TPU v7x, 32 devices: a whole 2x2x4 slice. The times are simulated.
32 devices in a mesh: dp: 8 (over z, y), region: 4 (over x, core).
Axes of the slice: x: 2, y: 2, z: 4, core: 2. Of those that a mesh axis runs over, the one named last changes fastest.
Arguments:
- travel_times: float32 [512, 128], P('dp'), may hold values from -60 to 60
- sensitivity: bfloat16 [512, 8, 128, 128], P('dp', 'region'), may hold values from -0.1875 to 0.1875
- tile_blocks: int32 [512, 8], P('dp', 'region'), may hold values from 0 to 1023
- face_blocks: int32 [1024, 2], P(('dp', 'region')), may hold values from 0 to 1023, as said below
- face_weights: float32 [1024, 128], P(('dp', 'region')), may hold values from 0.2 to 2
- face_count: int32 [32], P(('dp', 'region')), may hold values from 8 to 32, as said below
Outputs:
- solution: float32 [1024, 128], P('region')
Inputs may be any that keep to these rules, and one draw needn't show every extreme that they name: `face_blocks`: the first block of a face lies in the region of the device that holds the face, the second in that region or in the region one step up or down, the regions closing into a loop. `face_count`: entry k counts the faces in use among the 32 rows held by device k of dp+region; they are its first rows; some device holds 32.
All inputs are finite; a program needn't handle non-finite values.
Results may differ from a plain program's by a relative error of at most 0.0025.
The roundings to bfloat16 on the way count: a program that leaves them out, or rounds other values in their place, can miss the bound.
Values may be sent and summed in bfloat16 or wider, within the bound.
No kernel may reach another device: no remote copies, remote signals or barrier semaphores. Data moves between devices by JAX's collectives and lax.ppermute only.
A program may use at most 64 MiB of HBM per device.

v0:
```python
import jax
import jax.numpy as jnp
from jax import lax
from jax.sharding import PartitionSpec as P

ITERS = 2
NB_DEV = 256


smooth_weight = 1.0


def reduce_partials(partials):
    summed = lax.psum(partials, ("dp", "region"))
    return lax.dynamic_slice_in_dim(summed, lax.axis_index("region") * NB_DEV, NB_DEV, 0)


def piece_squares(piece):
    local_sq = jnp.sum(piece * piece)
    return lax.psum(local_sq, "region")


def model_field(piece):
    slab_half = piece.astype(jnp.bfloat16)
    return lax.all_gather(slab_half, "region", axis=0, tiled=True)


def left_squares(ray_sq, face_sq):
    return lax.psum(ray_sq, "dp") + lax.psum(face_sq, ("dp", "region"))


def local(travel_times, sensitivity, tile_blocks, face_blocks, face_weights, face_count):
    model_rows = NB_DEV * lax.axis_size("region")
    live_mask = (jnp.arange(face_blocks.shape[0]) < face_count[0]).astype(jnp.float32)
    face_scale = smooth_weight * face_weights * live_mask[:, None]
    first_block = face_blocks[:, 0]
    second_block = face_blocks[:, 1]
    flat_blocks = tile_blocks.reshape(-1)

    def transposed(left_rays, left_faces):
        rays_half = left_rays.astype(jnp.bfloat16)
        contrib = jnp.einsum(
            "tsrb,tr->tsb", sensitivity, rays_half, preferred_element_type=jnp.float32
        )
        contrib_rows = contrib.reshape(-1, contrib.shape[-1])
        face_term = face_scale * left_faces
        partials = jax.ops.segment_sum(contrib_rows, flat_blocks, num_segments=model_rows)
        partials = partials + jax.ops.segment_sum(face_term, first_block, num_segments=model_rows)
        partials = partials - jax.ops.segment_sum(face_term, second_block, num_segments=model_rows)
        return reduce_partials(partials)

    beta_value = jnp.sqrt(
        left_squares(jnp.sum(travel_times * travel_times), jnp.zeros((), jnp.float32))
    )
    left_rays = travel_times / beta_value
    left_faces = jnp.zeros(face_weights.shape, jnp.float32)
    right_vector = transposed(left_rays, left_faces)
    alpha_value = jnp.sqrt(piece_squares(right_vector))
    right_vector = right_vector / alpha_value
    direction = right_vector
    solution = jnp.zeros_like(right_vector)
    phi_bar = beta_value
    rho_bar = alpha_value
    for iteration in range(ITERS):
        full_model = model_field(right_vector)
        picked = full_model[tile_blocks]
        partial_value = jnp.einsum(
            "tsrb,tsb->tr", sensitivity, picked, preferred_element_type=jnp.float32
        )
        ray_pred = lax.psum(partial_value.astype(jnp.bfloat16), "region").astype(jnp.float32)
        face_pred = face_scale * (
            full_model[first_block].astype(jnp.float32)
            - full_model[second_block].astype(jnp.float32)
        )
        ray_pred, face_pred = (ray_pred, face_pred)
        left_rays = ray_pred - alpha_value * left_rays
        left_faces = face_pred - alpha_value * left_faces
        beta_value = jnp.sqrt(
            left_squares(jnp.sum(left_rays * left_rays), jnp.sum(left_faces * left_faces))
        )
        left_rays = left_rays / beta_value
        left_faces = left_faces / beta_value
        last_turn = iteration + 1 == ITERS
        if not last_turn:
            right_vector = transposed(left_rays, left_faces) - beta_value * right_vector
            alpha_new = jnp.sqrt(piece_squares(right_vector))
            right_vector = right_vector / alpha_new
        rho_value = jnp.sqrt(rho_bar * rho_bar + beta_value * beta_value)
        cosine = rho_bar / rho_value
        sine_value = beta_value / rho_value
        phi_value = cosine * phi_bar
        phi_bar = sine_value * phi_bar
        solution = solution + phi_value / rho_value * direction
        if not last_turn:
            rho_bar = -cosine * alpha_new
            direction = right_vector - sine_value * alpha_new / rho_value * direction
            alpha_value = alpha_new
    return solution


def solution(mesh):
    in_specs = (
        P("dp", None),
        P("dp", "region", None, None),
        P("dp", "region"),
        P(("dp", "region"), None),
        P(("dp", "region"), None),
        P(("dp", "region")),
    )
    out_specs = P("region", None)
    return jax.shard_map(local, mesh=mesh, in_specs=in_specs, out_specs=out_specs, check_vma=False)
```

profile of v0, /device:TPU:0, one launch (start us, length us, event | category | flops | bytes accessed | tf_op | source)
XLA Modules:
  0.0 538.3 jit_solution(2553015749312402894)
XLA Ops:
  6.5 0.8 fusion.24
  7.3 0.8 copy.9
  8.7 1.4 multiply_reduce_fusion.4
  10.1 0.1 broadcast_in_dim_reshape.4
  10.2 23.8 %psum.84 = f32[]{:T(128)} all-reduce(f32[]{:T(128)} %multiply_reduce_fusion.4), channel_id=1, replica_groups=mesh['dp'=8,'region'=4] {'dp'}, use_global_device_ids=true, to_apply=%region_1.0 | all-reduce | flops 1 | bytes 8 | tf_op jit(solution)/shard_map/psum | solution.py:29
  34.0 37.6 %psum.85 = f32[]{:T(128)} all-reduce(f32[]{:T(128)} %constant.5.clone.1), channel_id=1, replica_groups=mesh['dp'=8,'region'=4] {'dp','region'}, use_global_device_ids=true, to_apply=%region_2.0 | all-reduce | flops 1 | bytes 8 | tf_op jit(solution)/shard_map/psum | solution.py:29
  73.0 0.8 convert_bitcast_fusion.1
  73.7 0.8 multiply_multiply_fusion.1
  74.5 1.1 scatter_custom_fusion.1
  75.6 2.8 fusion.21
  78.5 1.3 scatter_custom_fusion
  79.7 0.9 sub.30
  80.7 0.1 copy.10
  80.8 0.1 reshape.15
  81.0 129.3 %all-reduce.3.cloned.1.call-done = f32[1024,128]{1,0:T(8,128)} async-done(((f32[1024,128]{1,0:T(8,128)}), f32[1024,128]{1,0:T(8,128)}) %all-reduce.3.cloned.1.call-update) | async-done | bytes 524304 | tf_op jit(solution)/shard_map/psum | solution.py:14
  210.2 1.5 multiply_reduce_fusion.1
  211.8 6.3 %psum.87 = f32[]{:T(128)} all-reduce(f32[]{:T(128)} %multiply_reduce_fusion.1), channel_id=1, replica_groups=mesh['dp'=8,'region'=4] {'region'}, use_global_device_ids=true, to_apply=%region_7.0 | all-reduce | flops 1 | bytes 8 | tf_op jit(solution)/shard_map/psum | solution.py:20
  218.8 0.9 fusion.26
  219.8 5.9 %all_gather.6 = bf16[1024,128]{1,0:T(8,128)(2,1)S(1)} all-gather(bf16[256,128]{1,0:T(8,128)(2,1)S(1)} %fusion.26), channel_id=1, replica_groups=mesh['dp'=8,'region'=4] {'region'}, dimensions={0}, use_global_device_ids=true | all-gather | bytes 327680 | tf_op jit(solution)/shard_map/all_gather | solution.py:25
  225.7 0.7 gather_fusion
  226.4 3.4 fusion.16
  229.8 11.6 %psum.88 = bf16[64,128]{1,0:T(8,128)(2,1)S(1)} all-reduce(bf16[64,128]{1,0:T(8,128)(2,1)S(1)} %convert_element_type.46), channel_id=1, replica_groups=mesh['dp'=8,'region'=4] {'region'}, use_global_device_ids=true, to_apply=%region_8.0 | all-reduce | flops 8192 | bytes 32768 | tf_op jit(solution)/shard_map/psum | solution.py:70
  241.4 0.6 multiply_reduce_fusion.3
  242.0 0.6 gather_fusion.2
  242.6 0.6 gather_fusion.1
  243.2 0.8 multiply_reduce_fusion.6
  244.0 19.8 %psum.89 = f32[]{:T(128)} all-reduce(f32[]{:T(128)} %multiply_reduce_fusion.3), channel_id=1, replica_groups=mesh['dp'=8,'region'=4] {'dp'}, use_global_device_ids=true, to_apply=%region_10.0 | all-reduce | flops 1 | bytes 8 | tf_op jit(solution)/shard_map/psum | solution.py:29
  263.8 37.1 %psum.90 = f32[]{:T(128)} all-reduce(f32[]{:T(128)} %multiply_reduce_fusion.6), channel_id=1, replica_groups=mesh['dp'=8,'region'=4] {'dp','region'}, use_global_device_ids=true, to_apply=%region_12.0 | all-reduce | flops 1 | bytes 8 | tf_op jit(solution)/shard_map/psum | solution.py:29
  302.2 0.1 multiply_multiply_fusion
  302.3 2.8 fusion.19
  305.2 0.8 scatter_custom_fusion.3
  306.0 1.3 scatter_custom_fusion.2
  307.3 0.9 sub.34
  308.3 129.4 %all-reduce.5.cloned.1.call-done = f32[1024,128]{1,0:T(8,128)} async-done(((f32[1024,128]{1,0:T(8,128)}), f32[1024,128]{1,0:T(8,128)}) %all-reduce.5.cloned.1.call-update) | async-done | bytes 524304 | tf_op jit(solution)/shard_map/psum | solution.py:14
  437.7 1.6 multiply_reduce_fusion
  439.3 6.4 %psum.92 = f32[]{:T(128)} all-reduce(f32[]{:T(128)} %multiply_reduce_fusion), channel_id=1, replica_groups=mesh['dp'=8,'region'=4] {'region'}, use_global_device_ids=true, to_apply=%region_17.0 | all-reduce | flops 1 | bytes 8 | tf_op jit(solution)/shard_map/psum | solution.py:20
  446.4 0.9 fusion.18
  447.3 5.9 %all_gather.7 = bf16[1024,128]{1,0:T(8,128)(2,1)S(1)} all-gather(bf16[256,128]{1,0:T(8,128)(2,1)S(1)} %fusion.18), channel_id=1, replica_groups=mesh['dp'=8,'region'=4] {'region'}, dimensions={0}, use_global_device_ids=true | all-gather | bytes 327680 | tf_op jit(solution)/shard_map/all_gather | solution.py:25
  453.2 0.7 gather_fusion.3
  453.9 0.6 gather_fusion.5
  454.5 0.6 gather_fusion.4
  455.2 3.4 fusion.14
  458.5 11.5 %psum.93 = bf16[64,128]{1,0:T(8,128)(2,1)S(1)} all-reduce(bf16[64,128]{1,0:T(8,128)(2,1)S(1)} %convert_element_type.52), channel_id=1, replica_groups=mesh['dp'=8,'region'=4] {'region'}, use_global_device_ids=true, to_apply=%region_18.0 | all-reduce | flops 8192 | bytes 32768 | tf_op jit(solution)/shard_map/psum | solution.py:70
  470.0 0.6 multiply_reduce_fusion.2
  470.6 19.8 %psum.94 = f32[]{:T(128)} all-reduce(f32[]{:T(128)} %multiply_reduce_fusion.2), channel_id=1, replica_groups=mesh['dp'=8,'region'=4] {'dp'}, use_global_device_ids=true, to_apply=%region_20.0 | all-reduce | flops 1 | bytes 8 | tf_op jit(solution)/shard_map/psum | solution.py:29
  490.5 0.8 multiply_reduce_fusion.5
  491.2 37.1 %psum.95 = f32[]{:T(128)} all-reduce(f32[]{:T(128)} %multiply_reduce_fusion.5), channel_id=1, replica_groups=mesh['dp'=8,'region'=4] {'dp','region'}, use_global_device_ids=true, to_apply=%region_22.0 | all-reduce | flops 1 | bytes 8 | tf_op jit(solution)/shard_map/psum | solution.py:29
  529.8 1.6 multiply_add_fusion
  (20 shorter events, 0.1 us)
Async XLA Ops:
  6.5 74.1 %copy-start.3 = (s32[64,2]{0,1:T(2,128)S(1)}, s32[64,2]{0,1:T(2,128)}, u32[]{:S(2)}) copy-start(s32[64,2]{0,1:T(2,128)} %param.8) | copy-start | bytes 1540
  6.5 203.7 %all-reduce.3.cloned.1.call-start = ((), (), s32[]{:S(2)}) async-start(), calls=%async_computation | async-start | bytes 1048576 | tf_op jit(solution)/shard_map/psum | solution.py:14
  78.5 162.9 %copy-start.1 = (f32[64,128]{1,0:T(8,128)S(1)}, f32[64,128]{1,0:T(8,128)}, u32[]{:S(2)}) copy-start(f32[64,128]{1,0:T(8,128)} %param.6) | copy-start | bytes 98308
  78.5 164.7 %copy-start.2 = (f32[32,128]{1,0:T(8,128)S(1)}, f32[32,128]{1,0:T(8,128)}, u32[]{:S(2)}) copy-start(f32[32,128]{1,0:T(8,128)} %param.10) | copy-start | bytes 49156
  80.6 357.1 %all-reduce.5.cloned.1.call-start = ((), (), s32[]{:S(2)}) async-start(), calls=%async_computation.1 | async-start | bytes 1048576 | tf_op jit(solution)/shard_map/psum | solution.py:14
  229.8 207.9 %copy-start = (f32[1024,128]{1,0:T(8,128)S(1)}, f32[1024,128]{1,0:T(8,128)}, u32[]{:S(2)}) copy-start(f32[1024,128]{1,0:T(8,128)} %all-reduce.3.cloned.1.call-done) | copy-start | bytes 1572868
Sparse Core Ops, SparseCore 0:
  80.7 129.4 all-reduce.2
  308.3 129.3 all-reduce.4
where the time goes:
time: 540 us; the launch traced here: 538 us
  waiting for transfers between devices  259 us (48%)
  blocking collectives  223 us (41%)
  between operations  20.1 us (4%)
  other arithmetic  19.3 us (4%)
  matrix products  12.4 us (2%)
    psum x2, waiting for transfers between devices, reduce_partials(): summed = lax.psum(partials, ('dp', 'region'))  259 us
    psum x6, blocking collectives, left_squares(): return lax.psum(ray_sq, 'dp') + lax.psum(face_sq, ('dp', 'region'))  175 us
    psum x2, blocking collectives, local(): lax.psum(partial_value.astype(jnp.bfloat16), 'region').astype(jnp.float32)  23.1 us
    psum x2, blocking collectives, piece_squares(): return lax.psum(local_sq, 'region')  12.7 us
    all_gather x2, blocking collectives, model_field(): return lax.all_gather(slab_half, 'region', axis=0, tiled=True)  11.9 us
  transfers between devices with their start and end apart: 2, of which 2 were waited for; matrix products, arithmetic and copies ran while one was open for 0% of the time, Pallas kernels for 0%

commit v1 on v0

v1 whole, which is shorter than its diff:
```python
import jax
import jax.numpy as jnp
from jax import lax
from jax.sharding import PartitionSpec as P

ITERS = 2
NB_DEV = 256


smooth_weight = 1.0


def butterfly_sum(x, axis):
    n = lax.axis_size(axis)
    if n & (n - 1):
        return lax.psum(x, axis)
    k = 1
    while k < n:
        x = x + lax.ppermute(x, axis, [(i, i ^ k) for i in range(n)])
        k *= 2
    return x


def halving_scatter(x, axis):
    n = lax.axis_size(axis)
    if n & (n - 1):
        summed = lax.psum(x, axis)
        rows = x.shape[0] // n
        return lax.dynamic_slice_in_dim(summed, lax.axis_index(axis) * rows, rows, 0)
    me = lax.axis_index(axis)
    k = n // 2
    while k >= 1:
        half = x.shape[0] // 2
        bit = (me // k) % 2
        keep = lax.dynamic_slice_in_dim(x, bit * half, half, 0)
        send = lax.dynamic_slice_in_dim(x, (1 - bit) * half, half, 0)
        x = keep + lax.ppermute(send, axis, [(i, i ^ k) for i in range(n)])
        k //= 2
    return x


def doubling_gather(x, axis):
    n = lax.axis_size(axis)
    if n & (n - 1):
        return lax.all_gather(x, axis, axis=0, tiled=True)
    me = lax.axis_index(axis)
    k = 1
    while k < n:
        other = lax.ppermute(x, axis, [(i, i ^ k) for i in range(n)])
        upper = (me // k) % 2 == 1
        x = jnp.where(upper, jnp.concatenate([other, x], 0), jnp.concatenate([x, other], 0))
        k *= 2
    return x


def local(travel_times, sensitivity, tile_blocks, face_blocks, face_weights, face_count):
    model_rows = NB_DEV * lax.axis_size("region")
    region = lax.axis_index("region")
    live_mask = (jnp.arange(face_blocks.shape[0]) < face_count[0]).astype(jnp.float32)
    face_scale = smooth_weight * face_weights * live_mask[:, None]
    first_block = face_blocks[:, 0]
    second_block = face_blocks[:, 1]
    flat_blocks = tile_blocks.reshape(-1)
    n_tiles = travel_times.shape[0]

    def transposed_part(left_rays, left_faces):
        rays_half = left_rays.astype(jnp.bfloat16)
        contrib = jnp.einsum(
            "tsrb,tr->tsb", sensitivity, rays_half, preferred_element_type=jnp.float32
        )
        contrib_rows = contrib.reshape(-1, contrib.shape[-1])
        face_term = face_scale * left_faces
        partials = jax.ops.segment_sum(contrib_rows, flat_blocks, num_segments=model_rows)
        partials = partials + jax.ops.segment_sum(face_term, first_block, num_segments=model_rows)
        partials = partials - jax.ops.segment_sum(face_term, second_block, num_segments=model_rows)
        piece = halving_scatter(partials, "region")
        return butterfly_sum(piece, "dp")

    def normalized_field(piece):
        field = doubling_gather(piece, "region")
        alpha = jnp.sqrt(jnp.sum(field * field))
        field = field / alpha
        return field, lax.dynamic_slice_in_dim(field, region * NB_DEV, NB_DEV, 0), alpha

    beta_value = jnp.sqrt(butterfly_sum(jnp.sum(travel_times * travel_times), "dp"))
    left_rays = travel_times / beta_value
    left_faces = jnp.zeros(face_weights.shape, jnp.float32)
    raw = transposed_part(left_rays, left_faces)
    full_model, right_vector, alpha_value = normalized_field(raw)
    direction = right_vector
    solution = jnp.zeros_like(right_vector)
    phi_bar = beta_value
    rho_bar = alpha_value
    for iteration in range(ITERS):
        full_half = full_model.astype(jnp.bfloat16)
        picked = full_half[tile_blocks]
        partial_value = jnp.einsum(
            "tsrb,tsb->tr", sensitivity, picked, preferred_element_type=jnp.float32
        )
        face_pred = face_scale * (
            full_half[first_block].astype(jnp.float32)
            - full_half[second_block].astype(jnp.float32)
        )
        left_faces = face_pred - alpha_value * left_faces
        face_sq = jnp.sum(left_faces * left_faces)
        packed = jnp.concatenate(
            [partial_value, jnp.broadcast_to(face_sq, (8, partial_value.shape[1]))], 0
        )
        packed = butterfly_sum(packed, "region")
        ray_pred = packed[:n_tiles]
        left_rays = ray_pred - alpha_value * left_rays
        beta_sq = butterfly_sum(jnp.sum(left_rays * left_rays) + packed[n_tiles, 0], "dp")
        beta_value = jnp.sqrt(beta_sq)
        left_rays = left_rays / beta_value
        left_faces = left_faces / beta_value
        last_turn = iteration + 1 == ITERS
        if not last_turn:
            raw = transposed_part(left_rays, left_faces) - beta_value * right_vector
            full_model, right_vector, alpha_new = normalized_field(raw)
        rho_value = jnp.sqrt(rho_bar * rho_bar + beta_value * beta_value)
        cosine = rho_bar / rho_value
        sine_value = beta_value / rho_value
        phi_value = cosine * phi_bar
        phi_bar = sine_value * phi_bar
        solution = solution + phi_value / rho_value * direction
        if not last_turn:
            rho_bar = -cosine * alpha_new
            direction = right_vector - sine_value * alpha_new / rho_value * direction
            alpha_value = alpha_new
    return solution


def solution(mesh):
    in_specs = (
        P("dp", None),
        P("dp", "region", None, None),
        P("dp", "region"),
        P(("dp", "region"), None),
        P(("dp", "region"), None),
        P(("dp", "region")),
    )
    out_specs = P("region", None)
    return jax.shard_map(local, mesh=mesh, in_specs=in_specs, out_specs=out_specs, check_vma=False)
```

time: 540 us -> 163 us (0.30)
  blocking collectives: 223 us -> 0 us
  waiting for transfers between devices: 259 us -> 73.6 us
  starting transfers between devices: 0.04 us -> 42 us
  between operations: 20.1 us -> 11.8 us
    psum x2 -> x0, waiting for transfers between devices: 259 us -> none  [reduce_partials(): summed = lax.psum(partials, ('dp', 'region'))]
    psum x10 -> x0, blocking collectives: 211 us -> none  [the longest x6 175 us: left_squares(): return lax.psum(ray_sq, 'dp') + lax.psum(face_sq, ('dp', 'region'))]
    ppermute x0 -> x27, waiting for transfers between devices: none -> 73.6 us  [the longest x19 45 us: butterfly_sum(): x = x + lax.ppermute(x, axis, [(i, i ^ k) for i in range(n)])]
    ppermute x0 -> x27, starting transfers between devices: none -> 42 us  [the longest x19 35.5 us: butterfly_sum(): x = x + lax.ppermute(x, axis, [(i, i ^ k) for i in range(n)])]
    all_gather x2 -> x0, blocking collectives: 11.9 us -> none  [model_field(): return lax.all_gather(slab_half, 'region', axis=0, tiled=True)]
  transfers between devices with their start and end apart: 2 -> 27, of which waited for: 2 -> 26; matrix products, arithmetic and copies ran while one was open for 0% -> 2% of each run, Pallas kernels for 0% -> 0%
where the time goes in v1:
time: 163 us; the launch traced here: 162 us
  waiting for transfers between devices  73.6 us (45%)
  starting transfers between devices  42 us (26%)
  other arithmetic  14.9 us (9%)
  matrix products  12.4 us (8%)
  between operations  11.8 us (7%)
  local copies, waits for them, and re-layouts  7.5 us (5%)
    ppermute x19, waiting for transfers between devices, butterfly_sum(): x = x + lax.ppermute(x, axis, [(i, i ^ k) for i in range(n)])  45 us
    ppermute x19, starting transfers between devices, butterfly_sum(): x = x + lax.ppermute(x, axis, [(i, i ^ k) for i in range(n)])  35.5 us
    ppermute x4, waiting for transfers between devices, doubling_gather(): other = lax.ppermute(x, axis, [(i, i ^ k) for i in range(n)])  16.1 us
    ppermute x4, waiting for transfers between devices, halving_scatter(): x = keep + lax.ppermute(send, axis, [(i, i ^ k) for i in range(n)])  12.4 us
    dot_general x2, matrix products, local(): jnp.einsum('tsrb,tsb->tr', sensitivity, picked, preferred_element_type=jn...  6.73 us
    dot_general x2, matrix products, transposed_part(): jnp.einsum('tsrb,tr->tsb', sensitivity, rays_half, preferred_element_type...  5.69 us
  transfers between devices with their start and end apart: 27, of which 26 were waited for; matrix products, arithmetic and copies ran while one was open for 2% of the time, Pallas kernels for 0%

profile of v1, /device:TPU:0, one launch (start us, length us, event | category | flops | bytes accessed | tf_op | source)
XLA Modules:
  0.0 162.1 jit_solution(18220338800903717780)
XLA Ops:
  0.0 1.4 multiply_reduce_fusion.3
  1.4 3.0 %collective-permute-start = (f32[]{:T(128)}, f32[]{:T(128)}, u32[]{:S(2)}, u32[]{:S(2)}) collective-permute-start(f32[]{:T(128)} %multiply_reduce_fusion.3), channel_id=1, source_target_pairs={{0,4},{4,0},{8,12},{12,8},{16,20},{20,16},{24,28},{28,24},{1,5},{5... | collective-permute-start | bytes 20 | tf_op jit(solution)/shard_map/ppermute | solution.py:19
  9.9 2.9 %collective-permute-start.1 = (f32[]{:T(128)}, f32[]{:T(128)}, u32[]{:S(2)}, u32[]{:S(2)}) collective-permute-start(f32[]{:T(128)} %add.163), channel_id=1, source_target_pairs={{0,8},{4,12},{8,0},{12,4},{16,24},{20,28},{24,16},{28,20},{1,9},{5... | collective-permute-start | bytes 20 | tf_op jit(solution)/shard_map/ppermute | solution.py:19
  14.1 4.0 %collective-permute-start.2 = (f32[]{:T(128)}, f32[]{:T(128)}, u32[]{:S(2)}, u32[]{:S(2)}) collective-permute-start(f32[]{:T(128)} %add.164), channel_id=1, source_target_pairs={{0,16},{4,20},{8,24},{12,28},{16,0},{20,4},{24,8},{28,12},{1,17},{... | collective-permute-start | bytes 20 | tf_op jit(solution)/shard_map/ppermute | solution.py:19
  20.0 2.9 %fusion.24 = f32[64,1,2,128]{3,1,2,0:T(1,128)S(1)} fusion(bf16[64,2,128,128]{3,2,1,0:T(8,128)(2,1)} %param.7, bf16[64,128,1,1]{1,0,2,3:T(8,128)(2,1)S(1)} %convert_bitcast_fusion.1), kind=kOutput, calls=%fused_computation.48 | convolution fusion | flops 4194304 | bytes 4276224 | tf_op jit(solution)/shard_map/tsrb,tr->tsb/dot_general | solution.py:68
  22.9 1.3 scatter_custom_fusion
  24.2 1.6 collective-permute-start.3
  25.8 4.9 %collective-permute-done.3 = f32[512,128]{1,0:T(8,128)S(1)} collective-permute-done((f32[512,128]{1,0:T(8,128)S(1)}, f32[512,128]{1,0:T(8,128)S(1)}, u32[]{:S(2)}, u32[]{:S(2)}) %collective-permute-start.3) | collective-permute-done | bytes 262176 | tf_op jit(solution)/shard_map/ppermute | solution.py:37
  30.8 1.3 collective-permute-done.4
  32.4 5.4 %collective-permute-done.5 = f32[256,128]{1,0:T(8,128)S(1)} collective-permute-done((f32[256,128]{1,0:T(8,128)S(1)}, f32[256,128]{1,0:T(8,128)S(1)}, u32[]{:S(2)}, u32[]{:S(2)}) %collective-permute-start.5) | collective-permute-done | bytes 131104 | tf_op jit(solution)/shard_map/ppermute | solution.py:19
  37.8 1.6 %collective-permute-start.6 = (f32[256,128]{1,0:T(8,128)S(1)}, f32[256,128]{1,0:T(8,128)S(1)}, u32[]{:S(2)}, u32[]{:S(2)}) collective-permute-start(f32[256,128]{1,0:T(8,128)S(1)} %add.173), channel_id=1, source_target_pairs={{0,8},{4,12},{8,0},{12,4},{16,24},{20,28},{24,16},{28,20},{1,9},{5... | collective-permute-start | bytes 393224 | tf_op jit(solution)/shard_map/ppermute | solution.py:19
  39.5 3.4 %collective-permute-done.6 = f32[256,128]{1,0:T(8,128)S(1)} collective-permute-done((f32[256,128]{1,0:T(8,128)S(1)}, f32[256,128]{1,0:T(8,128)S(1)}, u32[]{:S(2)}, u32[]{:S(2)}) %collective-permute-start.6) | collective-permute-done | bytes 131104 | tf_op jit(solution)/shard_map/ppermute | solution.py:19
  42.9 2.7 %collective-permute-start.7 = (f32[256,128]{1,0:T(8,128)S(1)}, f32[256,128]{1,0:T(8,128)S(1)}, u32[]{:S(2)}, u32[]{:S(2)}) collective-permute-start(f32[256,128]{1,0:T(8,128)S(1)} %add.174), channel_id=1, source_target_pairs={{0,16},{4,20},{8,24},{12,28},{16,0},{20,4},{24,8},{28,12},{1,17},{... | collective-permute-start | bytes 393224 | tf_op jit(solution)/shard_map/ppermute | solution.py:19
  45.5 4.7 %collective-permute-done.7 = f32[256,128]{1,0:T(8,128)S(1)} collective-permute-done((f32[256,128]{1,0:T(8,128)S(1)}, f32[256,128]{1,0:T(8,128)S(1)}, u32[]{:S(2)}, u32[]{:S(2)}) %collective-permute-start.7) | collective-permute-done | bytes 131104 | tf_op jit(solution)/shard_map/ppermute | solution.py:19
  50.3 1.3 collective-permute-done.8
  51.7 1.6 collective-permute-start.9
  53.5 6.6 %collective-permute-done.9 = f32[512,128]{1,0:T(8,128)S(1)} collective-permute-done((f32[512,128]{1,0:T(8,128)S(1)}, f32[512,128]{1,0:T(8,128)S(1)}, u32[]{:S(2)}, u32[]{:S(2)}) %collective-permute-start.9) | collective-permute-done | bytes 262176 | tf_op jit(solution)/shard_map/ppermute | solution.py:49
  62.3 3.4 %fusion.18 = f32[64,1,128,1]{2,1,3,0:T(1,128)S(1)} fusion(bf16[64,2,128,128]{3,2,1,0:T(8,128)(2,1)} %param.7, bf16[64,2,128,1]{2,1,0,3:T(2,128)(2,1)S(1)} %bitcast.40), kind=kOutput, calls=%fused_computation.40 | convolution fusion | flops 4194304 | bytes 4259840 | tf_op jit(solution)/shard_map/tsrb,tsb->tr/dot_general | solution.py:97
  68.3 1.2 collective-permute-done.10
  70.2 1.6 collective-permute-start.11
  71.7 2.5 %collective-permute-done.11 = f32[72,128]{1,0:T(8,128)S(1)} collective-permute-done((f32[72,128]{1,0:T(8,128)S(1)}, f32[72,128]{1,0:T(8,128)S(1)}, u32[]{:S(2)}, u32[]{:S(2)}) %collective-permute-start.11) | collective-permute-done | bytes 36896 | tf_op jit(solution)/shard_map/ppermute | solution.py:19
  76.7 1.8 %collective-permute-start.12 = (f32[]{:T(128)}, f32[]{:T(128)}, u32[]{:S(2)}, u32[]{:S(2)}) collective-permute-start(f32[]{:T(128)} %add.181), channel_id=1, source_target_pairs={{0,4},{4,0},{8,12},{12,8},{16,20},{20,16},{24,28},{28,24},{1,5},{5... | collective-permute-start | bytes 20 | tf_op jit(solution)/shard_map/ppermute | solution.py:19
  78.5 1.7 %collective-permute-done.12 = f32[]{:T(128)} collective-permute-done((f32[]{:T(128)}, f32[]{:T(128)}, u32[]{:S(2)}, u32[]{:S(2)}) %collective-permute-start.12) | collective-permute-done | bytes 36 | tf_op jit(solution)/shard_map/ppermute | solution.py:19
  80.9 2.0 %collective-permute-start.13 = (f32[]{:T(128)}, f32[]{:T(128)}, u32[]{:S(2)}, u32[]{:S(2)}) collective-permute-start(f32[]{:T(128)} %add.182), channel_id=1, source_target_pairs={{0,8},{4,12},{8,0},{12,4},{16,24},{20,28},{24,16},{28,20},{1,9},{5... | collective-permute-start | bytes 20 | tf_op jit(solution)/shard_map/ppermute | solution.py:19
  82.9 1.5 collective-permute-done.13
  85.1 3.4 %collective-permute-start.14 = (f32[]{:T(128)}, f32[]{:T(128)}, u32[]{:S(2)}, u32[]{:S(2)}) collective-permute-start(f32[]{:T(128)} %add.183), channel_id=1, source_target_pairs={{0,16},{4,20},{8,24},{12,28},{16,0},{20,4},{24,8},{28,12},{1,17},{... | collective-permute-start | bytes 20 | tf_op jit(solution)/shard_map/ppermute | solution.py:19
  90.3 2.8 %fusion.22 = f32[64,1,2,128]{3,1,2,0:T(1,128)S(1)} fusion(bf16[64,2,128,128]{3,2,1,0:T(8,128)(2,1)} %param.7, bf16[64,128,1,1]{1,0,2,3:T(8,128)(2,1)S(1)} %convert_bitcast_fusion), kind=kOutput, calls=%fused_computation.46 | convolution fusion | flops 4194304 | bytes 4276224 | tf_op jit(solution)/shard_map/tsrb,tr->tsb/dot_general | solution.py:68
  94.0 1.3 scatter_custom_fusion.2
  95.4 1.6 collective-permute-start.15
  96.9 4.9 %collective-permute-done.15 = f32[512,128]{1,0:T(8,128)S(1)} collective-permute-done((f32[512,128]{1,0:T(8,128)S(1)}, f32[512,128]{1,0:T(8,128)S(1)}, u32[]{:S(2)}, u32[]{:S(2)}) %collective-permute-start.15) | collective-permute-done | bytes 262176 | tf_op jit(solution)/shard_map/ppermute | solution.py:37
  101.9 1.3 collective-permute-done.16
  103.8 5.1 %collective-permute-done.17 = f32[256,128]{1,0:T(8,128)S(1)} collective-permute-done((f32[256,128]{1,0:T(8,128)S(1)}, f32[256,128]{1,0:T(8,128)S(1)}, u32[]{:S(2)}, u32[]{:S(2)}) %collective-permute-start.17) | collective-permute-done | bytes 131104 | tf_op jit(solution)/shard_map/ppermute | solution.py:19
  108.9 1.2 collective-permute-start.18
  110.1 3.8 %collective-permute-done.18 = f32[256,128]{1,0:T(8,128)S(1)} collective-permute-done((f32[256,128]{1,0:T(8,128)S(1)}, f32[256,128]{1,0:T(8,128)S(1)}, u32[]{:S(2)}, u32[]{:S(2)}) %collective-permute-start.18) | collective-permute-done | bytes 131104 | tf_op jit(solution)/shard_map/ppermute | solution.py:19
  114.0 2.1 %collective-permute-start.19 = (f32[256,128]{1,0:T(8,128)S(1)}, f32[256,128]{1,0:T(8,128)S(1)}, u32[]{:S(2)}, u32[]{:S(2)}) collective-permute-start(f32[256,128]{1,0:T(8,128)S(1)} %add.191), channel_id=1, source_target_pairs={{0,16},{4,20},{8,24},{12,28},{16,0},{20,4},{24,8},{28,12},{1,17},{... | collective-permute-start | bytes 393224 | tf_op jit(solution)/shard_map/ppermute | solution.py:19
  116.1 5.2 %collective-permute-done.19 = f32[256,128]{1,0:T(8,128)S(1)} collective-permute-done((f32[256,128]{1,0:T(8,128)S(1)}, f32[256,128]{1,0:T(8,128)S(1)}, u32[]{:S(2)}, u32[]{:S(2)}) %collective-permute-start.19) | collective-permute-done | bytes 131104 | tf_op jit(solution)/shard_map/ppermute | solution.py:19
  121.4 1.3 collective-permute-done.20
  122.8 1.6 collective-permute-start.21
  124.3 6.9 %collective-permute-done.21 = f32[512,128]{1,0:T(8,128)S(1)} collective-permute-done((f32[512,128]{1,0:T(8,128)S(1)}, f32[512,128]{1,0:T(8,128)S(1)}, u32[]{:S(2)}, u32[]{:S(2)}) %collective-permute-start.21) | collective-permute-done | bytes 262176 | tf_op jit(solution)/shard_map/ppermute | solution.py:49
  134.6 3.4 %fusion.16 = f32[64,1,128,1]{2,1,3,0:T(1,128)S(1)} fusion(bf16[64,2,128,128]{3,2,1,0:T(8,128)(2,1)} %param.7, bf16[64,2,128,1]{2,1,0,3:T(2,128)(2,1)S(1)} %bitcast.39), kind=kOutput, calls=%fused_computation.38 | convolution fusion | flops 4194304 | bytes 4259840 | tf_op jit(solution)/shard_map/tsrb,tsb->tr/dot_general | solution.py:97
  141.3 1.6 collective-permute-start.23
  143.1 2.2 %collective-permute-done.23 = f32[72,128]{1,0:T(8,128)S(1)} collective-permute-done((f32[72,128]{1,0:T(8,128)S(1)}, f32[72,128]{1,0:T(8,128)S(1)}, u32[]{:S(2)}, u32[]{:S(2)}) %collective-permute-start.23) | collective-permute-done | bytes 36896 | tf_op jit(solution)/shard_map/ppermute | solution.py:19
  147.8 1.8 %collective-permute-start.24 = (f32[]{:T(128)}, f32[]{:T(128)}, u32[]{:S(2)}, u32[]{:S(2)}) collective-permute-start(f32[]{:T(128)} %add.195), channel_id=1, source_target_pairs={{0,4},{4,0},{8,12},{12,8},{16,20},{20,16},{24,28},{28,24},{1,5},{5... | collective-permute-start | bytes 20 | tf_op jit(solution)/shard_map/ppermute | solution.py:19
  149.6 1.7 %collective-permute-done.24 = f32[]{:T(128)} collective-permute-done((f32[]{:T(128)}, f32[]{:T(128)}, u32[]{:S(2)}, u32[]{:S(2)}) %collective-permute-start.24) | collective-permute-done | bytes 36 | tf_op jit(solution)/shard_map/ppermute | solution.py:19
  152.0 1.8 %collective-permute-start.25 = (f32[]{:T(128)}, f32[]{:T(128)}, u32[]{:S(2)}, u32[]{:S(2)}) collective-permute-start(f32[]{:T(128)} %add.196), channel_id=1, source_target_pairs={{0,8},{4,12},{8,0},{12,4},{16,24},{20,28},{24,16},{28,20},{1,9},{5... | collective-permute-start | bytes 20 | tf_op jit(solution)/shard_map/ppermute | solution.py:19
  153.7 1.8 %collective-permute-done.25 = f32[]{:T(128)} collective-permute-done((f32[]{:T(128)}, f32[]{:T(128)}, u32[]{:S(2)}, u32[]{:S(2)}) %collective-permute-start.25) | collective-permute-done | bytes 36 | tf_op jit(solution)/shard_map/ppermute | solution.py:19
  156.2 3.1 %collective-permute-start.26 = (f32[]{:T(128)}, f32[]{:T(128)}, u32[]{:S(2)}, u32[]{:S(2)}) collective-permute-start(f32[]{:T(128)} %add.197), channel_id=1, source_target_pairs={{0,16},{4,20},{8,24},{12,28},{16,0},{20,4},{24,8},{28,12},{1,17},{... | collective-permute-start | bytes 20 | tf_op jit(solution)/shard_map/ppermute | solution.py:19
  159.3 1.3 collective-permute-done.26
  (76 shorter events, 23.0 us)
Async XLA Ops:
  1.4 7.2 %collective-permute-start = (f32[]{:T(128)}, f32[]{:T(128)}, u32[]{:S(2)}, u32[]{:S(2)}) collective-permute-start(f32[]{:T(128)} %multiply_reduce_fusion.3), channel_id=1, source_target_pairs={{0,4},{4,0},{8,12},{12,8},{16,20},{20,16},{24,28},{28,24},{1,5},{5... | collective-permute-start | bytes 20 | tf_op jit(solution)/shard_map/ppermute | solution.py:19
  9.9 3.6 %collective-permute-start.1 = (f32[]{:T(128)}, f32[]{:T(128)}, u32[]{:S(2)}, u32[]{:S(2)}) collective-permute-start(f32[]{:T(128)} %add.163), channel_id=1, source_target_pairs={{0,8},{4,12},{8,0},{12,4},{16,24},{20,28},{24,16},{28,20},{1,9},{5... | collective-permute-start | bytes 20 | tf_op jit(solution)/shard_map/ppermute | solution.py:19
  14.1 4.5 %collective-permute-start.2 = (f32[]{:T(128)}, f32[]{:T(128)}, u32[]{:S(2)}, u32[]{:S(2)}) collective-permute-start(f32[]{:T(128)} %add.164), channel_id=1, source_target_pairs={{0,16},{4,20},{8,24},{12,28},{16,0},{20,4},{24,8},{28,12},{1,17},{... | collective-permute-start | bytes 20 | tf_op jit(solution)/shard_map/ppermute | solution.py:19
  20.0 33.2 %copy-start.2 = (s32[64,2]{0,1:T(2,128)S(1)}, s32[64,2]{0,1:T(2,128)}, u32[]{:S(2)}) copy-start(s32[64,2]{0,1:T(2,128)} %param.8) | copy-start | bytes 1540
  24.2 6.4 %collective-permute-start.3 = (f32[512,128]{1,0:T(8,128)S(1)}, f32[512,128]{1,0:T(8,128)S(1)}, u32[]{:S(2)}, u32[]{:S(2)}) collective-permute-start(f32[512,128]{1,0:T(8,128)S(1)} %constant_dynamic-slice_fusion.3), channel_id=1, source_target_pairs={{0,2},{1,3},{2,0},{3,1},{4,6},{5,7},{6,4},{7,5},{8,10},{9,11},{10,... | collective-permute-start | bytes 786440 | tf_op jit(solution)/shard_map/ppermute | solution.py:37
  30.7 1.4 collective-permute-start.4
  32.1 34.8 %copy-start = (f32[32,128]{1,0:T(8,128)S(1)}, f32[32,128]{1,0:T(8,128)}, u32[]{:S(2)}) copy-start(f32[32,128]{1,0:T(8,128)} %param.10) | copy-start | bytes 49156
  32.2 5.6 %collective-permute-start.5 = (f32[256,128]{1,0:T(8,128)S(1)}, f32[256,128]{1,0:T(8,128)S(1)}, u32[]{:S(2)}, u32[]{:S(2)}) collective-permute-start(f32[256,128]{1,0:T(8,128)S(1)} %dynamic-slice_add_fusion.3), channel_id=1, source_target_pairs={{0,4},{4,0},{8,12},{12,8},{16,20},{20,16},{24,28},{28,24},{1,5},{5... | collective-permute-start | bytes 393224 | tf_op jit(solution)/shard_map/ppermute | solution.py:19
  37.8 36.4 %copy-start.1 = (f32[64,128]{1,0:T(8,128)S(1)}, f32[64,128]{1,0:T(8,128)}, u32[]{:S(2)}) copy-start(f32[64,128]{1,0:T(8,128)} %param.6) | copy-start | bytes 98308
  37.8 5.0 %collective-permute-start.6 = (f32[256,128]{1,0:T(8,128)S(1)}, f32[256,128]{1,0:T(8,128)S(1)}, u32[]{:S(2)}, u32[]{:S(2)}) collective-permute-start(f32[256,128]{1,0:T(8,128)S(1)} %add.173), channel_id=1, source_target_pairs={{0,8},{4,12},{8,0},{12,4},{16,24},{20,28},{24,16},{28,20},{1,9},{5... | collective-permute-start | bytes 393224 | tf_op jit(solution)/shard_map/ppermute | solution.py:19
  42.9 7.3 %collective-permute-start.7 = (f32[256,128]{1,0:T(8,128)S(1)}, f32[256,128]{1,0:T(8,128)S(1)}, u32[]{:S(2)}, u32[]{:S(2)}) collective-permute-start(f32[256,128]{1,0:T(8,128)S(1)} %add.174), channel_id=1, source_target_pairs={{0,16},{4,20},{8,24},{12,28},{16,0},{20,4},{24,8},{28,12},{1,17},{... | collective-permute-start | bytes 393224 | tf_op jit(solution)/shard_map/ppermute | solution.py:19
  50.2 1.4 collective-permute-start.8
  51.7 8.4 %collective-permute-start.9 = (f32[512,128]{1,0:T(8,128)S(1)}, f32[512,128]{1,0:T(8,128)S(1)}, u32[]{:S(2)}, u32[]{:S(2)}) collective-permute-start(f32[512,128]{1,0:T(8,128)S(1)} %maximum_select_fusion.2), channel_id=1, source_target_pairs={{0,2},{1,3},{2,0},{3,1},{4,6},{5,7},{6,4},{7,5},{8,10},{9,11},{10,... | collective-permute-start | bytes 786440 | tf_op jit(solution)/shard_map/ppermute | solution.py:49
  68.2 1.3 collective-permute-start.10
  70.2 4.0 %collective-permute-start.11 = (f32[72,128]{1,0:T(8,128)S(1)}, f32[72,128]{1,0:T(8,128)S(1)}, u32[]{:S(2)}, u32[]{:S(2)}) collective-permute-start(f32[72,128]{1,0:T(8,128)S(1)} %pad_add_fusion.2), channel_id=1, source_target_pairs={{0,2},{1,3},{2,0},{3,1},{4,6},{5,7},{6,4},{7,5},{8,10},{9,11},{10,... | collective-permute-start | bytes 110600 | tf_op jit(solution)/shard_map/ppermute | solution.py:19
  76.7 3.6 %collective-permute-start.12 = (f32[]{:T(128)}, f32[]{:T(128)}, u32[]{:S(2)}, u32[]{:S(2)}) collective-permute-start(f32[]{:T(128)} %add.181), channel_id=1, source_target_pairs={{0,4},{4,0},{8,12},{12,8},{16,20},{20,16},{24,28},{28,24},{1,5},{5... | collective-permute-start | bytes 20 | tf_op jit(solution)/shard_map/ppermute | solution.py:19
  80.9 3.6 %collective-permute-start.13 = (f32[]{:T(128)}, f32[]{:T(128)}, u32[]{:S(2)}, u32[]{:S(2)}) collective-permute-start(f32[]{:T(128)} %add.182), channel_id=1, source_target_pairs={{0,8},{4,12},{8,0},{12,4},{16,24},{20,28},{24,16},{28,20},{1,9},{5... | collective-permute-start | bytes 20 | tf_op jit(solution)/shard_map/ppermute | solution.py:19
  85.1 4.5 %collective-permute-start.14 = (f32[]{:T(128)}, f32[]{:T(128)}, u32[]{:S(2)}, u32[]{:S(2)}) collective-permute-start(f32[]{:T(128)} %add.183), channel_id=1, source_target_pairs={{0,16},{4,20},{8,24},{12,28},{16,0},{20,4},{24,8},{28,12},{1,17},{... | collective-permute-start | bytes 20 | tf_op jit(solution)/shard_map/ppermute | solution.py:19
  95.4 6.4 %collective-permute-start.15 = (f32[512,128]{1,0:T(8,128)S(1)}, f32[512,128]{1,0:T(8,128)S(1)}, u32[]{:S(2)}, u32[]{:S(2)}) collective-permute-start(f32[512,128]{1,0:T(8,128)S(1)} %constant_dynamic-slice_fusion.1), channel_id=1, source_target_pairs={{0,2},{1,3},{2,0},{3,1},{4,6},{5,7},{6,4},{7,5},{8,10},{9,11},{10,... | collective-permute-start | bytes 786440 | tf_op jit(solution)/shard_map/ppermute | solution.py:37
  101.8 1.4 collective-permute-start.16
  103.3 5.6 %collective-permute-start.17 = (f32[256,128]{1,0:T(8,128)S(1)}, f32[256,128]{1,0:T(8,128)S(1)}, u32[]{:S(2)}, u32[]{:S(2)}) collective-permute-start(f32[256,128]{1,0:T(8,128)S(1)} %dynamic-slice_add_fusion.2), channel_id=1, source_target_pairs={{0,4},{4,0},{8,12},{12,8},{16,20},{20,16},{24,28},{28,24},{1,5},{5... | collective-permute-start | bytes 393224 | tf_op jit(solution)/shard_map/ppermute | solution.py:19
  108.9 5.0 %collective-permute-start.18 = (f32[256,128]{1,0:T(8,128)S(1)}, f32[256,128]{1,0:T(8,128)S(1)}, u32[]{:S(2)}, u32[]{:S(2)}) collective-permute-start(f32[256,128]{1,0:T(8,128)S(1)} %add.190), channel_id=1, source_target_pairs={{0,8},{4,12},{8,0},{12,4},{16,24},{20,28},{24,16},{28,20},{1,9},{5... | collective-permute-start | bytes 393224 | tf_op jit(solution)/shard_map/ppermute | solution.py:19
  114.0 7.3 %collective-permute-start.19 = (f32[256,128]{1,0:T(8,128)S(1)}, f32[256,128]{1,0:T(8,128)S(1)}, u32[]{:S(2)}, u32[]{:S(2)}) collective-permute-start(f32[256,128]{1,0:T(8,128)S(1)} %add.191), channel_id=1, source_target_pairs={{0,16},{4,20},{8,24},{12,28},{16,0},{20,4},{24,8},{28,12},{1,17},{... | collective-permute-start | bytes 393224 | tf_op jit(solution)/shard_map/ppermute | solution.py:19
  121.3 1.4 collective-permute-start.20
  122.8 8.4 %collective-permute-start.21 = (f32[512,128]{1,0:T(8,128)S(1)}, f32[512,128]{1,0:T(8,128)S(1)}, u32[]{:S(2)}, u32[]{:S(2)}) collective-permute-start(f32[512,128]{1,0:T(8,128)S(1)} %maximum_select_fusion.3), channel_id=1, source_target_pairs={{0,2},{1,3},{2,0},{3,1},{4,6},{5,7},{6,4},{7,5},{8,10},{9,11},{10,... | collective-permute-start | bytes 786440 | tf_op jit(solution)/shard_map/ppermute | solution.py:49
  139.3 1.3 collective-permute-start.22
  141.3 4.0 %collective-permute-start.23 = (f32[72,128]{1,0:T(8,128)S(1)}, f32[72,128]{1,0:T(8,128)S(1)}, u32[]{:S(2)}, u32[]{:S(2)}) collective-permute-start(f32[72,128]{1,0:T(8,128)S(1)} %pad_add_fusion.1), channel_id=1, source_target_pairs={{0,2},{1,3},{2,0},{3,1},{4,6},{5,7},{6,4},{7,5},{8,10},{9,11},{10,... | collective-permute-start | bytes 110600 | tf_op jit(solution)/shard_map/ppermute | solution.py:19
  147.8 3.6 %collective-permute-start.24 = (f32[]{:T(128)}, f32[]{:T(128)}, u32[]{:S(2)}, u32[]{:S(2)}) collective-permute-start(f32[]{:T(128)} %add.195), channel_id=1, source_target_pairs={{0,4},{4,0},{8,12},{12,8},{16,20},{20,16},{24,28},{28,24},{1,5},{5... | collective-permute-start | bytes 20 | tf_op jit(solution)/shard_map/ppermute | solution.py:19
  152.0 3.6 %collective-permute-start.25 = (f32[]{:T(128)}, f32[]{:T(128)}, u32[]{:S(2)}, u32[]{:S(2)}) collective-permute-start(f32[]{:T(128)} %add.196), channel_id=1, source_target_pairs={{0,8},{4,12},{8,0},{12,4},{16,24},{20,28},{24,16},{28,20},{1,9},{5... | collective-permute-start | bytes 20 | tf_op jit(solution)/shard_map/ppermute | solution.py:19
  156.2 4.5 %collective-permute-start.26 = (f32[]{:T(128)}, f32[]{:T(128)}, u32[]{:S(2)}, u32[]{:S(2)}) collective-permute-start(f32[]{:T(128)} %add.197), channel_id=1, source_target_pairs={{0,16},{4,20},{8,24},{12,28},{16,0},{20,4},{24,8},{28,12},{1,17},{... | collective-permute-start | bytes 20 | tf_op jit(solution)/shard_map/ppermute | solution.py:19

commit v2 on v1

--- a/solution.py
+++ b/solution.py
@@ -28,14 +28,16 @@
         rows = x.shape[0] // n
         return lax.dynamic_slice_in_dim(summed, lax.axis_index(axis) * rows, rows, 0)
     me = lax.axis_index(axis)
-    k = n // 2
-    while k >= 1:
-        half = x.shape[0] // 2
+    levels = n.bit_length() - 1
+    x = x.reshape((2,) * levels + (x.shape[0] // n,) + x.shape[1:])
+    k = 1
+    while k < n:
+        place = x.ndim - 3
         bit = (me // k) % 2
-        keep = lax.dynamic_slice_in_dim(x, bit * half, half, 0)
-        send = lax.dynamic_slice_in_dim(x, (1 - bit) * half, half, 0)
+        keep = lax.dynamic_index_in_dim(x, bit, place, keepdims=False)
+        send = lax.dynamic_index_in_dim(x, 1 - bit, place, keepdims=False)
         x = keep + lax.ppermute(send, axis, [(i, i ^ k) for i in range(n)])
-        k //= 2
+        k *= 2
     return x
 
 
@@ -44,13 +46,15 @@
     if n & (n - 1):
         return lax.all_gather(x, axis, axis=0, tiled=True)
     me = lax.axis_index(axis)
-    k = 1
-    while k < n:
+    rows = x.shape[0]
+    k = n // 2
+    while k >= 1:
         other = lax.ppermute(x, axis, [(i, i ^ k) for i in range(n)])
         upper = (me // k) % 2 == 1
-        x = jnp.where(upper, jnp.concatenate([other, x], 0), jnp.concatenate([x, other], 0))
-        k *= 2
-    return x
+        place = x.ndim - 2
+        x = jnp.where(upper, jnp.stack([other, x], place), jnp.stack([x, other], place))
+        k //= 2
+    return x.reshape((n * rows,) + x.shape[-1:])
 
 
 def local(travel_times, sensitivity, tile_blocks, face_blocks, face_weights, face_count):

time: 163 us -> 154 us (0.945)
  waiting for transfers between devices: 73.6 us -> 65.5 us
    ppermute x4, waiting for transfers between devices: 16.1 us -> 9.65 us  [doubling_gather(): other = lax.ppermute(x, axis, [(i, i ^ k) for i in range(n)])]
where the time goes in v2:
time: 154 us
  waiting for transfers between devices  65.5 us (43%)
  starting transfers between devices  42.3 us (27%)
  other arithmetic  14.9 us (10%)
  matrix products  12.4 us (8%)
  between operations  11.1 us (7%)
  local copies, waits for them, and re-layouts  7.4 us (5%)
    ppermute x19, waiting for transfers between devices, butterfly_sum(): x = x + lax.ppermute(x, axis, [(i, i ^ k) for i in range(n)])  44.8 us
    ppermute x19, starting transfers between devices, butterfly_sum(): x = x + lax.ppermute(x, axis, [(i, i ^ k) for i in range(n)])  35.8 us
    ppermute x4, waiting for transfers between devices, halving_scatter(): x = keep + lax.ppermute(send, axis, [(i, i ^ k) for i in range(n)])  11.1 us
    ppermute x4, waiting for transfers between devices, doubling_gather(): other = lax.ppermute(x, axis, [(i, i ^ k) for i in range(n)])  9.65 us
    dot_general x2, matrix products, local(): jnp.einsum('tsrb,tsb->tr', sensitivity, picked, preferred_element_type=jn...  6.73 us
    dot_general x2, matrix products, transposed_part(): jnp.einsum('tsrb,tr->tsb', sensitivity, rays_half, preferred_element_type...  5.69 us
    ppermute x4, starting transfers between devices, halving_scatter(): x = keep + lax.ppermute(send, axis, [(i, i ^ k) for i in range(n)])  3.25 us
    ppermute x4, starting transfers between devices, doubling_gather(): other = lax.ppermute(x, axis, [(i, i ^ k) for i in range(n)])  3.25 us
  transfers between devices with their start and end apart: 27, of which 26 were waited for; matrix products, arithmetic and copies ran while one was open for 2% of the time, Pallas kernels for 0%

profile of v2, /device:TPU:0, one launch (start us, length us, event | category | flops | bytes accessed | tf_op | source)
XLA Modules:
  0.0 153.6 jit_solution(18077624724082490442)
XLA Ops:
  0.0 1.4 multiply_reduce_fusion.3
  1.4 3.0 %collective-permute-start = (f32[]{:T(128)}, f32[]{:T(128)}, u32[]{:S(2)}, u32[]{:S(2)}) collective-permute-start(f32[]{:T(128)} %multiply_reduce_fusion.3), channel_id=1, source_target_pairs={{0,4},{4,0},{8,12},{12,8},{16,20},{20,16},{24,28},{28,24},{1,5},{5... | collective-permute-start | bytes 20 | tf_op jit(solution)/shard_map/ppermute | solution.py:19
  9.8 2.9 %collective-permute-start.1 = (f32[]{:T(128)}, f32[]{:T(128)}, u32[]{:S(2)}, u32[]{:S(2)}) collective-permute-start(f32[]{:T(128)} %add.167), channel_id=1, source_target_pairs={{0,8},{4,12},{8,0},{12,4},{16,24},{20,28},{24,16},{28,20},{1,9},{5... | collective-permute-start | bytes 20 | tf_op jit(solution)/shard_map/ppermute | solution.py:19
  14.1 4.0 %collective-permute-start.2 = (f32[]{:T(128)}, f32[]{:T(128)}, u32[]{:S(2)}, u32[]{:S(2)}) collective-permute-start(f32[]{:T(128)} %add.168), channel_id=1, source_target_pairs={{0,16},{4,20},{8,24},{12,28},{16,0},{20,4},{24,8},{28,12},{1,17},{... | collective-permute-start | bytes 20 | tf_op jit(solution)/shard_map/ppermute | solution.py:19
  20.0 2.9 %fusion.24 = f32[64,1,2,128]{3,1,2,0:T(1,128)S(1)} fusion(bf16[64,2,128,128]{3,2,1,0:T(8,128)(2,1)} %param.7, bf16[64,128,1,1]{1,0,2,3:T(8,128)(2,1)S(1)} %convert_bitcast_fusion.1), kind=kOutput, calls=%fused_computation.54 | convolution fusion | flops 4194304 | bytes 4276224 | tf_op jit(solution)/shard_map/tsrb,tr->tsb/dot_general | solution.py:72
  22.9 1.3 scatter_custom_fusion
  24.4 1.5 collective-permute-done.3
  25.9 1.6 %collective-permute-start.4 = (f32[256,128]{1,0:T(8,128)S(1)}, f32[256,128]{1,0:T(8,128)S(1)}, u32[]{:S(2)}, u32[]{:S(2)}) collective-permute-start(f32[256,128]{1,0:T(8,128)S(1)} %dynamic-slice_bitcast_fusion.3), channel_id=1, source_target_pairs={{0,2},{1,3},{2,0},{3,1},{4,6},{5,7},{6,4},{7,5},{8,10},{9,11},{10,... | collective-permute-start | bytes 393224 | tf_op jit(solution)/shard_map/ppermute | solution.py:39
  27.5 4.0 %collective-permute-done.4 = f32[256,128]{1,0:T(8,128)S(1)} collective-permute-done((f32[256,128]{1,0:T(8,128)S(1)}, f32[256,128]{1,0:T(8,128)S(1)}, u32[]{:S(2)}, u32[]{:S(2)}) %collective-permute-start.4) | collective-permute-done | bytes 131104 | tf_op jit(solution)/shard_map/ppermute | solution.py:39
  31.9 4.7 %collective-permute-done.5 = f32[256,128]{1,0:T(8,128)S(1)} collective-permute-done((f32[256,128]{1,0:T(8,128)S(1)}, f32[256,128]{1,0:T(8,128)S(1)}, u32[]{:S(2)}, u32[]{:S(2)}) %collective-permute-start.5) | collective-permute-done | bytes 131104 | tf_op jit(solution)/shard_map/ppermute | solution.py:19
  36.6 1.6 %collective-permute-start.6 = (f32[256,128]{1,0:T(8,128)S(1)}, f32[256,128]{1,0:T(8,128)S(1)}, u32[]{:S(2)}, u32[]{:S(2)}) collective-permute-start(f32[256,128]{1,0:T(8,128)S(1)} %add.177), channel_id=1, source_target_pairs={{0,8},{4,12},{8,0},{12,4},{16,24},{20,28},{24,16},{28,20},{1,9},{5... | collective-permute-start | bytes 393224 | tf_op jit(solution)/shard_map/ppermute | solution.py:19
  38.2 3.4 %collective-permute-done.6 = f32[256,128]{1,0:T(8,128)S(1)} collective-permute-done((f32[256,128]{1,0:T(8,128)S(1)}, f32[256,128]{1,0:T(8,128)S(1)}, u32[]{:S(2)}, u32[]{:S(2)}) %collective-permute-start.6) | collective-permute-done | bytes 131104 | tf_op jit(solution)/shard_map/ppermute | solution.py:19
  41.6 3.1 %collective-permute-start.7 = (f32[256,128]{1,0:T(8,128)S(1)}, f32[256,128]{1,0:T(8,128)S(1)}, u32[]{:S(2)}, u32[]{:S(2)}) collective-permute-start(f32[256,128]{1,0:T(8,128)S(1)} %add.178), channel_id=1, source_target_pairs={{0,16},{4,20},{8,24},{12,28},{16,0},{20,4},{24,8},{28,12},{1,17},{... | collective-permute-start | bytes 393224 | tf_op jit(solution)/shard_map/ppermute | solution.py:19
  44.7 4.4 %collective-permute-done.7 = f32[256,128]{1,0:T(8,128)S(1)} collective-permute-done((f32[256,128]{1,0:T(8,128)S(1)}, f32[256,128]{1,0:T(8,128)S(1)}, u32[]{:S(2)}, u32[]{:S(2)}) %collective-permute-start.7) | collective-permute-done | bytes 131104 | tf_op jit(solution)/shard_map/ppermute | solution.py:19
  49.1 1.6 %collective-permute-start.8 = (f32[256,128]{1,0:T(8,128)S(1)}, f32[256,128]{1,0:T(8,128)S(1)}, u32[]{:S(2)}, u32[]{:S(2)}) collective-permute-start(f32[256,128]{1,0:T(8,128)S(1)} %add.179), channel_id=1, source_target_pairs={{0,2},{1,3},{2,0},{3,1},{4,6},{5,7},{6,4},{7,5},{8,10},{9,11},{10,... | collective-permute-start | bytes 393224 | tf_op jit(solution)/shard_map/ppermute | solution.py:52
  50.9 3.2 %collective-permute-done.8 = f32[256,128]{1,0:T(8,128)S(1)} collective-permute-done((f32[256,128]{1,0:T(8,128)S(1)}, f32[256,128]{1,0:T(8,128)S(1)}, u32[]{:S(2)}, u32[]{:S(2)}) %collective-permute-start.8) | collective-permute-done | bytes 131104 | tf_op jit(solution)/shard_map/ppermute | solution.py:52
  54.3 1.4 collective-permute-done.9
  58.0 3.4 %fusion.18 = f32[64,1,128,1]{2,1,3,0:T(1,128)S(1)} fusion(bf16[64,2,128,128]{3,2,1,0:T(8,128)(2,1)} %param.7, bf16[64,2,128,1]{2,1,0,3:T(2,128)(2,1)S(1)} %bitcast.93), kind=kOutput, calls=%fused_computation.46 | convolution fusion | flops 4194304 | bytes 4259840 | tf_op jit(solution)/shard_map/tsrb,tsb->tr/dot_general | solution.py:101
  65.9 1.6 %collective-permute-start.11 = (f32[72,128]{1,0:T(8,128)S(1)}, f32[72,128]{1,0:T(8,128)S(1)}, u32[]{:S(2)}, u32[]{:S(2)}) collective-permute-start(f32[72,128]{1,0:T(8,128)S(1)} %pad_add_fusion.2), channel_id=1, source_target_pairs={{0,2},{1,3},{2,0},{3,1},{4,6},{5,7},{6,4},{7,5},{8,10},{9,11},{10,... | collective-permute-start | bytes 110600 | tf_op jit(solution)/shard_map/ppermute | solution.py:19
  67.4 2.5 %collective-permute-done.11 = f32[72,128]{1,0:T(8,128)S(1)} collective-permute-done((f32[72,128]{1,0:T(8,128)S(1)}, f32[72,128]{1,0:T(8,128)S(1)}, u32[]{:S(2)}, u32[]{:S(2)}) %collective-permute-start.11) | collective-permute-done | bytes 36896 | tf_op jit(solution)/shard_map/ppermute | solution.py:19
  72.3 1.9 %collective-permute-start.12 = (f32[]{:T(128)}, f32[]{:T(128)}, u32[]{:S(2)}, u32[]{:S(2)}) collective-permute-start(f32[]{:T(128)} %add.185), channel_id=1, source_target_pairs={{0,4},{4,0},{8,12},{12,8},{16,20},{20,16},{24,28},{28,24},{1,5},{5... | collective-permute-start | bytes 20 | tf_op jit(solution)/shard_map/ppermute | solution.py:19
  74.1 1.8 %collective-permute-done.12 = f32[]{:T(128)} collective-permute-done((f32[]{:T(128)}, f32[]{:T(128)}, u32[]{:S(2)}, u32[]{:S(2)}) %collective-permute-start.12) | collective-permute-done | bytes 36 | tf_op jit(solution)/shard_map/ppermute | solution.py:19
  76.5 2.0 %collective-permute-start.13 = (f32[]{:T(128)}, f32[]{:T(128)}, u32[]{:S(2)}, u32[]{:S(2)}) collective-permute-start(f32[]{:T(128)} %add.186), channel_id=1, source_target_pairs={{0,8},{4,12},{8,0},{12,4},{16,24},{20,28},{24,16},{28,20},{1,9},{5... | collective-permute-start | bytes 20 | tf_op jit(solution)/shard_map/ppermute | solution.py:19
  78.6 1.7 %collective-permute-done.13 = f32[]{:T(128)} collective-permute-done((f32[]{:T(128)}, f32[]{:T(128)}, u32[]{:S(2)}, u32[]{:S(2)}) %collective-permute-start.13) | collective-permute-done | bytes 36 | tf_op jit(solution)/shard_map/ppermute | solution.py:19
  80.8 3.4 %collective-permute-start.14 = (f32[]{:T(128)}, f32[]{:T(128)}, u32[]{:S(2)}, u32[]{:S(2)}) collective-permute-start(f32[]{:T(128)} %add.187), channel_id=1, source_target_pairs={{0,16},{4,20},{8,24},{12,28},{16,0},{20,4},{24,8},{28,12},{1,17},{... | collective-permute-start | bytes 20 | tf_op jit(solution)/shard_map/ppermute | solution.py:19
  84.2 1.2 collective-permute-done.14
  86.1 2.8 %fusion.22 = f32[64,1,2,128]{3,1,2,0:T(1,128)S(1)} fusion(bf16[64,2,128,128]{3,2,1,0:T(8,128)(2,1)} %param.7, bf16[64,128,1,1]{1,0,2,3:T(8,128)(2,1)S(1)} %convert_bitcast_fusion), kind=kOutput, calls=%fused_computation.52 | convolution fusion | flops 4194304 | bytes 4276224 | tf_op jit(solution)/shard_map/tsrb,tr->tsb/dot_general | solution.py:72
  89.8 1.3 scatter_custom_fusion.2
  91.2 1.5 collective-permute-done.15
  92.8 1.6 %collective-permute-start.16 = (f32[256,128]{1,0:T(8,128)S(1)}, f32[256,128]{1,0:T(8,128)S(1)}, u32[]{:S(2)}, u32[]{:S(2)}) collective-permute-start(f32[256,128]{1,0:T(8,128)S(1)} %dynamic-slice_bitcast_fusion.2), channel_id=1, source_target_pairs={{0,2},{1,3},{2,0},{3,1},{4,6},{5,7},{6,4},{7,5},{8,10},{9,11},{10,... | collective-permute-start | bytes 393224 | tf_op jit(solution)/shard_map/ppermute | solution.py:39
  94.4 4.0 %collective-permute-done.16 = f32[256,128]{1,0:T(8,128)S(1)} collective-permute-done((f32[256,128]{1,0:T(8,128)S(1)}, f32[256,128]{1,0:T(8,128)S(1)}, u32[]{:S(2)}, u32[]{:S(2)}) %collective-permute-start.16) | collective-permute-done | bytes 131104 | tf_op jit(solution)/shard_map/ppermute | solution.py:39
  99.0 4.5 %collective-permute-done.17 = f32[256,128]{1,0:T(8,128)S(1)} collective-permute-done((f32[256,128]{1,0:T(8,128)S(1)}, f32[256,128]{1,0:T(8,128)S(1)}, u32[]{:S(2)}, u32[]{:S(2)}) %collective-permute-start.17) | collective-permute-done | bytes 131104 | tf_op jit(solution)/shard_map/ppermute | solution.py:19
  103.5 1.2 collective-permute-start.18
  104.7 3.8 %collective-permute-done.18 = f32[256,128]{1,0:T(8,128)S(1)} collective-permute-done((f32[256,128]{1,0:T(8,128)S(1)}, f32[256,128]{1,0:T(8,128)S(1)}, u32[]{:S(2)}, u32[]{:S(2)}) %collective-permute-start.18) | collective-permute-done | bytes 131104 | tf_op jit(solution)/shard_map/ppermute | solution.py:19
  108.6 2.1 %collective-permute-start.19 = (f32[256,128]{1,0:T(8,128)S(1)}, f32[256,128]{1,0:T(8,128)S(1)}, u32[]{:S(2)}, u32[]{:S(2)}) collective-permute-start(f32[256,128]{1,0:T(8,128)S(1)} %add.195), channel_id=1, source_target_pairs={{0,16},{4,20},{8,24},{12,28},{16,0},{20,4},{24,8},{28,12},{1,17},{... | collective-permute-start | bytes 393224 | tf_op jit(solution)/shard_map/ppermute | solution.py:19
  110.7 5.2 %collective-permute-done.19 = f32[256,128]{1,0:T(8,128)S(1)} collective-permute-done((f32[256,128]{1,0:T(8,128)S(1)}, f32[256,128]{1,0:T(8,128)S(1)}, u32[]{:S(2)}, u32[]{:S(2)}) %collective-permute-start.19) | collective-permute-done | bytes 131104 | tf_op jit(solution)/shard_map/ppermute | solution.py:19
  115.9 1.6 %collective-permute-start.20 = (f32[256,128]{1,0:T(8,128)S(1)}, f32[256,128]{1,0:T(8,128)S(1)}, u32[]{:S(2)}, u32[]{:S(2)}) collective-permute-start(f32[256,128]{1,0:T(8,128)S(1)} %multiply_subtract_fusion), channel_id=1, source_target_pairs={{0,2},{1,3},{2,0},{3,1},{4,6},{5,7},{6,4},{7,5},{8,10},{9,11},{10,... | collective-permute-start | bytes 393224 | tf_op jit(solution)/shard_map/ppermute | solution.py:52
  117.5 3.5 %collective-permute-done.20 = f32[256,128]{1,0:T(8,128)S(1)} collective-permute-done((f32[256,128]{1,0:T(8,128)S(1)}, f32[256,128]{1,0:T(8,128)S(1)}, u32[]{:S(2)}, u32[]{:S(2)}) %collective-permute-start.20) | collective-permute-done | bytes 131104 | tf_op jit(solution)/shard_map/ppermute | solution.py:52
  121.1 1.5 collective-permute-done.21
  126.0 3.4 %fusion.16 = f32[64,1,128,1]{2,1,3,0:T(1,128)S(1)} fusion(bf16[64,2,128,128]{3,2,1,0:T(8,128)(2,1)} %param.7, bf16[64,2,128,1]{2,1,0,3:T(2,128)(2,1)S(1)} %bitcast.92), kind=kOutput, calls=%fused_computation.44 | convolution fusion | flops 4194304 | bytes 4259840 | tf_op jit(solution)/shard_map/tsrb,tsb->tr/dot_general | solution.py:101
  132.7 1.6 %collective-permute-start.23 = (f32[72,128]{1,0:T(8,128)S(1)}, f32[72,128]{1,0:T(8,128)S(1)}, u32[]{:S(2)}, u32[]{:S(2)}) collective-permute-start(f32[72,128]{1,0:T(8,128)S(1)} %pad_add_fusion.1), channel_id=1, source_target_pairs={{0,2},{1,3},{2,0},{3,1},{4,6},{5,7},{6,4},{7,5},{8,10},{9,11},{10,... | collective-permute-start | bytes 110600 | tf_op jit(solution)/shard_map/ppermute | solution.py:19
  134.4 2.2 %collective-permute-done.23 = f32[72,128]{1,0:T(8,128)S(1)} collective-permute-done((f32[72,128]{1,0:T(8,128)S(1)}, f32[72,128]{1,0:T(8,128)S(1)}, u32[]{:S(2)}, u32[]{:S(2)}) %collective-permute-start.23) | collective-permute-done | bytes 36896 | tf_op jit(solution)/shard_map/ppermute | solution.py:19
  139.0 1.9 %collective-permute-start.24 = (f32[]{:T(128)}, f32[]{:T(128)}, u32[]{:S(2)}, u32[]{:S(2)}) collective-permute-start(f32[]{:T(128)} %add.199), channel_id=1, source_target_pairs={{0,4},{4,0},{8,12},{12,8},{16,20},{20,16},{24,28},{28,24},{1,5},{5... | collective-permute-start | bytes 20 | tf_op jit(solution)/shard_map/ppermute | solution.py:19
  140.9 1.8 %collective-permute-done.24 = f32[]{:T(128)} collective-permute-done((f32[]{:T(128)}, f32[]{:T(128)}, u32[]{:S(2)}, u32[]{:S(2)}) %collective-permute-start.24) | collective-permute-done | bytes 36 | tf_op jit(solution)/shard_map/ppermute | solution.py:19
  143.3 1.5 collective-permute-start.25
  144.8 2.2 %collective-permute-done.25 = f32[]{:T(128)} collective-permute-done((f32[]{:T(128)}, f32[]{:T(128)}, u32[]{:S(2)}, u32[]{:S(2)}) %collective-permute-start.25) | collective-permute-done | bytes 36 | tf_op jit(solution)/shard_map/ppermute | solution.py:19
  147.6 2.9 %collective-permute-start.26 = (f32[]{:T(128)}, f32[]{:T(128)}, u32[]{:S(2)}, u32[]{:S(2)}) collective-permute-start(f32[]{:T(128)} %add.201), channel_id=1, source_target_pairs={{0,16},{4,20},{8,24},{12,28},{16,0},{20,4},{24,8},{28,12},{1,17},{... | collective-permute-start | bytes 20 | tf_op jit(solution)/shard_map/ppermute | solution.py:19
  150.4 1.8 %collective-permute-done.26 = f32[]{:T(128)} collective-permute-done((f32[]{:T(128)}, f32[]{:T(128)}, u32[]{:S(2)}, u32[]{:S(2)}) %collective-permute-start.26) | collective-permute-done | bytes 36 | tf_op jit(solution)/shard_map/ppermute | solution.py:19
  (81 shorter events, 23.5 us)
Async XLA Ops:
  1.4 7.2 %collective-permute-start = (f32[]{:T(128)}, f32[]{:T(128)}, u32[]{:S(2)}, u32[]{:S(2)}) collective-permute-start(f32[]{:T(128)} %multiply_reduce_fusion.3), channel_id=1, source_target_pairs={{0,4},{4,0},{8,12},{12,8},{16,20},{20,16},{24,28},{28,24},{1,5},{5... | collective-permute-start | bytes 20 | tf_op jit(solution)/shard_map/ppermute | solution.py:19
  9.8 3.7 %collective-permute-start.1 = (f32[]{:T(128)}, f32[]{:T(128)}, u32[]{:S(2)}, u32[]{:S(2)}) collective-permute-start(f32[]{:T(128)} %add.167), channel_id=1, source_target_pairs={{0,8},{4,12},{8,0},{12,4},{16,24},{20,28},{24,16},{28,20},{1,9},{5... | collective-permute-start | bytes 20 | tf_op jit(solution)/shard_map/ppermute | solution.py:19
  14.1 4.6 %collective-permute-start.2 = (f32[]{:T(128)}, f32[]{:T(128)}, u32[]{:S(2)}, u32[]{:S(2)}) collective-permute-start(f32[]{:T(128)} %add.168), channel_id=1, source_target_pairs={{0,16},{4,20},{8,24},{12,28},{16,0},{20,4},{24,8},{28,12},{1,17},{... | collective-permute-start | bytes 20 | tf_op jit(solution)/shard_map/ppermute | solution.py:19
  20.0 30.6 %copy-start.2 = (s32[64,2]{0,1:T(2,128)S(1)}, s32[64,2]{0,1:T(2,128)}, u32[]{:S(2)}) copy-start(s32[64,2]{0,1:T(2,128)} %param.8) | copy-start | bytes 1540
  24.3 1.6 %collective-permute-start.3 = (f32[2,256,128]{2,1,0:T(8,128)S(1)}, f32[2,256,128]{2,1,0:T(8,128)S(1)}, u32[]{:S(2)}, u32[]{:S(2)}) collective-permute-start(f32[2,256,128]{2,1,0:T(8,128)S(1)} %dynamic-slice_bitcast_fusion.1), channel_id=1, source_target_pairs={{0,1},{1,0},{2,3},{3,2},{4,5},{5,4},{6,7},{7,6},{8,9},{9,8},{10,11... | collective-permute-start | bytes 786440 | tf_op jit(solution)/shard_map/ppermute | solution.py:39
  25.9 5.6 %collective-permute-start.4 = (f32[256,128]{1,0:T(8,128)S(1)}, f32[256,128]{1,0:T(8,128)S(1)}, u32[]{:S(2)}, u32[]{:S(2)}) collective-permute-start(f32[256,128]{1,0:T(8,128)S(1)} %dynamic-slice_bitcast_fusion.3), channel_id=1, source_target_pairs={{0,2},{1,3},{2,0},{3,1},{4,6},{5,7},{6,4},{7,5},{8,10},{9,11},{10,... | collective-permute-start | bytes 393224 | tf_op jit(solution)/shard_map/ppermute | solution.py:39
  31.5 5.0 %collective-permute-start.5 = (f32[256,128]{1,0:T(8,128)S(1)}, f32[256,128]{1,0:T(8,128)S(1)}, u32[]{:S(2)}, u32[]{:S(2)}) collective-permute-start(f32[256,128]{1,0:T(8,128)S(1)} %bitcast_add_fusion.3), channel_id=1, source_target_pairs={{0,4},{4,0},{8,12},{12,8},{16,20},{20,16},{24,28},{28,24},{1,5},{5... | collective-permute-start | bytes 393224 | tf_op jit(solution)/shard_map/ppermute | solution.py:19
  36.6 5.0 %collective-permute-start.6 = (f32[256,128]{1,0:T(8,128)S(1)}, f32[256,128]{1,0:T(8,128)S(1)}, u32[]{:S(2)}, u32[]{:S(2)}) collective-permute-start(f32[256,128]{1,0:T(8,128)S(1)} %add.177), channel_id=1, source_target_pairs={{0,8},{4,12},{8,0},{12,4},{16,24},{20,28},{24,16},{28,20},{1,9},{5... | collective-permute-start | bytes 393224 | tf_op jit(solution)/shard_map/ppermute | solution.py:19
  41.6 7.4 %collective-permute-start.7 = (f32[256,128]{1,0:T(8,128)S(1)}, f32[256,128]{1,0:T(8,128)S(1)}, u32[]{:S(2)}, u32[]{:S(2)}) collective-permute-start(f32[256,128]{1,0:T(8,128)S(1)} %add.178), channel_id=1, source_target_pairs={{0,16},{4,20},{8,24},{12,28},{16,0},{20,4},{24,8},{28,12},{1,17},{... | collective-permute-start | bytes 393224 | tf_op jit(solution)/shard_map/ppermute | solution.py:19
  49.1 5.0 %collective-permute-start.8 = (f32[256,128]{1,0:T(8,128)S(1)}, f32[256,128]{1,0:T(8,128)S(1)}, u32[]{:S(2)}, u32[]{:S(2)}) collective-permute-start(f32[256,128]{1,0:T(8,128)S(1)} %add.179), channel_id=1, source_target_pairs={{0,2},{1,3},{2,0},{3,1},{4,6},{5,7},{6,4},{7,5},{8,10},{9,11},{10,... | collective-permute-start | bytes 393224 | tf_op jit(solution)/shard_map/ppermute | solution.py:52
  54.2 1.6 %collective-permute-start.9 = (f32[2,256,128]{2,1,0:T(8,128)S(1)}, f32[2,256,128]{2,1,0:T(8,128)S(1)}, u32[]{:S(2)}, u32[]{:S(2)}) collective-permute-start(f32[2,256,128]{2,1,0:T(8,128)S(1)} %maximum_select_fusion.2), channel_id=1, source_target_pairs={{0,1},{1,0},{2,3},{3,2},{4,5},{5,4},{6,7},{7,6},{8,9},{9,8},{10,11... | collective-permute-start | bytes 786440 | tf_op jit(solution)/shard_map/ppermute | solution.py:52
  54.3 8.3 %copy-start = (f32[32,128]{1,0:T(8,128)S(1)}, f32[32,128]{1,0:T(8,128)}, u32[]{:S(2)}) copy-start(f32[32,128]{1,0:T(8,128)} %param.10) | copy-start | bytes 49156
  55.8 14.2 %copy-start.1 = (f32[64,128]{1,0:T(8,128)S(1)}, f32[64,128]{1,0:T(8,128)}, u32[]{:S(2)}) copy-start(f32[64,128]{1,0:T(8,128)} %param.6) | copy-start | bytes 98308
  64.0 1.3 collective-permute-start.10
  65.9 4.0 %collective-permute-start.11 = (f32[72,128]{1,0:T(8,128)S(1)}, f32[72,128]{1,0:T(8,128)S(1)}, u32[]{:S(2)}, u32[]{:S(2)}) collective-permute-start(f32[72,128]{1,0:T(8,128)S(1)} %pad_add_fusion.2), channel_id=1, source_target_pairs={{0,2},{1,3},{2,0},{3,1},{4,6},{5,7},{6,4},{7,5},{8,10},{9,11},{10,... | collective-permute-start | bytes 110600 | tf_op jit(solution)/shard_map/ppermute | solution.py:19
  72.3 3.7 %collective-permute-start.12 = (f32[]{:T(128)}, f32[]{:T(128)}, u32[]{:S(2)}, u32[]{:S(2)}) collective-permute-start(f32[]{:T(128)} %add.185), channel_id=1, source_target_pairs={{0,4},{4,0},{8,12},{12,8},{16,20},{20,16},{24,28},{28,24},{1,5},{5... | collective-permute-start | bytes 20 | tf_op jit(solution)/shard_map/ppermute | solution.py:19
  76.5 3.7 %collective-permute-start.13 = (f32[]{:T(128)}, f32[]{:T(128)}, u32[]{:S(2)}, u32[]{:S(2)}) collective-permute-start(f32[]{:T(128)} %add.186), channel_id=1, source_target_pairs={{0,8},{4,12},{8,0},{12,4},{16,24},{20,28},{24,16},{28,20},{1,9},{5... | collective-permute-start | bytes 20 | tf_op jit(solution)/shard_map/ppermute | solution.py:19
  80.8 4.6 %collective-permute-start.14 = (f32[]{:T(128)}, f32[]{:T(128)}, u32[]{:S(2)}, u32[]{:S(2)}) collective-permute-start(f32[]{:T(128)} %add.187), channel_id=1, source_target_pairs={{0,16},{4,20},{8,24},{12,28},{16,0},{20,4},{24,8},{28,12},{1,17},{... | collective-permute-start | bytes 20 | tf_op jit(solution)/shard_map/ppermute | solution.py:19
  91.2 1.6 %collective-permute-start.15 = (f32[2,256,128]{2,1,0:T(8,128)S(1)}, f32[2,256,128]{2,1,0:T(8,128)S(1)}, u32[]{:S(2)}, u32[]{:S(2)}) collective-permute-start(f32[2,256,128]{2,1,0:T(8,128)S(1)} %dynamic-slice_bitcast_fusion), channel_id=1, source_target_pairs={{0,1},{1,0},{2,3},{3,2},{4,5},{5,4},{6,7},{7,6},{8,9},{9,8},{10,11... | collective-permute-start | bytes 786440 | tf_op jit(solution)/shard_map/ppermute | solution.py:39
  92.8 5.6 %collective-permute-start.16 = (f32[256,128]{1,0:T(8,128)S(1)}, f32[256,128]{1,0:T(8,128)S(1)}, u32[]{:S(2)}, u32[]{:S(2)}) collective-permute-start(f32[256,128]{1,0:T(8,128)S(1)} %dynamic-slice_bitcast_fusion.2), channel_id=1, source_target_pairs={{0,2},{1,3},{2,0},{3,1},{4,6},{5,7},{6,4},{7,5},{8,10},{9,11},{10,... | collective-permute-start | bytes 393224 | tf_op jit(solution)/shard_map/ppermute | solution.py:39
  98.5 5.0 %collective-permute-start.17 = (f32[256,128]{1,0:T(8,128)S(1)}, f32[256,128]{1,0:T(8,128)S(1)}, u32[]{:S(2)}, u32[]{:S(2)}) collective-permute-start(f32[256,128]{1,0:T(8,128)S(1)} %bitcast_add_fusion.2), channel_id=1, source_target_pairs={{0,4},{4,0},{8,12},{12,8},{16,20},{20,16},{24,28},{28,24},{1,5},{5... | collective-permute-start | bytes 393224 | tf_op jit(solution)/shard_map/ppermute | solution.py:19
  103.5 5.0 %collective-permute-start.18 = (f32[256,128]{1,0:T(8,128)S(1)}, f32[256,128]{1,0:T(8,128)S(1)}, u32[]{:S(2)}, u32[]{:S(2)}) collective-permute-start(f32[256,128]{1,0:T(8,128)S(1)} %add.194), channel_id=1, source_target_pairs={{0,8},{4,12},{8,0},{12,4},{16,24},{20,28},{24,16},{28,20},{1,9},{5... | collective-permute-start | bytes 393224 | tf_op jit(solution)/shard_map/ppermute | solution.py:19
  108.6 7.3 %collective-permute-start.19 = (f32[256,128]{1,0:T(8,128)S(1)}, f32[256,128]{1,0:T(8,128)S(1)}, u32[]{:S(2)}, u32[]{:S(2)}) collective-permute-start(f32[256,128]{1,0:T(8,128)S(1)} %add.195), channel_id=1, source_target_pairs={{0,16},{4,20},{8,24},{12,28},{16,0},{20,4},{24,8},{28,12},{1,17},{... | collective-permute-start | bytes 393224 | tf_op jit(solution)/shard_map/ppermute | solution.py:19
  115.9 5.0 %collective-permute-start.20 = (f32[256,128]{1,0:T(8,128)S(1)}, f32[256,128]{1,0:T(8,128)S(1)}, u32[]{:S(2)}, u32[]{:S(2)}) collective-permute-start(f32[256,128]{1,0:T(8,128)S(1)} %multiply_subtract_fusion), channel_id=1, source_target_pairs={{0,2},{1,3},{2,0},{3,1},{4,6},{5,7},{6,4},{7,5},{8,10},{9,11},{10,... | collective-permute-start | bytes 393224 | tf_op jit(solution)/shard_map/ppermute | solution.py:52
  121.0 1.6 %collective-permute-start.21 = (f32[2,256,128]{2,1,0:T(8,128)S(1)}, f32[2,256,128]{2,1,0:T(8,128)S(1)}, u32[]{:S(2)}, u32[]{:S(2)}) collective-permute-start(f32[2,256,128]{2,1,0:T(8,128)S(1)} %maximum_select_fusion.4), channel_id=1, source_target_pairs={{0,1},{1,0},{2,3},{3,2},{4,5},{5,4},{6,7},{7,6},{8,9},{9,8},{10,11... | collective-permute-start | bytes 786440 | tf_op jit(solution)/shard_map/ppermute | solution.py:52
  130.7 1.3 collective-permute-start.22
  132.7 4.0 %collective-permute-start.23 = (f32[72,128]{1,0:T(8,128)S(1)}, f32[72,128]{1,0:T(8,128)S(1)}, u32[]{:S(2)}, u32[]{:S(2)}) collective-permute-start(f32[72,128]{1,0:T(8,128)S(1)} %pad_add_fusion.1), channel_id=1, source_target_pairs={{0,2},{1,3},{2,0},{3,1},{4,6},{5,7},{6,4},{7,5},{8,10},{9,11},{10,... | collective-permute-start | bytes 110600 | tf_op jit(solution)/shard_map/ppermute | solution.py:19
  139.0 3.7 %collective-permute-start.24 = (f32[]{:T(128)}, f32[]{:T(128)}, u32[]{:S(2)}, u32[]{:S(2)}) collective-permute-start(f32[]{:T(128)} %add.199), channel_id=1, source_target_pairs={{0,4},{4,0},{8,12},{12,8},{16,20},{20,16},{24,28},{28,24},{1,5},{5... | collective-permute-start | bytes 20 | tf_op jit(solution)/shard_map/ppermute | solution.py:19
  143.3 3.7 %collective-permute-start.25 = (f32[]{:T(128)}, f32[]{:T(128)}, u32[]{:S(2)}, u32[]{:S(2)}) collective-permute-start(f32[]{:T(128)} %add.200), channel_id=1, source_target_pairs={{0,8},{4,12},{8,0},{12,4},{16,24},{20,28},{24,16},{28,20},{1,9},{5... | collective-permute-start | bytes 20 | tf_op jit(solution)/shard_map/ppermute | solution.py:19
  147.6 4.6 %collective-permute-start.26 = (f32[]{:T(128)}, f32[]{:T(128)}, u32[]{:S(2)}, u32[]{:S(2)}) collective-permute-start(f32[]{:T(128)} %add.201), channel_id=1, source_target_pairs={{0,16},{4,20},{8,24},{12,28},{16,0},{20,4},{24,8},{28,12},{1,17},{... | collective-permute-start | bytes 20 | tf_op jit(solution)/shard_map/ppermute | solution.py:19

commit v3 on v2

--- a/solution.py
+++ b/solution.py
@@ -19,6 +19,16 @@
         x = x + lax.ppermute(x, axis, [(i, i ^ k) for i in range(n)])
         k *= 2
     return x
+
+
+def scalar_sum(value, axis):
+    n = lax.axis_size(axis)
+    spread = jnp.broadcast_to(value.astype(jnp.float32), (n, 1, 128))
+    got = lax.all_to_all(spread, axis, 0, 0, tiled=False)
+    total = got[0]
+    for j in range(1, n):
+        total = total + got[j]
+    return total[0, 0]
 
 
 def halving_scatter(x, axis):
@@ -86,7 +96,7 @@
         field = field / alpha
         return field, lax.dynamic_slice_in_dim(field, region * NB_DEV, NB_DEV, 0), alpha
 
-    beta_value = jnp.sqrt(butterfly_sum(jnp.sum(travel_times * travel_times), "dp"))
+    beta_value = jnp.sqrt(scalar_sum(jnp.sum(travel_times * travel_times), "dp"))
     left_rays = travel_times / beta_value
     left_faces = jnp.zeros(face_weights.shape, jnp.float32)
     raw = transposed_part(left_rays, left_faces)
@@ -113,7 +123,7 @@
         packed = butterfly_sum(packed, "region")
         ray_pred = packed[:n_tiles]
         left_rays = ray_pred - alpha_value * left_rays
-        beta_sq = butterfly_sum(jnp.sum(left_rays * left_rays) + packed[n_tiles, 0], "dp")
+        beta_sq = scalar_sum(jnp.sum(left_rays * left_rays) + packed[n_tiles, 0], "dp")
         beta_value = jnp.sqrt(beta_sq)
         left_rays = left_rays / beta_value
         left_faces = left_faces / beta_value

time: 154 us -> 145 us (0.942)
  starting transfers between devices: 42.3 us -> 24.5 us
  blocking collectives: 0 us -> 10.1 us
  between operations: 11.1 us -> 5.54 us
  local copies, waits for them, and re-layouts: 7.4 us -> 9.31 us
    ppermute x19 -> x10, starting transfers between devices: 35.8 us -> 7.42 us  [butterfly_sum(): x = x + lax.ppermute(x, axis, [(i, i ^ k) for i in range(n)])]
    all_to_all x0 -> x2, starting transfers between devices: none -> 10.6 us  [scalar_sum(): got = lax.all_to_all(spread, axis, 0, 0, tiled=False)]
    all_to_all x0 -> x1, blocking collectives: none -> 10.1 us  [scalar_sum(): got = lax.all_to_all(spread, axis, 0, 0, tiled=False)]
    all_to_all x0 -> x2, waiting for transfers between devices: none -> 8.26 us  [scalar_sum(): got = lax.all_to_all(spread, axis, 0, 0, tiled=False)]
    ppermute x19 -> x10, waiting for transfers between devices: 44.8 us -> 38 us  [butterfly_sum(): x = x + lax.ppermute(x, axis, [(i, i ^ k) for i in range(n)])]
    broadcast_in_dim x0 -> x3, local copies, waits for them, and re-layouts: none -> 1.88 us  [scalar_sum(): spread = jnp.broadcast_to(value.astype(jnp.float32), (n, 1, 128))]
  transfers between devices with their start and end apart: 27 -> 20, of which waited for: 26 -> 20; matrix products, arithmetic and copies ran while one was open for 2% -> 3% of each run, Pallas kernels for 0% -> 0%
where the time goes in v3:
time: 145 us; the launch traced here: 144 us
  waiting for transfers between devices  67 us (46%)
  starting transfers between devices  24.5 us (17%)
  other arithmetic  15 us (10%)
  matrix products  12.4 us (9%)
  blocking collectives  10.1 us (7%)
  local copies, waits for them, and re-layouts  9.31 us (6%)
  between operations  5.54 us (4%)
    ppermute x10, waiting for transfers between devices, butterfly_sum(): x = x + lax.ppermute(x, axis, [(i, i ^ k) for i in range(n)])  38 us
    ppermute x4, waiting for transfers between devices, halving_scatter(): x = keep + lax.ppermute(send, axis, [(i, i ^ k) for i in range(n)])  11.1 us
    all_to_all x2, starting transfers between devices, scalar_sum(): got = lax.all_to_all(spread, axis, 0, 0, tiled=False)  10.6 us
    all_to_all x1, blocking collectives, scalar_sum(): got = lax.all_to_all(spread, axis, 0, 0, tiled=False)  10.1 us
    ppermute x4, waiting for transfers between devices, doubling_gather(): other = lax.ppermute(x, axis, [(i, i ^ k) for i in range(n)])  9.65 us
    all_to_all x2, waiting for transfers between devices, scalar_sum(): got = lax.all_to_all(spread, axis, 0, 0, tiled=False)  8.26 us
    ppermute x10, starting transfers between devices, butterfly_sum(): x = x + lax.ppermute(x, axis, [(i, i ^ k) for i in range(n)])  7.42 us
    dot_general x2, matrix products, local(): jnp.einsum('tsrb,tsb->tr', sensitivity, picked, preferred_element_type=jn...  6.73 us
  transfers between devices with their start and end apart: 20, of which 20 were waited for; matrix products, arithmetic and copies ran while one was open for 3% of the time, Pallas kernels for 0%

profile of v3, /device:TPU:0, one launch (start us, length us, event | category | flops | bytes accessed | tf_op | source)
XLA Modules:
  0.0 143.9 jit_solution(15401473557402351116)
XLA Ops:
  0.0 1.4 %multiply_reduce_fusion.3 = f32[]{:T(128)} fusion(f32[64,128]{1,0:T(8,128)} %param.6), kind=kLoop, calls=%fused_computation.57 | loop fusion | flops 16383 | bytes 32772 | tf_op jit(solution)/shard_map/reduce_sum | solution.py:99
  1.5 1.3 broadcast_in_dim.12
  2.7 7.3 %all-to-all-start = ((f32[8,1,128]{2,1,0:T(1,128)}), f32[8,1,128]{2,1,0:T(1,128)S(1)}, u32[]{:S(2)}, u32[]{:S(2)}) async-start(f32[8,1,128]{2,1,0:T(1,128)} %broadcast_in_dim.12), calls=%async_computation | async-start | bytes 8192 | tf_op jit(solution)/shard_map/all_to_all | solution.py:27
  10.0 0.8 fusion.26
  10.8 0.8 copy.12
  12.3 0.8 multiply_multiply_fusion.1
  13.1 1.1 scatter_custom_fusion.1
  14.2 2.2 %all-to-all-done = f32[8,1,128]{2,1,0:T(1,128)S(1)} async-done(((f32[8,1,128]{2,1,0:T(1,128)}), f32[8,1,128]{2,1,0:T(1,128)S(1)}, u32[]{:S(2)}, u32[]{:S(2)}) %all-to-all-start) | async-done | bytes 4128 | tf_op jit(solution)/shard_map/all_to_all | solution.py:27
  16.5 0.8 convert_bitcast_fusion.1
  17.3 2.9 %fusion.24 = f32[64,1,2,128]{3,1,2,0:T(1,128)S(1)} fusion(bf16[64,2,128,128]{3,2,1,0:T(8,128)(2,1)} %param.7, bf16[64,128,1,1]{1,0,2,3:T(8,128)(2,1)S(1)} %convert_bitcast_fusion.1), kind=kOutput, calls=%fused_computation.54 | convolution fusion | flops 4194304 | bytes 4276224 | tf_op jit(solution)/shard_map/tsrb,tr->tsb/dot_general | solution.py:82
  20.1 1.3 scatter_custom_fusion
  21.6 1.5 %collective-permute-done = f32[2,256,128]{2,1,0:T(8,128)S(1)} collective-permute-done((f32[2,256,128]{2,1,0:T(8,128)S(1)}, f32[2,256,128]{2,1,0:T(8,128)S(1)}, u32[]{:S(2)}, u32[]{:S(2)}) %collective-permute-start) | collective-permute-done | bytes 262176 | tf_op jit(solution)/shard_map/ppermute | solution.py:49
  23.1 1.6 %collective-permute-start.1 = (f32[256,128]{1,0:T(8,128)S(1)}, f32[256,128]{1,0:T(8,128)S(1)}, u32[]{:S(2)}, u32[]{:S(2)}) collective-permute-start(f32[256,128]{1,0:T(8,128)S(1)} %dynamic-slice_bitcast_fusion.3), channel_id=1, source_target_pairs={{0,2},{1,3},{2,0},{3,1},{4,6},{5,7},{6,4},{7,5},{8,10},{9,11},{10,... | collective-permute-start | bytes 393224 | tf_op jit(solution)/shard_map/ppermute | solution.py:49
  24.7 4.0 %collective-permute-done.1 = f32[256,128]{1,0:T(8,128)S(1)} collective-permute-done((f32[256,128]{1,0:T(8,128)S(1)}, f32[256,128]{1,0:T(8,128)S(1)}, u32[]{:S(2)}, u32[]{:S(2)}) %collective-permute-start.1) | collective-permute-done | bytes 131104 | tf_op jit(solution)/shard_map/ppermute | solution.py:49
  29.4 4.4 %collective-permute-done.2 = f32[256,128]{1,0:T(8,128)S(1)} collective-permute-done((f32[256,128]{1,0:T(8,128)S(1)}, f32[256,128]{1,0:T(8,128)S(1)}, u32[]{:S(2)}, u32[]{:S(2)}) %collective-permute-start.2) | collective-permute-done | bytes 131104 | tf_op jit(solution)/shard_map/ppermute | solution.py:19
  34.4 4.4 %collective-permute-done.3 = f32[256,128]{1,0:T(8,128)S(1)} collective-permute-done((f32[256,128]{1,0:T(8,128)S(1)}, f32[256,128]{1,0:T(8,128)S(1)}, u32[]{:S(2)}, u32[]{:S(2)}) %collective-permute-start.3) | collective-permute-done | bytes 131104 | tf_op jit(solution)/shard_map/ppermute | solution.py:19
  38.9 0.8 collective-permute-start.4
  39.7 6.5 %collective-permute-done.4 = f32[256,128]{1,0:T(8,128)S(1)} collective-permute-done((f32[256,128]{1,0:T(8,128)S(1)}, f32[256,128]{1,0:T(8,128)S(1)}, u32[]{:S(2)}, u32[]{:S(2)}) %collective-permute-start.4) | collective-permute-done | bytes 131104 | tf_op jit(solution)/shard_map/ppermute | solution.py:19
  46.2 1.6 %collective-permute-start.5 = (f32[256,128]{1,0:T(8,128)S(1)}, f32[256,128]{1,0:T(8,128)S(1)}, u32[]{:S(2)}, u32[]{:S(2)}) collective-permute-start(f32[256,128]{1,0:T(8,128)S(1)} %add.406), channel_id=1, source_target_pairs={{0,2},{1,3},{2,0},{3,1},{4,6},{5,7},{6,4},{7,5},{8,10},{9,11},{10,... | collective-permute-start | bytes 393224 | tf_op jit(solution)/shard_map/ppermute | solution.py:62
  48.0 3.2 %collective-permute-done.5 = f32[256,128]{1,0:T(8,128)S(1)} collective-permute-done((f32[256,128]{1,0:T(8,128)S(1)}, f32[256,128]{1,0:T(8,128)S(1)}, u32[]{:S(2)}, u32[]{:S(2)}) %collective-permute-start.5) | collective-permute-done | bytes 131104 | tf_op jit(solution)/shard_map/ppermute | solution.py:62
  51.4 1.4 %collective-permute-done.6 = f32[2,256,128]{2,1,0:T(8,128)S(1)} collective-permute-done((f32[2,256,128]{2,1,0:T(8,128)S(1)}, f32[2,256,128]{2,1,0:T(8,128)S(1)}, u32[]{:S(2)}, u32[]{:S(2)}) %collective-permute-start.6) | collective-permute-done | bytes 262176 | tf_op jit(solution)/shard_map/ppermute | solution.py:62
  52.9 0.7 multiply_reduce_fusion.1
  54.5 0.7 gather_fusion
  55.2 3.4 %fusion.18 = f32[64,1,128,1]{2,1,3,0:T(1,128)S(1)} fusion(bf16[64,2,128,128]{3,2,1,0:T(8,128)(2,1)} %param.7, bf16[64,2,128,1]{2,1,0,3:T(2,128)(2,1)S(1)} %bitcast.105), kind=kOutput, calls=%fused_computation.46 | convolution fusion | flops 4194304 | bytes 4259840 | tf_op jit(solution)/shard_map/tsrb,tsb->tr/dot_general | solution.py:111
  61.3 1.1 collective-permute-done.7
  63.0 1.6 %collective-permute-start.8 = (f32[72,128]{1,0:T(8,128)S(1)}, f32[72,128]{1,0:T(8,128)S(1)}, u32[]{:S(2)}, u32[]{:S(2)}) collective-permute-start(f32[72,128]{1,0:T(8,128)S(1)} %pad_add_fusion.2), channel_id=1, source_target_pairs={{0,2},{1,3},{2,0},{3,1},{4,6},{5,7},{6,4},{7,5},{8,10},{9,11},{10,... | collective-permute-start | bytes 110600 | tf_op jit(solution)/shard_map/ppermute | solution.py:19
  64.6 2.5 %collective-permute-done.8 = f32[72,128]{1,0:T(8,128)S(1)} collective-permute-done((f32[72,128]{1,0:T(8,128)S(1)}, f32[72,128]{1,0:T(8,128)S(1)}, u32[]{:S(2)}, u32[]{:S(2)}) %collective-permute-start.8) | collective-permute-done | bytes 36896 | tf_op jit(solution)/shard_map/ppermute | solution.py:19
  69.4 10.1 %all_to_all.15 = f32[8,1,128]{2,1,0:T(1,128)S(1)} all-to-all(f32[8,1,128]{2,1,0:T(1,128)S(1)} %broadcast_in_dim.29), channel_id=1, replica_groups=mesh['dp'=8,'region'=4] {'dp'}, dimensions={0} | all-to-all | bytes 8192 | tf_op jit(solution)/shard_map/all_to_all | solution.py:27
  79.7 2.8 %fusion.22 = f32[64,1,2,128]{3,1,2,0:T(1,128)S(1)} fusion(bf16[64,2,128,128]{3,2,1,0:T(8,128)(2,1)} %param.7, bf16[64,128,1,1]{1,0,2,3:T(8,128)(2,1)S(1)} %convert_bitcast_fusion), kind=kOutput, calls=%fused_computation.52 | convolution fusion | flops 4194304 | bytes 4276224 | tf_op jit(solution)/shard_map/tsrb,tr->tsb/dot_general | solution.py:82
  82.5 0.8 scatter_custom_fusion.3
  83.4 1.3 scatter_custom_fusion.2
  84.8 1.5 %collective-permute-done.9 = f32[2,256,128]{2,1,0:T(8,128)S(1)} collective-permute-done((f32[2,256,128]{2,1,0:T(8,128)S(1)}, f32[2,256,128]{2,1,0:T(8,128)S(1)}, u32[]{:S(2)}, u32[]{:S(2)}) %collective-permute-start.9) | collective-permute-done | bytes 262176 | tf_op jit(solution)/shard_map/ppermute | solution.py:49
  86.4 1.6 %collective-permute-start.10 = (f32[256,128]{1,0:T(8,128)S(1)}, f32[256,128]{1,0:T(8,128)S(1)}, u32[]{:S(2)}, u32[]{:S(2)}) collective-permute-start(f32[256,128]{1,0:T(8,128)S(1)} %dynamic-slice_bitcast_fusion.2), channel_id=1, source_target_pairs={{0,2},{1,3},{2,0},{3,1},{4,6},{5,7},{6,4},{7,5},{8,10},{9,11},{10,... | collective-permute-start | bytes 393224 | tf_op jit(solution)/shard_map/ppermute | solution.py:49
  88.0 4.0 %collective-permute-done.10 = f32[256,128]{1,0:T(8,128)S(1)} collective-permute-done((f32[256,128]{1,0:T(8,128)S(1)}, f32[256,128]{1,0:T(8,128)S(1)}, u32[]{:S(2)}, u32[]{:S(2)}) %collective-permute-start.10) | collective-permute-done | bytes 131104 | tf_op jit(solution)/shard_map/ppermute | solution.py:49
  92.6 4.4 %collective-permute-done.11 = f32[256,128]{1,0:T(8,128)S(1)} collective-permute-done((f32[256,128]{1,0:T(8,128)S(1)}, f32[256,128]{1,0:T(8,128)S(1)}, u32[]{:S(2)}, u32[]{:S(2)}) %collective-permute-start.11) | collective-permute-done | bytes 131104 | tf_op jit(solution)/shard_map/ppermute | solution.py:19
  97.7 4.4 %collective-permute-done.12 = f32[256,128]{1,0:T(8,128)S(1)} collective-permute-done((f32[256,128]{1,0:T(8,128)S(1)}, f32[256,128]{1,0:T(8,128)S(1)}, u32[]{:S(2)}, u32[]{:S(2)}) %collective-permute-start.12) | collective-permute-done | bytes 131104 | tf_op jit(solution)/shard_map/ppermute | solution.py:19
  102.8 6.7 %collective-permute-done.13 = f32[256,128]{1,0:T(8,128)S(1)} collective-permute-done((f32[256,128]{1,0:T(8,128)S(1)}, f32[256,128]{1,0:T(8,128)S(1)}, u32[]{:S(2)}, u32[]{:S(2)}) %collective-permute-start.13) | collective-permute-done | bytes 131104 | tf_op jit(solution)/shard_map/ppermute | solution.py:19
  109.5 1.6 %collective-permute-start.14 = (f32[256,128]{1,0:T(8,128)S(1)}, f32[256,128]{1,0:T(8,128)S(1)}, u32[]{:S(2)}, u32[]{:S(2)}) collective-permute-start(f32[256,128]{1,0:T(8,128)S(1)} %multiply_subtract_fusion), channel_id=1, source_target_pairs={{0,2},{1,3},{2,0},{3,1},{4,6},{5,7},{6,4},{7,5},{8,10},{9,11},{10,... | collective-permute-start | bytes 393224 | tf_op jit(solution)/shard_map/ppermute | solution.py:62
  111.1 3.5 %collective-permute-done.14 = f32[256,128]{1,0:T(8,128)S(1)} collective-permute-done((f32[256,128]{1,0:T(8,128)S(1)}, f32[256,128]{1,0:T(8,128)S(1)}, u32[]{:S(2)}, u32[]{:S(2)}) %collective-permute-start.14) | collective-permute-done | bytes 131104 | tf_op jit(solution)/shard_map/ppermute | solution.py:62
  114.7 1.5 %collective-permute-done.15 = f32[2,256,128]{2,1,0:T(8,128)S(1)} collective-permute-done((f32[2,256,128]{2,1,0:T(8,128)S(1)}, f32[2,256,128]{2,1,0:T(8,128)S(1)}, u32[]{:S(2)}, u32[]{:S(2)}) %collective-permute-start.15) | collective-permute-done | bytes 262176 | tf_op jit(solution)/shard_map/ppermute | solution.py:62
  116.2 0.7 multiply_reduce_fusion
  117.7 0.7 gather_fusion.3
  119.6 3.4 %fusion.16 = f32[64,1,128,1]{2,1,3,0:T(1,128)S(1)} fusion(bf16[64,2,128,128]{3,2,1,0:T(8,128)(2,1)} %param.7, bf16[64,2,128,1]{2,1,0,3:T(2,128)(2,1)S(1)} %bitcast.104), kind=kOutput, calls=%fused_computation.44 | convolution fusion | flops 4194304 | bytes 4259840 | tf_op jit(solution)/shard_map/tsrb,tsb->tr/dot_general | solution.py:111
  124.5 1.1 collective-permute-done.16
  126.2 1.6 %collective-permute-start.17 = (f32[72,128]{1,0:T(8,128)S(1)}, f32[72,128]{1,0:T(8,128)S(1)}, u32[]{:S(2)}, u32[]{:S(2)}) collective-permute-start(f32[72,128]{1,0:T(8,128)S(1)} %pad_add_fusion.1), channel_id=1, source_target_pairs={{0,2},{1,3},{2,0},{3,1},{4,6},{5,7},{6,4},{7,5},{8,10},{9,11},{10,... | collective-permute-start | bytes 110600 | tf_op jit(solution)/shard_map/ppermute | solution.py:19
  127.8 2.5 %collective-permute-done.17 = f32[72,128]{1,0:T(8,128)S(1)} collective-permute-done((f32[72,128]{1,0:T(8,128)S(1)}, f32[72,128]{1,0:T(8,128)S(1)}, u32[]{:S(2)}, u32[]{:S(2)}) %collective-permute-start.17) | collective-permute-done | bytes 36896 | tf_op jit(solution)/shard_map/ppermute | solution.py:19
  133.3 3.3 %all-to-all-start.2 = ((f32[8,1,128]{2,1,0:T(1,128)}), f32[8,1,128]{2,1,0:T(1,128)S(1)}, u32[]{:S(2)}, u32[]{:S(2)}) async-start(f32[8,1,128]{2,1,0:T(1,128)} %broadcast_in_dim.30), calls=%async_computation.2 | async-start | bytes 8192 | tf_op jit(solution)/shard_map/all_to_all | solution.py:27
  136.8 6.1 %all-to-all-done.2 = f32[8,1,128]{2,1,0:T(1,128)S(1)} async-done(((f32[8,1,128]{2,1,0:T(1,128)}), f32[8,1,128]{2,1,0:T(1,128)S(1)}, u32[]{:S(2)}, u32[]{:S(2)}) %all-to-all-start.2) | async-done | bytes 4128 | tf_op jit(solution)/shard_map/all_to_all | solution.py:27
  (74 shorter events, 14.9 us)
Async XLA Ops:
  2.7 13.7 %all-to-all-start = ((f32[8,1,128]{2,1,0:T(1,128)}), f32[8,1,128]{2,1,0:T(1,128)S(1)}, u32[]{:S(2)}, u32[]{:S(2)}) async-start(f32[8,1,128]{2,1,0:T(1,128)} %broadcast_in_dim.12), calls=%async_computation | async-start | bytes 8192 | tf_op jit(solution)/shard_map/all_to_all | solution.py:27
  17.3 30.5 %copy-start.2 = (s32[64,2]{0,1:T(2,128)S(1)}, s32[64,2]{0,1:T(2,128)}, u32[]{:S(2)}) copy-start(s32[64,2]{0,1:T(2,128)} %param.8) | copy-start | bytes 1540
  21.5 1.6 %collective-permute-start = (f32[2,256,128]{2,1,0:T(8,128)S(1)}, f32[2,256,128]{2,1,0:T(8,128)S(1)}, u32[]{:S(2)}, u32[]{:S(2)}) collective-permute-start(f32[2,256,128]{2,1,0:T(8,128)S(1)} %dynamic-slice_bitcast_fusion.1), channel_id=1, source_target_pairs={{0,1},{1,0},{2,3},{3,2},{4,5},{5,4},{6,7},{7,6},{8,9},{9,8},{10,11... | collective-permute-start | bytes 786440 | tf_op jit(solution)/shard_map/ppermute | solution.py:49
  23.1 5.6 %collective-permute-start.1 = (f32[256,128]{1,0:T(8,128)S(1)}, f32[256,128]{1,0:T(8,128)S(1)}, u32[]{:S(2)}, u32[]{:S(2)}) collective-permute-start(f32[256,128]{1,0:T(8,128)S(1)} %dynamic-slice_bitcast_fusion.3), channel_id=1, source_target_pairs={{0,2},{1,3},{2,0},{3,1},{4,6},{5,7},{6,4},{7,5},{8,10},{9,11},{10,... | collective-permute-start | bytes 393224 | tf_op jit(solution)/shard_map/ppermute | solution.py:49
  28.8 5.0 %collective-permute-start.2 = (f32[256,128]{1,0:T(8,128)S(1)}, f32[256,128]{1,0:T(8,128)S(1)}, u32[]{:S(2)}, u32[]{:S(2)}) collective-permute-start(f32[256,128]{1,0:T(8,128)S(1)} %bitcast_add_fusion.3), channel_id=1, source_target_pairs={{0,4},{4,0},{8,12},{12,8},{16,20},{20,16},{24,28},{28,24},{1,5},{5... | collective-permute-start | bytes 393224 | tf_op jit(solution)/shard_map/ppermute | solution.py:19
  33.8 5.0 %collective-permute-start.3 = (f32[256,128]{1,0:T(8,128)S(1)}, f32[256,128]{1,0:T(8,128)S(1)}, u32[]{:S(2)}, u32[]{:S(2)}) collective-permute-start(f32[256,128]{1,0:T(8,128)S(1)} %add.404), channel_id=1, source_target_pairs={{0,8},{4,12},{8,0},{12,4},{16,24},{20,28},{24,16},{28,20},{1,9},{5... | collective-permute-start | bytes 393224 | tf_op jit(solution)/shard_map/ppermute | solution.py:19
  38.9 7.3 %collective-permute-start.4 = (f32[256,128]{1,0:T(8,128)S(1)}, f32[256,128]{1,0:T(8,128)S(1)}, u32[]{:S(2)}, u32[]{:S(2)}) collective-permute-start(f32[256,128]{1,0:T(8,128)S(1)} %add.405), channel_id=1, source_target_pairs={{0,16},{4,20},{8,24},{12,28},{16,0},{20,4},{24,8},{28,12},{1,17},{... | collective-permute-start | bytes 393224 | tf_op jit(solution)/shard_map/ppermute | solution.py:19
  46.2 5.0 %collective-permute-start.5 = (f32[256,128]{1,0:T(8,128)S(1)}, f32[256,128]{1,0:T(8,128)S(1)}, u32[]{:S(2)}, u32[]{:S(2)}) collective-permute-start(f32[256,128]{1,0:T(8,128)S(1)} %add.406), channel_id=1, source_target_pairs={{0,2},{1,3},{2,0},{3,1},{4,6},{5,7},{6,4},{7,5},{8,10},{9,11},{10,... | collective-permute-start | bytes 393224 | tf_op jit(solution)/shard_map/ppermute | solution.py:62
  51.3 1.6 %collective-permute-start.6 = (f32[2,256,128]{2,1,0:T(8,128)S(1)}, f32[2,256,128]{2,1,0:T(8,128)S(1)}, u32[]{:S(2)}, u32[]{:S(2)}) collective-permute-start(f32[2,256,128]{2,1,0:T(8,128)S(1)} %maximum_select_fusion.2), channel_id=1, source_target_pairs={{0,1},{1,0},{2,3},{3,2},{4,5},{5,4},{6,7},{7,6},{8,9},{9,8},{10,11... | collective-permute-start | bytes 786440 | tf_op jit(solution)/shard_map/ppermute | solution.py:62
  51.4 8.3 %copy-start = (f32[32,128]{1,0:T(8,128)S(1)}, f32[32,128]{1,0:T(8,128)}, u32[]{:S(2)}) copy-start(f32[32,128]{1,0:T(8,128)} %param.10) | copy-start | bytes 49156
  52.9 14.2 %copy-start.1 = (f32[64,128]{1,0:T(8,128)S(1)}, f32[64,128]{1,0:T(8,128)}, u32[]{:S(2)}) copy-start(f32[64,128]{1,0:T(8,128)} %param.6) | copy-start | bytes 98308
  61.1 1.3 collective-permute-start.7
  63.0 4.0 %collective-permute-start.8 = (f32[72,128]{1,0:T(8,128)S(1)}, f32[72,128]{1,0:T(8,128)S(1)}, u32[]{:S(2)}, u32[]{:S(2)}) collective-permute-start(f32[72,128]{1,0:T(8,128)S(1)} %pad_add_fusion.2), channel_id=1, source_target_pairs={{0,2},{1,3},{2,0},{3,1},{4,6},{5,7},{6,4},{7,5},{8,10},{9,11},{10,... | collective-permute-start | bytes 110600 | tf_op jit(solution)/shard_map/ppermute | solution.py:19
  84.7 1.6 %collective-permute-start.9 = (f32[2,256,128]{2,1,0:T(8,128)S(1)}, f32[2,256,128]{2,1,0:T(8,128)S(1)}, u32[]{:S(2)}, u32[]{:S(2)}) collective-permute-start(f32[2,256,128]{2,1,0:T(8,128)S(1)} %dynamic-slice_bitcast_fusion), channel_id=1, source_target_pairs={{0,1},{1,0},{2,3},{3,2},{4,5},{5,4},{6,7},{7,6},{8,9},{9,8},{10,11... | collective-permute-start | bytes 786440 | tf_op jit(solution)/shard_map/ppermute | solution.py:49
  86.4 5.6 %collective-permute-start.10 = (f32[256,128]{1,0:T(8,128)S(1)}, f32[256,128]{1,0:T(8,128)S(1)}, u32[]{:S(2)}, u32[]{:S(2)}) collective-permute-start(f32[256,128]{1,0:T(8,128)S(1)} %dynamic-slice_bitcast_fusion.2), channel_id=1, source_target_pairs={{0,2},{1,3},{2,0},{3,1},{4,6},{5,7},{6,4},{7,5},{8,10},{9,11},{10,... | collective-permute-start | bytes 393224 | tf_op jit(solution)/shard_map/ppermute | solution.py:49
  92.0 5.0 %collective-permute-start.11 = (f32[256,128]{1,0:T(8,128)S(1)}, f32[256,128]{1,0:T(8,128)S(1)}, u32[]{:S(2)}, u32[]{:S(2)}) collective-permute-start(f32[256,128]{1,0:T(8,128)S(1)} %bitcast_add_fusion.2), channel_id=1, source_target_pairs={{0,4},{4,0},{8,12},{12,8},{16,20},{20,16},{24,28},{28,24},{1,5},{5... | collective-permute-start | bytes 393224 | tf_op jit(solution)/shard_map/ppermute | solution.py:19
  97.1 5.0 %collective-permute-start.12 = (f32[256,128]{1,0:T(8,128)S(1)}, f32[256,128]{1,0:T(8,128)S(1)}, u32[]{:S(2)}, u32[]{:S(2)}) collective-permute-start(f32[256,128]{1,0:T(8,128)S(1)} %add.426), channel_id=1, source_target_pairs={{0,8},{4,12},{8,0},{12,4},{16,24},{20,28},{24,16},{28,20},{1,9},{5... | collective-permute-start | bytes 393224 | tf_op jit(solution)/shard_map/ppermute | solution.py:19
  102.1 7.3 %collective-permute-start.13 = (f32[256,128]{1,0:T(8,128)S(1)}, f32[256,128]{1,0:T(8,128)S(1)}, u32[]{:S(2)}, u32[]{:S(2)}) collective-permute-start(f32[256,128]{1,0:T(8,128)S(1)} %add.427), channel_id=1, source_target_pairs={{0,16},{4,20},{8,24},{12,28},{16,0},{20,4},{24,8},{28,12},{1,17},{... | collective-permute-start | bytes 393224 | tf_op jit(solution)/shard_map/ppermute | solution.py:19
  109.5 5.0 %collective-permute-start.14 = (f32[256,128]{1,0:T(8,128)S(1)}, f32[256,128]{1,0:T(8,128)S(1)}, u32[]{:S(2)}, u32[]{:S(2)}) collective-permute-start(f32[256,128]{1,0:T(8,128)S(1)} %multiply_subtract_fusion), channel_id=1, source_target_pairs={{0,2},{1,3},{2,0},{3,1},{4,6},{5,7},{6,4},{7,5},{8,10},{9,11},{10,... | collective-permute-start | bytes 393224 | tf_op jit(solution)/shard_map/ppermute | solution.py:62
  114.6 1.6 %collective-permute-start.15 = (f32[2,256,128]{2,1,0:T(8,128)S(1)}, f32[2,256,128]{2,1,0:T(8,128)S(1)}, u32[]{:S(2)}, u32[]{:S(2)}) collective-permute-start(f32[2,256,128]{2,1,0:T(8,128)S(1)} %maximum_select_fusion.4), channel_id=1, source_target_pairs={{0,1},{1,0},{2,3},{3,2},{4,5},{5,4},{6,7},{7,6},{8,9},{9,8},{10,11... | collective-permute-start | bytes 786440 | tf_op jit(solution)/shard_map/ppermute | solution.py:62
  124.3 1.3 collective-permute-start.16
  126.2 4.0 %collective-permute-start.17 = (f32[72,128]{1,0:T(8,128)S(1)}, f32[72,128]{1,0:T(8,128)S(1)}, u32[]{:S(2)}, u32[]{:S(2)}) collective-permute-start(f32[72,128]{1,0:T(8,128)S(1)} %pad_add_fusion.1), channel_id=1, source_target_pairs={{0,2},{1,3},{2,0},{3,1},{4,6},{5,7},{6,4},{7,5},{8,10},{9,11},{10,... | collective-permute-start | bytes 110600 | tf_op jit(solution)/shard_map/ppermute | solution.py:19
  133.3 9.6 %all-to-all-start.2 = ((f32[8,1,128]{2,1,0:T(1,128)}), f32[8,1,128]{2,1,0:T(1,128)S(1)}, u32[]{:S(2)}, u32[]{:S(2)}) async-start(f32[8,1,128]{2,1,0:T(1,128)} %broadcast_in_dim.30), calls=%async_computation.2 | async-start | bytes 8192 | tf_op jit(solution)/shard_map/all_to_all | solution.py:27

commit v4 on v3

--- a/solution.py
+++ b/solution.py
@@ -76,6 +76,17 @@
     second_block = face_blocks[:, 1]
     flat_blocks = tile_blocks.reshape(-1)
     n_tiles = travel_times.shape[0]
+    columns = jnp.arange(model_rows, dtype=jnp.int32)[None, :]
+    select = jnp.concatenate(
+        [
+            (flat_blocks[:, None] == columns).astype(jnp.float32),
+            (first_block[:, None] == columns).astype(jnp.float32)
+            - (second_block[:, None] == columns).astype(jnp.float32),
+        ],
+        0,
+    )
+    select_half = select.astype(jnp.bfloat16)
+    n_slots = flat_blocks.shape[0]
 
     def transposed_part(left_rays, left_faces):
         rays_half = left_rays.astype(jnp.bfloat16)
@@ -84,9 +95,13 @@
         )
         contrib_rows = contrib.reshape(-1, contrib.shape[-1])
         face_term = face_scale * left_faces
-        partials = jax.ops.segment_sum(contrib_rows, flat_blocks, num_segments=model_rows)
-        partials = partials + jax.ops.segment_sum(face_term, first_block, num_segments=model_rows)
-        partials = partials - jax.ops.segment_sum(face_term, second_block, num_segments=model_rows)
+        partials = lax.dot_general(
+            select,
+            jnp.concatenate([contrib_rows, face_term], 0),
+            (((0,), (0,)), ((), ())),
+            precision=lax.Precision.HIGHEST,
+            preferred_element_type=jnp.float32,
+        )
         piece = halving_scatter(partials, "region")
         return butterfly_sum(piece, "dp")
 
@@ -107,14 +122,12 @@
     rho_bar = alpha_value
     for iteration in range(ITERS):
         full_half = full_model.astype(jnp.bfloat16)
-        picked = full_half[tile_blocks]
+        rows = jnp.dot(select_half, full_half, preferred_element_type=jnp.float32)
+        picked = rows[:n_slots].astype(jnp.bfloat16).reshape(tile_blocks.shape + rows.shape[-1:])
         partial_value = jnp.einsum(
             "tsrb,tsb->tr", sensitivity, picked, preferred_element_type=jnp.float32
         )
-        face_pred = face_scale * (
-            full_half[first_block].astype(jnp.float32)
-            - full_half[second_block].astype(jnp.float32)
-        )
+        face_pred = face_scale * rows[n_slots:]
         left_faces = face_pred - alpha_value * left_faces
         face_sq = jnp.sum(left_faces * left_faces)
         packed = jnp.concatenate(

time: 145 us -> 140 us (0.966)
  other arithmetic: 15 us -> 9.69 us
  matrix products: 12.4 us -> 16.6 us
  local copies, waits for them, and re-layouts: 9.31 us -> 5.97 us
    dot_general x0 -> x4, matrix products: none -> 4.18 us  [the longest x2 3.71 us: transposed_part(): lax.dot_general(select, jnp.concatenate([contrib_rows, face_term], 0), ((...]
    gather x6 -> x0, local copies, waits for them, and re-layouts: 3.81 us -> none  [the longest x2 1.42 us: local(): picked = full_half[tile_blocks]]
    add x2 -> x0, other arithmetic: 2.51 us -> none  [transposed_part(): partials + jax.ops.segment_sum(face_term, first_block, num_segments=model...]
    scatter-add x2 -> x0, other arithmetic: 1.92 us -> none  [transposed_part(): jax.ops.segment_sum(face_term, second_block, num_segments=model_rows)]
  transfers between devices with their start and end apart: 20 -> 20, of which waited for: 20 -> 20; matrix products, arithmetic and copies ran while one was open for 3% -> 2% of each run, Pallas kernels for 0% -> 0%
where the time goes in v4:
time: 140 us
  waiting for transfers between devices  68.4 us (49%)
  starting transfers between devices  24.3 us (17%)
  matrix products  16.6 us (12%)
  other arithmetic  9.69 us (7%)
  blocking collectives  9.2 us (7%)
  local copies, waits for them, and re-layouts  5.97 us (4%)
  between operations  5.55 us (4%)
    ppermute x10, waiting for transfers between devices, butterfly_sum(): x = x + lax.ppermute(x, axis, [(i, i ^ k) for i in range(n)])  38.2 us
    ppermute x4, waiting for transfers between devices, halving_scatter(): x = keep + lax.ppermute(send, axis, [(i, i ^ k) for i in range(n)])  11.1 us
    all_to_all x2, starting transfers between devices, scalar_sum(): got = lax.all_to_all(spread, axis, 0, 0, tiled=False)  10.6 us
    ppermute x4, waiting for transfers between devices, doubling_gather(): other = lax.ppermute(x, axis, [(i, i ^ k) for i in range(n)])  9.92 us
    all_to_all x1, blocking collectives, scalar_sum(): got = lax.all_to_all(spread, axis, 0, 0, tiled=False)  9.2 us
    all_to_all x2, waiting for transfers between devices, scalar_sum(): got = lax.all_to_all(spread, axis, 0, 0, tiled=False)  9.16 us
    ppermute x10, starting transfers between devices, butterfly_sum(): x = x + lax.ppermute(x, axis, [(i, i ^ k) for i in range(n)])  7.2 us
    dot_general x2, matrix products, local(): jnp.einsum('tsrb,tsb->tr', sensitivity, picked, preferred_element_type=jn...  6.73 us
  transfers between devices with their start and end apart: 20, of which 20 were waited for; matrix products, arithmetic and copies ran while one was open for 2% of the time, Pallas kernels for 0%

profile of v4, /device:TPU:0, one launch (start us, length us, event | category | flops | bytes accessed | tf_op | source)
XLA Modules:
  0.0 139.7 jit_solution(8020593380665998775)
XLA Ops:
  0.0 1.4 multiply_reduce_fusion.3
  1.4 1.2 broadcast_in_dim.18
  2.5 7.3 %all-to-all-start = ((f32[8,1,128]{2,1,0:T(1,128)}), f32[8,1,128]{2,1,0:T(1,128)S(1)}, u32[]{:S(2)}, u32[]{:S(2)}) async-start(f32[8,1,128]{2,1,0:T(1,128)} %broadcast_in_dim.18), calls=%async_computation | async-start | bytes 8192 | tf_op jit(solution)/shard_map/all_to_all | solution.py:27
  9.8 0.8 slice_bitcast_fusion.1
  10.6 0.8 copy.10
  12.3 0.8 multiply_multiply_fusion.1
  13.1 3.1 %all-to-all-done = f32[8,1,128]{2,1,0:T(1,128)S(1)} async-done(((f32[8,1,128]{2,1,0:T(1,128)}), f32[8,1,128]{2,1,0:T(1,128)S(1)}, u32[]{:S(2)}, u32[]{:S(2)}) %all-to-all-start) | async-done | bytes 4128 | tf_op jit(solution)/shard_map/all_to_all | solution.py:27
  16.3 0.8 convert_bitcast_fusion.1
  17.1 2.8 %fusion.26 = f32[64,1,2,128]{3,1,2,0:T(1,128)S(1)} fusion(bf16[64,2,128,128]{3,2,1,0:T(8,128)(2,1)} %param.7, bf16[64,128,1,1]{1,0,2,3:T(8,128)(2,1)S(1)} %convert_bitcast_fusion.1), kind=kOutput, calls=%fused_computation.51 | convolution fusion | flops 4194304 | bytes 4276224 | tf_op jit(solution)/shard_map/tsrb,tr->tsb/dot_general | solution.py:93
  19.9 1.9 %fusion.3 = f32[1024,128]{1,0:T(8,128)S(1)} fusion(f32[32,1024]{1,0:T(8,128)S(1)} %convert_subtract_fusion, f32[128,1024]{1,0:T(8,128)S(1)} %fusion, f32[32,128]{1,0:T(8,128)S(1)} %multiply_multiply_fusion.1, f32[128,128]{1,0:T(8,128)S(1)} %bitcast.107), kind=kOutput, calls=%fused_computation.9 | convolution fusion | flops 251842560 | bytes 1261568 | tf_op jit(solution)/shard_map/dot_general | solution.py:98
  21.9 1.5 %collective-permute-done = f32[2,256,128]{2,1,0:T(8,128)S(1)} collective-permute-done((f32[2,256,128]{2,1,0:T(8,128)S(1)}, f32[2,256,128]{2,1,0:T(8,128)S(1)}, u32[]{:S(2)}, u32[]{:S(2)}) %collective-permute-start) | collective-permute-done | bytes 262176 | tf_op jit(solution)/shard_map/ppermute | solution.py:49
  23.4 1.6 %collective-permute-start.1 = (f32[256,128]{1,0:T(8,128)S(1)}, f32[256,128]{1,0:T(8,128)S(1)}, u32[]{:S(2)}, u32[]{:S(2)}) collective-permute-start(f32[256,128]{1,0:T(8,128)S(1)} %dynamic-slice_bitcast_fusion.3), channel_id=1, source_target_pairs={{0,2},{1,3},{2,0},{3,1},{4,6},{5,7},{6,4},{7,5},{8,10},{9,11},{10,... | collective-permute-start | bytes 393224 | tf_op jit(solution)/shard_map/ppermute | solution.py:49
  25.0 4.0 %collective-permute-done.1 = f32[256,128]{1,0:T(8,128)S(1)} collective-permute-done((f32[256,128]{1,0:T(8,128)S(1)}, f32[256,128]{1,0:T(8,128)S(1)}, u32[]{:S(2)}, u32[]{:S(2)}) %collective-permute-start.1) | collective-permute-done | bytes 131104 | tf_op jit(solution)/shard_map/ppermute | solution.py:49
  29.7 4.4 %collective-permute-done.2 = f32[256,128]{1,0:T(8,128)S(1)} collective-permute-done((f32[256,128]{1,0:T(8,128)S(1)}, f32[256,128]{1,0:T(8,128)S(1)}, u32[]{:S(2)}, u32[]{:S(2)}) %collective-permute-start.2) | collective-permute-done | bytes 131104 | tf_op jit(solution)/shard_map/ppermute | solution.py:19
  34.7 4.4 %collective-permute-done.3 = f32[256,128]{1,0:T(8,128)S(1)} collective-permute-done((f32[256,128]{1,0:T(8,128)S(1)}, f32[256,128]{1,0:T(8,128)S(1)}, u32[]{:S(2)}, u32[]{:S(2)}) %collective-permute-start.3) | collective-permute-done | bytes 131104 | tf_op jit(solution)/shard_map/ppermute | solution.py:19
  39.8 6.7 %collective-permute-done.4 = f32[256,128]{1,0:T(8,128)S(1)} collective-permute-done((f32[256,128]{1,0:T(8,128)S(1)}, f32[256,128]{1,0:T(8,128)S(1)}, u32[]{:S(2)}, u32[]{:S(2)}) %collective-permute-start.4) | collective-permute-done | bytes 131104 | tf_op jit(solution)/shard_map/ppermute | solution.py:19
  46.5 1.6 %collective-permute-start.5 = (f32[256,128]{1,0:T(8,128)S(1)}, f32[256,128]{1,0:T(8,128)S(1)}, u32[]{:S(2)}, u32[]{:S(2)}) collective-permute-start(f32[256,128]{1,0:T(8,128)S(1)} %add.367), channel_id=1, source_target_pairs={{0,2},{1,3},{2,0},{3,1},{4,6},{5,7},{6,4},{7,5},{8,10},{9,11},{10,... | collective-permute-start | bytes 393224 | tf_op jit(solution)/shard_map/ppermute | solution.py:62
  48.1 3.5 %collective-permute-done.5 = f32[256,128]{1,0:T(8,128)S(1)} collective-permute-done((f32[256,128]{1,0:T(8,128)S(1)}, f32[256,128]{1,0:T(8,128)S(1)}, u32[]{:S(2)}, u32[]{:S(2)}) %collective-permute-start.5) | collective-permute-done | bytes 131104 | tf_op jit(solution)/shard_map/ppermute | solution.py:62
  51.7 1.5 %collective-permute-done.6 = f32[2,256,128]{2,1,0:T(8,128)S(1)} collective-permute-done((f32[2,256,128]{2,1,0:T(8,128)S(1)}, f32[2,256,128]{2,1,0:T(8,128)S(1)}, u32[]{:S(2)}, u32[]{:S(2)}) %collective-permute-start.6) | collective-permute-done | bytes 262176 | tf_op jit(solution)/shard_map/ppermute | solution.py:62
  53.2 0.7 multiply_reduce_fusion.1
  55.0 3.4 %fusion.18 = f32[64,1,128,1]{2,1,3,0:T(1,128)S(1)} fusion(bf16[64,2,128,128]{3,2,1,0:T(8,128)(2,1)} %param.7, bf16[64,2,128,1]{2,1,0,3:T(2,128)(2,1)S(1)} %bitcast.102), kind=kOutput, calls=%fused_computation.43 | convolution fusion | flops 4194304 | bytes 4259840 | tf_op jit(solution)/shard_map/tsrb,tsb->tr/dot_general | solution.py:127
  58.3 0.7 multiply_reduce_fusion.4
  59.9 1.1 collective-permute-done.7
  61.0 0.7 pad_add_fusion.1
  61.6 1.6 %collective-permute-start.8 = (f32[72,128]{1,0:T(8,128)S(1)}, f32[72,128]{1,0:T(8,128)S(1)}, u32[]{:S(2)}, u32[]{:S(2)}) collective-permute-start(f32[72,128]{1,0:T(8,128)S(1)} %pad_add_fusion.1), channel_id=1, source_target_pairs={{0,2},{1,3},{2,0},{3,1},{4,6},{5,7},{6,4},{7,5},{8,10},{9,11},{10,... | collective-permute-start | bytes 110600 | tf_op jit(solution)/shard_map/ppermute | solution.py:19
  63.2 2.5 %collective-permute-done.8 = f32[72,128]{1,0:T(8,128)S(1)} collective-permute-done((f32[72,128]{1,0:T(8,128)S(1)}, f32[72,128]{1,0:T(8,128)S(1)}, u32[]{:S(2)}, u32[]{:S(2)}) %collective-permute-start.8) | collective-permute-done | bytes 36896 | tf_op jit(solution)/shard_map/ppermute | solution.py:19
  68.2 9.2 %all_to_all.15 = f32[8,1,128]{2,1,0:T(1,128)S(1)} all-to-all(f32[8,1,128]{2,1,0:T(1,128)S(1)} %broadcast_in_dim.21), channel_id=1, replica_groups=mesh['dp'=8,'region'=4] {'dp'}, dimensions={0} | all-to-all | bytes 8192 | tf_op jit(solution)/shard_map/all_to_all | solution.py:27
  77.6 2.8 %fusion.24 = f32[64,1,2,128]{3,1,2,0:T(1,128)S(1)} fusion(bf16[64,2,128,128]{3,2,1,0:T(8,128)(2,1)} %param.7, bf16[64,128,1,1]{1,0,2,3:T(8,128)(2,1)S(1)} %convert_bitcast_fusion), kind=kOutput, calls=%fused_computation.49 | convolution fusion | flops 4194304 | bytes 4276224 | tf_op jit(solution)/shard_map/tsrb,tr->tsb/dot_general | solution.py:93
  80.5 1.9 %fusion.1 = f32[1024,128]{1,0:T(8,128)S(1)} fusion(f32[32,1024]{1,0:T(8,128)S(1)} %convert_subtract_fusion, f32[128,1024]{1,0:T(8,128)S(1)} %fusion, f32[32,128]{1,0:T(8,128)S(1)} %multiply_multiply_fusion, f32[128,128]{1,0:T(8,128)S(1)} %bitcast.108), kind=kOutput, calls=%fused_computation.7 | convolution fusion | flops 251842560 | bytes 1261568 | tf_op jit(solution)/shard_map/dot_general | solution.py:98
  82.4 1.5 %collective-permute-done.9 = f32[2,256,128]{2,1,0:T(8,128)S(1)} collective-permute-done((f32[2,256,128]{2,1,0:T(8,128)S(1)}, f32[2,256,128]{2,1,0:T(8,128)S(1)}, u32[]{:S(2)}, u32[]{:S(2)}) %collective-permute-start.9) | collective-permute-done | bytes 262176 | tf_op jit(solution)/shard_map/ppermute | solution.py:49
  84.0 1.6 %collective-permute-start.10 = (f32[256,128]{1,0:T(8,128)S(1)}, f32[256,128]{1,0:T(8,128)S(1)}, u32[]{:S(2)}, u32[]{:S(2)}) collective-permute-start(f32[256,128]{1,0:T(8,128)S(1)} %dynamic-slice_bitcast_fusion.2), channel_id=1, source_target_pairs={{0,2},{1,3},{2,0},{3,1},{4,6},{5,7},{6,4},{7,5},{8,10},{9,11},{10,... | collective-permute-start | bytes 393224 | tf_op jit(solution)/shard_map/ppermute | solution.py:49
  85.6 4.0 %collective-permute-done.10 = f32[256,128]{1,0:T(8,128)S(1)} collective-permute-done((f32[256,128]{1,0:T(8,128)S(1)}, f32[256,128]{1,0:T(8,128)S(1)}, u32[]{:S(2)}, u32[]{:S(2)}) %collective-permute-start.10) | collective-permute-done | bytes 131104 | tf_op jit(solution)/shard_map/ppermute | solution.py:49
  90.3 4.4 %collective-permute-done.11 = f32[256,128]{1,0:T(8,128)S(1)} collective-permute-done((f32[256,128]{1,0:T(8,128)S(1)}, f32[256,128]{1,0:T(8,128)S(1)}, u32[]{:S(2)}, u32[]{:S(2)}) %collective-permute-start.11) | collective-permute-done | bytes 131104 | tf_op jit(solution)/shard_map/ppermute | solution.py:19
  95.3 4.4 %collective-permute-done.12 = f32[256,128]{1,0:T(8,128)S(1)} collective-permute-done((f32[256,128]{1,0:T(8,128)S(1)}, f32[256,128]{1,0:T(8,128)S(1)}, u32[]{:S(2)}, u32[]{:S(2)}) %collective-permute-start.12) | collective-permute-done | bytes 131104 | tf_op jit(solution)/shard_map/ppermute | solution.py:19
  100.4 6.7 %collective-permute-done.13 = f32[256,128]{1,0:T(8,128)S(1)} collective-permute-done((f32[256,128]{1,0:T(8,128)S(1)}, f32[256,128]{1,0:T(8,128)S(1)}, u32[]{:S(2)}, u32[]{:S(2)}) %collective-permute-start.13) | collective-permute-done | bytes 131104 | tf_op jit(solution)/shard_map/ppermute | solution.py:19
  107.1 1.6 %collective-permute-start.14 = (f32[256,128]{1,0:T(8,128)S(1)}, f32[256,128]{1,0:T(8,128)S(1)}, u32[]{:S(2)}, u32[]{:S(2)}) collective-permute-start(f32[256,128]{1,0:T(8,128)S(1)} %multiply_subtract_fusion), channel_id=1, source_target_pairs={{0,2},{1,3},{2,0},{3,1},{4,6},{5,7},{6,4},{7,5},{8,10},{9,11},{10,... | collective-permute-start | bytes 393224 | tf_op jit(solution)/shard_map/ppermute | solution.py:62
  108.7 3.5 %collective-permute-done.14 = f32[256,128]{1,0:T(8,128)S(1)} collective-permute-done((f32[256,128]{1,0:T(8,128)S(1)}, f32[256,128]{1,0:T(8,128)S(1)}, u32[]{:S(2)}, u32[]{:S(2)}) %collective-permute-start.14) | collective-permute-done | bytes 131104 | tf_op jit(solution)/shard_map/ppermute | solution.py:62
  112.3 1.5 %collective-permute-done.15 = f32[2,256,128]{2,1,0:T(8,128)S(1)} collective-permute-done((f32[2,256,128]{2,1,0:T(8,128)S(1)}, f32[2,256,128]{2,1,0:T(8,128)S(1)}, u32[]{:S(2)}, u32[]{:S(2)}) %collective-permute-start.15) | collective-permute-done | bytes 262176 | tf_op jit(solution)/shard_map/ppermute | solution.py:62
  113.8 0.7 multiply_reduce_fusion
  115.5 0.7 fusion.30
  116.2 3.4 %fusion.16 = f32[64,1,128,1]{2,1,3,0:T(1,128)S(1)} fusion(bf16[64,2,128,128]{3,2,1,0:T(8,128)(2,1)} %param.7, bf16[64,2,128,1]{2,1,0,3:T(2,128)(2,1)S(1)} %bitcast.101), kind=kOutput, calls=%fused_computation.41 | convolution fusion | flops 4194304 | bytes 4259840 | tf_op jit(solution)/shard_map/tsrb,tsb->tr/dot_general | solution.py:127
  119.5 0.7 concatenate.47
  120.4 1.1 collective-permute-done.16
  122.2 1.6 %collective-permute-start.17 = (f32[72,128]{1,0:T(8,128)S(1)}, f32[72,128]{1,0:T(8,128)S(1)}, u32[]{:S(2)}, u32[]{:S(2)}) collective-permute-start(f32[72,128]{1,0:T(8,128)S(1)} %pad_add_fusion), channel_id=1, source_target_pairs={{0,2},{1,3},{2,0},{3,1},{4,6},{5,7},{6,4},{7,5},{8,10},{9,11},{10,... | collective-permute-start | bytes 110600 | tf_op jit(solution)/shard_map/ppermute | solution.py:19
  123.7 2.5 %collective-permute-done.17 = f32[72,128]{1,0:T(8,128)S(1)} collective-permute-done((f32[72,128]{1,0:T(8,128)S(1)}, f32[72,128]{1,0:T(8,128)S(1)}, u32[]{:S(2)}, u32[]{:S(2)}) %collective-permute-start.17) | collective-permute-done | bytes 36896 | tf_op jit(solution)/shard_map/ppermute | solution.py:19
  129.1 3.3 %all-to-all-start.2 = ((f32[8,1,128]{2,1,0:T(1,128)}), f32[8,1,128]{2,1,0:T(1,128)S(1)}, u32[]{:S(2)}, u32[]{:S(2)}) async-start(f32[8,1,128]{2,1,0:T(1,128)} %broadcast_in_dim.22), calls=%async_computation.2 | async-start | bytes 8192 | tf_op jit(solution)/shard_map/all_to_all | solution.py:27
  132.7 6.1 %all-to-all-done.2 = f32[8,1,128]{2,1,0:T(1,128)S(1)} async-done(((f32[8,1,128]{2,1,0:T(1,128)}), f32[8,1,128]{2,1,0:T(1,128)S(1)}, u32[]{:S(2)}, u32[]{:S(2)}) %all-to-all-start.2) | async-done | bytes 4128 | tf_op jit(solution)/shard_map/all_to_all | solution.py:27
  139.0 0.7 multiply_add_fusion
  (60 shorter events, 10.1 us)
Async XLA Ops:
  2.5 13.7 %all-to-all-start = ((f32[8,1,128]{2,1,0:T(1,128)}), f32[8,1,128]{2,1,0:T(1,128)S(1)}, u32[]{:S(2)}, u32[]{:S(2)}) async-start(f32[8,1,128]{2,1,0:T(1,128)} %broadcast_in_dim.18), calls=%async_computation | async-start | bytes 8192 | tf_op jit(solution)/shard_map/all_to_all | solution.py:27
  21.8 1.6 %collective-permute-start = (f32[2,256,128]{2,1,0:T(8,128)S(1)}, f32[2,256,128]{2,1,0:T(8,128)S(1)}, u32[]{:S(2)}, u32[]{:S(2)}) collective-permute-start(f32[2,256,128]{2,1,0:T(8,128)S(1)} %dynamic-slice_bitcast_fusion.1), channel_id=1, source_target_pairs={{0,1},{1,0},{2,3},{3,2},{4,5},{5,4},{6,7},{7,6},{8,9},{9,8},{10,11... | collective-permute-start | bytes 786440 | tf_op jit(solution)/shard_map/ppermute | solution.py:49
  23.4 5.6 %collective-permute-start.1 = (f32[256,128]{1,0:T(8,128)S(1)}, f32[256,128]{1,0:T(8,128)S(1)}, u32[]{:S(2)}, u32[]{:S(2)}) collective-permute-start(f32[256,128]{1,0:T(8,128)S(1)} %dynamic-slice_bitcast_fusion.3), channel_id=1, source_target_pairs={{0,2},{1,3},{2,0},{3,1},{4,6},{5,7},{6,4},{7,5},{8,10},{9,11},{10,... | collective-permute-start | bytes 393224 | tf_op jit(solution)/shard_map/ppermute | solution.py:49
  29.1 5.0 %collective-permute-start.2 = (f32[256,128]{1,0:T(8,128)S(1)}, f32[256,128]{1,0:T(8,128)S(1)}, u32[]{:S(2)}, u32[]{:S(2)}) collective-permute-start(f32[256,128]{1,0:T(8,128)S(1)} %bitcast_add_fusion.3), channel_id=1, source_target_pairs={{0,4},{4,0},{8,12},{12,8},{16,20},{20,16},{24,28},{28,24},{1,5},{5... | collective-permute-start | bytes 393224 | tf_op jit(solution)/shard_map/ppermute | solution.py:19
  34.1 5.0 %collective-permute-start.3 = (f32[256,128]{1,0:T(8,128)S(1)}, f32[256,128]{1,0:T(8,128)S(1)}, u32[]{:S(2)}, u32[]{:S(2)}) collective-permute-start(f32[256,128]{1,0:T(8,128)S(1)} %add.365), channel_id=1, source_target_pairs={{0,8},{4,12},{8,0},{12,4},{16,24},{20,28},{24,16},{28,20},{1,9},{5... | collective-permute-start | bytes 393224 | tf_op jit(solution)/shard_map/ppermute | solution.py:19
  39.2 7.3 %collective-permute-start.4 = (f32[256,128]{1,0:T(8,128)S(1)}, f32[256,128]{1,0:T(8,128)S(1)}, u32[]{:S(2)}, u32[]{:S(2)}) collective-permute-start(f32[256,128]{1,0:T(8,128)S(1)} %add.366), channel_id=1, source_target_pairs={{0,16},{4,20},{8,24},{12,28},{16,0},{20,4},{24,8},{28,12},{1,17},{... | collective-permute-start | bytes 393224 | tf_op jit(solution)/shard_map/ppermute | solution.py:19
  46.5 5.0 %collective-permute-start.5 = (f32[256,128]{1,0:T(8,128)S(1)}, f32[256,128]{1,0:T(8,128)S(1)}, u32[]{:S(2)}, u32[]{:S(2)}) collective-permute-start(f32[256,128]{1,0:T(8,128)S(1)} %add.367), channel_id=1, source_target_pairs={{0,2},{1,3},{2,0},{3,1},{4,6},{5,7},{6,4},{7,5},{8,10},{9,11},{10,... | collective-permute-start | bytes 393224 | tf_op jit(solution)/shard_map/ppermute | solution.py:62
  51.6 1.6 %collective-permute-start.6 = (f32[2,256,128]{2,1,0:T(8,128)S(1)}, f32[2,256,128]{2,1,0:T(8,128)S(1)}, u32[]{:S(2)}, u32[]{:S(2)}) collective-permute-start(f32[2,256,128]{2,1,0:T(8,128)S(1)} %maximum_select_fusion.2), channel_id=1, source_target_pairs={{0,1},{1,0},{2,3},{3,2},{4,5},{5,4},{6,7},{7,6},{8,9},{9,8},{10,11... | collective-permute-start | bytes 786440 | tf_op jit(solution)/shard_map/ppermute | solution.py:62
  51.7 6.6 %copy-start.1 = (f32[32,128]{1,0:T(8,128)S(1)}, f32[32,128]{1,0:T(8,128)}, u32[]{:S(2)}) copy-start(f32[32,128]{1,0:T(8,128)} %param.10) | copy-start | bytes 49156
  53.2 12.5 %copy-start = (f32[64,128]{1,0:T(8,128)S(1)}, f32[64,128]{1,0:T(8,128)}, u32[]{:S(2)}) copy-start(f32[64,128]{1,0:T(8,128)} %param.6) | copy-start | bytes 98308
  59.7 1.3 collective-permute-start.7
  61.6 4.0 %collective-permute-start.8 = (f32[72,128]{1,0:T(8,128)S(1)}, f32[72,128]{1,0:T(8,128)S(1)}, u32[]{:S(2)}, u32[]{:S(2)}) collective-permute-start(f32[72,128]{1,0:T(8,128)S(1)} %pad_add_fusion.1), channel_id=1, source_target_pairs={{0,2},{1,3},{2,0},{3,1},{4,6},{5,7},{6,4},{7,5},{8,10},{9,11},{10,... | collective-permute-start | bytes 110600 | tf_op jit(solution)/shard_map/ppermute | solution.py:19
  82.3 1.6 %collective-permute-start.9 = (f32[2,256,128]{2,1,0:T(8,128)S(1)}, f32[2,256,128]{2,1,0:T(8,128)S(1)}, u32[]{:S(2)}, u32[]{:S(2)}) collective-permute-start(f32[2,256,128]{2,1,0:T(8,128)S(1)} %dynamic-slice_bitcast_fusion), channel_id=1, source_target_pairs={{0,1},{1,0},{2,3},{3,2},{4,5},{5,4},{6,7},{7,6},{8,9},{9,8},{10,11... | collective-permute-start | bytes 786440 | tf_op jit(solution)/shard_map/ppermute | solution.py:49
  84.0 5.6 %collective-permute-start.10 = (f32[256,128]{1,0:T(8,128)S(1)}, f32[256,128]{1,0:T(8,128)S(1)}, u32[]{:S(2)}, u32[]{:S(2)}) collective-permute-start(f32[256,128]{1,0:T(8,128)S(1)} %dynamic-slice_bitcast_fusion.2), channel_id=1, source_target_pairs={{0,2},{1,3},{2,0},{3,1},{4,6},{5,7},{6,4},{7,5},{8,10},{9,11},{10,... | collective-permute-start | bytes 393224 | tf_op jit(solution)/shard_map/ppermute | solution.py:49
  89.6 5.0 %collective-permute-start.11 = (f32[256,128]{1,0:T(8,128)S(1)}, f32[256,128]{1,0:T(8,128)S(1)}, u32[]{:S(2)}, u32[]{:S(2)}) collective-permute-start(f32[256,128]{1,0:T(8,128)S(1)} %bitcast_add_fusion.2), channel_id=1, source_target_pairs={{0,4},{4,0},{8,12},{12,8},{16,20},{20,16},{24,28},{28,24},{1,5},{5... | collective-permute-start | bytes 393224 | tf_op jit(solution)/shard_map/ppermute | solution.py:19
  94.7 5.0 %collective-permute-start.12 = (f32[256,128]{1,0:T(8,128)S(1)}, f32[256,128]{1,0:T(8,128)S(1)}, u32[]{:S(2)}, u32[]{:S(2)}) collective-permute-start(f32[256,128]{1,0:T(8,128)S(1)} %add.383), channel_id=1, source_target_pairs={{0,8},{4,12},{8,0},{12,4},{16,24},{20,28},{24,16},{28,20},{1,9},{5... | collective-permute-start | bytes 393224 | tf_op jit(solution)/shard_map/ppermute | solution.py:19
  99.7 7.3 %collective-permute-start.13 = (f32[256,128]{1,0:T(8,128)S(1)}, f32[256,128]{1,0:T(8,128)S(1)}, u32[]{:S(2)}, u32[]{:S(2)}) collective-permute-start(f32[256,128]{1,0:T(8,128)S(1)} %add.384), channel_id=1, source_target_pairs={{0,16},{4,20},{8,24},{12,28},{16,0},{20,4},{24,8},{28,12},{1,17},{... | collective-permute-start | bytes 393224 | tf_op jit(solution)/shard_map/ppermute | solution.py:19
  107.1 5.0 %collective-permute-start.14 = (f32[256,128]{1,0:T(8,128)S(1)}, f32[256,128]{1,0:T(8,128)S(1)}, u32[]{:S(2)}, u32[]{:S(2)}) collective-permute-start(f32[256,128]{1,0:T(8,128)S(1)} %multiply_subtract_fusion), channel_id=1, source_target_pairs={{0,2},{1,3},{2,0},{3,1},{4,6},{5,7},{6,4},{7,5},{8,10},{9,11},{10,... | collective-permute-start | bytes 393224 | tf_op jit(solution)/shard_map/ppermute | solution.py:62
  112.2 1.6 %collective-permute-start.15 = (f32[2,256,128]{2,1,0:T(8,128)S(1)}, f32[2,256,128]{2,1,0:T(8,128)S(1)}, u32[]{:S(2)}, u32[]{:S(2)}) collective-permute-start(f32[2,256,128]{2,1,0:T(8,128)S(1)} %maximum_select_fusion.4), channel_id=1, source_target_pairs={{0,1},{1,0},{2,3},{3,2},{4,5},{5,4},{6,7},{7,6},{8,9},{9,8},{10,11... | collective-permute-start | bytes 786440 | tf_op jit(solution)/shard_map/ppermute | solution.py:62
  120.2 1.3 collective-permute-start.16
  122.2 4.0 %collective-permute-start.17 = (f32[72,128]{1,0:T(8,128)S(1)}, f32[72,128]{1,0:T(8,128)S(1)}, u32[]{:S(2)}, u32[]{:S(2)}) collective-permute-start(f32[72,128]{1,0:T(8,128)S(1)} %pad_add_fusion), channel_id=1, source_target_pairs={{0,2},{1,3},{2,0},{3,1},{4,6},{5,7},{6,4},{7,5},{8,10},{9,11},{10,... | collective-permute-start | bytes 110600 | tf_op jit(solution)/shard_map/ppermute | solution.py:19
  129.1 9.6 %all-to-all-start.2 = ((f32[8,1,128]{2,1,0:T(1,128)}), f32[8,1,128]{2,1,0:T(1,128)S(1)}, u32[]{:S(2)}, u32[]{:S(2)}) async-start(f32[8,1,128]{2,1,0:T(1,128)} %broadcast_in_dim.22), calls=%async_computation.2 | async-start | bytes 8192 | tf_op jit(solution)/shard_map/all_to_all | solution.py:27

commit v5 on v4

--- a/solution.py
+++ b/solution.py
@@ -56,47 +56,57 @@
     if n & (n - 1):
         return lax.all_gather(x, axis, axis=0, tiled=True)
     me = lax.axis_index(axis)
-    rows = x.shape[0]
+    rows, trailing = x.shape[0], x.shape[1:]
     k = n // 2
+    place = 0
     while k >= 1:
         other = lax.ppermute(x, axis, [(i, i ^ k) for i in range(n)])
         upper = (me // k) % 2 == 1
-        place = x.ndim - 2
         x = jnp.where(upper, jnp.stack([other, x], place), jnp.stack([x, other], place))
+        place += 1
         k //= 2
-    return x.reshape((n * rows,) + x.shape[-1:])
+    return x.reshape((n * rows,) + trailing)
 
 
 def local(travel_times, sensitivity, tile_blocks, face_blocks, face_weights, face_count):
     model_rows = NB_DEV * lax.axis_size("region")
     region = lax.axis_index("region")
-    live_mask = (jnp.arange(face_blocks.shape[0]) < face_count[0]).astype(jnp.float32)
+    n_faces = face_blocks.shape[0]
+    group_blocks = doubling_gather(face_blocks, "region")
+    group_weights = doubling_gather(face_weights, "region")
+    group_count = doubling_gather(face_count, "region")
+    group_rows = jnp.arange(group_blocks.shape[0])
+    group_live = (group_rows % n_faces < group_count[group_rows // n_faces]).astype(jnp.float32)
+    group_scale = smooth_weight * group_weights * group_live[:, None]
+    live_mask = (jnp.arange(n_faces) < face_count[0]).astype(jnp.float32)
     face_scale = smooth_weight * face_weights * live_mask[:, None]
     first_block = face_blocks[:, 0]
     second_block = face_blocks[:, 1]
     flat_blocks = tile_blocks.reshape(-1)
     n_tiles = travel_times.shape[0]
+    n_slots = flat_blocks.shape[0]
     columns = jnp.arange(model_rows, dtype=jnp.int32)[None, :]
-    select = jnp.concatenate(
-        [
-            (flat_blocks[:, None] == columns).astype(jnp.float32),
-            (first_block[:, None] == columns).astype(jnp.float32)
-            - (second_block[:, None] == columns).astype(jnp.float32),
-        ],
-        0,
+
+    def hits(blocks):
+        return (blocks[:, None] == columns).astype(jnp.float32)
+
+    own_select = jnp.concatenate(
+        [hits(flat_blocks), hits(first_block) - hits(second_block)], 0
     )
-    select_half = select.astype(jnp.bfloat16)
-    n_slots = flat_blocks.shape[0]
+    group_select = jnp.concatenate(
+        [hits(flat_blocks), hits(group_blocks[:, 0]) - hits(group_blocks[:, 1])], 0
+    ).astype(jnp.bfloat16)
 
-    def transposed_part(left_rays, left_faces):
+    def transposed_part(left_rays, group_faces):
         rays_half = left_rays.astype(jnp.bfloat16)
         contrib = jnp.einsum(
             "tsrb,tr->tsb", sensitivity, rays_half, preferred_element_type=jnp.float32
         )
         contrib_rows = contrib.reshape(-1, contrib.shape[-1])
+        left_faces = lax.dynamic_slice_in_dim(group_faces, region * n_faces, n_faces, 0)
         face_term = face_scale * left_faces
         partials = lax.dot_general(
-            select,
+            own_select,
             jnp.concatenate([contrib_rows, face_term], 0),
             (((0,), (0,)), ((), ())),
             precision=lax.Precision.HIGHEST,
@@ -113,7 +123,7 @@
 
     beta_value = jnp.sqrt(scalar_sum(jnp.sum(travel_times * travel_times), "dp"))
     left_rays = travel_times / beta_value
-    left_faces = jnp.zeros(face_weights.shape, jnp.float32)
+    left_faces = jnp.zeros(group_weights.shape, jnp.float32)
     raw = transposed_part(left_rays, left_faces)
     full_model, right_vector, alpha_value = normalized_field(raw)
     direction = right_vector
@@ -122,21 +132,17 @@
     rho_bar = alpha_value
     for iteration in range(ITERS):
         full_half = full_model.astype(jnp.bfloat16)
-        rows = jnp.dot(select_half, full_half, preferred_element_type=jnp.float32)
+        rows = jnp.dot(group_select, full_half, preferred_element_type=jnp.float32)
         picked = rows[:n_slots].astype(jnp.bfloat16).reshape(tile_blocks.shape + rows.shape[-1:])
         partial_value = jnp.einsum(
             "tsrb,tsb->tr", sensitivity, picked, preferred_element_type=jnp.float32
         )
-        face_pred = face_scale * rows[n_slots:]
+        ray_pred = butterfly_sum(partial_value, "region")
+        face_pred = group_scale * rows[n_slots:]
         left_faces = face_pred - alpha_value * left_faces
         face_sq = jnp.sum(left_faces * left_faces)
-        packed = jnp.concatenate(
-            [partial_value, jnp.broadcast_to(face_sq, (8, partial_value.shape[1]))], 0
-        )
-        packed = butterfly_sum(packed, "region")
-        ray_pred = packed[:n_tiles]
         left_rays = ray_pred - alpha_value * left_rays
-        beta_sq = scalar_sum(jnp.sum(left_rays * left_rays) + packed[n_tiles, 0], "dp")
+        beta_sq = scalar_sum(jnp.sum(left_rays * left_rays) + face_sq, "dp")
         beta_value = jnp.sqrt(beta_sq)
         left_rays = left_rays / beta_value
         left_faces = left_faces / beta_value

time: 140 us -> 142 us (1.014)
  blocking collectives: 9.2 us -> 0 us
  waiting for transfers between devices: 68.4 us -> 75 us
  other arithmetic: 9.69 us -> 13 us
  starting transfers between devices: 24.3 us -> 25.9 us
    all_to_all x1 -> x0, blocking collectives: 9.2 us -> none  [scalar_sum(): got = lax.all_to_all(spread, axis, 0, 0, tiled=False)]
    all_to_all x2 -> x3, waiting for transfers between devices: 9.16 us -> 15.5 us  [scalar_sum(): got = lax.all_to_all(spread, axis, 0, 0, tiled=False)]
    all_to_all x2 -> x3, starting transfers between devices: 10.6 us -> 13.9 us  [scalar_sum(): got = lax.all_to_all(spread, axis, 0, 0, tiled=False)]
    ppermute x4 -> x10, waiting for transfers between devices: 9.92 us -> 12.7 us  [doubling_gather(): other = lax.ppermute(x, axis, [(i, i ^ k) for i in range(n)])]
    convert_element_type x2, other arithmetic: 0.11 us -> 2.59 us  [the longest x1 2.59 us: local(): (group_rows % n_faces < group_count[group_rows // n_faces]).astype(jnp.fl...]
    ppermute x10, waiting for transfers between devices: 38.2 us -> 35.8 us  [butterfly_sum(): x = x + lax.ppermute(x, axis, [(i, i ^ k) for i in range(n)])]
    ppermute x4 -> x10, starting transfers between devices: 3.25 us -> 5.56 us  [doubling_gather(): other = lax.ppermute(x, axis, [(i, i ^ k) for i in range(n)])]
    ppermute x10, starting transfers between devices: 7.2 us -> 5.09 us  [butterfly_sum(): x = x + lax.ppermute(x, axis, [(i, i ^ k) for i in range(n)])]
  transfers between devices with their start and end apart: 20 -> 27, of which waited for: 20 -> 21; matrix products, arithmetic and copies ran while one was open for 2% -> 10% of each run, Pallas kernels for 0% -> 0%
where the time goes in v5:
time: 142 us; the launch traced here: 141 us
  waiting for transfers between devices  75 us (53%)
  starting transfers between devices  25.9 us (18%)
  matrix products  16.7 us (12%)
  other arithmetic  13 us (9%)
  between operations  5.69 us (4%)
  local copies, waits for them, and re-layouts  5.08 us (4%)
    ppermute x10, waiting for transfers between devices, butterfly_sum(): x = x + lax.ppermute(x, axis, [(i, i ^ k) for i in range(n)])  35.8 us
    all_to_all x3, waiting for transfers between devices, scalar_sum(): got = lax.all_to_all(spread, axis, 0, 0, tiled=False)  15.5 us
    all_to_all x3, starting transfers between devices, scalar_sum(): got = lax.all_to_all(spread, axis, 0, 0, tiled=False)  13.9 us
    ppermute x10, waiting for transfers between devices, doubling_gather(): other = lax.ppermute(x, axis, [(i, i ^ k) for i in range(n)])  12.7 us
    ppermute x4, waiting for transfers between devices, halving_scatter(): x = keep + lax.ppermute(send, axis, [(i, i ^ k) for i in range(n)])  11 us
    dot_general x2, matrix products, local(): jnp.einsum('tsrb,tsb->tr', sensitivity, picked, preferred_element_type=jn...  6.74 us
    dot_general x2, matrix products, transposed_part(): jnp.einsum('tsrb,tr->tsb', sensitivity, rays_half, preferred_element_type...  5.68 us
    ppermute x10, starting transfers between devices, doubling_gather(): other = lax.ppermute(x, axis, [(i, i ^ k) for i in range(n)])  5.56 us
  transfers between devices with their start and end apart: 27, of which 21 were waited for; matrix products, arithmetic and copies ran while one was open for 10% of the time, Pallas kernels for 0%

profile of v5, /device:TPU:0, one launch (start us, length us, event | category | flops | bytes accessed | tf_op | source)
XLA Modules:
  0.0 141.3 jit_solution(6674043241484741667)
XLA Ops:
  0.0 1.4 multiply_reduce_fusion.5
  1.4 1.1 broadcast_in_dim.6
  2.5 7.3 %all-to-all-start = ((f32[8,1,128]{2,1,0:T(1,128)}), f32[8,1,128]{2,1,0:T(1,128)S(1)}, u32[]{:S(2)}, u32[]{:S(2)}) async-start(f32[8,1,128]{2,1,0:T(1,128)} %broadcast_in_dim.6), calls=%async_computation | async-start | bytes 8192 | tf_op jit(solution)/shard_map/all_to_all | solution.py:27
  9.8 0.8 slice_bitcast_fusion.3
  10.5 0.8 copy.11
  12.3 0.8 multiply_multiply_fusion
  13.1 3.0 %all-to-all-done = f32[8,1,128]{2,1,0:T(1,128)S(1)} async-done(((f32[8,1,128]{2,1,0:T(1,128)}), f32[8,1,128]{2,1,0:T(1,128)S(1)}, u32[]{:S(2)}, u32[]{:S(2)}) %all-to-all-start) | async-done | bytes 4128 | tf_op jit(solution)/shard_map/all_to_all | solution.py:27
  16.3 0.8 convert_bitcast_fusion.1
  17.0 2.8 %fusion.26 = f32[64,1,2,128]{3,1,2,0:T(1,128)S(1)} fusion(bf16[64,2,128,128]{3,2,1,0:T(8,128)(2,1)} %param.7, bf16[64,128,1,1]{1,0,2,3:T(8,128)(2,1)S(1)} %convert_bitcast_fusion.1), kind=kOutput, calls=%fused_computation.62 | convolution fusion | flops 4194304 | bytes 4276224 | tf_op jit(solution)/shard_map/tsrb,tr->tsb/dot_general | solution.py:102
  19.9 1.9 %fusion.1 = f32[1024,128]{1,0:T(8,128)S(1)} fusion(f32[32,1024]{1,0:T(8,128)S(1)} %convert_subtract_fusion, f32[128,1024]{1,0:T(8,128)S(1)} %get-tuple-element.16, f32[32,128]{1,0:T(8,128)S(1)} %multiply_multiply_fusion, f32[128,128]{1,0:T(8,128)S(1)} %bitcast.145), kind=kOutput, calls=%fused_computation.2 | convolution fusion | flops 251842560 | bytes 1261568 | tf_op jit(solution)/shard_map/dot_general | solution.py:108
  21.9 1.6 %collective-permute-start.7 = (s32[32,2]{0,1:T(2,128)S(1)}, s32[32,2]{0,1:T(2,128)S(1)}, u32[]{:S(2)}, u32[]{:S(2)}) collective-permute-start(s32[32,2]{0,1:T(2,128)S(1)} %copy-done.2), channel_id=1, source_target_pairs={{0,2},{1,3},{2,0},{3,1},{4,6},{5,7},{6,4},{7,5},{8,10},{9,11},{10,... | collective-permute-start | bytes 776 | tf_op jit(solution)/shard_map/ppermute | solution.py:63
  24.0 1.5 %collective-permute-start.11 = (f32[32,128]{1,0:T(8,128)S(1)}, f32[32,128]{1,0:T(8,128)S(1)}, u32[]{:S(2)}, u32[]{:S(2)}) collective-permute-start(f32[32,128]{1,0:T(8,128)S(1)} %copy-done.1), channel_id=1, source_target_pairs={{0,2},{1,3},{2,0},{3,1},{4,6},{5,7},{6,4},{7,5},{8,10},{9,11},{10,... | collective-permute-start | bytes 49160 | tf_op jit(solution)/shard_map/ppermute | solution.py:63
  25.4 1.6 %collective-permute-done.13 = s32[1]{0:T(128)} collective-permute-done((s32[1]{0:T(128)}, s32[1]{0:T(128)}, u32[]{:S(2)}, u32[]{:S(2)}) %collective-permute-start.13) | collective-permute-done | bytes 36 | tf_op jit(solution)/shard_map/ppermute | solution.py:63
  27.0 0.8 broadcast_select_fusion.2
  27.8 0.8 broadcast_select_fusion.1
  29.5 0.7 fusion.36
  30.1 4.5 %collective-permute-done.1 = f32[256,128]{1,0:T(8,128)S(1)} collective-permute-done((f32[256,128]{1,0:T(8,128)S(1)}, f32[256,128]{1,0:T(8,128)S(1)}, u32[]{:S(2)}, u32[]{:S(2)}) %collective-permute-start.1) | collective-permute-done | bytes 131104 | tf_op jit(solution)/shard_map/ppermute | solution.py:49
  35.3 2.6 %compare_convert_fusion = f32[128]{0:T(128)S(1)} fusion(s32[]{:T(128)} %bitcast.43, s32[]{:T(128)} %bitcast.44, s32[]{:T(128)} %bitcast.46, s32[]{:T(128)} %bitcast.45), kind=kLoop, calls=%fused_computation.82 | loop fusion | flops 3200 | bytes 528 | tf_op jit(solution)/shard_map/convert_element_type | solution.py:79
  38.0 1.9 %collective-permute-done.2 = f32[256,128]{1,0:T(8,128)S(1)} collective-permute-done((f32[256,128]{1,0:T(8,128)S(1)}, f32[256,128]{1,0:T(8,128)S(1)}, u32[]{:S(2)}, u32[]{:S(2)}) %collective-permute-start.2) | collective-permute-done | bytes 131104 | tf_op jit(solution)/shard_map/ppermute | solution.py:19
  40.6 4.3 %collective-permute-done.3 = f32[256,128]{1,0:T(8,128)S(1)} collective-permute-done((f32[256,128]{1,0:T(8,128)S(1)}, f32[256,128]{1,0:T(8,128)S(1)}, u32[]{:S(2)}, u32[]{:S(2)}) %collective-permute-start.3) | collective-permute-done | bytes 131104 | tf_op jit(solution)/shard_map/ppermute | solution.py:19
  44.9 0.6 collective-permute-start.4
  45.5 6.7 %collective-permute-done.4 = f32[256,128]{1,0:T(8,128)S(1)} collective-permute-done((f32[256,128]{1,0:T(8,128)S(1)}, f32[256,128]{1,0:T(8,128)S(1)}, u32[]{:S(2)}, u32[]{:S(2)}) %collective-permute-start.4) | collective-permute-done | bytes 131104 | tf_op jit(solution)/shard_map/ppermute | solution.py:19
  53.0 4.3 %collective-permute-done.5 = f32[256,128]{1,0:T(8,128)S(1)} collective-permute-done((f32[256,128]{1,0:T(8,128)S(1)}, f32[256,128]{1,0:T(8,128)S(1)}, u32[]{:S(2)}, u32[]{:S(2)}) %collective-permute-start.5) | collective-permute-done | bytes 131104 | tf_op jit(solution)/shard_map/ppermute | solution.py:63
  58.0 0.9 collective-permute-done.6
  58.9 0.7 multiply_reduce_fusion.1
  60.7 3.4 %fusion.22 = f32[64,1,128,1]{2,1,3,0:T(1,128)S(1)} fusion(bf16[64,2,128,128]{3,2,1,0:T(8,128)(2,1)} %param.7, bf16[64,2,128,1]{2,1,0,3:T(2,128)(2,1)S(1)} %bitcast.142), kind=kOutput, calls=%fused_computation.55 | convolution fusion | flops 4194304 | bytes 4259840 | tf_op jit(solution)/shard_map/tsrb,tsb->tr/dot_general | solution.py:137
  64.3 1.1 collective-permute-done.9
  65.9 0.8 multiply_reduce_fusion.2
  66.6 2.6 %collective-permute-done.10 = f32[64,128]{1,0:T(8,128)S(1)} collective-permute-done((f32[64,128]{1,0:T(8,128)S(1)}, f32[64,128]{1,0:T(8,128)S(1)}, u32[]{:S(2)}, u32[]{:S(2)}) %collective-permute-start.10) | collective-permute-done | bytes 32800 | tf_op jit(solution)/shard_map/ppermute | solution.py:19
  71.8 3.3 %all-to-all-start.1 = ((f32[8,1,128]{2,1,0:T(1,128)}), f32[8,1,128]{2,1,0:T(1,128)S(1)}, u32[]{:S(2)}, u32[]{:S(2)}) async-start(f32[8,1,128]{2,1,0:T(1,128)} %broadcast_in_dim.7), calls=%async_computation.1 | async-start | bytes 8192 | tf_op jit(solution)/shard_map/all_to_all | solution.py:27
  75.1 6.3 %all-to-all-done.1 = f32[8,1,128]{2,1,0:T(1,128)S(1)} async-done(((f32[8,1,128]{2,1,0:T(1,128)}), f32[8,1,128]{2,1,0:T(1,128)S(1)}, u32[]{:S(2)}, u32[]{:S(2)}) %all-to-all-start.1) | async-done | bytes 4128 | tf_op jit(solution)/shard_map/all_to_all | solution.py:27
  81.7 2.8 %fusion.24 = f32[64,1,2,128]{3,1,2,0:T(1,128)S(1)} fusion(bf16[64,2,128,128]{3,2,1,0:T(8,128)(2,1)} %param.7, bf16[64,128,1,1]{1,0,2,3:T(8,128)(2,1)S(1)} %convert_bitcast_fusion), kind=kOutput, calls=%fused_computation.60 | convolution fusion | flops 4194304 | bytes 4276224 | tf_op jit(solution)/shard_map/tsrb,tr->tsb/dot_general | solution.py:102
  84.6 1.9 %fusion = f32[1024,128]{1,0:T(8,128)S(1)} fusion(f32[32,1024]{1,0:T(8,128)S(1)} %convert_subtract_fusion, f32[128,1024]{1,0:T(8,128)S(1)} %get-tuple-element.16, f32[32,128]{1,0:T(8,128)S(1)} %dynamic-slice_multiply_fusion, f32[128,128]{1,0:T(8,128)S(1)} %bitcast.144), kind=kOutput, calls=%fused_computation.1 | convolution fusion | flops 251842560 | bytes 1261568 | tf_op jit(solution)/shard_map/dot_general | solution.py:108
  86.5 1.5 %collective-permute-done.15 = f32[2,256,128]{2,1,0:T(8,128)S(1)} collective-permute-done((f32[2,256,128]{2,1,0:T(8,128)S(1)}, f32[2,256,128]{2,1,0:T(8,128)S(1)}, u32[]{:S(2)}, u32[]{:S(2)}) %collective-permute-start.15) | collective-permute-done | bytes 262176 | tf_op jit(solution)/shard_map/ppermute | solution.py:49
  88.7 5.0 %collective-permute-done.16 = f32[256,128]{1,0:T(8,128)S(1)} collective-permute-done((f32[256,128]{1,0:T(8,128)S(1)}, f32[256,128]{1,0:T(8,128)S(1)}, u32[]{:S(2)}, u32[]{:S(2)}) %collective-permute-start.16) | collective-permute-done | bytes 131104 | tf_op jit(solution)/shard_map/ppermute | solution.py:49
  94.4 4.4 %collective-permute-done.17 = f32[256,128]{1,0:T(8,128)S(1)} collective-permute-done((f32[256,128]{1,0:T(8,128)S(1)}, f32[256,128]{1,0:T(8,128)S(1)}, u32[]{:S(2)}, u32[]{:S(2)}) %collective-permute-start.17) | collective-permute-done | bytes 131104 | tf_op jit(solution)/shard_map/ppermute | solution.py:19
  99.4 4.4 %collective-permute-done.18 = f32[256,128]{1,0:T(8,128)S(1)} collective-permute-done((f32[256,128]{1,0:T(8,128)S(1)}, f32[256,128]{1,0:T(8,128)S(1)}, u32[]{:S(2)}, u32[]{:S(2)}) %collective-permute-start.18) | collective-permute-done | bytes 131104 | tf_op jit(solution)/shard_map/ppermute | solution.py:19
  104.5 6.7 %collective-permute-done.19 = f32[256,128]{1,0:T(8,128)S(1)} collective-permute-done((f32[256,128]{1,0:T(8,128)S(1)}, f32[256,128]{1,0:T(8,128)S(1)}, u32[]{:S(2)}, u32[]{:S(2)}) %collective-permute-start.19) | collective-permute-done | bytes 131104 | tf_op jit(solution)/shard_map/ppermute | solution.py:19
  111.8 4.4 %collective-permute-done.20 = f32[256,128]{1,0:T(8,128)S(1)} collective-permute-done((f32[256,128]{1,0:T(8,128)S(1)}, f32[256,128]{1,0:T(8,128)S(1)}, u32[]{:S(2)}, u32[]{:S(2)}) %collective-permute-start.20) | collective-permute-done | bytes 131104 | tf_op jit(solution)/shard_map/ppermute | solution.py:63
  116.4 1.5 %collective-permute-done.21 = f32[2,256,128]{2,1,0:T(8,128)S(1)} collective-permute-done((f32[2,256,128]{2,1,0:T(8,128)S(1)}, f32[2,256,128]{2,1,0:T(8,128)S(1)}, u32[]{:S(2)}, u32[]{:S(2)}) %collective-permute-start.21) | collective-permute-done | bytes 262176 | tf_op jit(solution)/shard_map/ppermute | solution.py:63
  117.9 0.7 multiply_reduce_fusion
  119.7 3.4 %fusion.20 = f32[64,1,128,1]{2,1,3,0:T(1,128)S(1)} fusion(bf16[64,2,128,128]{3,2,1,0:T(8,128)(2,1)} %param.7, bf16[64,2,128,1]{2,1,0,3:T(2,128)(2,1)S(1)} %bitcast.143), kind=kOutput, calls=%fused_computation.53 | convolution fusion | flops 4194304 | bytes 4259840 | tf_op jit(solution)/shard_map/tsrb,tsb->tr/dot_general | solution.py:137
  123.2 1.1 collective-permute-done.22
  124.8 0.8 fusion.18
  125.6 2.6 %collective-permute-done.23 = f32[64,128]{1,0:T(8,128)S(1)} collective-permute-done((f32[64,128]{1,0:T(8,128)S(1)}, f32[64,128]{1,0:T(8,128)S(1)}, u32[]{:S(2)}, u32[]{:S(2)}) %collective-permute-start.23) | collective-permute-done | bytes 32800 | tf_op jit(solution)/shard_map/ppermute | solution.py:19
  130.7 3.3 %all-to-all-start.2 = ((f32[8,1,128]{2,1,0:T(1,128)}), f32[8,1,128]{2,1,0:T(1,128)S(1)}, u32[]{:S(2)}, u32[]{:S(2)}) async-start(f32[8,1,128]{2,1,0:T(1,128)} %broadcast_in_dim.16), calls=%async_computation.2 | async-start | bytes 8192 | tf_op jit(solution)/shard_map/all_to_all | solution.py:27
  134.3 6.1 %all-to-all-done.2 = f32[8,1,128]{2,1,0:T(1,128)S(1)} async-done(((f32[8,1,128]{2,1,0:T(1,128)}), f32[8,1,128]{2,1,0:T(1,128)S(1)}, u32[]{:S(2)}, u32[]{:S(2)}) %all-to-all-start.2) | async-done | bytes 4128 | tf_op jit(solution)/shard_map/all_to_all | solution.py:27
  140.6 0.7 multiply_add_fusion
  (87 shorter events, 12.9 us)
Async XLA Ops:
  0.0 21.9 %copy-start.2 = (s32[32,2]{0,1:T(2,128)S(1)}, s32[32,2]{0,1:T(2,128)}, u32[]{:S(2)}) copy-start(s32[32,2]{0,1:T(2,128)} %param.9) | copy-start | bytes 772
  0.0 24.0 %copy-start.1 = (f32[32,128]{1,0:T(8,128)S(1)}, f32[32,128]{1,0:T(8,128)}, u32[]{:S(2)}) copy-start(f32[32,128]{1,0:T(8,128)} %param.10) | copy-start | bytes 49156
  2.5 13.7 %all-to-all-start = ((f32[8,1,128]{2,1,0:T(1,128)}), f32[8,1,128]{2,1,0:T(1,128)S(1)}, u32[]{:S(2)}, u32[]{:S(2)}) async-start(f32[8,1,128]{2,1,0:T(1,128)} %broadcast_in_dim.6), calls=%async_computation | async-start | bytes 8192 | tf_op jit(solution)/shard_map/all_to_all | solution.py:27
  21.8 6.8 %collective-permute-start = (f32[2,256,128]{2,1,0:T(8,128)S(1)}, f32[2,256,128]{2,1,0:T(8,128)S(1)}, u32[]{:S(2)}, u32[]{:S(2)}) collective-permute-start(f32[2,256,128]{2,1,0:T(8,128)S(1)} %dynamic-slice_bitcast_fusion.1), channel_id=1, source_target_pairs={{0,1},{1,0},{2,3},{3,2},{4,5},{5,4},{6,7},{7,6},{8,9},{9,8},{10,11... | collective-permute-start | bytes 786440 | tf_op jit(solution)/shard_map/ppermute | solution.py:49
  21.9 16.0 %collective-permute-start.7 = (s32[32,2]{0,1:T(2,128)S(1)}, s32[32,2]{0,1:T(2,128)S(1)}, u32[]{:S(2)}, u32[]{:S(2)}) collective-permute-start(s32[32,2]{0,1:T(2,128)S(1)} %copy-done.2), channel_id=1, source_target_pairs={{0,2},{1,3},{2,0},{3,1},{4,6},{5,7},{6,4},{7,5},{8,10},{9,11},{10,... | collective-permute-start | bytes 776 | tf_op jit(solution)/shard_map/ppermute | solution.py:63
  23.4 3.6 %collective-permute-start.13 = (s32[1]{0:T(128)}, s32[1]{0:T(128)}, u32[]{:S(2)}, u32[]{:S(2)}) collective-permute-start(s32[1]{0:T(128)} %param.11), channel_id=1, source_target_pairs={{0,2},{1,3},{2,0},{3,1},{4,6},{5,7},{6,4},{7,5},{8,10},{9,11},{10,... | collective-permute-start | bytes 20 | tf_op jit(solution)/shard_map/ppermute | solution.py:63
  24.0 33.4 %collective-permute-start.11 = (f32[32,128]{1,0:T(8,128)S(1)}, f32[32,128]{1,0:T(8,128)S(1)}, u32[]{:S(2)}, u32[]{:S(2)}) collective-permute-start(f32[32,128]{1,0:T(8,128)S(1)} %copy-done.1), channel_id=1, source_target_pairs={{0,2},{1,3},{2,0},{3,1},{4,6},{5,7},{6,4},{7,5},{8,10},{9,11},{10,... | collective-permute-start | bytes 49160 | tf_op jit(solution)/shard_map/ppermute | solution.py:63
  27.8 1.5 %collective-permute-start.14 = (s32[2,1]{0,1:T(1,128)S(1)}, s32[2,1]{0,1:T(1,128)S(1)}, u32[]{:S(2)}, u32[]{:S(2)}) collective-permute-start(s32[2,1]{0,1:T(1,128)S(1)} %broadcast_select_fusion.2), channel_id=1, source_target_pairs={{0,1},{1,0},{2,3},{3,2},{4,5},{5,4},{6,7},{7,6},{8,9},{9,8},{10,11... | collective-permute-start | bytes 32 | tf_op jit(solution)/shard_map/ppermute | solution.py:63
  28.7 6.0 %collective-permute-start.1 = (f32[256,128]{1,0:T(8,128)S(1)}, f32[256,128]{1,0:T(8,128)S(1)}, u32[]{:S(2)}, u32[]{:S(2)}) collective-permute-start(f32[256,128]{1,0:T(8,128)S(1)} %dynamic-slice_bitcast_fusion.3), channel_id=1, source_target_pairs={{0,2},{1,3},{2,0},{3,1},{4,6},{5,7},{6,4},{7,5},{8,10},{9,11},{10,... | collective-permute-start | bytes 393224 | tf_op jit(solution)/shard_map/ppermute | solution.py:49
  34.6 5.2 %collective-permute-start.2 = (f32[256,128]{1,0:T(8,128)S(1)}, f32[256,128]{1,0:T(8,128)S(1)}, u32[]{:S(2)}, u32[]{:S(2)}) collective-permute-start(f32[256,128]{1,0:T(8,128)S(1)} %bitcast_add_fusion.3), channel_id=1, source_target_pairs={{0,4},{4,0},{8,12},{12,8},{16,20},{20,16},{24,28},{28,24},{1,5},{5... | collective-permute-start | bytes 393224 | tf_op jit(solution)/shard_map/ppermute | solution.py:19
  37.9 2.6 %collective-permute-start.8 = (s32[2,32,2]{1,2,0:T(2,128)S(1)}, s32[2,32,2]{1,2,0:T(2,128)S(1)}, u32[]{:S(2)}, u32[]{:S(2)}) collective-permute-start(s32[2,32,2]{1,2,0:T(2,128)S(1)} %add_select_fusion.1), channel_id=1, source_target_pairs={{0,1},{1,0},{2,3},{3,2},{4,5},{5,4},{6,7},{7,6},{8,9},{9,8},{10,11... | collective-permute-start | bytes 1544 | tf_op jit(solution)/shard_map/ppermute | solution.py:63
  39.8 5.0 %collective-permute-start.3 = (f32[256,128]{1,0:T(8,128)S(1)}, f32[256,128]{1,0:T(8,128)S(1)}, u32[]{:S(2)}, u32[]{:S(2)}) collective-permute-start(f32[256,128]{1,0:T(8,128)S(1)} %add.401), channel_id=1, source_target_pairs={{0,8},{4,12},{8,0},{12,4},{16,24},{20,28},{24,16},{28,20},{1,9},{5... | collective-permute-start | bytes 393224 | tf_op jit(solution)/shard_map/ppermute | solution.py:19
  44.9 7.3 %collective-permute-start.4 = (f32[256,128]{1,0:T(8,128)S(1)}, f32[256,128]{1,0:T(8,128)S(1)}, u32[]{:S(2)}, u32[]{:S(2)}) collective-permute-start(f32[256,128]{1,0:T(8,128)S(1)} %add.402), channel_id=1, source_target_pairs={{0,16},{4,20},{8,24},{12,28},{16,0},{20,4},{24,8},{28,12},{1,17},{... | collective-permute-start | bytes 393224 | tf_op jit(solution)/shard_map/ppermute | solution.py:19
  52.2 5.0 %collective-permute-start.5 = (f32[256,128]{1,0:T(8,128)S(1)}, f32[256,128]{1,0:T(8,128)S(1)}, u32[]{:S(2)}, u32[]{:S(2)}) collective-permute-start(f32[256,128]{1,0:T(8,128)S(1)} %add.403), channel_id=1, source_target_pairs={{0,2},{1,3},{2,0},{3,1},{4,6},{5,7},{6,4},{7,5},{8,10},{9,11},{10,... | collective-permute-start | bytes 393224 | tf_op jit(solution)/shard_map/ppermute | solution.py:63
  57.3 1.6 %collective-permute-start.6 = (f32[2,256,128]{2,1,0:T(8,128)S(1)}, f32[2,256,128]{2,1,0:T(8,128)S(1)}, u32[]{:S(2)}, u32[]{:S(2)}) collective-permute-start(f32[2,256,128]{2,1,0:T(8,128)S(1)} %maximum_select_fusion.2), channel_id=1, source_target_pairs={{0,1},{1,0},{2,3},{3,2},{4,5},{5,4},{6,7},{7,6},{8,9},{9,8},{10,11... | collective-permute-start | bytes 786440 | tf_op jit(solution)/shard_map/ppermute | solution.py:63
  57.4 6.9 %collective-permute-start.12 = (f32[2,32,128]{2,1,0:T(8,128)S(1)}, f32[2,32,128]{2,1,0:T(8,128)S(1)}, u32[]{:S(2)}, u32[]{:S(2)}) collective-permute-start(f32[2,32,128]{2,1,0:T(8,128)S(1)} %maximum_select_fusion.7), channel_id=1, source_target_pairs={{0,1},{1,0},{2,3},{3,2},{4,5},{5,4},{6,7},{7,6},{8,9},{9,8},{10,11... | collective-permute-start | bytes 98312 | tf_op jit(solution)/shard_map/ppermute | solution.py:63
  58.9 10.4 %copy-start = (f32[64,128]{1,0:T(8,128)S(1)}, f32[64,128]{1,0:T(8,128)}, u32[]{:S(2)}) copy-start(f32[64,128]{1,0:T(8,128)} %param.6) | copy-start | bytes 98308
  64.1 1.2 collective-permute-start.9
  65.3 3.9 %collective-permute-start.10 = (f32[64,128]{1,0:T(8,128)S(1)}, f32[64,128]{1,0:T(8,128)S(1)}, u32[]{:S(2)}, u32[]{:S(2)}) collective-permute-start(f32[64,128]{1,0:T(8,128)S(1)} %add.404), channel_id=1, source_target_pairs={{0,2},{1,3},{2,0},{3,1},{4,6},{5,7},{6,4},{7,5},{8,10},{9,11},{10,... | collective-permute-start | bytes 98312 | tf_op jit(solution)/shard_map/ppermute | solution.py:19
  71.8 9.6 %all-to-all-start.1 = ((f32[8,1,128]{2,1,0:T(1,128)}), f32[8,1,128]{2,1,0:T(1,128)S(1)}, u32[]{:S(2)}, u32[]{:S(2)}) async-start(f32[8,1,128]{2,1,0:T(1,128)} %broadcast_in_dim.7), calls=%async_computation.1 | async-start | bytes 8192 | tf_op jit(solution)/shard_map/all_to_all | solution.py:27
  86.5 1.6 %collective-permute-start.15 = (f32[2,256,128]{2,1,0:T(8,128)S(1)}, f32[2,256,128]{2,1,0:T(8,128)S(1)}, u32[]{:S(2)}, u32[]{:S(2)}) collective-permute-start(f32[2,256,128]{2,1,0:T(8,128)S(1)} %dynamic-slice_bitcast_fusion), channel_id=1, source_target_pairs={{0,1},{1,0},{2,3},{3,2},{4,5},{5,4},{6,7},{7,6},{8,9},{9,8},{10,11... | collective-permute-start | bytes 786440 | tf_op jit(solution)/shard_map/ppermute | solution.py:49
  88.1 5.6 %collective-permute-start.16 = (f32[256,128]{1,0:T(8,128)S(1)}, f32[256,128]{1,0:T(8,128)S(1)}, u32[]{:S(2)}, u32[]{:S(2)}) collective-permute-start(f32[256,128]{1,0:T(8,128)S(1)} %dynamic-slice_bitcast_fusion.2), channel_id=1, source_target_pairs={{0,2},{1,3},{2,0},{3,1},{4,6},{5,7},{6,4},{7,5},{8,10},{9,11},{10,... | collective-permute-start | bytes 393224 | tf_op jit(solution)/shard_map/ppermute | solution.py:49
  93.7 5.0 %collective-permute-start.17 = (f32[256,128]{1,0:T(8,128)S(1)}, f32[256,128]{1,0:T(8,128)S(1)}, u32[]{:S(2)}, u32[]{:S(2)}) collective-permute-start(f32[256,128]{1,0:T(8,128)S(1)} %bitcast_add_fusion.2), channel_id=1, source_target_pairs={{0,4},{4,0},{8,12},{12,8},{16,20},{20,16},{24,28},{28,24},{1,5},{5... | collective-permute-start | bytes 393224 | tf_op jit(solution)/shard_map/ppermute | solution.py:19
  98.8 5.0 %collective-permute-start.18 = (f32[256,128]{1,0:T(8,128)S(1)}, f32[256,128]{1,0:T(8,128)S(1)}, u32[]{:S(2)}, u32[]{:S(2)}) collective-permute-start(f32[256,128]{1,0:T(8,128)S(1)} %add.423), channel_id=1, source_target_pairs={{0,8},{4,12},{8,0},{12,4},{16,24},{20,28},{24,16},{28,20},{1,9},{5... | collective-permute-start | bytes 393224 | tf_op jit(solution)/shard_map/ppermute | solution.py:19
  103.9 7.3 %collective-permute-start.19 = (f32[256,128]{1,0:T(8,128)S(1)}, f32[256,128]{1,0:T(8,128)S(1)}, u32[]{:S(2)}, u32[]{:S(2)}) collective-permute-start(f32[256,128]{1,0:T(8,128)S(1)} %add.424), channel_id=1, source_target_pairs={{0,16},{4,20},{8,24},{12,28},{16,0},{20,4},{24,8},{28,12},{1,17},{... | collective-permute-start | bytes 393224 | tf_op jit(solution)/shard_map/ppermute | solution.py:19
  111.2 5.0 %collective-permute-start.20 = (f32[256,128]{1,0:T(8,128)S(1)}, f32[256,128]{1,0:T(8,128)S(1)}, u32[]{:S(2)}, u32[]{:S(2)}) collective-permute-start(f32[256,128]{1,0:T(8,128)S(1)} %multiply_subtract_fusion), channel_id=1, source_target_pairs={{0,2},{1,3},{2,0},{3,1},{4,6},{5,7},{6,4},{7,5},{8,10},{9,11},{10,... | collective-permute-start | bytes 393224 | tf_op jit(solution)/shard_map/ppermute | solution.py:63
  116.3 1.6 %collective-permute-start.21 = (f32[2,256,128]{2,1,0:T(8,128)S(1)}, f32[2,256,128]{2,1,0:T(8,128)S(1)}, u32[]{:S(2)}, u32[]{:S(2)}) collective-permute-start(f32[2,256,128]{2,1,0:T(8,128)S(1)} %maximum_select_fusion.4), channel_id=1, source_target_pairs={{0,1},{1,0},{2,3},{3,2},{4,5},{5,4},{6,7},{7,6},{8,9},{9,8},{10,11... | collective-permute-start | bytes 786440 | tf_op jit(solution)/shard_map/ppermute | solution.py:63
  123.0 1.2 collective-permute-start.22
  124.3 3.9 %collective-permute-start.23 = (f32[64,128]{1,0:T(8,128)S(1)}, f32[64,128]{1,0:T(8,128)S(1)}, u32[]{:S(2)}, u32[]{:S(2)}) collective-permute-start(f32[64,128]{1,0:T(8,128)S(1)} %add.426), channel_id=1, source_target_pairs={{0,2},{1,3},{2,0},{3,1},{4,6},{5,7},{6,4},{7,5},{8,10},{9,11},{10,... | collective-permute-start | bytes 98312 | tf_op jit(solution)/shard_map/ppermute | solution.py:19
  130.7 9.6 %all-to-all-start.2 = ((f32[8,1,128]{2,1,0:T(1,128)}), f32[8,1,128]{2,1,0:T(1,128)S(1)}, u32[]{:S(2)}, u32[]{:S(2)}) async-start(f32[8,1,128]{2,1,0:T(1,128)} %broadcast_in_dim.16), calls=%async_computation.2 | async-start | bytes 8192 | tf_op jit(solution)/shard_map/all_to_all | solution.py:27

commit v6 on v5

--- a/solution.py
+++ b/solution.py
@@ -123,6 +123,9 @@
 
     beta_value = jnp.sqrt(scalar_sum(jnp.sum(travel_times * travel_times), "dp"))
     left_rays = travel_times / beta_value
+    left_rays, group_select, group_scale = lax.optimization_barrier(
+        (left_rays, group_select, group_scale)
+    )
     left_faces = jnp.zeros(group_weights.shape, jnp.float32)
     raw = transposed_part(left_rays, left_faces)
     full_model, right_vector, alpha_value = normalized_field(raw)

time: 142 us -> 149 us (1.049)
  starting transfers between devices: 25.9 us -> 33.6 us
  waiting for transfers between devices: 75 us -> 71.7 us
  other arithmetic: 13 us -> 15.7 us
    ppermute x10, starting transfers between devices: 5.09 us -> 10.4 us  [butterfly_sum(): x = x + lax.ppermute(x, axis, [(i, i ^ k) for i in range(n)])]
    select_n x13, other arithmetic: 1.65 us -> 4.66 us  [doubling_gather(): jnp.where(upper, jnp.stack([other, x], place), jnp.stack([x, other], place))]
    all_to_all x3, waiting for transfers between devices: 15.5 us -> 12.5 us  [scalar_sum(): got = lax.all_to_all(spread, axis, 0, 0, tiled=False)]
    all_to_all x3, starting transfers between devices: 13.9 us -> 16.4 us  [scalar_sum(): got = lax.all_to_all(spread, axis, 0, 0, tiled=False)]
    ppermute x10, waiting for transfers between devices: 35.8 us -> 33.7 us  [butterfly_sum(): x = x + lax.ppermute(x, axis, [(i, i ^ k) for i in range(n)])]
    ppermute x4, waiting for transfers between devices: 11 us -> 12.9 us  [halving_scatter(): x = keep + lax.ppermute(send, axis, [(i, i ^ k) for i in range(n)])]
  transfers between devices with their start and end apart: 27 -> 27, of which waited for: 21 -> 23; matrix products, arithmetic and copies ran while one was open for 10% -> 8% of each run, Pallas kernels for 0% -> 0%
where the time goes in v6:
time: 149 us; the launch traced here: 148 us
  waiting for transfers between devices  71.7 us (48%)
  starting transfers between devices  33.6 us (23%)
  matrix products  16.7 us (11%)
  other arithmetic  15.7 us (11%)
  between operations  5.5 us (4%)
  local copies, waits for them, and re-layouts  5.17 us (3%)
    ppermute x10, waiting for transfers between devices, butterfly_sum(): x = x + lax.ppermute(x, axis, [(i, i ^ k) for i in range(n)])  33.7 us
    all_to_all x3, starting transfers between devices, scalar_sum(): got = lax.all_to_all(spread, axis, 0, 0, tiled=False)  16.4 us
    ppermute x4, waiting for transfers between devices, halving_scatter(): x = keep + lax.ppermute(send, axis, [(i, i ^ k) for i in range(n)])  12.9 us
    ppermute x10, waiting for transfers between devices, doubling_gather(): other = lax.ppermute(x, axis, [(i, i ^ k) for i in range(n)])  12.6 us
    all_to_all x3, waiting for transfers between devices, scalar_sum(): got = lax.all_to_all(spread, axis, 0, 0, tiled=False)  12.5 us
    ppermute x10, starting transfers between devices, butterfly_sum(): x = x + lax.ppermute(x, axis, [(i, i ^ k) for i in range(n)])  10.4 us
    dot_general x2, matrix products, local(): jnp.einsum('tsrb,tsb->tr', sensitivity, picked, preferred_element_type=jn...  6.74 us
    dot_general x2, matrix products, transposed_part(): jnp.einsum('tsrb,tr->tsb', sensitivity, rays_half, preferred_element_type...  5.68 us
  transfers between devices with their start and end apart: 27, of which 23 were waited for; matrix products, arithmetic and copies ran while one was open for 8% of the time, Pallas kernels for 0%

profile of v6, /device:TPU:0, one launch (start us, length us, event | category | flops | bytes accessed | tf_op | source)
XLA Modules:
  0.0 148.4 jit_solution(9802758918566344348)
XLA Ops:
  0.0 1.4 multiply_reduce_fusion.5
  1.4 1.2 broadcast_in_dim.6
  2.6 7.3 %all-to-all-start = ((f32[8,1,128]{2,1,0:T(1,128)}), f32[8,1,128]{2,1,0:T(1,128)S(1)}, u32[]{:S(2)}, u32[]{:S(2)}) async-start(f32[8,1,128]{2,1,0:T(1,128)} %broadcast_in_dim.6), calls=%async_computation | async-start | bytes 8192 | tf_op jit(solution)/shard_map/all_to_all | solution.py:27
  9.9 1.5 %collective-permute-start = (s32[32,2]{0,1:T(2,128)}, s32[32,2]{0,1:T(2,128)S(1)}, u32[]{:S(2)}, u32[]{:S(2)}) collective-permute-start(s32[32,2]{0,1:T(2,128)} %param.9), channel_id=1, source_target_pairs={{0,2},{1,3},{2,0},{3,1},{4,6},{5,7},{6,4},{7,5},{8,10},{9,11},{10,... | collective-permute-start | bytes 776 | tf_op jit(solution)/shard_map/ppermute | solution.py:63
  12.0 1.5 %collective-permute-start.4 = (s32[1]{0:T(128)}, s32[1]{0:T(128)}, u32[]{:S(2)}, u32[]{:S(2)}) collective-permute-start(s32[1]{0:T(128)} %param.11), channel_id=1, source_target_pairs={{0,2},{1,3},{2,0},{3,1},{4,6},{5,7},{6,4},{7,5},{8,10},{9,11},{10,... | collective-permute-start | bytes 20 | tf_op jit(solution)/shard_map/ppermute | solution.py:63
  13.4 0.8 slice_bitcast_fusion.3
  14.9 0.8 copy.12
  15.9 0.8 multiply_multiply_fusion
  16.8 0.7 broadcast_select_fusion.2
  19.5 2.5 %compare_convert_fusion.1 = f32[128]{0:T(128)S(1)} fusion(s32[]{:T(128)} %bitcast.22, s32[]{:T(128)} %bitcast.23, s32[]{:T(128)} %bitcast.25, s32[]{:T(128)} %bitcast.24), kind=kLoop, calls=%fused_computation.83 | loop fusion | flops 3200 | bytes 528 | tf_op jit(solution)/shard_map/convert_element_type | solution.py:79
  22.0 0.8 add_select_fusion.1
  23.0 0.8 add_select_fusion.2
  24.4 0.8 broadcast_divide_fusion.2
  25.2 0.8 maximum_select_fusion.7
  26.2 0.8 maximum_select_fusion.8
  27.3 2.8 %fusion.26 = f32[64,1,2,128]{3,1,2,0:T(1,128)S(1)} fusion(bf16[64,2,128,128]{3,2,1,0:T(8,128)(2,1)} %param.7, bf16[64,128,1,1]{1,0,2,3:T(8,128)(2,1)S(1)} %convert_bitcast_fusion.1), kind=kOutput, calls=%fused_computation.62 | convolution fusion | flops 4194304 | bytes 4276224 | tf_op jit(solution)/shard_map/tsrb,tr->tsb/dot_general | solution.py:102
  30.1 1.9 %fusion.1 = f32[1024,128]{1,0:T(8,128)S(1)} fusion(f32[32,1024]{1,0:T(8,128)S(1)} %convert_subtract_fusion, f32[128,1024]{1,0:T(8,128)S(1)} %get-tuple-element.22, f32[32,128]{1,0:T(8,128)S(1)} %multiply_multiply_fusion, f32[128,128]{1,0:T(8,128)S(1)} %bitcast.139), kind=kOutput, calls=%fused_computation.2 | convolution fusion | flops 251842560 | bytes 1261568 | tf_op jit(solution)/shard_map/dot_general | solution.py:108
  32.3 1.3 collective-permute-done.6
  34.3 5.1 %collective-permute-done.7 = f32[256,128]{1,0:T(8,128)S(1)} collective-permute-done((f32[256,128]{1,0:T(8,128)S(1)}, f32[256,128]{1,0:T(8,128)S(1)}, u32[]{:S(2)}, u32[]{:S(2)}) %collective-permute-start.7) | collective-permute-done | bytes 131104 | tf_op jit(solution)/shard_map/ppermute | solution.py:49
  39.4 2.1 %collective-permute-start.8 = (f32[256,128]{1,0:T(8,128)S(1)}, f32[256,128]{1,0:T(8,128)S(1)}, u32[]{:S(2)}, u32[]{:S(2)}) collective-permute-start(f32[256,128]{1,0:T(8,128)S(1)} %bitcast_add_fusion.3), channel_id=1, source_target_pairs={{0,4},{4,0},{8,12},{12,8},{16,20},{20,16},{24,28},{28,24},{1,5},{5... | collective-permute-start | bytes 393224 | tf_op jit(solution)/shard_map/ppermute | solution.py:19
  41.5 3.0 %collective-permute-done.8 = f32[256,128]{1,0:T(8,128)S(1)} collective-permute-done((f32[256,128]{1,0:T(8,128)S(1)}, f32[256,128]{1,0:T(8,128)S(1)}, u32[]{:S(2)}, u32[]{:S(2)}) %collective-permute-start.8) | collective-permute-done | bytes 131104 | tf_op jit(solution)/shard_map/ppermute | solution.py:19
  44.5 2.0 %collective-permute-start.9 = (f32[256,128]{1,0:T(8,128)S(1)}, f32[256,128]{1,0:T(8,128)S(1)}, u32[]{:S(2)}, u32[]{:S(2)}) collective-permute-start(f32[256,128]{1,0:T(8,128)S(1)} %add.404), channel_id=1, source_target_pairs={{0,8},{4,12},{8,0},{12,4},{16,24},{20,28},{24,16},{28,20},{1,9},{5... | collective-permute-start | bytes 393224 | tf_op jit(solution)/shard_map/ppermute | solution.py:19
  46.5 3.0 %collective-permute-done.9 = f32[256,128]{1,0:T(8,128)S(1)} collective-permute-done((f32[256,128]{1,0:T(8,128)S(1)}, f32[256,128]{1,0:T(8,128)S(1)}, u32[]{:S(2)}, u32[]{:S(2)}) %collective-permute-start.9) | collective-permute-done | bytes 131104 | tf_op jit(solution)/shard_map/ppermute | solution.py:19
  49.6 3.1 %collective-permute-start.10 = (f32[256,128]{1,0:T(8,128)S(1)}, f32[256,128]{1,0:T(8,128)S(1)}, u32[]{:S(2)}, u32[]{:S(2)}) collective-permute-start(f32[256,128]{1,0:T(8,128)S(1)} %add.405), channel_id=1, source_target_pairs={{0,16},{4,20},{8,24},{12,28},{16,0},{20,4},{24,8},{28,12},{1,17},{... | collective-permute-start | bytes 393224 | tf_op jit(solution)/shard_map/ppermute | solution.py:19
  52.7 4.4 %collective-permute-done.10 = f32[256,128]{1,0:T(8,128)S(1)} collective-permute-done((f32[256,128]{1,0:T(8,128)S(1)}, f32[256,128]{1,0:T(8,128)S(1)}, u32[]{:S(2)}, u32[]{:S(2)}) %collective-permute-start.10) | collective-permute-done | bytes 131104 | tf_op jit(solution)/shard_map/ppermute | solution.py:19
  57.7 4.4 %collective-permute-done.11 = f32[256,128]{1,0:T(8,128)S(1)} collective-permute-done((f32[256,128]{1,0:T(8,128)S(1)}, f32[256,128]{1,0:T(8,128)S(1)}, u32[]{:S(2)}, u32[]{:S(2)}) %collective-permute-start.11) | collective-permute-done | bytes 131104 | tf_op jit(solution)/shard_map/ppermute | solution.py:63
  62.2 1.5 %collective-permute-done.12 = f32[2,256,128]{2,1,0:T(8,128)S(1)} collective-permute-done((f32[2,256,128]{2,1,0:T(8,128)S(1)}, f32[2,256,128]{2,1,0:T(8,128)S(1)}, u32[]{:S(2)}, u32[]{:S(2)}) %collective-permute-start.12) | collective-permute-done | bytes 262176 | tf_op jit(solution)/shard_map/ppermute | solution.py:63
  63.7 0.7 multiply_reduce_fusion.1
  65.6 3.4 %fusion.22 = f32[64,1,128,1]{2,1,3,0:T(1,128)S(1)} fusion(bf16[64,2,128,128]{3,2,1,0:T(8,128)(2,1)} %param.7, bf16[64,2,128,1]{2,1,0,3:T(2,128)(2,1)S(1)} %bitcast.136), kind=kOutput, calls=%fused_computation.55 | convolution fusion | flops 4194304 | bytes 4259840 | tf_op jit(solution)/shard_map/tsrb,tsb->tr/dot_general | solution.py:140
  69.1 1.1 collective-permute-done.13
  71.4 2.7 %collective-permute-done.14 = f32[64,128]{1,0:T(8,128)S(1)} collective-permute-done((f32[64,128]{1,0:T(8,128)S(1)}, f32[64,128]{1,0:T(8,128)S(1)}, u32[]{:S(2)}, u32[]{:S(2)}) %collective-permute-start.14) | collective-permute-done | bytes 32800 | tf_op jit(solution)/shard_map/ppermute | solution.py:19
  76.6 5.8 %all-to-all-start.1 = ((f32[8,1,128]{2,1,0:T(1,128)}), f32[8,1,128]{2,1,0:T(1,128)S(1)}, u32[]{:S(2)}, u32[]{:S(2)}) async-start(f32[8,1,128]{2,1,0:T(1,128)} %broadcast_in_dim.7), calls=%async_computation.1 | async-start | bytes 8192 | tf_op jit(solution)/shard_map/all_to_all | solution.py:27
  82.4 6.4 %all-to-all-done.1 = f32[8,1,128]{2,1,0:T(1,128)S(1)} async-done(((f32[8,1,128]{2,1,0:T(1,128)}), f32[8,1,128]{2,1,0:T(1,128)S(1)}, u32[]{:S(2)}, u32[]{:S(2)}) %all-to-all-start.1) | async-done | bytes 4128 | tf_op jit(solution)/shard_map/all_to_all | solution.py:27
  88.9 2.8 %fusion.24 = f32[64,1,2,128]{3,1,2,0:T(1,128)S(1)} fusion(bf16[64,2,128,128]{3,2,1,0:T(8,128)(2,1)} %param.7, bf16[64,128,1,1]{1,0,2,3:T(8,128)(2,1)S(1)} %convert_bitcast_fusion), kind=kOutput, calls=%fused_computation.60 | convolution fusion | flops 4194304 | bytes 4276224 | tf_op jit(solution)/shard_map/tsrb,tr->tsb/dot_general | solution.py:102
  91.8 1.9 %fusion = f32[1024,128]{1,0:T(8,128)S(1)} fusion(f32[32,1024]{1,0:T(8,128)S(1)} %convert_subtract_fusion, f32[128,1024]{1,0:T(8,128)S(1)} %get-tuple-element.22, f32[32,128]{1,0:T(8,128)S(1)} %dynamic-slice_multiply_fusion, f32[128,128]{1,0:T(8,128)S(1)} %bitcast.138), kind=kOutput, calls=%fused_computation.1 | convolution fusion | flops 251842560 | bytes 1261568 | tf_op jit(solution)/shard_map/dot_general | solution.py:108
  93.8 1.5 %collective-permute-done.15 = f32[2,256,128]{2,1,0:T(8,128)S(1)} collective-permute-done((f32[2,256,128]{2,1,0:T(8,128)S(1)}, f32[2,256,128]{2,1,0:T(8,128)S(1)}, u32[]{:S(2)}, u32[]{:S(2)}) %collective-permute-start.15) | collective-permute-done | bytes 262176 | tf_op jit(solution)/shard_map/ppermute | solution.py:49
  96.0 5.0 %collective-permute-done.16 = f32[256,128]{1,0:T(8,128)S(1)} collective-permute-done((f32[256,128]{1,0:T(8,128)S(1)}, f32[256,128]{1,0:T(8,128)S(1)}, u32[]{:S(2)}, u32[]{:S(2)}) %collective-permute-start.16) | collective-permute-done | bytes 131104 | tf_op jit(solution)/shard_map/ppermute | solution.py:49
  101.6 4.4 %collective-permute-done.17 = f32[256,128]{1,0:T(8,128)S(1)} collective-permute-done((f32[256,128]{1,0:T(8,128)S(1)}, f32[256,128]{1,0:T(8,128)S(1)}, u32[]{:S(2)}, u32[]{:S(2)}) %collective-permute-start.17) | collective-permute-done | bytes 131104 | tf_op jit(solution)/shard_map/ppermute | solution.py:19
  106.6 4.4 %collective-permute-done.18 = f32[256,128]{1,0:T(8,128)S(1)} collective-permute-done((f32[256,128]{1,0:T(8,128)S(1)}, f32[256,128]{1,0:T(8,128)S(1)}, u32[]{:S(2)}, u32[]{:S(2)}) %collective-permute-start.18) | collective-permute-done | bytes 131104 | tf_op jit(solution)/shard_map/ppermute | solution.py:19
  111.7 6.7 %collective-permute-done.19 = f32[256,128]{1,0:T(8,128)S(1)} collective-permute-done((f32[256,128]{1,0:T(8,128)S(1)}, f32[256,128]{1,0:T(8,128)S(1)}, u32[]{:S(2)}, u32[]{:S(2)}) %collective-permute-start.19) | collective-permute-done | bytes 131104 | tf_op jit(solution)/shard_map/ppermute | solution.py:19
  119.1 4.4 %collective-permute-done.20 = f32[256,128]{1,0:T(8,128)S(1)} collective-permute-done((f32[256,128]{1,0:T(8,128)S(1)}, f32[256,128]{1,0:T(8,128)S(1)}, u32[]{:S(2)}, u32[]{:S(2)}) %collective-permute-start.20) | collective-permute-done | bytes 131104 | tf_op jit(solution)/shard_map/ppermute | solution.py:63
  123.6 1.5 %collective-permute-done.21 = f32[2,256,128]{2,1,0:T(8,128)S(1)} collective-permute-done((f32[2,256,128]{2,1,0:T(8,128)S(1)}, f32[2,256,128]{2,1,0:T(8,128)S(1)}, u32[]{:S(2)}, u32[]{:S(2)}) %collective-permute-start.21) | collective-permute-done | bytes 262176 | tf_op jit(solution)/shard_map/ppermute | solution.py:63
  125.1 0.7 multiply_reduce_fusion
  126.9 3.4 %fusion.20 = f32[64,1,128,1]{2,1,3,0:T(1,128)S(1)} fusion(bf16[64,2,128,128]{3,2,1,0:T(8,128)(2,1)} %param.7, bf16[64,2,128,1]{2,1,0,3:T(2,128)(2,1)S(1)} %bitcast.137), kind=kOutput, calls=%fused_computation.53 | convolution fusion | flops 4194304 | bytes 4259840 | tf_op jit(solution)/shard_map/tsrb,tsb->tr/dot_general | solution.py:140
  130.4 1.1 collective-permute-done.22
  132.6 2.8 %collective-permute-done.23 = f32[64,128]{1,0:T(8,128)S(1)} collective-permute-done((f32[64,128]{1,0:T(8,128)S(1)}, f32[64,128]{1,0:T(8,128)S(1)}, u32[]{:S(2)}, u32[]{:S(2)}) %collective-permute-start.23) | collective-permute-done | bytes 32800 | tf_op jit(solution)/shard_map/ppermute | solution.py:19
  137.8 3.3 %all-to-all-start.2 = ((f32[8,1,128]{2,1,0:T(1,128)}), f32[8,1,128]{2,1,0:T(1,128)S(1)}, u32[]{:S(2)}, u32[]{:S(2)}) async-start(f32[8,1,128]{2,1,0:T(1,128)} %broadcast_in_dim.16), calls=%async_computation.2 | async-start | bytes 8192 | tf_op jit(solution)/shard_map/all_to_all | solution.py:27
  141.4 6.1 %all-to-all-done.2 = f32[8,1,128]{2,1,0:T(1,128)S(1)} async-done(((f32[8,1,128]{2,1,0:T(1,128)}), f32[8,1,128]{2,1,0:T(1,128)S(1)}, u32[]{:S(2)}, u32[]{:S(2)}) %all-to-all-start.2) | async-done | bytes 4128 | tf_op jit(solution)/shard_map/all_to_all | solution.py:27
  (87 shorter events, 15.8 us)
Async XLA Ops:
  2.6 21.6 %all-to-all-start = ((f32[8,1,128]{2,1,0:T(1,128)}), f32[8,1,128]{2,1,0:T(1,128)S(1)}, u32[]{:S(2)}, u32[]{:S(2)}) async-start(f32[8,1,128]{2,1,0:T(1,128)} %broadcast_in_dim.6), calls=%async_computation | async-start | bytes 8192 | tf_op jit(solution)/shard_map/all_to_all | solution.py:27
  9.9 12.1 %collective-permute-start = (s32[32,2]{0,1:T(2,128)}, s32[32,2]{0,1:T(2,128)S(1)}, u32[]{:S(2)}, u32[]{:S(2)}) collective-permute-start(s32[32,2]{0,1:T(2,128)} %param.9), channel_id=1, source_target_pairs={{0,2},{1,3},{2,0},{3,1},{4,6},{5,7},{6,4},{7,5},{8,10},{9,11},{10,... | collective-permute-start | bytes 776 | tf_op jit(solution)/shard_map/ppermute | solution.py:63
  11.4 13.7 %collective-permute-start.2 = (f32[32,128]{1,0:T(8,128)}, f32[32,128]{1,0:T(8,128)S(1)}, u32[]{:S(2)}, u32[]{:S(2)}) collective-permute-start(f32[32,128]{1,0:T(8,128)} %param.10), channel_id=1, source_target_pairs={{0,2},{1,3},{2,0},{3,1},{4,6},{5,7},{6,4},{7,5},{8,10},{9,11},{10,... | collective-permute-start | bytes 49160 | tf_op jit(solution)/shard_map/ppermute | solution.py:63
  12.0 4.9 %collective-permute-start.4 = (s32[1]{0:T(128)}, s32[1]{0:T(128)}, u32[]{:S(2)}, u32[]{:S(2)}) collective-permute-start(s32[1]{0:T(128)} %param.11), channel_id=1, source_target_pairs={{0,2},{1,3},{2,0},{3,1},{4,6},{5,7},{6,4},{7,5},{8,10},{9,11},{10,... | collective-permute-start | bytes 20 | tf_op jit(solution)/shard_map/ppermute | solution.py:63
  17.5 1.1 collective-permute-start.5
  22.8 1.2 collective-permute-start.1
  26.0 1.2 collective-permute-start.3
  32.0 1.6 %collective-permute-start.6 = (f32[2,256,128]{2,1,0:T(8,128)S(1)}, f32[2,256,128]{2,1,0:T(8,128)S(1)}, u32[]{:S(2)}, u32[]{:S(2)}) collective-permute-start(f32[2,256,128]{2,1,0:T(8,128)S(1)} %dynamic-slice_bitcast_fusion.1), channel_id=1, source_target_pairs={{0,1},{1,0},{2,3},{3,2},{4,5},{5,4},{6,7},{7,6},{8,9},{9,8},{10,11... | collective-permute-start | bytes 786440 | tf_op jit(solution)/shard_map/ppermute | solution.py:49
  33.7 5.7 %collective-permute-start.7 = (f32[256,128]{1,0:T(8,128)S(1)}, f32[256,128]{1,0:T(8,128)S(1)}, u32[]{:S(2)}, u32[]{:S(2)}) collective-permute-start(f32[256,128]{1,0:T(8,128)S(1)} %dynamic-slice_bitcast_fusion.3), channel_id=1, source_target_pairs={{0,2},{1,3},{2,0},{3,1},{4,6},{5,7},{6,4},{7,5},{8,10},{9,11},{10,... | collective-permute-start | bytes 393224 | tf_op jit(solution)/shard_map/ppermute | solution.py:49
  39.4 5.1 %collective-permute-start.8 = (f32[256,128]{1,0:T(8,128)S(1)}, f32[256,128]{1,0:T(8,128)S(1)}, u32[]{:S(2)}, u32[]{:S(2)}) collective-permute-start(f32[256,128]{1,0:T(8,128)S(1)} %bitcast_add_fusion.3), channel_id=1, source_target_pairs={{0,4},{4,0},{8,12},{12,8},{16,20},{20,16},{24,28},{28,24},{1,5},{5... | collective-permute-start | bytes 393224 | tf_op jit(solution)/shard_map/ppermute | solution.py:19
  44.5 5.0 %collective-permute-start.9 = (f32[256,128]{1,0:T(8,128)S(1)}, f32[256,128]{1,0:T(8,128)S(1)}, u32[]{:S(2)}, u32[]{:S(2)}) collective-permute-start(f32[256,128]{1,0:T(8,128)S(1)} %add.404), channel_id=1, source_target_pairs={{0,8},{4,12},{8,0},{12,4},{16,24},{20,28},{24,16},{28,20},{1,9},{5... | collective-permute-start | bytes 393224 | tf_op jit(solution)/shard_map/ppermute | solution.py:19
  49.6 7.5 %collective-permute-start.10 = (f32[256,128]{1,0:T(8,128)S(1)}, f32[256,128]{1,0:T(8,128)S(1)}, u32[]{:S(2)}, u32[]{:S(2)}) collective-permute-start(f32[256,128]{1,0:T(8,128)S(1)} %add.405), channel_id=1, source_target_pairs={{0,16},{4,20},{8,24},{12,28},{16,0},{20,4},{24,8},{28,12},{1,17},{... | collective-permute-start | bytes 393224 | tf_op jit(solution)/shard_map/ppermute | solution.py:19
  57.1 5.0 %collective-permute-start.11 = (f32[256,128]{1,0:T(8,128)S(1)}, f32[256,128]{1,0:T(8,128)S(1)}, u32[]{:S(2)}, u32[]{:S(2)}) collective-permute-start(f32[256,128]{1,0:T(8,128)S(1)} %add.406), channel_id=1, source_target_pairs={{0,2},{1,3},{2,0},{3,1},{4,6},{5,7},{6,4},{7,5},{8,10},{9,11},{10,... | collective-permute-start | bytes 393224 | tf_op jit(solution)/shard_map/ppermute | solution.py:63
  62.1 1.6 %collective-permute-start.12 = (f32[2,256,128]{2,1,0:T(8,128)S(1)}, f32[2,256,128]{2,1,0:T(8,128)S(1)}, u32[]{:S(2)}, u32[]{:S(2)}) collective-permute-start(f32[2,256,128]{2,1,0:T(8,128)S(1)} %maximum_select_fusion.2), channel_id=1, source_target_pairs={{0,1},{1,0},{2,3},{3,2},{4,5},{5,4},{6,7},{7,6},{8,9},{9,8},{10,11... | collective-permute-start | bytes 786440 | tf_op jit(solution)/shard_map/ppermute | solution.py:63
  65.6 26.2 %copy-start = (f32[32,128]{1,0:T(8,128)S(1)}, f32[32,128]{1,0:T(8,128)}, u32[]{:S(2)}) copy-start(f32[32,128]{1,0:T(8,128)} %param.10) | copy-start | bytes 49156
  69.0 1.2 collective-permute-start.13
  70.2 3.9 %collective-permute-start.14 = (f32[64,128]{1,0:T(8,128)S(1)}, f32[64,128]{1,0:T(8,128)S(1)}, u32[]{:S(2)}, u32[]{:S(2)}) collective-permute-start(f32[64,128]{1,0:T(8,128)S(1)} %add.407), channel_id=1, source_target_pairs={{0,2},{1,3},{2,0},{3,1},{4,6},{5,7},{6,4},{7,5},{8,10},{9,11},{10,... | collective-permute-start | bytes 98312 | tf_op jit(solution)/shard_map/ppermute | solution.py:19
  76.6 12.2 %all-to-all-start.1 = ((f32[8,1,128]{2,1,0:T(1,128)}), f32[8,1,128]{2,1,0:T(1,128)S(1)}, u32[]{:S(2)}, u32[]{:S(2)}) async-start(f32[8,1,128]{2,1,0:T(1,128)} %broadcast_in_dim.7), calls=%async_computation.1 | async-start | bytes 8192 | tf_op jit(solution)/shard_map/all_to_all | solution.py:27
  93.7 1.6 %collective-permute-start.15 = (f32[2,256,128]{2,1,0:T(8,128)S(1)}, f32[2,256,128]{2,1,0:T(8,128)S(1)}, u32[]{:S(2)}, u32[]{:S(2)}) collective-permute-start(f32[2,256,128]{2,1,0:T(8,128)S(1)} %dynamic-slice_bitcast_fusion), channel_id=1, source_target_pairs={{0,1},{1,0},{2,3},{3,2},{4,5},{5,4},{6,7},{7,6},{8,9},{9,8},{10,11... | collective-permute-start | bytes 786440 | tf_op jit(solution)/shard_map/ppermute | solution.py:49
  95.4 5.6 %collective-permute-start.16 = (f32[256,128]{1,0:T(8,128)S(1)}, f32[256,128]{1,0:T(8,128)S(1)}, u32[]{:S(2)}, u32[]{:S(2)}) collective-permute-start(f32[256,128]{1,0:T(8,128)S(1)} %dynamic-slice_bitcast_fusion.2), channel_id=1, source_target_pairs={{0,2},{1,3},{2,0},{3,1},{4,6},{5,7},{6,4},{7,5},{8,10},{9,11},{10,... | collective-permute-start | bytes 393224 | tf_op jit(solution)/shard_map/ppermute | solution.py:49
  101.0 5.0 %collective-permute-start.17 = (f32[256,128]{1,0:T(8,128)S(1)}, f32[256,128]{1,0:T(8,128)S(1)}, u32[]{:S(2)}, u32[]{:S(2)}) collective-permute-start(f32[256,128]{1,0:T(8,128)S(1)} %bitcast_add_fusion.2), channel_id=1, source_target_pairs={{0,4},{4,0},{8,12},{12,8},{16,20},{20,16},{24,28},{28,24},{1,5},{5... | collective-permute-start | bytes 393224 | tf_op jit(solution)/shard_map/ppermute | solution.py:19
  106.0 5.0 %collective-permute-start.18 = (f32[256,128]{1,0:T(8,128)S(1)}, f32[256,128]{1,0:T(8,128)S(1)}, u32[]{:S(2)}, u32[]{:S(2)}) collective-permute-start(f32[256,128]{1,0:T(8,128)S(1)} %add.423), channel_id=1, source_target_pairs={{0,8},{4,12},{8,0},{12,4},{16,24},{20,28},{24,16},{28,20},{1,9},{5... | collective-permute-start | bytes 393224 | tf_op jit(solution)/shard_map/ppermute | solution.py:19
  111.1 7.3 %collective-permute-start.19 = (f32[256,128]{1,0:T(8,128)S(1)}, f32[256,128]{1,0:T(8,128)S(1)}, u32[]{:S(2)}, u32[]{:S(2)}) collective-permute-start(f32[256,128]{1,0:T(8,128)S(1)} %add.424), channel_id=1, source_target_pairs={{0,16},{4,20},{8,24},{12,28},{16,0},{20,4},{24,8},{28,12},{1,17},{... | collective-permute-start | bytes 393224 | tf_op jit(solution)/shard_map/ppermute | solution.py:19
  118.5 5.0 %collective-permute-start.20 = (f32[256,128]{1,0:T(8,128)S(1)}, f32[256,128]{1,0:T(8,128)S(1)}, u32[]{:S(2)}, u32[]{:S(2)}) collective-permute-start(f32[256,128]{1,0:T(8,128)S(1)} %multiply_subtract_fusion), channel_id=1, source_target_pairs={{0,2},{1,3},{2,0},{3,1},{4,6},{5,7},{6,4},{7,5},{8,10},{9,11},{10,... | collective-permute-start | bytes 393224 | tf_op jit(solution)/shard_map/ppermute | solution.py:63
  123.5 1.6 %collective-permute-start.21 = (f32[2,256,128]{2,1,0:T(8,128)S(1)}, f32[2,256,128]{2,1,0:T(8,128)S(1)}, u32[]{:S(2)}, u32[]{:S(2)}) collective-permute-start(f32[2,256,128]{2,1,0:T(8,128)S(1)} %maximum_select_fusion.4), channel_id=1, source_target_pairs={{0,1},{1,0},{2,3},{3,2},{4,5},{5,4},{6,7},{7,6},{8,9},{9,8},{10,11... | collective-permute-start | bytes 786440 | tf_op jit(solution)/shard_map/ppermute | solution.py:63
  130.3 1.2 collective-permute-start.22
  131.5 3.9 %collective-permute-start.23 = (f32[64,128]{1,0:T(8,128)S(1)}, f32[64,128]{1,0:T(8,128)S(1)}, u32[]{:S(2)}, u32[]{:S(2)}) collective-permute-start(f32[64,128]{1,0:T(8,128)S(1)} %add.426), channel_id=1, source_target_pairs={{0,2},{1,3},{2,0},{3,1},{4,6},{5,7},{6,4},{7,5},{8,10},{9,11},{10,... | collective-permute-start | bytes 98312 | tf_op jit(solution)/shard_map/ppermute | solution.py:19
  137.8 9.6 %all-to-all-start.2 = ((f32[8,1,128]{2,1,0:T(1,128)}), f32[8,1,128]{2,1,0:T(1,128)S(1)}, u32[]{:S(2)}, u32[]{:S(2)}) async-start(f32[8,1,128]{2,1,0:T(1,128)} %broadcast_in_dim.16), calls=%async_computation.2 | async-start | bytes 8192 | tf_op jit(solution)/shard_map/all_to_all | solution.py:27

commit v7 on v4

--- a/solution.py
+++ b/solution.py
@@ -22,7 +22,7 @@
 
 
 def scalar_sum(value, axis):
-    n = lax.axis_size(axis)
+    n = lax.psum(1, axis)
     spread = jnp.broadcast_to(value.astype(jnp.float32), (n, 1, 128))
     got = lax.all_to_all(spread, axis, 0, 0, tiled=False)
     total = got[0]
@@ -68,7 +68,8 @@
 
 
 def local(travel_times, sensitivity, tile_blocks, face_blocks, face_weights, face_count):
-    model_rows = NB_DEV * lax.axis_size("region")
+    n_region = lax.axis_size("region")
+    model_rows = NB_DEV * n_region
     region = lax.axis_index("region")
     live_mask = (jnp.arange(face_blocks.shape[0]) < face_count[0]).astype(jnp.float32)
     face_scale = smooth_weight * face_weights * live_mask[:, None]
@@ -127,16 +128,18 @@
         partial_value = jnp.einsum(
             "tsrb,tsb->tr", sensitivity, picked, preferred_element_type=jnp.float32
         )
+        ray_pred = butterfly_sum(partial_value, "region")
         face_pred = face_scale * rows[n_slots:]
         left_faces = face_pred - alpha_value * left_faces
         face_sq = jnp.sum(left_faces * left_faces)
-        packed = jnp.concatenate(
-            [partial_value, jnp.broadcast_to(face_sq, (8, partial_value.shape[1]))], 0
-        )
-        packed = butterfly_sum(packed, "region")
-        ray_pred = packed[:n_tiles]
         left_rays = ray_pred - alpha_value * left_rays
-        beta_sq = scalar_sum(jnp.sum(left_rays * left_rays) + packed[n_tiles, 0], "dp")
+        if n_tiles % n_region == 0:
+            share = n_tiles // n_region
+            own_rays = lax.dynamic_slice_in_dim(left_rays, region * share, share, 0)
+            ray_sq = jnp.sum(own_rays * own_rays)
+        else:
+            ray_sq = jnp.where(region == 0, jnp.sum(left_rays * left_rays), 0.0)
+        beta_sq = scalar_sum(ray_sq + face_sq, ("dp", "region"))
         beta_value = jnp.sqrt(beta_sq)
         left_rays = left_rays / beta_value
         left_faces = left_faces / beta_value

time: 140 us -> 136 us (0.971)
  starting transfers between devices: 24.3 us -> 20.5 us
  local copies, waits for them, and re-layouts: 5.97 us -> 3.59 us
  waiting for transfers between devices: 68.4 us -> 70.4 us
  transfers between devices with their start and end apart: 20 -> 20, of which waited for: 20 -> 20; matrix products, arithmetic and copies ran while one was open for 2% -> 3% of each run, Pallas kernels for 0% -> 0%
where the time goes in v7:
time: 136 us; the launch traced here: 135 us
  waiting for transfers between devices  70.4 us (52%)
  starting transfers between devices  20.5 us (15%)
  matrix products  16.6 us (12%)
  blocking collectives  9.91 us (7%)
  other arithmetic  8.48 us (6%)
  between operations  5.52 us (4%)
  local copies, waits for them, and re-layouts  3.59 us (3%)
    ppermute x10, waiting for transfers between devices, butterfly_sum(): x = x + lax.ppermute(x, axis, [(i, i ^ k) for i in range(n)])  37.6 us
    ppermute x4, waiting for transfers between devices, halving_scatter(): x = keep + lax.ppermute(send, axis, [(i, i ^ k) for i in range(n)])  12.1 us
    ppermute x4, waiting for transfers between devices, doubling_gather(): other = lax.ppermute(x, axis, [(i, i ^ k) for i in range(n)])  10.9 us
    all_to_all x1, blocking collectives, scalar_sum(): got = lax.all_to_all(spread, axis, 0, 0, tiled=False)  9.91 us
    all_to_all x2, waiting for transfers between devices, scalar_sum(): got = lax.all_to_all(spread, axis, 0, 0, tiled=False)  9.91 us
    all_to_all x2, starting transfers between devices, scalar_sum(): got = lax.all_to_all(spread, axis, 0, 0, tiled=False)  9.82 us
    dot_general x2, matrix products, local(): jnp.einsum('tsrb,tsb->tr', sensitivity, picked, preferred_element_type=jn...  6.74 us
    ppermute x10, starting transfers between devices, butterfly_sum(): x = x + lax.ppermute(x, axis, [(i, i ^ k) for i in range(n)])  6.08 us
  transfers between devices with their start and end apart: 20, of which 20 were waited for; matrix products, arithmetic and copies ran while one was open for 3% of the time, Pallas kernels for 0%

profile of v7, /device:TPU:0, one launch (start us, length us, event | category | flops | bytes accessed | tf_op | source)
XLA Modules:
  0.0 135.0 jit_solution(30642521058630251)
XLA Ops:
  0.0 1.4 %multiply_reduce_fusion.2 = f32[]{:T(128)} fusion(f32[64,128]{1,0:T(8,128)} %param.6), kind=kLoop, calls=%fused_computation.50 | loop fusion | flops 16383 | bytes 32772 | tf_op jit(solution)/shard_map/reduce_sum | solution.py:115
  1.4 1.2 broadcast_in_dim.16
  2.5 7.3 %all-to-all-start = ((f32[8,1,128]{2,1,0:T(1,128)}), f32[8,1,128]{2,1,0:T(1,128)S(1)}, u32[]{:S(2)}, u32[]{:S(2)}) async-start(f32[8,1,128]{2,1,0:T(1,128)} %broadcast_in_dim.16), calls=%async_computation | async-start | bytes 8192 | tf_op jit(solution)/shard_map/all_to_all | solution.py:27
  9.8 0.8 slice_bitcast_fusion.31
  10.6 0.8 copy.10
  12.3 0.8 multiply_multiply_fusion.1
  13.1 3.1 %all-to-all-done = f32[8,1,128]{2,1,0:T(1,128)S(1)} async-done(((f32[8,1,128]{2,1,0:T(1,128)}), f32[8,1,128]{2,1,0:T(1,128)S(1)}, u32[]{:S(2)}, u32[]{:S(2)}) %all-to-all-start) | async-done | bytes 4128 | tf_op jit(solution)/shard_map/all_to_all | solution.py:27
  16.3 0.8 convert_bitcast_fusion.1
  17.1 2.8 %fusion.24 = f32[64,1,2,128]{3,1,2,0:T(1,128)S(1)} fusion(bf16[64,2,128,128]{3,2,1,0:T(8,128)(2,1)} %param.7, bf16[64,128,1,1]{1,0,2,3:T(8,128)(2,1)S(1)} %convert_bitcast_fusion.1), kind=kOutput, calls=%fused_computation.47 | convolution fusion | flops 4194304 | bytes 4276224 | tf_op jit(solution)/shard_map/tsrb,tr->tsb/dot_general | solution.py:94
  19.9 1.9 %fusion.3 = f32[1024,128]{1,0:T(8,128)S(1)} fusion(f32[32,1024]{1,0:T(8,128)S(1)} %convert_subtract_fusion, f32[128,1024]{1,0:T(8,128)S(1)} %fusion, f32[32,128]{1,0:T(8,128)S(1)} %multiply_multiply_fusion.1, f32[128,128]{1,0:T(8,128)S(1)} %bitcast.281), kind=kOutput, calls=%fused_computation.9 | convolution fusion | flops 251842560 | bytes 1261568 | tf_op jit(solution)/shard_map/dot_general | solution.py:99
  21.9 1.5 %collective-permute-done = f32[2,256,128]{2,1,0:T(8,128)S(1)} collective-permute-done((f32[2,256,128]{2,1,0:T(8,128)S(1)}, f32[2,256,128]{2,1,0:T(8,128)S(1)}, u32[]{:S(2)}, u32[]{:S(2)}) %collective-permute-start) | collective-permute-done | bytes 262176 | tf_op jit(solution)/shard_map/ppermute | solution.py:49
  23.4 1.6 %collective-permute-start.1 = (f32[256,128]{1,0:T(8,128)S(1)}, f32[256,128]{1,0:T(8,128)S(1)}, u32[]{:S(2)}, u32[]{:S(2)}) collective-permute-start(f32[256,128]{1,0:T(8,128)S(1)} %dynamic-slice_bitcast_fusion.3), channel_id=1, source_target_pairs={{0,2},{1,3},{2,0},{3,1},{4,6},{5,7},{6,4},{7,5},{8,10},{9,11},{10,... | collective-permute-start | bytes 393224 | tf_op jit(solution)/shard_map/ppermute | solution.py:49
  25.0 4.0 %collective-permute-done.1 = f32[256,128]{1,0:T(8,128)S(1)} collective-permute-done((f32[256,128]{1,0:T(8,128)S(1)}, f32[256,128]{1,0:T(8,128)S(1)}, u32[]{:S(2)}, u32[]{:S(2)}) %collective-permute-start.1) | collective-permute-done | bytes 131104 | tf_op jit(solution)/shard_map/ppermute | solution.py:49
  29.1 0.6 collective-permute-start.2
  29.7 4.4 %collective-permute-done.2 = f32[256,128]{1,0:T(8,128)S(1)} collective-permute-done((f32[256,128]{1,0:T(8,128)S(1)}, f32[256,128]{1,0:T(8,128)S(1)}, u32[]{:S(2)}, u32[]{:S(2)}) %collective-permute-start.2) | collective-permute-done | bytes 131104 | tf_op jit(solution)/shard_map/ppermute | solution.py:19
  34.7 4.4 %collective-permute-done.3 = f32[256,128]{1,0:T(8,128)S(1)} collective-permute-done((f32[256,128]{1,0:T(8,128)S(1)}, f32[256,128]{1,0:T(8,128)S(1)}, u32[]{:S(2)}, u32[]{:S(2)}) %collective-permute-start.3) | collective-permute-done | bytes 131104 | tf_op jit(solution)/shard_map/ppermute | solution.py:19
  39.2 0.6 collective-permute-start.4
  39.8 6.7 %collective-permute-done.4 = f32[256,128]{1,0:T(8,128)S(1)} collective-permute-done((f32[256,128]{1,0:T(8,128)S(1)}, f32[256,128]{1,0:T(8,128)S(1)}, u32[]{:S(2)}, u32[]{:S(2)}) %collective-permute-start.4) | collective-permute-done | bytes 131104 | tf_op jit(solution)/shard_map/ppermute | solution.py:19
  46.5 1.6 %collective-permute-start.5 = (f32[256,128]{1,0:T(8,128)S(1)}, f32[256,128]{1,0:T(8,128)S(1)}, u32[]{:S(2)}, u32[]{:S(2)}) collective-permute-start(f32[256,128]{1,0:T(8,128)S(1)} %add.895), channel_id=1, source_target_pairs={{0,2},{1,3},{2,0},{3,1},{4,6},{5,7},{6,4},{7,5},{8,10},{9,11},{10,... | collective-permute-start | bytes 393224 | tf_op jit(solution)/shard_map/ppermute | solution.py:62
  48.1 3.5 %collective-permute-done.5 = f32[256,128]{1,0:T(8,128)S(1)} collective-permute-done((f32[256,128]{1,0:T(8,128)S(1)}, f32[256,128]{1,0:T(8,128)S(1)}, u32[]{:S(2)}, u32[]{:S(2)}) %collective-permute-start.5) | collective-permute-done | bytes 131104 | tf_op jit(solution)/shard_map/ppermute | solution.py:62
  51.7 1.5 %collective-permute-done.6 = f32[2,256,128]{2,1,0:T(8,128)S(1)} collective-permute-done((f32[2,256,128]{2,1,0:T(8,128)S(1)}, f32[2,256,128]{2,1,0:T(8,128)S(1)}, u32[]{:S(2)}, u32[]{:S(2)}) %collective-permute-start.6) | collective-permute-done | bytes 262176 | tf_op jit(solution)/shard_map/ppermute | solution.py:62
  53.2 0.7 multiply_reduce_fusion.1
  55.0 3.4 %fusion.18 = f32[64,1,128,1]{2,1,3,0:T(1,128)S(1)} fusion(bf16[64,2,128,128]{3,2,1,0:T(8,128)(2,1)} %param.7, bf16[64,2,128,1]{2,1,0,3:T(2,128)(2,1)S(1)} %bitcast.279), kind=kOutput, calls=%fused_computation.43 | convolution fusion | flops 4194304 | bytes 4259840 | tf_op jit(solution)/shard_map/tsrb,tsb->tr/dot_general | solution.py:128
  58.5 1.1 collective-permute-done.7
  59.6 1.5 %collective-permute-start.8 = (f32[64,128]{1,0:T(8,128)S(1)}, f32[64,128]{1,0:T(8,128)S(1)}, u32[]{:S(2)}, u32[]{:S(2)}) collective-permute-start(f32[64,128]{1,0:T(8,128)S(1)} %add.896), channel_id=1, source_target_pairs={{0,2},{1,3},{2,0},{3,1},{4,6},{5,7},{6,4},{7,5},{8,10},{9,11},{10,... | collective-permute-start | bytes 98312 | tf_op jit(solution)/shard_map/ppermute | solution.py:19
  61.1 0.8 multiply_reduce_fusion.3
  61.8 1.7 %collective-permute-done.8 = f32[64,128]{1,0:T(8,128)S(1)} collective-permute-done((f32[64,128]{1,0:T(8,128)S(1)}, f32[64,128]{1,0:T(8,128)S(1)}, u32[]{:S(2)}, u32[]{:S(2)}) %collective-permute-start.8) | collective-permute-done | bytes 32800 | tf_op jit(solution)/shard_map/ppermute | solution.py:19
  65.5 9.9 %all_to_all.15 = f32[32,1,128]{2,1,0:T(1,128)S(1)} all-to-all(f32[32,1,128]{2,1,0:T(1,128)S(1)} %broadcast_in_dim.19), channel_id=1, replica_groups=mesh['dp'=8,'region'=4] {'dp','region'}, dimensions={0} | all-to-all | bytes 32768 | tf_op jit(solution)/shard_map/all_to_all | solution.py:27
  75.6 2.8 %fusion.22 = f32[64,1,2,128]{3,1,2,0:T(1,128)S(1)} fusion(bf16[64,2,128,128]{3,2,1,0:T(8,128)(2,1)} %param.7, bf16[64,128,1,1]{1,0,2,3:T(8,128)(2,1)S(1)} %get-tuple-element.5), kind=kOutput, calls=%fused_computation.45 | convolution fusion | flops 4194304 | bytes 4276224 | tf_op jit(solution)/shard_map/tsrb,tr->tsb/dot_general | solution.py:94
  78.4 1.9 %fusion.1 = f32[1024,128]{1,0:T(8,128)S(1)} fusion(f32[32,1024]{1,0:T(8,128)S(1)} %convert_subtract_fusion, f32[128,1024]{1,0:T(8,128)S(1)} %fusion, f32[32,128]{1,0:T(8,128)S(1)} %multiply_multiply_fusion, f32[128,128]{1,0:T(8,128)S(1)} %bitcast.282), kind=kOutput, calls=%fused_computation.7 | convolution fusion | flops 251842560 | bytes 1261568 | tf_op jit(solution)/shard_map/dot_general | solution.py:99
  80.4 1.5 %collective-permute-done.9 = f32[2,256,128]{2,1,0:T(8,128)S(1)} collective-permute-done((f32[2,256,128]{2,1,0:T(8,128)S(1)}, f32[2,256,128]{2,1,0:T(8,128)S(1)}, u32[]{:S(2)}, u32[]{:S(2)}) %collective-permute-start.9) | collective-permute-done | bytes 262176 | tf_op jit(solution)/shard_map/ppermute | solution.py:49
  82.6 5.0 %collective-permute-done.10 = f32[256,128]{1,0:T(8,128)S(1)} collective-permute-done((f32[256,128]{1,0:T(8,128)S(1)}, f32[256,128]{1,0:T(8,128)S(1)}, u32[]{:S(2)}, u32[]{:S(2)}) %collective-permute-start.10) | collective-permute-done | bytes 131104 | tf_op jit(solution)/shard_map/ppermute | solution.py:49
  88.2 4.4 %collective-permute-done.11 = f32[256,128]{1,0:T(8,128)S(1)} collective-permute-done((f32[256,128]{1,0:T(8,128)S(1)}, f32[256,128]{1,0:T(8,128)S(1)}, u32[]{:S(2)}, u32[]{:S(2)}) %collective-permute-start.11) | collective-permute-done | bytes 131104 | tf_op jit(solution)/shard_map/ppermute | solution.py:19
  92.7 0.6 collective-permute-start.12
  93.3 4.4 %collective-permute-done.12 = f32[256,128]{1,0:T(8,128)S(1)} collective-permute-done((f32[256,128]{1,0:T(8,128)S(1)}, f32[256,128]{1,0:T(8,128)S(1)}, u32[]{:S(2)}, u32[]{:S(2)}) %collective-permute-start.12) | collective-permute-done | bytes 131104 | tf_op jit(solution)/shard_map/ppermute | solution.py:19
  97.7 0.7 collective-permute-start.13
  98.4 6.7 %collective-permute-done.13 = f32[256,128]{1,0:T(8,128)S(1)} collective-permute-done((f32[256,128]{1,0:T(8,128)S(1)}, f32[256,128]{1,0:T(8,128)S(1)}, u32[]{:S(2)}, u32[]{:S(2)}) %collective-permute-start.13) | collective-permute-done | bytes 131104 | tf_op jit(solution)/shard_map/ppermute | solution.py:19
  105.7 4.4 %collective-permute-done.14 = f32[256,128]{1,0:T(8,128)S(1)} collective-permute-done((f32[256,128]{1,0:T(8,128)S(1)}, f32[256,128]{1,0:T(8,128)S(1)}, u32[]{:S(2)}, u32[]{:S(2)}) %collective-permute-start.14) | collective-permute-done | bytes 131104 | tf_op jit(solution)/shard_map/ppermute | solution.py:62
  110.3 1.5 %collective-permute-done.15 = f32[2,256,128]{2,1,0:T(8,128)S(1)} collective-permute-done((f32[2,256,128]{2,1,0:T(8,128)S(1)}, f32[2,256,128]{2,1,0:T(8,128)S(1)}, u32[]{:S(2)}, u32[]{:S(2)}) %collective-permute-start.15) | collective-permute-done | bytes 262176 | tf_op jit(solution)/shard_map/ppermute | solution.py:62
  111.7 0.7 multiply_reduce_fusion
  113.5 3.4 %fusion.16 = f32[64,1,128,1]{2,1,3,0:T(1,128)S(1)} fusion(bf16[64,2,128,128]{3,2,1,0:T(8,128)(2,1)} %param.7, bf16[64,2,128,1]{2,1,0,3:T(2,128)(2,1)S(1)} %bitcast.280), kind=kOutput, calls=%fused_computation.41 | convolution fusion | flops 4194304 | bytes 4259840 | tf_op jit(solution)/shard_map/tsrb,tsb->tr/dot_general | solution.py:128
  117.0 1.1 collective-permute-done.16
  118.6 0.7 fusion.28
  119.3 2.7 %collective-permute-done.17 = f32[64,128]{1,0:T(8,128)S(1)} collective-permute-done((f32[64,128]{1,0:T(8,128)S(1)}, f32[64,128]{1,0:T(8,128)S(1)}, u32[]{:S(2)}, u32[]{:S(2)}) %collective-permute-start.17) | collective-permute-done | bytes 32800 | tf_op jit(solution)/shard_map/ppermute | solution.py:19
  123.8 0.6 broadcast_in_dim.20
  124.4 2.5 %all-to-all-start.2 = ((f32[32,1,128]{2,1,0:T(1,128)}), f32[32,1,128]{2,1,0:T(1,128)S(1)}, u32[]{:S(2)}, u32[]{:S(2)}) async-start(f32[32,1,128]{2,1,0:T(1,128)} %broadcast_in_dim.20), calls=%async_computation.2 | async-start | bytes 32768 | tf_op jit(solution)/shard_map/all_to_all | solution.py:27
  127.2 6.8 %all-to-all-done.2 = f32[32,1,128]{2,1,0:T(1,128)S(1)} async-done(((f32[32,1,128]{2,1,0:T(1,128)}), f32[32,1,128]{2,1,0:T(1,128)S(1)}, u32[]{:S(2)}, u32[]{:S(2)}) %all-to-all-start.2) | async-done | bytes 16416 | tf_op jit(solution)/shard_map/all_to_all | solution.py:27
  134.3 0.7 multiply_add_fusion
  (55 shorter events, 6.3 us)
Async XLA Ops:
  2.5 13.7 %all-to-all-start = ((f32[8,1,128]{2,1,0:T(1,128)}), f32[8,1,128]{2,1,0:T(1,128)S(1)}, u32[]{:S(2)}, u32[]{:S(2)}) async-start(f32[8,1,128]{2,1,0:T(1,128)} %broadcast_in_dim.16), calls=%async_computation | async-start | bytes 8192 | tf_op jit(solution)/shard_map/all_to_all | solution.py:27
  21.8 1.6 %collective-permute-start = (f32[2,256,128]{2,1,0:T(8,128)S(1)}, f32[2,256,128]{2,1,0:T(8,128)S(1)}, u32[]{:S(2)}, u32[]{:S(2)}) collective-permute-start(f32[2,256,128]{2,1,0:T(8,128)S(1)} %dynamic-slice_bitcast_fusion.1), channel_id=1, source_target_pairs={{0,1},{1,0},{2,3},{3,2},{4,5},{5,4},{6,7},{7,6},{8,9},{9,8},{10,11... | collective-permute-start | bytes 786440 | tf_op jit(solution)/shard_map/ppermute | solution.py:49
  23.4 5.6 %collective-permute-start.1 = (f32[256,128]{1,0:T(8,128)S(1)}, f32[256,128]{1,0:T(8,128)S(1)}, u32[]{:S(2)}, u32[]{:S(2)}) collective-permute-start(f32[256,128]{1,0:T(8,128)S(1)} %dynamic-slice_bitcast_fusion.3), channel_id=1, source_target_pairs={{0,2},{1,3},{2,0},{3,1},{4,6},{5,7},{6,4},{7,5},{8,10},{9,11},{10,... | collective-permute-start | bytes 393224 | tf_op jit(solution)/shard_map/ppermute | solution.py:49
  29.1 5.0 %collective-permute-start.2 = (f32[256,128]{1,0:T(8,128)S(1)}, f32[256,128]{1,0:T(8,128)S(1)}, u32[]{:S(2)}, u32[]{:S(2)}) collective-permute-start(f32[256,128]{1,0:T(8,128)S(1)} %bitcast_add_fusion.3), channel_id=1, source_target_pairs={{0,4},{4,0},{8,12},{12,8},{16,20},{20,16},{24,28},{28,24},{1,5},{5... | collective-permute-start | bytes 393224 | tf_op jit(solution)/shard_map/ppermute | solution.py:19
  34.1 5.0 %collective-permute-start.3 = (f32[256,128]{1,0:T(8,128)S(1)}, f32[256,128]{1,0:T(8,128)S(1)}, u32[]{:S(2)}, u32[]{:S(2)}) collective-permute-start(f32[256,128]{1,0:T(8,128)S(1)} %add.893), channel_id=1, source_target_pairs={{0,8},{4,12},{8,0},{12,4},{16,24},{20,28},{24,16},{28,20},{1,9},{5... | collective-permute-start | bytes 393224 | tf_op jit(solution)/shard_map/ppermute | solution.py:19
  39.2 7.3 %collective-permute-start.4 = (f32[256,128]{1,0:T(8,128)S(1)}, f32[256,128]{1,0:T(8,128)S(1)}, u32[]{:S(2)}, u32[]{:S(2)}) collective-permute-start(f32[256,128]{1,0:T(8,128)S(1)} %add.894), channel_id=1, source_target_pairs={{0,16},{4,20},{8,24},{12,28},{16,0},{20,4},{24,8},{28,12},{1,17},{... | collective-permute-start | bytes 393224 | tf_op jit(solution)/shard_map/ppermute | solution.py:19
  46.5 5.0 %collective-permute-start.5 = (f32[256,128]{1,0:T(8,128)S(1)}, f32[256,128]{1,0:T(8,128)S(1)}, u32[]{:S(2)}, u32[]{:S(2)}) collective-permute-start(f32[256,128]{1,0:T(8,128)S(1)} %add.895), channel_id=1, source_target_pairs={{0,2},{1,3},{2,0},{3,1},{4,6},{5,7},{6,4},{7,5},{8,10},{9,11},{10,... | collective-permute-start | bytes 393224 | tf_op jit(solution)/shard_map/ppermute | solution.py:62
  51.6 1.6 %collective-permute-start.6 = (f32[2,256,128]{2,1,0:T(8,128)S(1)}, f32[2,256,128]{2,1,0:T(8,128)S(1)}, u32[]{:S(2)}, u32[]{:S(2)}) collective-permute-start(f32[2,256,128]{2,1,0:T(8,128)S(1)} %maximum_select_fusion.2), channel_id=1, source_target_pairs={{0,1},{1,0},{2,3},{3,2},{4,5},{5,4},{6,7},{7,6},{8,9},{9,8},{10,11... | collective-permute-start | bytes 786440 | tf_op jit(solution)/shard_map/ppermute | solution.py:62
  51.7 9.4 %copy-start.1 = (f32[32,128]{1,0:T(8,128)S(1)}, f32[32,128]{1,0:T(8,128)}, u32[]{:S(2)}) copy-start(f32[32,128]{1,0:T(8,128)} %param.10) | copy-start | bytes 49156
  53.2 10.3 %copy-start = (f32[64,128]{1,0:T(8,128)S(1)}, f32[64,128]{1,0:T(8,128)}, u32[]{:S(2)}) copy-start(f32[64,128]{1,0:T(8,128)} %param.6) | copy-start | bytes 98308
  58.3 1.2 collective-permute-start.7
  59.6 3.9 %collective-permute-start.8 = (f32[64,128]{1,0:T(8,128)S(1)}, f32[64,128]{1,0:T(8,128)S(1)}, u32[]{:S(2)}, u32[]{:S(2)}) collective-permute-start(f32[64,128]{1,0:T(8,128)S(1)} %add.896), channel_id=1, source_target_pairs={{0,2},{1,3},{2,0},{3,1},{4,6},{5,7},{6,4},{7,5},{8,10},{9,11},{10,... | collective-permute-start | bytes 98312 | tf_op jit(solution)/shard_map/ppermute | solution.py:19
  80.3 1.6 %collective-permute-start.9 = (f32[2,256,128]{2,1,0:T(8,128)S(1)}, f32[2,256,128]{2,1,0:T(8,128)S(1)}, u32[]{:S(2)}, u32[]{:S(2)}) collective-permute-start(f32[2,256,128]{2,1,0:T(8,128)S(1)} %dynamic-slice_bitcast_fusion), channel_id=1, source_target_pairs={{0,1},{1,0},{2,3},{3,2},{4,5},{5,4},{6,7},{7,6},{8,9},{9,8},{10,11... | collective-permute-start | bytes 786440 | tf_op jit(solution)/shard_map/ppermute | solution.py:49
  82.0 5.6 %collective-permute-start.10 = (f32[256,128]{1,0:T(8,128)S(1)}, f32[256,128]{1,0:T(8,128)S(1)}, u32[]{:S(2)}, u32[]{:S(2)}) collective-permute-start(f32[256,128]{1,0:T(8,128)S(1)} %dynamic-slice_bitcast_fusion.2), channel_id=1, source_target_pairs={{0,2},{1,3},{2,0},{3,1},{4,6},{5,7},{6,4},{7,5},{8,10},{9,11},{10,... | collective-permute-start | bytes 393224 | tf_op jit(solution)/shard_map/ppermute | solution.py:49
  87.6 5.0 %collective-permute-start.11 = (f32[256,128]{1,0:T(8,128)S(1)}, f32[256,128]{1,0:T(8,128)S(1)}, u32[]{:S(2)}, u32[]{:S(2)}) collective-permute-start(f32[256,128]{1,0:T(8,128)S(1)} %bitcast_add_fusion.2), channel_id=1, source_target_pairs={{0,4},{4,0},{8,12},{12,8},{16,20},{20,16},{24,28},{28,24},{1,5},{5... | collective-permute-start | bytes 393224 | tf_op jit(solution)/shard_map/ppermute | solution.py:19
  92.7 5.0 %collective-permute-start.12 = (f32[256,128]{1,0:T(8,128)S(1)}, f32[256,128]{1,0:T(8,128)S(1)}, u32[]{:S(2)}, u32[]{:S(2)}) collective-permute-start(f32[256,128]{1,0:T(8,128)S(1)} %add.936), channel_id=1, source_target_pairs={{0,8},{4,12},{8,0},{12,4},{16,24},{20,28},{24,16},{28,20},{1,9},{5... | collective-permute-start | bytes 393224 | tf_op jit(solution)/shard_map/ppermute | solution.py:19
  97.7 7.3 %collective-permute-start.13 = (f32[256,128]{1,0:T(8,128)S(1)}, f32[256,128]{1,0:T(8,128)S(1)}, u32[]{:S(2)}, u32[]{:S(2)}) collective-permute-start(f32[256,128]{1,0:T(8,128)S(1)} %add.937), channel_id=1, source_target_pairs={{0,16},{4,20},{8,24},{12,28},{16,0},{20,4},{24,8},{28,12},{1,17},{... | collective-permute-start | bytes 393224 | tf_op jit(solution)/shard_map/ppermute | solution.py:19
  105.1 5.0 %collective-permute-start.14 = (f32[256,128]{1,0:T(8,128)S(1)}, f32[256,128]{1,0:T(8,128)S(1)}, u32[]{:S(2)}, u32[]{:S(2)}) collective-permute-start(f32[256,128]{1,0:T(8,128)S(1)} %multiply_subtract_fusion), channel_id=1, source_target_pairs={{0,2},{1,3},{2,0},{3,1},{4,6},{5,7},{6,4},{7,5},{8,10},{9,11},{10,... | collective-permute-start | bytes 393224 | tf_op jit(solution)/shard_map/ppermute | solution.py:62
  110.1 1.6 %collective-permute-start.15 = (f32[2,256,128]{2,1,0:T(8,128)S(1)}, f32[2,256,128]{2,1,0:T(8,128)S(1)}, u32[]{:S(2)}, u32[]{:S(2)}) collective-permute-start(f32[2,256,128]{2,1,0:T(8,128)S(1)} %maximum_select_fusion.4), channel_id=1, source_target_pairs={{0,1},{1,0},{2,3},{3,2},{4,5},{5,4},{6,7},{7,6},{8,9},{9,8},{10,11... | collective-permute-start | bytes 786440 | tf_op jit(solution)/shard_map/ppermute | solution.py:62
  116.9 1.2 collective-permute-start.16
  118.1 3.9 %collective-permute-start.17 = (f32[64,128]{1,0:T(8,128)S(1)}, f32[64,128]{1,0:T(8,128)S(1)}, u32[]{:S(2)}, u32[]{:S(2)}) collective-permute-start(f32[64,128]{1,0:T(8,128)S(1)} %add.939), channel_id=1, source_target_pairs={{0,2},{1,3},{2,0},{3,1},{4,6},{5,7},{6,4},{7,5},{8,10},{9,11},{10,... | collective-permute-start | bytes 98312 | tf_op jit(solution)/shard_map/ppermute | solution.py:19
  124.4 9.6 %all-to-all-start.2 = ((f32[32,1,128]{2,1,0:T(1,128)}), f32[32,1,128]{2,1,0:T(1,128)S(1)}, u32[]{:S(2)}, u32[]{:S(2)}) async-start(f32[32,1,128]{2,1,0:T(1,128)} %broadcast_in_dim.20), calls=%async_computation.2 | async-start | bytes 32768 | tf_op jit(solution)/shard_map/all_to_all | solution.py:27

commit v8 on v7

--- a/solution.py
+++ b/solution.py
@@ -23,12 +23,9 @@
 
 def scalar_sum(value, axis):
     n = lax.psum(1, axis)
-    spread = jnp.broadcast_to(value.astype(jnp.float32), (n, 1, 128))
-    got = lax.all_to_all(spread, axis, 0, 0, tiled=False)
-    total = got[0]
-    for j in range(1, n):
-        total = total + got[j]
-    return total[0, 0]
+    spread = jnp.broadcast_to(value.astype(jnp.float32), (n,))
+    got = lax.all_to_all(spread, axis, 0, 0, tiled=True)
+    return jnp.sum(got)
 
 
 def halving_scatter(x, axis):

time: 136 us -> 140 us (1.029)
  between operations: 5.52 us -> 7.48 us
  other arithmetic: 8.48 us -> 10.4 us
    reduce_sum x0 -> x3, other arithmetic: none -> 1.88 us  [scalar_sum(): return jnp.sum(got)]
where the time goes in v8:
time: 140 us; the launch traced here: 139 us
  waiting for transfers between devices  70.3 us (50%)
  starting transfers between devices  20.5 us (15%)
  matrix products  16.6 us (12%)
  other arithmetic  10.4 us (7%)
  blocking collectives  9.93 us (7%)
  between operations  7.48 us (5%)
  local copies, waits for them, and re-layouts  3.72 us (3%)
    ppermute x10, waiting for transfers between devices, butterfly_sum(): x = x + lax.ppermute(x, axis, [(i, i ^ k) for i in range(n)])  37.4 us
    ppermute x4, waiting for transfers between devices, halving_scatter(): x = keep + lax.ppermute(send, axis, [(i, i ^ k) for i in range(n)])  12.1 us
    ppermute x4, waiting for transfers between devices, doubling_gather(): other = lax.ppermute(x, axis, [(i, i ^ k) for i in range(n)])  10.9 us
    all_to_all x2, waiting for transfers between devices, scalar_sum(): got = lax.all_to_all(spread, axis, 0, 0, tiled=True)  10 us
    all_to_all x1, blocking collectives, scalar_sum(): got = lax.all_to_all(spread, axis, 0, 0, tiled=True)  9.93 us
    all_to_all x2, starting transfers between devices, scalar_sum(): got = lax.all_to_all(spread, axis, 0, 0, tiled=True)  9.82 us
    dot_general x2, matrix products, local(): jnp.einsum('tsrb,tsb->tr', sensitivity, picked, preferred_element_type=jn...  6.74 us
    ppermute x10, starting transfers between devices, butterfly_sum(): x = x + lax.ppermute(x, axis, [(i, i ^ k) for i in range(n)])  6.08 us
  transfers between devices with their start and end apart: 20, of which 20 were waited for; matrix products, arithmetic and copies ran while one was open for 3% of the time, Pallas kernels for 0%

profile of v8, /device:TPU:0, one launch (start us, length us, event | category | flops | bytes accessed | tf_op | source)
XLA Modules:
  0.0 139.0 jit_solution(17589139600685843137)
XLA Ops:
  0.0 1.4 %multiply_reduce_fusion.2 = f32[]{:T(128)} fusion(f32[64,128]{1,0:T(8,128)} %param.6), kind=kLoop, calls=%fused_computation.50 | loop fusion | flops 16383 | bytes 32772 | tf_op jit(solution)/shard_map/reduce_sum | solution.py:112
  1.5 1.3 broadcast_in_dim.16
  2.7 7.3 %all-to-all-start = ((f32[8,1,1]{2,1,0:T(1,128)}), f32[8,1,1]{2,1,0:T(1,128)S(1)}, u32[]{:S(2)}, u32[]{:S(2)}) async-start(f32[8,1,1]{2,1,0:T(1,128)} %broadcast_in_dim.16), calls=%async_computation | async-start | bytes 8192 | tf_op jit(solution)/shard_map/all_to_all | solution.py:27
  10.0 0.8 slice_bitcast_fusion.1
  10.8 0.8 copy.18
  12.6 0.8 multiply_multiply_fusion.1
  13.4 3.0 %all-to-all-done = f32[8,1,1]{2,1,0:T(1,128)S(1)} async-done(((f32[8,1,1]{2,1,0:T(1,128)}), f32[8,1,1]{2,1,0:T(1,128)S(1)}, u32[]{:S(2)}, u32[]{:S(2)}) %all-to-all-start) | async-done | bytes 64 | tf_op jit(solution)/shard_map/all_to_all | solution.py:27
  17.7 0.8 convert_bitcast_fusion.1
  18.5 2.8 %fusion.24 = f32[64,1,2,128]{3,1,2,0:T(1,128)S(1)} fusion(bf16[64,2,128,128]{3,2,1,0:T(8,128)(2,1)} %param.7, bf16[64,128,1,1]{1,0,2,3:T(8,128)(2,1)S(1)} %convert_bitcast_fusion.1), kind=kOutput, calls=%fused_computation.47 | convolution fusion | flops 4194304 | bytes 4276224 | tf_op jit(solution)/shard_map/tsrb,tr->tsb/dot_general | solution.py:91
  21.3 1.9 %fusion.3 = f32[1024,128]{1,0:T(8,128)S(1)} fusion(f32[32,1024]{1,0:T(8,128)S(1)} %convert_subtract_fusion, f32[128,1024]{1,0:T(8,128)S(1)} %fusion, f32[32,128]{1,0:T(8,128)S(1)} %multiply_multiply_fusion.1, f32[128,128]{1,0:T(8,128)S(1)} %bitcast.89), kind=kOutput, calls=%fused_computation.9 | convolution fusion | flops 251842560 | bytes 1261568 | tf_op jit(solution)/shard_map/dot_general | solution.py:96
  23.3 1.5 %collective-permute-done = f32[2,256,128]{2,1,0:T(8,128)S(1)} collective-permute-done((f32[2,256,128]{2,1,0:T(8,128)S(1)}, f32[2,256,128]{2,1,0:T(8,128)S(1)}, u32[]{:S(2)}, u32[]{:S(2)}) %collective-permute-start) | collective-permute-done | bytes 262176 | tf_op jit(solution)/shard_map/ppermute | solution.py:46
  24.9 1.6 %collective-permute-start.1 = (f32[256,128]{1,0:T(8,128)S(1)}, f32[256,128]{1,0:T(8,128)S(1)}, u32[]{:S(2)}, u32[]{:S(2)}) collective-permute-start(f32[256,128]{1,0:T(8,128)S(1)} %dynamic-slice_bitcast_fusion.3), channel_id=1, source_target_pairs={{0,2},{1,3},{2,0},{3,1},{4,6},{5,7},{6,4},{7,5},{8,10},{9,11},{10,... | collective-permute-start | bytes 393224 | tf_op jit(solution)/shard_map/ppermute | solution.py:46
  26.4 4.0 %collective-permute-done.1 = f32[256,128]{1,0:T(8,128)S(1)} collective-permute-done((f32[256,128]{1,0:T(8,128)S(1)}, f32[256,128]{1,0:T(8,128)S(1)}, u32[]{:S(2)}, u32[]{:S(2)}) %collective-permute-start.1) | collective-permute-done | bytes 131104 | tf_op jit(solution)/shard_map/ppermute | solution.py:46
  31.1 4.4 %collective-permute-done.2 = f32[256,128]{1,0:T(8,128)S(1)} collective-permute-done((f32[256,128]{1,0:T(8,128)S(1)}, f32[256,128]{1,0:T(8,128)S(1)}, u32[]{:S(2)}, u32[]{:S(2)}) %collective-permute-start.2) | collective-permute-done | bytes 131104 | tf_op jit(solution)/shard_map/ppermute | solution.py:19
  36.2 4.4 %collective-permute-done.3 = f32[256,128]{1,0:T(8,128)S(1)} collective-permute-done((f32[256,128]{1,0:T(8,128)S(1)}, f32[256,128]{1,0:T(8,128)S(1)}, u32[]{:S(2)}, u32[]{:S(2)}) %collective-permute-start.3) | collective-permute-done | bytes 131104 | tf_op jit(solution)/shard_map/ppermute | solution.py:19
  40.6 0.6 collective-permute-start.4
  41.2 6.7 %collective-permute-done.4 = f32[256,128]{1,0:T(8,128)S(1)} collective-permute-done((f32[256,128]{1,0:T(8,128)S(1)}, f32[256,128]{1,0:T(8,128)S(1)}, u32[]{:S(2)}, u32[]{:S(2)}) %collective-permute-start.4) | collective-permute-done | bytes 131104 | tf_op jit(solution)/shard_map/ppermute | solution.py:19
  48.0 1.6 %collective-permute-start.5 = (f32[256,128]{1,0:T(8,128)S(1)}, f32[256,128]{1,0:T(8,128)S(1)}, u32[]{:S(2)}, u32[]{:S(2)}) collective-permute-start(f32[256,128]{1,0:T(8,128)S(1)} %add.110), channel_id=1, source_target_pairs={{0,2},{1,3},{2,0},{3,1},{4,6},{5,7},{6,4},{7,5},{8,10},{9,11},{10,... | collective-permute-start | bytes 393224 | tf_op jit(solution)/shard_map/ppermute | solution.py:59
  49.5 3.5 %collective-permute-done.5 = f32[256,128]{1,0:T(8,128)S(1)} collective-permute-done((f32[256,128]{1,0:T(8,128)S(1)}, f32[256,128]{1,0:T(8,128)S(1)}, u32[]{:S(2)}, u32[]{:S(2)}) %collective-permute-start.5) | collective-permute-done | bytes 131104 | tf_op jit(solution)/shard_map/ppermute | solution.py:59
  53.1 1.5 %collective-permute-done.6 = f32[2,256,128]{2,1,0:T(8,128)S(1)} collective-permute-done((f32[2,256,128]{2,1,0:T(8,128)S(1)}, f32[2,256,128]{2,1,0:T(8,128)S(1)}, u32[]{:S(2)}, u32[]{:S(2)}) %collective-permute-start.6) | collective-permute-done | bytes 262176 | tf_op jit(solution)/shard_map/ppermute | solution.py:59
  54.6 0.7 multiply_reduce_fusion.1
  56.4 3.4 %fusion.18 = f32[64,1,128,1]{2,1,3,0:T(1,128)S(1)} fusion(bf16[64,2,128,128]{3,2,1,0:T(8,128)(2,1)} %param.7, bf16[64,2,128,1]{2,1,0,3:T(2,128)(2,1)S(1)} %bitcast.87), kind=kOutput, calls=%fused_computation.43 | convolution fusion | flops 4194304 | bytes 4259840 | tf_op jit(solution)/shard_map/tsrb,tsb->tr/dot_general | solution.py:125
  59.9 1.1 collective-permute-done.7
  61.0 1.5 %collective-permute-start.8 = (f32[64,128]{1,0:T(8,128)S(1)}, f32[64,128]{1,0:T(8,128)S(1)}, u32[]{:S(2)}, u32[]{:S(2)}) collective-permute-start(f32[64,128]{1,0:T(8,128)S(1)} %add.111), channel_id=1, source_target_pairs={{0,2},{1,3},{2,0},{3,1},{4,6},{5,7},{6,4},{7,5},{8,10},{9,11},{10,... | collective-permute-start | bytes 98312 | tf_op jit(solution)/shard_map/ppermute | solution.py:19
  62.5 0.8 multiply_reduce_fusion.3
  63.2 1.7 %collective-permute-done.8 = f32[64,128]{1,0:T(8,128)S(1)} collective-permute-done((f32[64,128]{1,0:T(8,128)S(1)}, f32[64,128]{1,0:T(8,128)S(1)}, u32[]{:S(2)}, u32[]{:S(2)}) %collective-permute-start.8) | collective-permute-done | bytes 32800 | tf_op jit(solution)/shard_map/ppermute | solution.py:19
  66.9 9.9 %all_to_all.18 = f32[32,1,1]{2,1,0:T(1,128)S(1)} all-to-all(f32[32,1,1]{2,1,0:T(1,128)S(1)} %broadcast_in_dim.19), channel_id=1, replica_groups=mesh['dp'=8,'region'=4] {'dp','region'}, dimensions={0} | all-to-all | bytes 256 | tf_op jit(solution)/shard_map/all_to_all | solution.py:27
  76.8 0.6 reduce_sum.95
  78.2 2.8 %fusion.22 = f32[64,1,2,128]{3,1,2,0:T(1,128)S(1)} fusion(bf16[64,2,128,128]{3,2,1,0:T(8,128)(2,1)} %param.7, bf16[64,128,1,1]{1,0,2,3:T(8,128)(2,1)S(1)} %get-tuple-element.5), kind=kOutput, calls=%fused_computation.45 | convolution fusion | flops 4194304 | bytes 4276224 | tf_op jit(solution)/shard_map/tsrb,tr->tsb/dot_general | solution.py:91
  81.1 1.9 %fusion.1 = f32[1024,128]{1,0:T(8,128)S(1)} fusion(f32[32,1024]{1,0:T(8,128)S(1)} %convert_subtract_fusion, f32[128,1024]{1,0:T(8,128)S(1)} %fusion, f32[32,128]{1,0:T(8,128)S(1)} %multiply_multiply_fusion, f32[128,128]{1,0:T(8,128)S(1)} %bitcast.90), kind=kOutput, calls=%fused_computation.7 | convolution fusion | flops 251842560 | bytes 1261568 | tf_op jit(solution)/shard_map/dot_general | solution.py:96
  83.1 1.5 %collective-permute-done.9 = f32[2,256,128]{2,1,0:T(8,128)S(1)} collective-permute-done((f32[2,256,128]{2,1,0:T(8,128)S(1)}, f32[2,256,128]{2,1,0:T(8,128)S(1)}, u32[]{:S(2)}, u32[]{:S(2)}) %collective-permute-start.9) | collective-permute-done | bytes 262176 | tf_op jit(solution)/shard_map/ppermute | solution.py:46
  85.2 5.0 %collective-permute-done.10 = f32[256,128]{1,0:T(8,128)S(1)} collective-permute-done((f32[256,128]{1,0:T(8,128)S(1)}, f32[256,128]{1,0:T(8,128)S(1)}, u32[]{:S(2)}, u32[]{:S(2)}) %collective-permute-start.10) | collective-permute-done | bytes 131104 | tf_op jit(solution)/shard_map/ppermute | solution.py:46
  90.9 4.4 %collective-permute-done.11 = f32[256,128]{1,0:T(8,128)S(1)} collective-permute-done((f32[256,128]{1,0:T(8,128)S(1)}, f32[256,128]{1,0:T(8,128)S(1)}, u32[]{:S(2)}, u32[]{:S(2)}) %collective-permute-start.11) | collective-permute-done | bytes 131104 | tf_op jit(solution)/shard_map/ppermute | solution.py:19
  95.3 0.6 collective-permute-start.12
  96.0 4.4 %collective-permute-done.12 = f32[256,128]{1,0:T(8,128)S(1)} collective-permute-done((f32[256,128]{1,0:T(8,128)S(1)}, f32[256,128]{1,0:T(8,128)S(1)}, u32[]{:S(2)}, u32[]{:S(2)}) %collective-permute-start.12) | collective-permute-done | bytes 131104 | tf_op jit(solution)/shard_map/ppermute | solution.py:19
  100.4 0.7 collective-permute-start.13
  101.0 6.7 %collective-permute-done.13 = f32[256,128]{1,0:T(8,128)S(1)} collective-permute-done((f32[256,128]{1,0:T(8,128)S(1)}, f32[256,128]{1,0:T(8,128)S(1)}, u32[]{:S(2)}, u32[]{:S(2)}) %collective-permute-start.13) | collective-permute-done | bytes 131104 | tf_op jit(solution)/shard_map/ppermute | solution.py:19
  108.3 4.4 %collective-permute-done.14 = f32[256,128]{1,0:T(8,128)S(1)} collective-permute-done((f32[256,128]{1,0:T(8,128)S(1)}, f32[256,128]{1,0:T(8,128)S(1)}, u32[]{:S(2)}, u32[]{:S(2)}) %collective-permute-start.14) | collective-permute-done | bytes 131104 | tf_op jit(solution)/shard_map/ppermute | solution.py:59
  112.9 1.5 %collective-permute-done.15 = f32[2,256,128]{2,1,0:T(8,128)S(1)} collective-permute-done((f32[2,256,128]{2,1,0:T(8,128)S(1)}, f32[2,256,128]{2,1,0:T(8,128)S(1)}, u32[]{:S(2)}, u32[]{:S(2)}) %collective-permute-start.15) | collective-permute-done | bytes 262176 | tf_op jit(solution)/shard_map/ppermute | solution.py:59
  114.4 0.7 multiply_reduce_fusion
  116.1 3.4 %fusion.16 = f32[64,1,128,1]{2,1,3,0:T(1,128)S(1)} fusion(bf16[64,2,128,128]{3,2,1,0:T(8,128)(2,1)} %param.7, bf16[64,2,128,1]{2,1,0,3:T(2,128)(2,1)S(1)} %bitcast.88), kind=kOutput, calls=%fused_computation.41 | convolution fusion | flops 4194304 | bytes 4259840 | tf_op jit(solution)/shard_map/tsrb,tsb->tr/dot_general | solution.py:125
  119.8 0.9 collective-permute-done.16
  121.3 0.8 fusion.28
  122.0 2.6 %collective-permute-done.17 = f32[64,128]{1,0:T(8,128)S(1)} collective-permute-done((f32[64,128]{1,0:T(8,128)S(1)}, f32[64,128]{1,0:T(8,128)S(1)}, u32[]{:S(2)}, u32[]{:S(2)}) %collective-permute-start.17) | collective-permute-done | bytes 32800 | tf_op jit(solution)/shard_map/ppermute | solution.py:19
  127.2 2.5 %all-to-all-start.2 = ((f32[32,1,1]{2,1,0:T(1,128)}), f32[32,1,1]{2,1,0:T(1,128)S(1)}, u32[]{:S(2)}, u32[]{:S(2)}) async-start(f32[32,1,1]{2,1,0:T(1,128)} %broadcast_in_dim.20), calls=%async_computation.2 | async-start | bytes 32768 | tf_op jit(solution)/shard_map/all_to_all | solution.py:27
  129.8 7.0 %all-to-all-done.2 = f32[32,1,1]{2,1,0:T(1,128)S(1)} async-done(((f32[32,1,1]{2,1,0:T(1,128)}), f32[32,1,1]{2,1,0:T(1,128)S(1)}, u32[]{:S(2)}, u32[]{:S(2)}) %all-to-all-start.2) | async-done | bytes 160 | tf_op jit(solution)/shard_map/all_to_all | solution.py:27
  136.8 0.6 reduce_sum.99
  138.3 0.7 multiply_add_fusion
  (55 shorter events, 8.0 us)
Async XLA Ops:
  2.7 13.7 %all-to-all-start = ((f32[8,1,1]{2,1,0:T(1,128)}), f32[8,1,1]{2,1,0:T(1,128)S(1)}, u32[]{:S(2)}, u32[]{:S(2)}) async-start(f32[8,1,1]{2,1,0:T(1,128)} %broadcast_in_dim.16), calls=%async_computation | async-start | bytes 8192 | tf_op jit(solution)/shard_map/all_to_all | solution.py:27
  23.2 1.6 %collective-permute-start = (f32[2,256,128]{2,1,0:T(8,128)S(1)}, f32[2,256,128]{2,1,0:T(8,128)S(1)}, u32[]{:S(2)}, u32[]{:S(2)}) collective-permute-start(f32[2,256,128]{2,1,0:T(8,128)S(1)} %dynamic-slice_bitcast_fusion.1), channel_id=1, source_target_pairs={{0,1},{1,0},{2,3},{3,2},{4,5},{5,4},{6,7},{7,6},{8,9},{9,8},{10,11... | collective-permute-start | bytes 786440 | tf_op jit(solution)/shard_map/ppermute | solution.py:46
  24.9 5.6 %collective-permute-start.1 = (f32[256,128]{1,0:T(8,128)S(1)}, f32[256,128]{1,0:T(8,128)S(1)}, u32[]{:S(2)}, u32[]{:S(2)}) collective-permute-start(f32[256,128]{1,0:T(8,128)S(1)} %dynamic-slice_bitcast_fusion.3), channel_id=1, source_target_pairs={{0,2},{1,3},{2,0},{3,1},{4,6},{5,7},{6,4},{7,5},{8,10},{9,11},{10,... | collective-permute-start | bytes 393224 | tf_op jit(solution)/shard_map/ppermute | solution.py:46
  30.5 5.0 %collective-permute-start.2 = (f32[256,128]{1,0:T(8,128)S(1)}, f32[256,128]{1,0:T(8,128)S(1)}, u32[]{:S(2)}, u32[]{:S(2)}) collective-permute-start(f32[256,128]{1,0:T(8,128)S(1)} %bitcast_add_fusion.3), channel_id=1, source_target_pairs={{0,4},{4,0},{8,12},{12,8},{16,20},{20,16},{24,28},{28,24},{1,5},{5... | collective-permute-start | bytes 393224 | tf_op jit(solution)/shard_map/ppermute | solution.py:19
  35.5 5.0 %collective-permute-start.3 = (f32[256,128]{1,0:T(8,128)S(1)}, f32[256,128]{1,0:T(8,128)S(1)}, u32[]{:S(2)}, u32[]{:S(2)}) collective-permute-start(f32[256,128]{1,0:T(8,128)S(1)} %add.108), channel_id=1, source_target_pairs={{0,8},{4,12},{8,0},{12,4},{16,24},{20,28},{24,16},{28,20},{1,9},{5... | collective-permute-start | bytes 393224 | tf_op jit(solution)/shard_map/ppermute | solution.py:19
  40.6 7.3 %collective-permute-start.4 = (f32[256,128]{1,0:T(8,128)S(1)}, f32[256,128]{1,0:T(8,128)S(1)}, u32[]{:S(2)}, u32[]{:S(2)}) collective-permute-start(f32[256,128]{1,0:T(8,128)S(1)} %add.109), channel_id=1, source_target_pairs={{0,16},{4,20},{8,24},{12,28},{16,0},{20,4},{24,8},{28,12},{1,17},{... | collective-permute-start | bytes 393224 | tf_op jit(solution)/shard_map/ppermute | solution.py:19
  48.0 5.0 %collective-permute-start.5 = (f32[256,128]{1,0:T(8,128)S(1)}, f32[256,128]{1,0:T(8,128)S(1)}, u32[]{:S(2)}, u32[]{:S(2)}) collective-permute-start(f32[256,128]{1,0:T(8,128)S(1)} %add.110), channel_id=1, source_target_pairs={{0,2},{1,3},{2,0},{3,1},{4,6},{5,7},{6,4},{7,5},{8,10},{9,11},{10,... | collective-permute-start | bytes 393224 | tf_op jit(solution)/shard_map/ppermute | solution.py:59
  53.0 1.6 %collective-permute-start.6 = (f32[2,256,128]{2,1,0:T(8,128)S(1)}, f32[2,256,128]{2,1,0:T(8,128)S(1)}, u32[]{:S(2)}, u32[]{:S(2)}) collective-permute-start(f32[2,256,128]{2,1,0:T(8,128)S(1)} %maximum_select_fusion.2), channel_id=1, source_target_pairs={{0,1},{1,0},{2,3},{3,2},{4,5},{5,4},{6,7},{7,6},{8,9},{9,8},{10,11... | collective-permute-start | bytes 786440 | tf_op jit(solution)/shard_map/ppermute | solution.py:59
  53.1 9.4 %copy-start.1 = (f32[32,128]{1,0:T(8,128)S(1)}, f32[32,128]{1,0:T(8,128)}, u32[]{:S(2)}) copy-start(f32[32,128]{1,0:T(8,128)} %param.10) | copy-start | bytes 49156
  54.6 10.3 %copy-start = (f32[64,128]{1,0:T(8,128)S(1)}, f32[64,128]{1,0:T(8,128)}, u32[]{:S(2)}) copy-start(f32[64,128]{1,0:T(8,128)} %param.6) | copy-start | bytes 98308
  59.8 1.2 collective-permute-start.7
  61.0 3.9 %collective-permute-start.8 = (f32[64,128]{1,0:T(8,128)S(1)}, f32[64,128]{1,0:T(8,128)S(1)}, u32[]{:S(2)}, u32[]{:S(2)}) collective-permute-start(f32[64,128]{1,0:T(8,128)S(1)} %add.111), channel_id=1, source_target_pairs={{0,2},{1,3},{2,0},{3,1},{4,6},{5,7},{6,4},{7,5},{8,10},{9,11},{10,... | collective-permute-start | bytes 98312 | tf_op jit(solution)/shard_map/ppermute | solution.py:19
  83.0 1.6 %collective-permute-start.9 = (f32[2,256,128]{2,1,0:T(8,128)S(1)}, f32[2,256,128]{2,1,0:T(8,128)S(1)}, u32[]{:S(2)}, u32[]{:S(2)}) collective-permute-start(f32[2,256,128]{2,1,0:T(8,128)S(1)} %dynamic-slice_bitcast_fusion), channel_id=1, source_target_pairs={{0,1},{1,0},{2,3},{3,2},{4,5},{5,4},{6,7},{7,6},{8,9},{9,8},{10,11... | collective-permute-start | bytes 786440 | tf_op jit(solution)/shard_map/ppermute | solution.py:46
  84.6 5.6 %collective-permute-start.10 = (f32[256,128]{1,0:T(8,128)S(1)}, f32[256,128]{1,0:T(8,128)S(1)}, u32[]{:S(2)}, u32[]{:S(2)}) collective-permute-start(f32[256,128]{1,0:T(8,128)S(1)} %dynamic-slice_bitcast_fusion.2), channel_id=1, source_target_pairs={{0,2},{1,3},{2,0},{3,1},{4,6},{5,7},{6,4},{7,5},{8,10},{9,11},{10,... | collective-permute-start | bytes 393224 | tf_op jit(solution)/shard_map/ppermute | solution.py:46
  90.3 5.0 %collective-permute-start.11 = (f32[256,128]{1,0:T(8,128)S(1)}, f32[256,128]{1,0:T(8,128)S(1)}, u32[]{:S(2)}, u32[]{:S(2)}) collective-permute-start(f32[256,128]{1,0:T(8,128)S(1)} %bitcast_add_fusion.2), channel_id=1, source_target_pairs={{0,4},{4,0},{8,12},{12,8},{16,20},{20,16},{24,28},{28,24},{1,5},{5... | collective-permute-start | bytes 393224 | tf_op jit(solution)/shard_map/ppermute | solution.py:19
  95.3 5.0 %collective-permute-start.12 = (f32[256,128]{1,0:T(8,128)S(1)}, f32[256,128]{1,0:T(8,128)S(1)}, u32[]{:S(2)}, u32[]{:S(2)}) collective-permute-start(f32[256,128]{1,0:T(8,128)S(1)} %add.119), channel_id=1, source_target_pairs={{0,8},{4,12},{8,0},{12,4},{16,24},{20,28},{24,16},{28,20},{1,9},{5... | collective-permute-start | bytes 393224 | tf_op jit(solution)/shard_map/ppermute | solution.py:19
  100.4 7.3 %collective-permute-start.13 = (f32[256,128]{1,0:T(8,128)S(1)}, f32[256,128]{1,0:T(8,128)S(1)}, u32[]{:S(2)}, u32[]{:S(2)}) collective-permute-start(f32[256,128]{1,0:T(8,128)S(1)} %add.120), channel_id=1, source_target_pairs={{0,16},{4,20},{8,24},{12,28},{16,0},{20,4},{24,8},{28,12},{1,17},{... | collective-permute-start | bytes 393224 | tf_op jit(solution)/shard_map/ppermute | solution.py:19
  107.7 5.0 %collective-permute-start.14 = (f32[256,128]{1,0:T(8,128)S(1)}, f32[256,128]{1,0:T(8,128)S(1)}, u32[]{:S(2)}, u32[]{:S(2)}) collective-permute-start(f32[256,128]{1,0:T(8,128)S(1)} %multiply_subtract_fusion), channel_id=1, source_target_pairs={{0,2},{1,3},{2,0},{3,1},{4,6},{5,7},{6,4},{7,5},{8,10},{9,11},{10,... | collective-permute-start | bytes 393224 | tf_op jit(solution)/shard_map/ppermute | solution.py:59
  112.8 1.6 %collective-permute-start.15 = (f32[2,256,128]{2,1,0:T(8,128)S(1)}, f32[2,256,128]{2,1,0:T(8,128)S(1)}, u32[]{:S(2)}, u32[]{:S(2)}) collective-permute-start(f32[2,256,128]{2,1,0:T(8,128)S(1)} %maximum_select_fusion.4), channel_id=1, source_target_pairs={{0,1},{1,0},{2,3},{3,2},{4,5},{5,4},{6,7},{7,6},{8,9},{9,8},{10,11... | collective-permute-start | bytes 786440 | tf_op jit(solution)/shard_map/ppermute | solution.py:59
  119.5 1.2 collective-permute-start.16
  120.7 3.9 %collective-permute-start.17 = (f32[64,128]{1,0:T(8,128)S(1)}, f32[64,128]{1,0:T(8,128)S(1)}, u32[]{:S(2)}, u32[]{:S(2)}) collective-permute-start(f32[64,128]{1,0:T(8,128)S(1)} %add.122), channel_id=1, source_target_pairs={{0,2},{1,3},{2,0},{3,1},{4,6},{5,7},{6,4},{7,5},{8,10},{9,11},{10,... | collective-permute-start | bytes 98312 | tf_op jit(solution)/shard_map/ppermute | solution.py:19
  127.2 9.6 %all-to-all-start.2 = ((f32[32,1,1]{2,1,0:T(1,128)}), f32[32,1,1]{2,1,0:T(1,128)S(1)}, u32[]{:S(2)}, u32[]{:S(2)}) async-start(f32[32,1,1]{2,1,0:T(1,128)} %broadcast_in_dim.20), calls=%async_computation.2 | async-start | bytes 32768 | tf_op jit(solution)/shard_map/all_to_all | solution.py:27

commit v9 on v7

--- a/solution.py
+++ b/solution.py
@@ -87,6 +87,7 @@
         0,
     )
     select_half = select.astype(jnp.bfloat16)
+    select_triple = jnp.concatenate([select_half] * 3, 0)
     n_slots = flat_blocks.shape[0]
 
     def transposed_part(left_rays, left_faces):
@@ -96,11 +97,15 @@
         )
         contrib_rows = contrib.reshape(-1, contrib.shape[-1])
         face_term = face_scale * left_faces
+        terms = jnp.concatenate([contrib_rows, face_term], 0)
+        high = terms.astype(jnp.bfloat16)
+        rest = terms - high.astype(jnp.float32)
+        middle = rest.astype(jnp.bfloat16)
+        low = (rest - middle.astype(jnp.float32)).astype(jnp.bfloat16)
         partials = lax.dot_general(
-            select,
-            jnp.concatenate([contrib_rows, face_term], 0),
+            select_triple,
+            jnp.concatenate([high, middle, low], 0),
             (((0,), (0,)), ((), ())),
-            precision=lax.Precision.HIGHEST,
             preferred_element_type=jnp.float32,
         )
         piece = halving_scatter(partials, "region")

time: 136 us -> 133 us (0.978)
  matrix products: 16.6 us -> 13.8 us
    dot_general x2, matrix products: 3.71 us -> 0.94 us  [transposed_part(): lax.dot_general(select_triple, jnp.concatenate([high, middle, low], 0), (...]
  transfers between devices with their start and end apart: 20 -> 20, of which waited for: 20 -> 20; matrix products, arithmetic and copies ran while one was open for 3% -> 4% of each run, Pallas kernels for 0% -> 0%
where the time goes in v9:
time: 133 us
  waiting for transfers between devices  69.7 us (52%)
  starting transfers between devices  20.5 us (15%)
  matrix products  13.8 us (10%)
  blocking collectives  10.4 us (8%)
  other arithmetic  9.2 us (7%)
  between operations  5.65 us (4%)
  local copies, waits for them, and re-layouts  3.59 us (3%)
    ppermute x10, waiting for transfers between devices, butterfly_sum(): x = x + lax.ppermute(x, axis, [(i, i ^ k) for i in range(n)])  37.5 us
    ppermute x4, waiting for transfers between devices, halving_scatter(): x = keep + lax.ppermute(send, axis, [(i, i ^ k) for i in range(n)])  12.1 us
    ppermute x4, waiting for transfers between devices, doubling_gather(): other = lax.ppermute(x, axis, [(i, i ^ k) for i in range(n)])  10.7 us
    all_to_all x1, blocking collectives, scalar_sum(): got = lax.all_to_all(spread, axis, 0, 0, tiled=False)  10.4 us
    all_to_all x2, starting transfers between devices, scalar_sum(): got = lax.all_to_all(spread, axis, 0, 0, tiled=False)  9.82 us
    all_to_all x2, waiting for transfers between devices, scalar_sum(): got = lax.all_to_all(spread, axis, 0, 0, tiled=False)  9.46 us
    dot_general x2, matrix products, local(): jnp.einsum('tsrb,tsb->tr', sensitivity, picked, preferred_element_type=jn...  6.74 us
    ppermute x10, starting transfers between devices, butterfly_sum(): x = x + lax.ppermute(x, axis, [(i, i ^ k) for i in range(n)])  6.09 us
  transfers between devices with their start and end apart: 20, of which 20 were waited for; matrix products, arithmetic and copies ran while one was open for 4% of the time, Pallas kernels for 0%

profile of v9, /device:TPU:0, one launch (start us, length us, event | category | flops | bytes accessed | tf_op | source)
XLA Modules:
  0.0 132.8 jit_solution(12277149112628622177)
XLA Ops:
  0.0 1.4 %multiply_reduce_fusion.2 = f32[]{:T(128)} fusion(f32[64,128]{1,0:T(8,128)} %param.6), kind=kLoop, calls=%fused_computation.66 | loop fusion | flops 16383 | bytes 32772 | tf_op jit(solution)/shard_map/reduce_sum | solution.py:120
  1.4 1.2 broadcast_in_dim.16
  2.5 7.3 %all-to-all-start = ((f32[8,1,128]{2,1,0:T(1,128)}), f32[8,1,128]{2,1,0:T(1,128)S(1)}, u32[]{:S(2)}, u32[]{:S(2)}) async-start(f32[8,1,128]{2,1,0:T(1,128)} %broadcast_in_dim.16), calls=%async_computation | async-start | bytes 8192 | tf_op jit(solution)/shard_map/all_to_all | solution.py:27
  9.8 0.8 copy.10
  10.8 0.8 slice_bitcast_fusion.31
  12.8 0.8 multiply_multiply_fusion.1
  13.6 2.6 %all-to-all-done = f32[8,1,128]{2,1,0:T(1,128)S(1)} async-done(((f32[8,1,128]{2,1,0:T(1,128)}), f32[8,1,128]{2,1,0:T(1,128)S(1)}, u32[]{:S(2)}, u32[]{:S(2)}) %all-to-all-start) | async-done | bytes 4128 | tf_op jit(solution)/shard_map/all_to_all | solution.py:27
  16.3 0.8 convert_bitcast_fusion.1
  17.1 2.8 %fusion.31 = f32[64,1,2,128]{3,1,2,0:T(1,128)S(1)} fusion(bf16[64,2,128,128]{3,2,1,0:T(8,128)(2,1)} %param.7, bf16[64,128,1,1]{1,0,2,3:T(8,128)(2,1)S(1)} %convert_bitcast_fusion.1), kind=kOutput, calls=%fused_computation.63 | convolution fusion | flops 4194304 | bytes 4276224 | tf_op jit(solution)/shard_map/tsrb,tr->tsb/dot_general | solution.py:95
  20.6 1.5 %collective-permute-done = f32[2,256,128]{2,1,0:T(8,128)S(1)} collective-permute-done((f32[2,256,128]{2,1,0:T(8,128)S(1)}, f32[2,256,128]{2,1,0:T(8,128)S(1)}, u32[]{:S(2)}, u32[]{:S(2)}) %collective-permute-start) | collective-permute-done | bytes 262176 | tf_op jit(solution)/shard_map/ppermute | solution.py:49
  22.1 1.6 %collective-permute-start.1 = (f32[256,128]{1,0:T(8,128)S(1)}, f32[256,128]{1,0:T(8,128)S(1)}, u32[]{:S(2)}, u32[]{:S(2)}) collective-permute-start(f32[256,128]{1,0:T(8,128)S(1)} %dynamic-slice_bitcast_fusion.3), channel_id=1, source_target_pairs={{0,2},{1,3},{2,0},{3,1},{4,6},{5,7},{6,4},{7,5},{8,10},{9,11},{10,... | collective-permute-start | bytes 393224 | tf_op jit(solution)/shard_map/ppermute | solution.py:49
  23.7 4.0 %collective-permute-done.1 = f32[256,128]{1,0:T(8,128)S(1)} collective-permute-done((f32[256,128]{1,0:T(8,128)S(1)}, f32[256,128]{1,0:T(8,128)S(1)}, u32[]{:S(2)}, u32[]{:S(2)}) %collective-permute-start.1) | collective-permute-done | bytes 131104 | tf_op jit(solution)/shard_map/ppermute | solution.py:49
  27.7 0.6 collective-permute-start.2
  28.3 4.4 %collective-permute-done.2 = f32[256,128]{1,0:T(8,128)S(1)} collective-permute-done((f32[256,128]{1,0:T(8,128)S(1)}, f32[256,128]{1,0:T(8,128)S(1)}, u32[]{:S(2)}, u32[]{:S(2)}) %collective-permute-start.2) | collective-permute-done | bytes 131104 | tf_op jit(solution)/shard_map/ppermute | solution.py:19
  33.4 4.4 %collective-permute-done.3 = f32[256,128]{1,0:T(8,128)S(1)} collective-permute-done((f32[256,128]{1,0:T(8,128)S(1)}, f32[256,128]{1,0:T(8,128)S(1)}, u32[]{:S(2)}, u32[]{:S(2)}) %collective-permute-start.3) | collective-permute-done | bytes 131104 | tf_op jit(solution)/shard_map/ppermute | solution.py:19
  37.8 0.6 collective-permute-start.4
  38.5 6.7 %collective-permute-done.4 = f32[256,128]{1,0:T(8,128)S(1)} collective-permute-done((f32[256,128]{1,0:T(8,128)S(1)}, f32[256,128]{1,0:T(8,128)S(1)}, u32[]{:S(2)}, u32[]{:S(2)}) %collective-permute-start.4) | collective-permute-done | bytes 131104 | tf_op jit(solution)/shard_map/ppermute | solution.py:19
  45.2 1.6 %collective-permute-start.5 = (f32[256,128]{1,0:T(8,128)S(1)}, f32[256,128]{1,0:T(8,128)S(1)}, u32[]{:S(2)}, u32[]{:S(2)}) collective-permute-start(f32[256,128]{1,0:T(8,128)S(1)} %add.895), channel_id=1, source_target_pairs={{0,2},{1,3},{2,0},{3,1},{4,6},{5,7},{6,4},{7,5},{8,10},{9,11},{10,... | collective-permute-start | bytes 393224 | tf_op jit(solution)/shard_map/ppermute | solution.py:62
  46.9 3.4 %collective-permute-done.5 = f32[256,128]{1,0:T(8,128)S(1)} collective-permute-done((f32[256,128]{1,0:T(8,128)S(1)}, f32[256,128]{1,0:T(8,128)S(1)}, u32[]{:S(2)}, u32[]{:S(2)}) %collective-permute-start.5) | collective-permute-done | bytes 131104 | tf_op jit(solution)/shard_map/ppermute | solution.py:62
  50.5 1.4 %collective-permute-done.6 = f32[2,256,128]{2,1,0:T(8,128)S(1)} collective-permute-done((f32[2,256,128]{2,1,0:T(8,128)S(1)}, f32[2,256,128]{2,1,0:T(8,128)S(1)}, u32[]{:S(2)}, u32[]{:S(2)}) %collective-permute-start.6) | collective-permute-done | bytes 262176 | tf_op jit(solution)/shard_map/ppermute | solution.py:62
  51.8 0.7 multiply_reduce_fusion.1
  53.6 3.4 %fusion.25 = f32[64,1,128,1]{2,1,3,0:T(1,128)S(1)} fusion(bf16[64,2,128,128]{3,2,1,0:T(8,128)(2,1)} %param.7, bf16[64,2,128,1]{2,1,0,3:T(2,128)(2,1)S(1)} %bitcast.285), kind=kOutput, calls=%fused_computation.57 | convolution fusion | flops 4194304 | bytes 4259840 | tf_op jit(solution)/shard_map/tsrb,tsb->tr/dot_general | solution.py:133
  57.2 1.1 collective-permute-done.7
  58.2 1.5 %collective-permute-start.8 = (f32[64,128]{1,0:T(8,128)S(1)}, f32[64,128]{1,0:T(8,128)S(1)}, u32[]{:S(2)}, u32[]{:S(2)}) collective-permute-start(f32[64,128]{1,0:T(8,128)S(1)} %add.896), channel_id=1, source_target_pairs={{0,2},{1,3},{2,0},{3,1},{4,6},{5,7},{6,4},{7,5},{8,10},{9,11},{10,... | collective-permute-start | bytes 98312 | tf_op jit(solution)/shard_map/ppermute | solution.py:19
  59.7 0.7 multiply_reduce_fusion.3
  60.5 1.7 %collective-permute-done.8 = f32[64,128]{1,0:T(8,128)S(1)} collective-permute-done((f32[64,128]{1,0:T(8,128)S(1)}, f32[64,128]{1,0:T(8,128)S(1)}, u32[]{:S(2)}, u32[]{:S(2)}) %collective-permute-start.8) | collective-permute-done | bytes 32800 | tf_op jit(solution)/shard_map/ppermute | solution.py:19
  62.2 0.6 multiply_reduce_fusion.4
  64.1 10.4 %all_to_all.15 = f32[32,1,128]{2,1,0:T(1,128)S(1)} all-to-all(f32[32,1,128]{2,1,0:T(1,128)S(1)} %broadcast_in_dim.19), channel_id=1, replica_groups=mesh['dp'=8,'region'=4] {'dp','region'}, dimensions={0} | all-to-all | bytes 32768 | tf_op jit(solution)/shard_map/all_to_all | solution.py:27
  74.7 2.8 %fusion.29 = f32[64,1,2,128]{3,1,2,0:T(1,128)S(1)} fusion(bf16[64,2,128,128]{3,2,1,0:T(8,128)(2,1)} %param.7, bf16[64,128,1,1]{1,0,2,3:T(8,128)(2,1)S(1)} %get-tuple-element.5), kind=kOutput, calls=%fused_computation.61 | convolution fusion | flops 4194304 | bytes 4276224 | tf_op jit(solution)/shard_map/tsrb,tr->tsb/dot_general | solution.py:95
  78.2 1.5 %collective-permute-done.9 = f32[2,256,128]{2,1,0:T(8,128)S(1)} collective-permute-done((f32[2,256,128]{2,1,0:T(8,128)S(1)}, f32[2,256,128]{2,1,0:T(8,128)S(1)}, u32[]{:S(2)}, u32[]{:S(2)}) %collective-permute-start.9) | collective-permute-done | bytes 262176 | tf_op jit(solution)/shard_map/ppermute | solution.py:49
  80.3 5.0 %collective-permute-done.10 = f32[256,128]{1,0:T(8,128)S(1)} collective-permute-done((f32[256,128]{1,0:T(8,128)S(1)}, f32[256,128]{1,0:T(8,128)S(1)}, u32[]{:S(2)}, u32[]{:S(2)}) %collective-permute-start.10) | collective-permute-done | bytes 131104 | tf_op jit(solution)/shard_map/ppermute | solution.py:49
  85.4 0.6 collective-permute-start.11
  86.0 4.4 %collective-permute-done.11 = f32[256,128]{1,0:T(8,128)S(1)} collective-permute-done((f32[256,128]{1,0:T(8,128)S(1)}, f32[256,128]{1,0:T(8,128)S(1)}, u32[]{:S(2)}, u32[]{:S(2)}) %collective-permute-start.11) | collective-permute-done | bytes 131104 | tf_op jit(solution)/shard_map/ppermute | solution.py:19
  90.4 0.6 collective-permute-start.12
  91.1 4.4 %collective-permute-done.12 = f32[256,128]{1,0:T(8,128)S(1)} collective-permute-done((f32[256,128]{1,0:T(8,128)S(1)}, f32[256,128]{1,0:T(8,128)S(1)}, u32[]{:S(2)}, u32[]{:S(2)}) %collective-permute-start.12) | collective-permute-done | bytes 131104 | tf_op jit(solution)/shard_map/ppermute | solution.py:19
  95.5 0.7 collective-permute-start.13
  96.1 6.7 %collective-permute-done.13 = f32[256,128]{1,0:T(8,128)S(1)} collective-permute-done((f32[256,128]{1,0:T(8,128)S(1)}, f32[256,128]{1,0:T(8,128)S(1)}, u32[]{:S(2)}, u32[]{:S(2)}) %collective-permute-start.13) | collective-permute-done | bytes 131104 | tf_op jit(solution)/shard_map/ppermute | solution.py:19
  103.4 4.4 %collective-permute-done.14 = f32[256,128]{1,0:T(8,128)S(1)} collective-permute-done((f32[256,128]{1,0:T(8,128)S(1)}, f32[256,128]{1,0:T(8,128)S(1)}, u32[]{:S(2)}, u32[]{:S(2)}) %collective-permute-start.14) | collective-permute-done | bytes 131104 | tf_op jit(solution)/shard_map/ppermute | solution.py:62
  108.0 1.5 %collective-permute-done.15 = f32[2,256,128]{2,1,0:T(8,128)S(1)} collective-permute-done((f32[2,256,128]{2,1,0:T(8,128)S(1)}, f32[2,256,128]{2,1,0:T(8,128)S(1)}, u32[]{:S(2)}, u32[]{:S(2)}) %collective-permute-start.15) | collective-permute-done | bytes 262176 | tf_op jit(solution)/shard_map/ppermute | solution.py:62
  109.5 0.7 multiply_reduce_fusion
  111.2 3.4 %fusion.23 = f32[64,1,128,1]{2,1,3,0:T(1,128)S(1)} fusion(bf16[64,2,128,128]{3,2,1,0:T(8,128)(2,1)} %param.7, bf16[64,2,128,1]{2,1,0,3:T(2,128)(2,1)S(1)} %bitcast.286), kind=kOutput, calls=%fused_computation.55 | convolution fusion | flops 4194304 | bytes 4259840 | tf_op jit(solution)/shard_map/tsrb,tsb->tr/dot_general | solution.py:133
  114.8 1.1 collective-permute-done.16
  116.4 0.7 fusion.38
  117.1 2.7 %collective-permute-done.17 = f32[64,128]{1,0:T(8,128)S(1)} collective-permute-done((f32[64,128]{1,0:T(8,128)S(1)}, f32[64,128]{1,0:T(8,128)S(1)}, u32[]{:S(2)}, u32[]{:S(2)}) %collective-permute-start.17) | collective-permute-done | bytes 32800 | tf_op jit(solution)/shard_map/ppermute | solution.py:19
  121.6 0.6 broadcast_in_dim.20
  122.3 2.5 %all-to-all-start.2 = ((f32[32,1,128]{2,1,0:T(1,128)}), f32[32,1,128]{2,1,0:T(1,128)S(1)}, u32[]{:S(2)}, u32[]{:S(2)}) async-start(f32[32,1,128]{2,1,0:T(1,128)} %broadcast_in_dim.20), calls=%async_computation.2 | async-start | bytes 32768 | tf_op jit(solution)/shard_map/all_to_all | solution.py:27
  125.0 6.8 %all-to-all-done.2 = f32[32,1,128]{2,1,0:T(1,128)S(1)} async-done(((f32[32,1,128]{2,1,0:T(1,128)}), f32[32,1,128]{2,1,0:T(1,128)S(1)}, u32[]{:S(2)}, u32[]{:S(2)}) %all-to-all-start.2) | async-done | bytes 16416 | tf_op jit(solution)/shard_map/all_to_all | solution.py:27
  132.1 0.7 multiply_add_fusion
  (65 shorter events, 6.7 us)
Async XLA Ops:
  2.5 13.7 %all-to-all-start = ((f32[8,1,128]{2,1,0:T(1,128)}), f32[8,1,128]{2,1,0:T(1,128)S(1)}, u32[]{:S(2)}, u32[]{:S(2)}) async-start(f32[8,1,128]{2,1,0:T(1,128)} %broadcast_in_dim.16), calls=%async_computation | async-start | bytes 8192 | tf_op jit(solution)/shard_map/all_to_all | solution.py:27
  20.4 1.6 %collective-permute-start = (f32[2,256,128]{2,1,0:T(8,128)S(1)}, f32[2,256,128]{2,1,0:T(8,128)S(1)}, u32[]{:S(2)}, u32[]{:S(2)}) collective-permute-start(f32[2,256,128]{2,1,0:T(8,128)S(1)} %dynamic-slice_bitcast_fusion.1), channel_id=1, source_target_pairs={{0,1},{1,0},{2,3},{3,2},{4,5},{5,4},{6,7},{7,6},{8,9},{9,8},{10,11... | collective-permute-start | bytes 786440 | tf_op jit(solution)/shard_map/ppermute | solution.py:49
  22.1 5.6 %collective-permute-start.1 = (f32[256,128]{1,0:T(8,128)S(1)}, f32[256,128]{1,0:T(8,128)S(1)}, u32[]{:S(2)}, u32[]{:S(2)}) collective-permute-start(f32[256,128]{1,0:T(8,128)S(1)} %dynamic-slice_bitcast_fusion.3), channel_id=1, source_target_pairs={{0,2},{1,3},{2,0},{3,1},{4,6},{5,7},{6,4},{7,5},{8,10},{9,11},{10,... | collective-permute-start | bytes 393224 | tf_op jit(solution)/shard_map/ppermute | solution.py:49
  27.7 5.0 %collective-permute-start.2 = (f32[256,128]{1,0:T(8,128)S(1)}, f32[256,128]{1,0:T(8,128)S(1)}, u32[]{:S(2)}, u32[]{:S(2)}) collective-permute-start(f32[256,128]{1,0:T(8,128)S(1)} %bitcast_add_fusion.3), channel_id=1, source_target_pairs={{0,4},{4,0},{8,12},{12,8},{16,20},{20,16},{24,28},{28,24},{1,5},{5... | collective-permute-start | bytes 393224 | tf_op jit(solution)/shard_map/ppermute | solution.py:19
  32.8 5.0 %collective-permute-start.3 = (f32[256,128]{1,0:T(8,128)S(1)}, f32[256,128]{1,0:T(8,128)S(1)}, u32[]{:S(2)}, u32[]{:S(2)}) collective-permute-start(f32[256,128]{1,0:T(8,128)S(1)} %add.893), channel_id=1, source_target_pairs={{0,8},{4,12},{8,0},{12,4},{16,24},{20,28},{24,16},{28,20},{1,9},{5... | collective-permute-start | bytes 393224 | tf_op jit(solution)/shard_map/ppermute | solution.py:19
  37.8 7.3 %collective-permute-start.4 = (f32[256,128]{1,0:T(8,128)S(1)}, f32[256,128]{1,0:T(8,128)S(1)}, u32[]{:S(2)}, u32[]{:S(2)}) collective-permute-start(f32[256,128]{1,0:T(8,128)S(1)} %add.894), channel_id=1, source_target_pairs={{0,16},{4,20},{8,24},{12,28},{16,0},{20,4},{24,8},{28,12},{1,17},{... | collective-permute-start | bytes 393224 | tf_op jit(solution)/shard_map/ppermute | solution.py:19
  45.2 5.0 %collective-permute-start.5 = (f32[256,128]{1,0:T(8,128)S(1)}, f32[256,128]{1,0:T(8,128)S(1)}, u32[]{:S(2)}, u32[]{:S(2)}) collective-permute-start(f32[256,128]{1,0:T(8,128)S(1)} %add.895), channel_id=1, source_target_pairs={{0,2},{1,3},{2,0},{3,1},{4,6},{5,7},{6,4},{7,5},{8,10},{9,11},{10,... | collective-permute-start | bytes 393224 | tf_op jit(solution)/shard_map/ppermute | solution.py:62
  50.2 1.6 %collective-permute-start.6 = (f32[2,256,128]{2,1,0:T(8,128)S(1)}, f32[2,256,128]{2,1,0:T(8,128)S(1)}, u32[]{:S(2)}, u32[]{:S(2)}) collective-permute-start(f32[2,256,128]{2,1,0:T(8,128)S(1)} %maximum_select_fusion.2), channel_id=1, source_target_pairs={{0,1},{1,0},{2,3},{3,2},{4,5},{5,4},{6,7},{7,6},{8,9},{9,8},{10,11... | collective-permute-start | bytes 786440 | tf_op jit(solution)/shard_map/ppermute | solution.py:62
  50.4 9.3 %copy-start.1 = (f32[32,128]{1,0:T(8,128)S(1)}, f32[32,128]{1,0:T(8,128)}, u32[]{:S(2)}) copy-start(f32[32,128]{1,0:T(8,128)} %param.10) | copy-start | bytes 49156
  50.4 11.7 %copy-start = (f32[64,128]{1,0:T(8,128)S(1)}, f32[64,128]{1,0:T(8,128)}, u32[]{:S(2)}) copy-start(f32[64,128]{1,0:T(8,128)} %param.6) | copy-start | bytes 98308
  57.0 1.2 collective-permute-start.7
  58.2 3.9 %collective-permute-start.8 = (f32[64,128]{1,0:T(8,128)S(1)}, f32[64,128]{1,0:T(8,128)S(1)}, u32[]{:S(2)}, u32[]{:S(2)}) collective-permute-start(f32[64,128]{1,0:T(8,128)S(1)} %add.896), channel_id=1, source_target_pairs={{0,2},{1,3},{2,0},{3,1},{4,6},{5,7},{6,4},{7,5},{8,10},{9,11},{10,... | collective-permute-start | bytes 98312 | tf_op jit(solution)/shard_map/ppermute | solution.py:19
  78.1 1.6 %collective-permute-start.9 = (f32[2,256,128]{2,1,0:T(8,128)S(1)}, f32[2,256,128]{2,1,0:T(8,128)S(1)}, u32[]{:S(2)}, u32[]{:S(2)}) collective-permute-start(f32[2,256,128]{2,1,0:T(8,128)S(1)} %dynamic-slice_bitcast_fusion), channel_id=1, source_target_pairs={{0,1},{1,0},{2,3},{3,2},{4,5},{5,4},{6,7},{7,6},{8,9},{9,8},{10,11... | collective-permute-start | bytes 786440 | tf_op jit(solution)/shard_map/ppermute | solution.py:49
  79.8 5.6 %collective-permute-start.10 = (f32[256,128]{1,0:T(8,128)S(1)}, f32[256,128]{1,0:T(8,128)S(1)}, u32[]{:S(2)}, u32[]{:S(2)}) collective-permute-start(f32[256,128]{1,0:T(8,128)S(1)} %dynamic-slice_bitcast_fusion.2), channel_id=1, source_target_pairs={{0,2},{1,3},{2,0},{3,1},{4,6},{5,7},{6,4},{7,5},{8,10},{9,11},{10,... | collective-permute-start | bytes 393224 | tf_op jit(solution)/shard_map/ppermute | solution.py:49
  85.4 5.0 %collective-permute-start.11 = (f32[256,128]{1,0:T(8,128)S(1)}, f32[256,128]{1,0:T(8,128)S(1)}, u32[]{:S(2)}, u32[]{:S(2)}) collective-permute-start(f32[256,128]{1,0:T(8,128)S(1)} %bitcast_add_fusion.2), channel_id=1, source_target_pairs={{0,4},{4,0},{8,12},{12,8},{16,20},{20,16},{24,28},{28,24},{1,5},{5... | collective-permute-start | bytes 393224 | tf_op jit(solution)/shard_map/ppermute | solution.py:19
  90.4 5.0 %collective-permute-start.12 = (f32[256,128]{1,0:T(8,128)S(1)}, f32[256,128]{1,0:T(8,128)S(1)}, u32[]{:S(2)}, u32[]{:S(2)}) collective-permute-start(f32[256,128]{1,0:T(8,128)S(1)} %add.936), channel_id=1, source_target_pairs={{0,8},{4,12},{8,0},{12,4},{16,24},{20,28},{24,16},{28,20},{1,9},{5... | collective-permute-start | bytes 393224 | tf_op jit(solution)/shard_map/ppermute | solution.py:19
  95.5 7.3 %collective-permute-start.13 = (f32[256,128]{1,0:T(8,128)S(1)}, f32[256,128]{1,0:T(8,128)S(1)}, u32[]{:S(2)}, u32[]{:S(2)}) collective-permute-start(f32[256,128]{1,0:T(8,128)S(1)} %add.937), channel_id=1, source_target_pairs={{0,16},{4,20},{8,24},{12,28},{16,0},{20,4},{24,8},{28,12},{1,17},{... | collective-permute-start | bytes 393224 | tf_op jit(solution)/shard_map/ppermute | solution.py:19
  102.8 5.0 %collective-permute-start.14 = (f32[256,128]{1,0:T(8,128)S(1)}, f32[256,128]{1,0:T(8,128)S(1)}, u32[]{:S(2)}, u32[]{:S(2)}) collective-permute-start(f32[256,128]{1,0:T(8,128)S(1)} %multiply_subtract_fusion), channel_id=1, source_target_pairs={{0,2},{1,3},{2,0},{3,1},{4,6},{5,7},{6,4},{7,5},{8,10},{9,11},{10,... | collective-permute-start | bytes 393224 | tf_op jit(solution)/shard_map/ppermute | solution.py:62
  107.9 1.6 %collective-permute-start.15 = (f32[2,256,128]{2,1,0:T(8,128)S(1)}, f32[2,256,128]{2,1,0:T(8,128)S(1)}, u32[]{:S(2)}, u32[]{:S(2)}) collective-permute-start(f32[2,256,128]{2,1,0:T(8,128)S(1)} %maximum_select_fusion.4), channel_id=1, source_target_pairs={{0,1},{1,0},{2,3},{3,2},{4,5},{5,4},{6,7},{7,6},{8,9},{9,8},{10,11... | collective-permute-start | bytes 786440 | tf_op jit(solution)/shard_map/ppermute | solution.py:62
  114.6 1.2 collective-permute-start.16
  115.8 3.9 %collective-permute-start.17 = (f32[64,128]{1,0:T(8,128)S(1)}, f32[64,128]{1,0:T(8,128)S(1)}, u32[]{:S(2)}, u32[]{:S(2)}) collective-permute-start(f32[64,128]{1,0:T(8,128)S(1)} %add.939), channel_id=1, source_target_pairs={{0,2},{1,3},{2,0},{3,1},{4,6},{5,7},{6,4},{7,5},{8,10},{9,11},{10,... | collective-permute-start | bytes 98312 | tf_op jit(solution)/shard_map/ppermute | solution.py:19
  122.3 9.6 %all-to-all-start.2 = ((f32[32,1,128]{2,1,0:T(1,128)}), f32[32,1,128]{2,1,0:T(1,128)S(1)}, u32[]{:S(2)}, u32[]{:S(2)}) async-start(f32[32,1,128]{2,1,0:T(1,128)} %broadcast_in_dim.20), calls=%async_computation.2 | async-start | bytes 32768 | tf_op jit(solution)/shard_map/all_to_all | solution.py:27

commit v10 on v9

--- a/solution.py
+++ b/solution.py
@@ -98,10 +98,12 @@
         contrib_rows = contrib.reshape(-1, contrib.shape[-1])
         face_term = face_scale * left_faces
         terms = jnp.concatenate([contrib_rows, face_term], 0)
-        high = terms.astype(jnp.bfloat16)
-        rest = terms - high.astype(jnp.float32)
-        middle = rest.astype(jnp.bfloat16)
-        low = (rest - middle.astype(jnp.float32)).astype(jnp.bfloat16)
+        high_wide = lax.reduce_precision(terms, exponent_bits=8, mantissa_bits=7)
+        rest = terms - high_wide
+        middle_wide = lax.reduce_precision(rest, exponent_bits=8, mantissa_bits=7)
+        high = high_wide.astype(jnp.bfloat16)
+        middle = middle_wide.astype(jnp.bfloat16)
+        low = (rest - middle_wide).astype(jnp.bfloat16)
         partials = lax.dot_general(
             select_triple,
             jnp.concatenate([high, middle, low], 0),

time: 133 us -> 133 us (level)
  no operation moved by 1% of the time
where the time goes in v10:
time: 133 us
  waiting for transfers between devices  69.7 us (52%)
  starting transfers between devices  20.5 us (15%)
  matrix products  13.8 us (10%)
  blocking collectives  10.4 us (8%)
  other arithmetic  9.2 us (7%)
  between operations  5.63 us (4%)
  local copies, waits for them, and re-layouts  3.59 us (3%)
    ppermute x10, waiting for transfers between devices, butterfly_sum(): x = x + lax.ppermute(x, axis, [(i, i ^ k) for i in range(n)])  37.5 us
    ppermute x4, waiting for transfers between devices, halving_scatter(): x = keep + lax.ppermute(send, axis, [(i, i ^ k) for i in range(n)])  12 us
    ppermute x4, waiting for transfers between devices, doubling_gather(): other = lax.ppermute(x, axis, [(i, i ^ k) for i in range(n)])  10.7 us
    all_to_all x1, blocking collectives, scalar_sum(): got = lax.all_to_all(spread, axis, 0, 0, tiled=False)  10.4 us
    all_to_all x2, starting transfers between devices, scalar_sum(): got = lax.all_to_all(spread, axis, 0, 0, tiled=False)  9.82 us
    all_to_all x2, waiting for transfers between devices, scalar_sum(): got = lax.all_to_all(spread, axis, 0, 0, tiled=False)  9.46 us
    dot_general x2, matrix products, local(): jnp.einsum('tsrb,tsb->tr', sensitivity, picked, preferred_element_type=jn...  6.74 us
    ppermute x10, starting transfers between devices, butterfly_sum(): x = x + lax.ppermute(x, axis, [(i, i ^ k) for i in range(n)])  6.09 us
  transfers between devices with their start and end apart: 20, of which 20 were waited for; matrix products, arithmetic and copies ran while one was open for 4% of the time, Pallas kernels for 0%

profile of v10, /device:TPU:0, one launch (start us, length us, event | category | flops | bytes accessed | tf_op | source)
XLA Modules:
  0.0 132.8 jit_solution(12528024267863035946)
XLA Ops:
  0.0 1.4 %multiply_reduce_fusion.2 = f32[]{:T(128)} fusion(f32[64,128]{1,0:T(8,128)} %param.6), kind=kLoop, calls=%fused_computation.68 | loop fusion | flops 16383 | bytes 32772 | tf_op jit(solution)/shard_map/reduce_sum | solution.py:122
  1.4 1.2 broadcast_in_dim.16
  2.5 7.3 %all-to-all-start = ((f32[8,1,128]{2,1,0:T(1,128)}), f32[8,1,128]{2,1,0:T(1,128)S(1)}, u32[]{:S(2)}, u32[]{:S(2)}) async-start(f32[8,1,128]{2,1,0:T(1,128)} %broadcast_in_dim.16), calls=%async_computation | async-start | bytes 8192 | tf_op jit(solution)/shard_map/all_to_all | solution.py:27
  9.8 0.8 copy.10
  10.8 0.8 slice_bitcast_fusion.31
  12.8 0.8 multiply_multiply_fusion.1
  13.6 2.6 %all-to-all-done = f32[8,1,128]{2,1,0:T(1,128)S(1)} async-done(((f32[8,1,128]{2,1,0:T(1,128)}), f32[8,1,128]{2,1,0:T(1,128)S(1)}, u32[]{:S(2)}, u32[]{:S(2)}) %all-to-all-start) | async-done | bytes 4128 | tf_op jit(solution)/shard_map/all_to_all | solution.py:27
  16.3 0.8 convert_bitcast_fusion.1
  17.1 2.8 %fusion.29 = f32[64,1,2,128]{3,1,2,0:T(1,128)S(1)} fusion(bf16[64,2,128,128]{3,2,1,0:T(8,128)(2,1)} %param.7, bf16[64,128,1,1]{1,0,2,3:T(8,128)(2,1)S(1)} %convert_bitcast_fusion.1), kind=kOutput, calls=%fused_computation.65 | convolution fusion | flops 4194304 | bytes 4276224 | tf_op jit(solution)/shard_map/tsrb,tr->tsb/dot_general | solution.py:95
  20.6 1.5 %collective-permute-done = f32[2,256,128]{2,1,0:T(8,128)S(1)} collective-permute-done((f32[2,256,128]{2,1,0:T(8,128)S(1)}, f32[2,256,128]{2,1,0:T(8,128)S(1)}, u32[]{:S(2)}, u32[]{:S(2)}) %collective-permute-start) | collective-permute-done | bytes 262176 | tf_op jit(solution)/shard_map/ppermute | solution.py:49
  22.1 1.6 %collective-permute-start.1 = (f32[256,128]{1,0:T(8,128)S(1)}, f32[256,128]{1,0:T(8,128)S(1)}, u32[]{:S(2)}, u32[]{:S(2)}) collective-permute-start(f32[256,128]{1,0:T(8,128)S(1)} %dynamic-slice_bitcast_fusion.3), channel_id=1, source_target_pairs={{0,2},{1,3},{2,0},{3,1},{4,6},{5,7},{6,4},{7,5},{8,10},{9,11},{10,... | collective-permute-start | bytes 393224 | tf_op jit(solution)/shard_map/ppermute | solution.py:49
  23.7 4.0 %collective-permute-done.1 = f32[256,128]{1,0:T(8,128)S(1)} collective-permute-done((f32[256,128]{1,0:T(8,128)S(1)}, f32[256,128]{1,0:T(8,128)S(1)}, u32[]{:S(2)}, u32[]{:S(2)}) %collective-permute-start.1) | collective-permute-done | bytes 131104 | tf_op jit(solution)/shard_map/ppermute | solution.py:49
  27.7 0.6 collective-permute-start.2
  28.3 4.4 %collective-permute-done.2 = f32[256,128]{1,0:T(8,128)S(1)} collective-permute-done((f32[256,128]{1,0:T(8,128)S(1)}, f32[256,128]{1,0:T(8,128)S(1)}, u32[]{:S(2)}, u32[]{:S(2)}) %collective-permute-start.2) | collective-permute-done | bytes 131104 | tf_op jit(solution)/shard_map/ppermute | solution.py:19
  33.4 4.4 %collective-permute-done.3 = f32[256,128]{1,0:T(8,128)S(1)} collective-permute-done((f32[256,128]{1,0:T(8,128)S(1)}, f32[256,128]{1,0:T(8,128)S(1)}, u32[]{:S(2)}, u32[]{:S(2)}) %collective-permute-start.3) | collective-permute-done | bytes 131104 | tf_op jit(solution)/shard_map/ppermute | solution.py:19
  37.8 0.6 collective-permute-start.4
  38.5 6.7 %collective-permute-done.4 = f32[256,128]{1,0:T(8,128)S(1)} collective-permute-done((f32[256,128]{1,0:T(8,128)S(1)}, f32[256,128]{1,0:T(8,128)S(1)}, u32[]{:S(2)}, u32[]{:S(2)}) %collective-permute-start.4) | collective-permute-done | bytes 131104 | tf_op jit(solution)/shard_map/ppermute | solution.py:19
  45.2 1.6 %collective-permute-start.5 = (f32[256,128]{1,0:T(8,128)S(1)}, f32[256,128]{1,0:T(8,128)S(1)}, u32[]{:S(2)}, u32[]{:S(2)}) collective-permute-start(f32[256,128]{1,0:T(8,128)S(1)} %add.895), channel_id=1, source_target_pairs={{0,2},{1,3},{2,0},{3,1},{4,6},{5,7},{6,4},{7,5},{8,10},{9,11},{10,... | collective-permute-start | bytes 393224 | tf_op jit(solution)/shard_map/ppermute | solution.py:62
  46.9 3.4 %collective-permute-done.5 = f32[256,128]{1,0:T(8,128)S(1)} collective-permute-done((f32[256,128]{1,0:T(8,128)S(1)}, f32[256,128]{1,0:T(8,128)S(1)}, u32[]{:S(2)}, u32[]{:S(2)}) %collective-permute-start.5) | collective-permute-done | bytes 131104 | tf_op jit(solution)/shard_map/ppermute | solution.py:62
  50.5 1.4 %collective-permute-done.6 = f32[2,256,128]{2,1,0:T(8,128)S(1)} collective-permute-done((f32[2,256,128]{2,1,0:T(8,128)S(1)}, f32[2,256,128]{2,1,0:T(8,128)S(1)}, u32[]{:S(2)}, u32[]{:S(2)}) %collective-permute-start.6) | collective-permute-done | bytes 262176 | tf_op jit(solution)/shard_map/ppermute | solution.py:62
  51.8 0.7 multiply_reduce_fusion.1
  53.6 3.4 %fusion.25 = f32[64,1,128,1]{2,1,3,0:T(1,128)S(1)} fusion(bf16[64,2,128,128]{3,2,1,0:T(8,128)(2,1)} %param.7, bf16[64,2,128,1]{2,1,0,3:T(2,128)(2,1)S(1)} %bitcast.281), kind=kOutput, calls=%fused_computation.61 | convolution fusion | flops 4194304 | bytes 4259840 | tf_op jit(solution)/shard_map/tsrb,tsb->tr/dot_general | solution.py:135
  57.1 1.1 collective-permute-done.7
  58.2 1.5 %collective-permute-start.8 = (f32[64,128]{1,0:T(8,128)S(1)}, f32[64,128]{1,0:T(8,128)S(1)}, u32[]{:S(2)}, u32[]{:S(2)}) collective-permute-start(f32[64,128]{1,0:T(8,128)S(1)} %add.896), channel_id=1, source_target_pairs={{0,2},{1,3},{2,0},{3,1},{4,6},{5,7},{6,4},{7,5},{8,10},{9,11},{10,... | collective-permute-start | bytes 98312 | tf_op jit(solution)/shard_map/ppermute | solution.py:19
  59.7 0.7 multiply_reduce_fusion.3
  60.5 1.7 %collective-permute-done.8 = f32[64,128]{1,0:T(8,128)S(1)} collective-permute-done((f32[64,128]{1,0:T(8,128)S(1)}, f32[64,128]{1,0:T(8,128)S(1)}, u32[]{:S(2)}, u32[]{:S(2)}) %collective-permute-start.8) | collective-permute-done | bytes 32800 | tf_op jit(solution)/shard_map/ppermute | solution.py:19
  62.2 0.6 multiply_reduce_fusion.4
  64.1 10.4 %all_to_all.15 = f32[32,1,128]{2,1,0:T(1,128)S(1)} all-to-all(f32[32,1,128]{2,1,0:T(1,128)S(1)} %broadcast_in_dim.19), channel_id=1, replica_groups=mesh['dp'=8,'region'=4] {'dp','region'}, dimensions={0} | all-to-all | bytes 32768 | tf_op jit(solution)/shard_map/all_to_all | solution.py:27
  74.7 2.8 %fusion.27 = f32[64,1,2,128]{3,1,2,0:T(1,128)S(1)} fusion(bf16[64,2,128,128]{3,2,1,0:T(8,128)(2,1)} %param.7, bf16[64,128,1,1]{1,0,2,3:T(8,128)(2,1)S(1)} %get-tuple-element.5), kind=kOutput, calls=%fused_computation.63 | convolution fusion | flops 4194304 | bytes 4276224 | tf_op jit(solution)/shard_map/tsrb,tr->tsb/dot_general | solution.py:95
  78.2 1.5 %collective-permute-done.9 = f32[2,256,128]{2,1,0:T(8,128)S(1)} collective-permute-done((f32[2,256,128]{2,1,0:T(8,128)S(1)}, f32[2,256,128]{2,1,0:T(8,128)S(1)}, u32[]{:S(2)}, u32[]{:S(2)}) %collective-permute-start.9) | collective-permute-done | bytes 262176 | tf_op jit(solution)/shard_map/ppermute | solution.py:49
  80.3 5.0 %collective-permute-done.10 = f32[256,128]{1,0:T(8,128)S(1)} collective-permute-done((f32[256,128]{1,0:T(8,128)S(1)}, f32[256,128]{1,0:T(8,128)S(1)}, u32[]{:S(2)}, u32[]{:S(2)}) %collective-permute-start.10) | collective-permute-done | bytes 131104 | tf_op jit(solution)/shard_map/ppermute | solution.py:49
  85.4 0.6 collective-permute-start.11
  86.0 4.4 %collective-permute-done.11 = f32[256,128]{1,0:T(8,128)S(1)} collective-permute-done((f32[256,128]{1,0:T(8,128)S(1)}, f32[256,128]{1,0:T(8,128)S(1)}, u32[]{:S(2)}, u32[]{:S(2)}) %collective-permute-start.11) | collective-permute-done | bytes 131104 | tf_op jit(solution)/shard_map/ppermute | solution.py:19
  90.4 0.6 collective-permute-start.12
  91.1 4.4 %collective-permute-done.12 = f32[256,128]{1,0:T(8,128)S(1)} collective-permute-done((f32[256,128]{1,0:T(8,128)S(1)}, f32[256,128]{1,0:T(8,128)S(1)}, u32[]{:S(2)}, u32[]{:S(2)}) %collective-permute-start.12) | collective-permute-done | bytes 131104 | tf_op jit(solution)/shard_map/ppermute | solution.py:19
  95.5 0.7 collective-permute-start.13
  96.1 6.7 %collective-permute-done.13 = f32[256,128]{1,0:T(8,128)S(1)} collective-permute-done((f32[256,128]{1,0:T(8,128)S(1)}, f32[256,128]{1,0:T(8,128)S(1)}, u32[]{:S(2)}, u32[]{:S(2)}) %collective-permute-start.13) | collective-permute-done | bytes 131104 | tf_op jit(solution)/shard_map/ppermute | solution.py:19
  103.4 4.4 %collective-permute-done.14 = f32[256,128]{1,0:T(8,128)S(1)} collective-permute-done((f32[256,128]{1,0:T(8,128)S(1)}, f32[256,128]{1,0:T(8,128)S(1)}, u32[]{:S(2)}, u32[]{:S(2)}) %collective-permute-start.14) | collective-permute-done | bytes 131104 | tf_op jit(solution)/shard_map/ppermute | solution.py:62
  108.0 1.5 %collective-permute-done.15 = f32[2,256,128]{2,1,0:T(8,128)S(1)} collective-permute-done((f32[2,256,128]{2,1,0:T(8,128)S(1)}, f32[2,256,128]{2,1,0:T(8,128)S(1)}, u32[]{:S(2)}, u32[]{:S(2)}) %collective-permute-start.15) | collective-permute-done | bytes 262176 | tf_op jit(solution)/shard_map/ppermute | solution.py:62
  109.5 0.7 multiply_reduce_fusion
  111.2 3.4 %fusion.23 = f32[64,1,128,1]{2,1,3,0:T(1,128)S(1)} fusion(bf16[64,2,128,128]{3,2,1,0:T(8,128)(2,1)} %param.7, bf16[64,2,128,1]{2,1,0,3:T(2,128)(2,1)S(1)} %bitcast.282), kind=kOutput, calls=%fused_computation.59 | convolution fusion | flops 4194304 | bytes 4259840 | tf_op jit(solution)/shard_map/tsrb,tsb->tr/dot_general | solution.py:135
  114.8 1.1 collective-permute-done.16
  116.4 0.7 fusion.36
  117.1 2.7 %collective-permute-done.17 = f32[64,128]{1,0:T(8,128)S(1)} collective-permute-done((f32[64,128]{1,0:T(8,128)S(1)}, f32[64,128]{1,0:T(8,128)S(1)}, u32[]{:S(2)}, u32[]{:S(2)}) %collective-permute-start.17) | collective-permute-done | bytes 32800 | tf_op jit(solution)/shard_map/ppermute | solution.py:19
  121.6 0.6 broadcast_in_dim.20
  122.2 2.5 %all-to-all-start.2 = ((f32[32,1,128]{2,1,0:T(1,128)}), f32[32,1,128]{2,1,0:T(1,128)S(1)}, u32[]{:S(2)}, u32[]{:S(2)}) async-start(f32[32,1,128]{2,1,0:T(1,128)} %broadcast_in_dim.20), calls=%async_computation.2 | async-start | bytes 32768 | tf_op jit(solution)/shard_map/all_to_all | solution.py:27
  125.0 6.9 %all-to-all-done.2 = f32[32,1,128]{2,1,0:T(1,128)S(1)} async-done(((f32[32,1,128]{2,1,0:T(1,128)}), f32[32,1,128]{2,1,0:T(1,128)S(1)}, u32[]{:S(2)}, u32[]{:S(2)}) %all-to-all-start.2) | async-done | bytes 16416 | tf_op jit(solution)/shard_map/all_to_all | solution.py:27
  132.1 0.7 multiply_add_fusion
  (63 shorter events, 6.7 us)
Async XLA Ops:
  2.5 13.7 %all-to-all-start = ((f32[8,1,128]{2,1,0:T(1,128)}), f32[8,1,128]{2,1,0:T(1,128)S(1)}, u32[]{:S(2)}, u32[]{:S(2)}) async-start(f32[8,1,128]{2,1,0:T(1,128)} %broadcast_in_dim.16), calls=%async_computation | async-start | bytes 8192 | tf_op jit(solution)/shard_map/all_to_all | solution.py:27
  20.4 1.6 %collective-permute-start = (f32[2,256,128]{2,1,0:T(8,128)S(1)}, f32[2,256,128]{2,1,0:T(8,128)S(1)}, u32[]{:S(2)}, u32[]{:S(2)}) collective-permute-start(f32[2,256,128]{2,1,0:T(8,128)S(1)} %dynamic-slice_bitcast_fusion.1), channel_id=1, source_target_pairs={{0,1},{1,0},{2,3},{3,2},{4,5},{5,4},{6,7},{7,6},{8,9},{9,8},{10,11... | collective-permute-start | bytes 786440 | tf_op jit(solution)/shard_map/ppermute | solution.py:49
  22.1 5.6 %collective-permute-start.1 = (f32[256,128]{1,0:T(8,128)S(1)}, f32[256,128]{1,0:T(8,128)S(1)}, u32[]{:S(2)}, u32[]{:S(2)}) collective-permute-start(f32[256,128]{1,0:T(8,128)S(1)} %dynamic-slice_bitcast_fusion.3), channel_id=1, source_target_pairs={{0,2},{1,3},{2,0},{3,1},{4,6},{5,7},{6,4},{7,5},{8,10},{9,11},{10,... | collective-permute-start | bytes 393224 | tf_op jit(solution)/shard_map/ppermute | solution.py:49
  27.7 5.0 %collective-permute-start.2 = (f32[256,128]{1,0:T(8,128)S(1)}, f32[256,128]{1,0:T(8,128)S(1)}, u32[]{:S(2)}, u32[]{:S(2)}) collective-permute-start(f32[256,128]{1,0:T(8,128)S(1)} %bitcast_add_fusion.3), channel_id=1, source_target_pairs={{0,4},{4,0},{8,12},{12,8},{16,20},{20,16},{24,28},{28,24},{1,5},{5... | collective-permute-start | bytes 393224 | tf_op jit(solution)/shard_map/ppermute | solution.py:19
  32.8 5.0 %collective-permute-start.3 = (f32[256,128]{1,0:T(8,128)S(1)}, f32[256,128]{1,0:T(8,128)S(1)}, u32[]{:S(2)}, u32[]{:S(2)}) collective-permute-start(f32[256,128]{1,0:T(8,128)S(1)} %add.893), channel_id=1, source_target_pairs={{0,8},{4,12},{8,0},{12,4},{16,24},{20,28},{24,16},{28,20},{1,9},{5... | collective-permute-start | bytes 393224 | tf_op jit(solution)/shard_map/ppermute | solution.py:19
  37.8 7.3 %collective-permute-start.4 = (f32[256,128]{1,0:T(8,128)S(1)}, f32[256,128]{1,0:T(8,128)S(1)}, u32[]{:S(2)}, u32[]{:S(2)}) collective-permute-start(f32[256,128]{1,0:T(8,128)S(1)} %add.894), channel_id=1, source_target_pairs={{0,16},{4,20},{8,24},{12,28},{16,0},{20,4},{24,8},{28,12},{1,17},{... | collective-permute-start | bytes 393224 | tf_op jit(solution)/shard_map/ppermute | solution.py:19
  45.2 5.0 %collective-permute-start.5 = (f32[256,128]{1,0:T(8,128)S(1)}, f32[256,128]{1,0:T(8,128)S(1)}, u32[]{:S(2)}, u32[]{:S(2)}) collective-permute-start(f32[256,128]{1,0:T(8,128)S(1)} %add.895), channel_id=1, source_target_pairs={{0,2},{1,3},{2,0},{3,1},{4,6},{5,7},{6,4},{7,5},{8,10},{9,11},{10,... | collective-permute-start | bytes 393224 | tf_op jit(solution)/shard_map/ppermute | solution.py:62
  50.2 1.6 %collective-permute-start.6 = (f32[2,256,128]{2,1,0:T(8,128)S(1)}, f32[2,256,128]{2,1,0:T(8,128)S(1)}, u32[]{:S(2)}, u32[]{:S(2)}) collective-permute-start(f32[2,256,128]{2,1,0:T(8,128)S(1)} %maximum_select_fusion.2), channel_id=1, source_target_pairs={{0,1},{1,0},{2,3},{3,2},{4,5},{5,4},{6,7},{7,6},{8,9},{9,8},{10,11... | collective-permute-start | bytes 786440 | tf_op jit(solution)/shard_map/ppermute | solution.py:62
  50.4 9.3 %copy-start.1 = (f32[32,128]{1,0:T(8,128)S(1)}, f32[32,128]{1,0:T(8,128)}, u32[]{:S(2)}) copy-start(f32[32,128]{1,0:T(8,128)} %param.10) | copy-start | bytes 49156
  50.4 11.7 %copy-start = (f32[64,128]{1,0:T(8,128)S(1)}, f32[64,128]{1,0:T(8,128)}, u32[]{:S(2)}) copy-start(f32[64,128]{1,0:T(8,128)} %param.6) | copy-start | bytes 98308
  57.0 1.2 collective-permute-start.7
  58.2 3.9 %collective-permute-start.8 = (f32[64,128]{1,0:T(8,128)S(1)}, f32[64,128]{1,0:T(8,128)S(1)}, u32[]{:S(2)}, u32[]{:S(2)}) collective-permute-start(f32[64,128]{1,0:T(8,128)S(1)} %add.896), channel_id=1, source_target_pairs={{0,2},{1,3},{2,0},{3,1},{4,6},{5,7},{6,4},{7,5},{8,10},{9,11},{10,... | collective-permute-start | bytes 98312 | tf_op jit(solution)/shard_map/ppermute | solution.py:19
  78.1 1.6 %collective-permute-start.9 = (f32[2,256,128]{2,1,0:T(8,128)S(1)}, f32[2,256,128]{2,1,0:T(8,128)S(1)}, u32[]{:S(2)}, u32[]{:S(2)}) collective-permute-start(f32[2,256,128]{2,1,0:T(8,128)S(1)} %dynamic-slice_bitcast_fusion), channel_id=1, source_target_pairs={{0,1},{1,0},{2,3},{3,2},{4,5},{5,4},{6,7},{7,6},{8,9},{9,8},{10,11... | collective-permute-start | bytes 786440 | tf_op jit(solution)/shard_map/ppermute | solution.py:49
  79.7 5.6 %collective-permute-start.10 = (f32[256,128]{1,0:T(8,128)S(1)}, f32[256,128]{1,0:T(8,128)S(1)}, u32[]{:S(2)}, u32[]{:S(2)}) collective-permute-start(f32[256,128]{1,0:T(8,128)S(1)} %dynamic-slice_bitcast_fusion.2), channel_id=1, source_target_pairs={{0,2},{1,3},{2,0},{3,1},{4,6},{5,7},{6,4},{7,5},{8,10},{9,11},{10,... | collective-permute-start | bytes 393224 | tf_op jit(solution)/shard_map/ppermute | solution.py:49
  85.4 5.0 %collective-permute-start.11 = (f32[256,128]{1,0:T(8,128)S(1)}, f32[256,128]{1,0:T(8,128)S(1)}, u32[]{:S(2)}, u32[]{:S(2)}) collective-permute-start(f32[256,128]{1,0:T(8,128)S(1)} %bitcast_add_fusion.2), channel_id=1, source_target_pairs={{0,4},{4,0},{8,12},{12,8},{16,20},{20,16},{24,28},{28,24},{1,5},{5... | collective-permute-start | bytes 393224 | tf_op jit(solution)/shard_map/ppermute | solution.py:19
  90.4 5.0 %collective-permute-start.12 = (f32[256,128]{1,0:T(8,128)S(1)}, f32[256,128]{1,0:T(8,128)S(1)}, u32[]{:S(2)}, u32[]{:S(2)}) collective-permute-start(f32[256,128]{1,0:T(8,128)S(1)} %add.936), channel_id=1, source_target_pairs={{0,8},{4,12},{8,0},{12,4},{16,24},{20,28},{24,16},{28,20},{1,9},{5... | collective-permute-start | bytes 393224 | tf_op jit(solution)/shard_map/ppermute | solution.py:19
  95.5 7.3 %collective-permute-start.13 = (f32[256,128]{1,0:T(8,128)S(1)}, f32[256,128]{1,0:T(8,128)S(1)}, u32[]{:S(2)}, u32[]{:S(2)}) collective-permute-start(f32[256,128]{1,0:T(8,128)S(1)} %add.937), channel_id=1, source_target_pairs={{0,16},{4,20},{8,24},{12,28},{16,0},{20,4},{24,8},{28,12},{1,17},{... | collective-permute-start | bytes 393224 | tf_op jit(solution)/shard_map/ppermute | solution.py:19
  102.8 5.0 %collective-permute-start.14 = (f32[256,128]{1,0:T(8,128)S(1)}, f32[256,128]{1,0:T(8,128)S(1)}, u32[]{:S(2)}, u32[]{:S(2)}) collective-permute-start(f32[256,128]{1,0:T(8,128)S(1)} %multiply_subtract_fusion), channel_id=1, source_target_pairs={{0,2},{1,3},{2,0},{3,1},{4,6},{5,7},{6,4},{7,5},{8,10},{9,11},{10,... | collective-permute-start | bytes 393224 | tf_op jit(solution)/shard_map/ppermute | solution.py:62
  107.9 1.6 %collective-permute-start.15 = (f32[2,256,128]{2,1,0:T(8,128)S(1)}, f32[2,256,128]{2,1,0:T(8,128)S(1)}, u32[]{:S(2)}, u32[]{:S(2)}) collective-permute-start(f32[2,256,128]{2,1,0:T(8,128)S(1)} %maximum_select_fusion.4), channel_id=1, source_target_pairs={{0,1},{1,0},{2,3},{3,2},{4,5},{5,4},{6,7},{7,6},{8,9},{9,8},{10,11... | collective-permute-start | bytes 786440 | tf_op jit(solution)/shard_map/ppermute | solution.py:62
  114.6 1.2 collective-permute-start.16
  115.8 3.9 %collective-permute-start.17 = (f32[64,128]{1,0:T(8,128)S(1)}, f32[64,128]{1,0:T(8,128)S(1)}, u32[]{:S(2)}, u32[]{:S(2)}) collective-permute-start(f32[64,128]{1,0:T(8,128)S(1)} %add.939), channel_id=1, source_target_pairs={{0,2},{1,3},{2,0},{3,1},{4,6},{5,7},{6,4},{7,5},{8,10},{9,11},{10,... | collective-permute-start | bytes 98312 | tf_op jit(solution)/shard_map/ppermute | solution.py:19
  122.2 9.6 %all-to-all-start.2 = ((f32[32,1,128]{2,1,0:T(1,128)}), f32[32,1,128]{2,1,0:T(1,128)S(1)}, u32[]{:S(2)}, u32[]{:S(2)}) async-start(f32[32,1,128]{2,1,0:T(1,128)} %broadcast_in_dim.20), calls=%async_computation.2 | async-start | bytes 32768 | tf_op jit(solution)/shard_map/all_to_all | solution.py:27

commit v11 on v10

--- a/solution.py
+++ b/solution.py
@@ -21,14 +21,17 @@
     return x
 
 
-def scalar_sum(value, axis):
+def square_sum(rows, axis):
     n = lax.psum(1, axis)
-    spread = jnp.broadcast_to(value.astype(jnp.float32), (n, 1, 128))
-    got = lax.all_to_all(spread, axis, 0, 0, tiled=False)
+    squares = rows * rows
+    spread = jnp.dot(
+        jnp.ones((n, squares.shape[0]), jnp.float32), squares, precision=lax.Precision.HIGHEST
+    )
+    got = lax.all_to_all(spread[:, None, :], axis, 0, 0, tiled=False)
     total = got[0]
     for j in range(1, n):
         total = total + got[j]
-    return total[0, 0]
+    return jnp.sum(total)
 
 
 def halving_scatter(x, axis):
@@ -119,7 +122,7 @@
         field = field / alpha
         return field, lax.dynamic_slice_in_dim(field, region * NB_DEV, NB_DEV, 0), alpha
 
-    beta_value = jnp.sqrt(scalar_sum(jnp.sum(travel_times * travel_times), "dp"))
+    beta_value = jnp.sqrt(square_sum(travel_times, "dp"))
     left_rays = travel_times / beta_value
     left_faces = jnp.zeros(face_weights.shape, jnp.float32)
     raw = transposed_part(left_rays, left_faces)
@@ -138,15 +141,13 @@
         ray_pred = butterfly_sum(partial_value, "region")
         face_pred = face_scale * rows[n_slots:]
         left_faces = face_pred - alpha_value * left_faces
-        face_sq = jnp.sum(left_faces * left_faces)
         left_rays = ray_pred - alpha_value * left_rays
         if n_tiles % n_region == 0:
             share = n_tiles // n_region
             own_rays = lax.dynamic_slice_in_dim(left_rays, region * share, share, 0)
-            ray_sq = jnp.sum(own_rays * own_rays)
         else:
-            ray_sq = jnp.where(region == 0, jnp.sum(left_rays * left_rays), 0.0)
-        beta_sq = scalar_sum(ray_sq + face_sq, ("dp", "region"))
+            own_rays = jnp.where(region == 0, left_rays, 0.0)
+        beta_sq = square_sum(jnp.concatenate([own_rays, left_faces], 0), ("dp", "region"))
         beta_value = jnp.sqrt(beta_sq)
         left_rays = left_rays / beta_value
         left_faces = left_faces / beta_value

time: 133 us -> 132 us (level)
  matrix products: 13.8 us -> 16.2 us
  other arithmetic: 9.2 us -> 7.09 us
  local copies, waits for them, and re-layouts: 3.59 us -> 1.82 us
    dot_general x0 -> x3, matrix products: none -> 2.39 us  [square_sum(): jnp.dot(jnp.ones((n, squares.shape[0]), jnp.float32), squares, precision=...]
    reduce_sum x5 -> x3, other arithmetic: 4.05 us -> 1.87 us  [square_sum(): return jnp.sum(total)]
    broadcast_in_dim x3 -> x0, local copies, waits for them, and re-layouts: 1.78 us -> none  [scalar_sum(): spread = jnp.broadcast_to(value.astype(jnp.float32), (n, 1, 128))]
  transfers between devices with their start and end apart: 20 -> 20, of which waited for: 20 -> 20; matrix products, arithmetic and copies ran while one was open for 4% -> 3% of each run, Pallas kernels for 0% -> 0%
where the time goes in v11:
time: 132 us
  waiting for transfers between devices  71 us (54%)
  starting transfers between devices  20.5 us (16%)
  matrix products  16.2 us (12%)
  blocking collectives  10.4 us (8%)
  other arithmetic  7.09 us (5%)
  between operations  4.85 us (4%)
  local copies, waits for them, and re-layouts  1.82 us (1%)
    ppermute x10, waiting for transfers between devices, butterfly_sum(): x = x + lax.ppermute(x, axis, [(i, i ^ k) for i in range(n)])  38.8 us
    ppermute x4, waiting for transfers between devices, halving_scatter(): x = keep + lax.ppermute(send, axis, [(i, i ^ k) for i in range(n)])  12.1 us
    ppermute x4, waiting for transfers between devices, doubling_gather(): other = lax.ppermute(x, axis, [(i, i ^ k) for i in range(n)])  10.7 us
    all_to_all x1, blocking collectives, square_sum(): got = lax.all_to_all(spread[:, None, :], axis, 0, 0, tiled=False)  10.4 us
    all_to_all x2, starting transfers between devices, square_sum(): got = lax.all_to_all(spread[:, None, :], axis, 0, 0, tiled=False)  9.82 us
    all_to_all x2, waiting for transfers between devices, square_sum(): got = lax.all_to_all(spread[:, None, :], axis, 0, 0, tiled=False)  9.46 us
    dot_general x2, matrix products, local(): jnp.einsum('tsrb,tsb->tr', sensitivity, picked, preferred_element_type=jn...  6.74 us
    ppermute x10, starting transfers between devices, butterfly_sum(): x = x + lax.ppermute(x, axis, [(i, i ^ k) for i in range(n)])  6.09 us
  transfers between devices with their start and end apart: 20, of which 20 were waited for; matrix products, arithmetic and copies ran while one was open for 3% of the time, Pallas kernels for 0%

profile of v11, /device:TPU:0, one launch (start us, length us, event | category | flops | bytes accessed | tf_op | source)
XLA Modules:
  0.0 131.9 jit_solution(11717498167353531293)
XLA Ops:
  0.0 1.5 %fusion.31 = f32[8,128]{1,0:T(8,128)} fusion(f32[64,128]{1,0:T(8,128)} %param.6), kind=kOutput, calls=%fused_computation.68 | convolution fusion | flops 794624 | bytes 36864 | tf_op jit(solution)/shard_map/dot_general | solution.py:27
  1.5 7.3 %all-to-all-start = ((f32[8,1,128]{2,1,0:T(1,128)}), f32[8,1,128]{2,1,0:T(1,128)S(1)}, u32[]{:S(2)}, u32[]{:S(2)}) async-start(f32[8,1,128]{2,1,0:T(1,128)} %bitcast.3), calls=%async_computation | async-start | bytes 8192 | tf_op jit(solution)/shard_map/all_to_all | solution.py:30
  8.8 0.8 copy.14
  9.8 0.8 slice_bitcast_fusion.31
  11.8 0.8 multiply_multiply_fusion.1
  12.6 2.6 %all-to-all-done = f32[8,1,128]{2,1,0:T(1,128)S(1)} async-done(((f32[8,1,128]{2,1,0:T(1,128)}), f32[8,1,128]{2,1,0:T(1,128)S(1)}, u32[]{:S(2)}, u32[]{:S(2)}) %all-to-all-start) | async-done | bytes 4128 | tf_op jit(solution)/shard_map/all_to_all | solution.py:30
  15.2 0.6 fusion.82
  16.5 0.8 convert_bitcast_fusion.1
  17.2 2.8 %fusion.29 = f32[64,1,2,128]{3,1,2,0:T(1,128)S(1)} fusion(bf16[64,2,128,128]{3,2,1,0:T(8,128)(2,1)} %param.7, bf16[64,128,1,1]{1,0,2,3:T(8,128)(2,1)S(1)} %convert_bitcast_fusion.1), kind=kOutput, calls=%fused_computation.65 | convolution fusion | flops 4194304 | bytes 4276224 | tf_op jit(solution)/shard_map/tsrb,tr->tsb/dot_general | solution.py:98
  20.7 1.5 %collective-permute-done = f32[2,256,128]{2,1,0:T(8,128)S(1)} collective-permute-done((f32[2,256,128]{2,1,0:T(8,128)S(1)}, f32[2,256,128]{2,1,0:T(8,128)S(1)}, u32[]{:S(2)}, u32[]{:S(2)}) %collective-permute-start) | collective-permute-done | bytes 262176 | tf_op jit(solution)/shard_map/ppermute | solution.py:52
  22.3 1.6 %collective-permute-start.1 = (f32[256,128]{1,0:T(8,128)S(1)}, f32[256,128]{1,0:T(8,128)S(1)}, u32[]{:S(2)}, u32[]{:S(2)}) collective-permute-start(f32[256,128]{1,0:T(8,128)S(1)} %dynamic-slice_bitcast_fusion.3), channel_id=1, source_target_pairs={{0,2},{1,3},{2,0},{3,1},{4,6},{5,7},{6,4},{7,5},{8,10},{9,11},{10,... | collective-permute-start | bytes 393224 | tf_op jit(solution)/shard_map/ppermute | solution.py:52
  23.8 4.0 %collective-permute-done.1 = f32[256,128]{1,0:T(8,128)S(1)} collective-permute-done((f32[256,128]{1,0:T(8,128)S(1)}, f32[256,128]{1,0:T(8,128)S(1)}, u32[]{:S(2)}, u32[]{:S(2)}) %collective-permute-start.1) | collective-permute-done | bytes 131104 | tf_op jit(solution)/shard_map/ppermute | solution.py:52
  27.9 0.6 collective-permute-start.2
  28.5 4.4 %collective-permute-done.2 = f32[256,128]{1,0:T(8,128)S(1)} collective-permute-done((f32[256,128]{1,0:T(8,128)S(1)}, f32[256,128]{1,0:T(8,128)S(1)}, u32[]{:S(2)}, u32[]{:S(2)}) %collective-permute-start.2) | collective-permute-done | bytes 131104 | tf_op jit(solution)/shard_map/ppermute | solution.py:19
  33.0 0.6 collective-permute-start.3
  33.6 4.4 %collective-permute-done.3 = f32[256,128]{1,0:T(8,128)S(1)} collective-permute-done((f32[256,128]{1,0:T(8,128)S(1)}, f32[256,128]{1,0:T(8,128)S(1)}, u32[]{:S(2)}, u32[]{:S(2)}) %collective-permute-start.3) | collective-permute-done | bytes 131104 | tf_op jit(solution)/shard_map/ppermute | solution.py:19
  38.0 0.6 collective-permute-start.4
  38.6 6.7 %collective-permute-done.4 = f32[256,128]{1,0:T(8,128)S(1)} collective-permute-done((f32[256,128]{1,0:T(8,128)S(1)}, f32[256,128]{1,0:T(8,128)S(1)}, u32[]{:S(2)}, u32[]{:S(2)}) %collective-permute-start.4) | collective-permute-done | bytes 131104 | tf_op jit(solution)/shard_map/ppermute | solution.py:19
  45.4 1.6 %collective-permute-start.5 = (f32[256,128]{1,0:T(8,128)S(1)}, f32[256,128]{1,0:T(8,128)S(1)}, u32[]{:S(2)}, u32[]{:S(2)}) collective-permute-start(f32[256,128]{1,0:T(8,128)S(1)} %add.889), channel_id=1, source_target_pairs={{0,2},{1,3},{2,0},{3,1},{4,6},{5,7},{6,4},{7,5},{8,10},{9,11},{10,... | collective-permute-start | bytes 393224 | tf_op jit(solution)/shard_map/ppermute | solution.py:65
  47.0 3.4 %collective-permute-done.5 = f32[256,128]{1,0:T(8,128)S(1)} collective-permute-done((f32[256,128]{1,0:T(8,128)S(1)}, f32[256,128]{1,0:T(8,128)S(1)}, u32[]{:S(2)}, u32[]{:S(2)}) %collective-permute-start.5) | collective-permute-done | bytes 131104 | tf_op jit(solution)/shard_map/ppermute | solution.py:65
  50.7 1.4 %collective-permute-done.6 = f32[2,256,128]{2,1,0:T(8,128)S(1)} collective-permute-done((f32[2,256,128]{2,1,0:T(8,128)S(1)}, f32[2,256,128]{2,1,0:T(8,128)S(1)}, u32[]{:S(2)}, u32[]{:S(2)}) %collective-permute-start.6) | collective-permute-done | bytes 262176 | tf_op jit(solution)/shard_map/ppermute | solution.py:65
  52.0 0.7 multiply_reduce_fusion.1
  53.8 3.4 %fusion.25 = f32[64,1,128,1]{2,1,3,0:T(1,128)S(1)} fusion(bf16[64,2,128,128]{3,2,1,0:T(8,128)(2,1)} %param.7, bf16[64,2,128,1]{2,1,0,3:T(2,128)(2,1)S(1)} %bitcast.286), kind=kOutput, calls=%fused_computation.61 | convolution fusion | flops 4194304 | bytes 4259840 | tf_op jit(solution)/shard_map/tsrb,tsb->tr/dot_general | solution.py:138
  57.3 1.1 collective-permute-done.7
  58.4 1.5 %collective-permute-start.8 = (f32[64,128]{1,0:T(8,128)S(1)}, f32[64,128]{1,0:T(8,128)S(1)}, u32[]{:S(2)}, u32[]{:S(2)}) collective-permute-start(f32[64,128]{1,0:T(8,128)S(1)} %add.890), channel_id=1, source_target_pairs={{0,2},{1,3},{2,0},{3,1},{4,6},{5,7},{6,4},{7,5},{8,10},{9,11},{10,... | collective-permute-start | bytes 98312 | tf_op jit(solution)/shard_map/ppermute | solution.py:19
  60.0 2.3 %collective-permute-done.8 = f32[64,128]{1,0:T(8,128)S(1)} collective-permute-done((f32[64,128]{1,0:T(8,128)S(1)}, f32[64,128]{1,0:T(8,128)S(1)}, u32[]{:S(2)}, u32[]{:S(2)}) %collective-permute-start.8) | collective-permute-done | bytes 32800 | tf_op jit(solution)/shard_map/ppermute | solution.py:19
  62.5 10.4 %all_to_all.15 = f32[32,1,128]{2,1,0:T(1,128)S(1)} all-to-all(f32[32,1,128]{2,1,0:T(1,128)S(1)} %bitcast.294), channel_id=1, replica_groups=mesh['dp'=8,'region'=4] {'dp','region'}, dimensions={0} | all-to-all | bytes 32768 | tf_op jit(solution)/shard_map/all_to_all | solution.py:30
  72.9 0.6 fusion.66
  74.3 2.8 %fusion.27 = f32[64,1,2,128]{3,1,2,0:T(1,128)S(1)} fusion(bf16[64,2,128,128]{3,2,1,0:T(8,128)(2,1)} %param.7, bf16[64,128,1,1]{1,0,2,3:T(8,128)(2,1)S(1)} %get-tuple-element.5), kind=kOutput, calls=%fused_computation.63 | convolution fusion | flops 4194304 | bytes 4276224 | tf_op jit(solution)/shard_map/tsrb,tr->tsb/dot_general | solution.py:98
  77.7 1.5 %collective-permute-done.9 = f32[2,256,128]{2,1,0:T(8,128)S(1)} collective-permute-done((f32[2,256,128]{2,1,0:T(8,128)S(1)}, f32[2,256,128]{2,1,0:T(8,128)S(1)}, u32[]{:S(2)}, u32[]{:S(2)}) %collective-permute-start.9) | collective-permute-done | bytes 262176 | tf_op jit(solution)/shard_map/ppermute | solution.py:52
  79.9 5.0 %collective-permute-done.10 = f32[256,128]{1,0:T(8,128)S(1)} collective-permute-done((f32[256,128]{1,0:T(8,128)S(1)}, f32[256,128]{1,0:T(8,128)S(1)}, u32[]{:S(2)}, u32[]{:S(2)}) %collective-permute-start.10) | collective-permute-done | bytes 131104 | tf_op jit(solution)/shard_map/ppermute | solution.py:52
  84.9 0.6 collective-permute-start.11
  85.6 4.4 %collective-permute-done.11 = f32[256,128]{1,0:T(8,128)S(1)} collective-permute-done((f32[256,128]{1,0:T(8,128)S(1)}, f32[256,128]{1,0:T(8,128)S(1)}, u32[]{:S(2)}, u32[]{:S(2)}) %collective-permute-start.11) | collective-permute-done | bytes 131104 | tf_op jit(solution)/shard_map/ppermute | solution.py:19
  90.0 0.6 collective-permute-start.12
  90.6 4.4 %collective-permute-done.12 = f32[256,128]{1,0:T(8,128)S(1)} collective-permute-done((f32[256,128]{1,0:T(8,128)S(1)}, f32[256,128]{1,0:T(8,128)S(1)}, u32[]{:S(2)}, u32[]{:S(2)}) %collective-permute-start.12) | collective-permute-done | bytes 131104 | tf_op jit(solution)/shard_map/ppermute | solution.py:19
  95.1 0.7 collective-permute-start.13
  95.7 6.7 %collective-permute-done.13 = f32[256,128]{1,0:T(8,128)S(1)} collective-permute-done((f32[256,128]{1,0:T(8,128)S(1)}, f32[256,128]{1,0:T(8,128)S(1)}, u32[]{:S(2)}, u32[]{:S(2)}) %collective-permute-start.13) | collective-permute-done | bytes 131104 | tf_op jit(solution)/shard_map/ppermute | solution.py:19
  103.0 4.4 %collective-permute-done.14 = f32[256,128]{1,0:T(8,128)S(1)} collective-permute-done((f32[256,128]{1,0:T(8,128)S(1)}, f32[256,128]{1,0:T(8,128)S(1)}, u32[]{:S(2)}, u32[]{:S(2)}) %collective-permute-start.14) | collective-permute-done | bytes 131104 | tf_op jit(solution)/shard_map/ppermute | solution.py:65
  107.6 1.5 %collective-permute-done.15 = f32[2,256,128]{2,1,0:T(8,128)S(1)} collective-permute-done((f32[2,256,128]{2,1,0:T(8,128)S(1)}, f32[2,256,128]{2,1,0:T(8,128)S(1)}, u32[]{:S(2)}, u32[]{:S(2)}) %collective-permute-start.15) | collective-permute-done | bytes 262176 | tf_op jit(solution)/shard_map/ppermute | solution.py:65
  109.1 0.7 multiply_reduce_fusion
  110.8 3.4 %fusion.23 = f32[64,1,128,1]{2,1,3,0:T(1,128)S(1)} fusion(bf16[64,2,128,128]{3,2,1,0:T(8,128)(2,1)} %param.7, bf16[64,2,128,1]{2,1,0,3:T(2,128)(2,1)S(1)} %bitcast.287), kind=kOutput, calls=%fused_computation.59 | convolution fusion | flops 4194304 | bytes 4259840 | tf_op jit(solution)/shard_map/tsrb,tsb->tr/dot_general | solution.py:138
  114.3 1.1 collective-permute-done.16
  116.0 3.3 %collective-permute-done.17 = f32[64,128]{1,0:T(8,128)S(1)} collective-permute-done((f32[64,128]{1,0:T(8,128)S(1)}, f32[64,128]{1,0:T(8,128)S(1)}, u32[]{:S(2)}, u32[]{:S(2)}) %collective-permute-start.17) | collective-permute-done | bytes 32800 | tf_op jit(solution)/shard_map/ppermute | solution.py:19
  119.3 0.8 fusion.39
  120.1 2.5 %all-to-all-start.2 = ((f32[32,1,128]{2,1,0:T(1,128)}), f32[32,1,128]{2,1,0:T(1,128)S(1)}, u32[]{:S(2)}, u32[]{:S(2)}) async-start(f32[32,1,128]{2,1,0:T(1,128)} %bitcast.65), calls=%async_computation.2 | async-start | bytes 32768 | tf_op jit(solution)/shard_map/all_to_all | solution.py:30
  122.9 6.8 %all-to-all-done.2 = f32[32,1,128]{2,1,0:T(1,128)S(1)} async-done(((f32[32,1,128]{2,1,0:T(1,128)}), f32[32,1,128]{2,1,0:T(1,128)S(1)}, u32[]{:S(2)}, u32[]{:S(2)}) %all-to-all-start.2) | async-done | bytes 16416 | tf_op jit(solution)/shard_map/all_to_all | solution.py:30
  129.7 0.6 fusion.49
  131.2 0.7 multiply_add_fusion
  (62 shorter events, 5.7 us)
Async XLA Ops:
  1.5 13.7 %all-to-all-start = ((f32[8,1,128]{2,1,0:T(1,128)}), f32[8,1,128]{2,1,0:T(1,128)S(1)}, u32[]{:S(2)}, u32[]{:S(2)}) async-start(f32[8,1,128]{2,1,0:T(1,128)} %bitcast.3), calls=%async_computation | async-start | bytes 8192 | tf_op jit(solution)/shard_map/all_to_all | solution.py:30
  20.6 1.6 %collective-permute-start = (f32[2,256,128]{2,1,0:T(8,128)S(1)}, f32[2,256,128]{2,1,0:T(8,128)S(1)}, u32[]{:S(2)}, u32[]{:S(2)}) collective-permute-start(f32[2,256,128]{2,1,0:T(8,128)S(1)} %dynamic-slice_bitcast_fusion.1), channel_id=1, source_target_pairs={{0,1},{1,0},{2,3},{3,2},{4,5},{5,4},{6,7},{7,6},{8,9},{9,8},{10,11... | collective-permute-start | bytes 786440 | tf_op jit(solution)/shard_map/ppermute | solution.py:52
  22.3 5.6 %collective-permute-start.1 = (f32[256,128]{1,0:T(8,128)S(1)}, f32[256,128]{1,0:T(8,128)S(1)}, u32[]{:S(2)}, u32[]{:S(2)}) collective-permute-start(f32[256,128]{1,0:T(8,128)S(1)} %dynamic-slice_bitcast_fusion.3), channel_id=1, source_target_pairs={{0,2},{1,3},{2,0},{3,1},{4,6},{5,7},{6,4},{7,5},{8,10},{9,11},{10,... | collective-permute-start | bytes 393224 | tf_op jit(solution)/shard_map/ppermute | solution.py:52
  27.9 5.0 %collective-permute-start.2 = (f32[256,128]{1,0:T(8,128)S(1)}, f32[256,128]{1,0:T(8,128)S(1)}, u32[]{:S(2)}, u32[]{:S(2)}) collective-permute-start(f32[256,128]{1,0:T(8,128)S(1)} %bitcast_add_fusion.3), channel_id=1, source_target_pairs={{0,4},{4,0},{8,12},{12,8},{16,20},{20,16},{24,28},{28,24},{1,5},{5... | collective-permute-start | bytes 393224 | tf_op jit(solution)/shard_map/ppermute | solution.py:19
  33.0 5.0 %collective-permute-start.3 = (f32[256,128]{1,0:T(8,128)S(1)}, f32[256,128]{1,0:T(8,128)S(1)}, u32[]{:S(2)}, u32[]{:S(2)}) collective-permute-start(f32[256,128]{1,0:T(8,128)S(1)} %add.887), channel_id=1, source_target_pairs={{0,8},{4,12},{8,0},{12,4},{16,24},{20,28},{24,16},{28,20},{1,9},{5... | collective-permute-start | bytes 393224 | tf_op jit(solution)/shard_map/ppermute | solution.py:19
  38.0 7.3 %collective-permute-start.4 = (f32[256,128]{1,0:T(8,128)S(1)}, f32[256,128]{1,0:T(8,128)S(1)}, u32[]{:S(2)}, u32[]{:S(2)}) collective-permute-start(f32[256,128]{1,0:T(8,128)S(1)} %add.888), channel_id=1, source_target_pairs={{0,16},{4,20},{8,24},{12,28},{16,0},{20,4},{24,8},{28,12},{1,17},{... | collective-permute-start | bytes 393224 | tf_op jit(solution)/shard_map/ppermute | solution.py:19
  45.4 5.0 %collective-permute-start.5 = (f32[256,128]{1,0:T(8,128)S(1)}, f32[256,128]{1,0:T(8,128)S(1)}, u32[]{:S(2)}, u32[]{:S(2)}) collective-permute-start(f32[256,128]{1,0:T(8,128)S(1)} %add.889), channel_id=1, source_target_pairs={{0,2},{1,3},{2,0},{3,1},{4,6},{5,7},{6,4},{7,5},{8,10},{9,11},{10,... | collective-permute-start | bytes 393224 | tf_op jit(solution)/shard_map/ppermute | solution.py:65
  50.4 1.6 %collective-permute-start.6 = (f32[2,256,128]{2,1,0:T(8,128)S(1)}, f32[2,256,128]{2,1,0:T(8,128)S(1)}, u32[]{:S(2)}, u32[]{:S(2)}) collective-permute-start(f32[2,256,128]{2,1,0:T(8,128)S(1)} %maximum_select_fusion.2), channel_id=1, source_target_pairs={{0,1},{1,0},{2,3},{3,2},{4,5},{5,4},{6,7},{7,6},{8,9},{9,8},{10,11... | collective-permute-start | bytes 786440 | tf_op jit(solution)/shard_map/ppermute | solution.py:65
  50.6 9.3 %copy-start.1 = (f32[32,128]{1,0:T(8,128)S(1)}, f32[32,128]{1,0:T(8,128)}, u32[]{:S(2)}) copy-start(f32[32,128]{1,0:T(8,128)} %param.10) | copy-start | bytes 49156
  50.6 11.7 %copy-start = (f32[64,128]{1,0:T(8,128)S(1)}, f32[64,128]{1,0:T(8,128)}, u32[]{:S(2)}) copy-start(f32[64,128]{1,0:T(8,128)} %param.6) | copy-start | bytes 98308
  57.2 1.2 collective-permute-start.7
  58.4 3.9 %collective-permute-start.8 = (f32[64,128]{1,0:T(8,128)S(1)}, f32[64,128]{1,0:T(8,128)S(1)}, u32[]{:S(2)}, u32[]{:S(2)}) collective-permute-start(f32[64,128]{1,0:T(8,128)S(1)} %add.890), channel_id=1, source_target_pairs={{0,2},{1,3},{2,0},{3,1},{4,6},{5,7},{6,4},{7,5},{8,10},{9,11},{10,... | collective-permute-start | bytes 98312 | tf_op jit(solution)/shard_map/ppermute | solution.py:19
  77.7 1.6 %collective-permute-start.9 = (f32[2,256,128]{2,1,0:T(8,128)S(1)}, f32[2,256,128]{2,1,0:T(8,128)S(1)}, u32[]{:S(2)}, u32[]{:S(2)}) collective-permute-start(f32[2,256,128]{2,1,0:T(8,128)S(1)} %dynamic-slice_bitcast_fusion), channel_id=1, source_target_pairs={{0,1},{1,0},{2,3},{3,2},{4,5},{5,4},{6,7},{7,6},{8,9},{9,8},{10,11... | collective-permute-start | bytes 786440 | tf_op jit(solution)/shard_map/ppermute | solution.py:52
  79.3 5.6 %collective-permute-start.10 = (f32[256,128]{1,0:T(8,128)S(1)}, f32[256,128]{1,0:T(8,128)S(1)}, u32[]{:S(2)}, u32[]{:S(2)}) collective-permute-start(f32[256,128]{1,0:T(8,128)S(1)} %dynamic-slice_bitcast_fusion.2), channel_id=1, source_target_pairs={{0,2},{1,3},{2,0},{3,1},{4,6},{5,7},{6,4},{7,5},{8,10},{9,11},{10,... | collective-permute-start | bytes 393224 | tf_op jit(solution)/shard_map/ppermute | solution.py:52
  84.9 5.0 %collective-permute-start.11 = (f32[256,128]{1,0:T(8,128)S(1)}, f32[256,128]{1,0:T(8,128)S(1)}, u32[]{:S(2)}, u32[]{:S(2)}) collective-permute-start(f32[256,128]{1,0:T(8,128)S(1)} %bitcast_add_fusion.2), channel_id=1, source_target_pairs={{0,4},{4,0},{8,12},{12,8},{16,20},{20,16},{24,28},{28,24},{1,5},{5... | collective-permute-start | bytes 393224 | tf_op jit(solution)/shard_map/ppermute | solution.py:19
  90.0 5.0 %collective-permute-start.12 = (f32[256,128]{1,0:T(8,128)S(1)}, f32[256,128]{1,0:T(8,128)S(1)}, u32[]{:S(2)}, u32[]{:S(2)}) collective-permute-start(f32[256,128]{1,0:T(8,128)S(1)} %add.929), channel_id=1, source_target_pairs={{0,8},{4,12},{8,0},{12,4},{16,24},{20,28},{24,16},{28,20},{1,9},{5... | collective-permute-start | bytes 393224 | tf_op jit(solution)/shard_map/ppermute | solution.py:19
  95.1 7.3 %collective-permute-start.13 = (f32[256,128]{1,0:T(8,128)S(1)}, f32[256,128]{1,0:T(8,128)S(1)}, u32[]{:S(2)}, u32[]{:S(2)}) collective-permute-start(f32[256,128]{1,0:T(8,128)S(1)} %add.930), channel_id=1, source_target_pairs={{0,16},{4,20},{8,24},{12,28},{16,0},{20,4},{24,8},{28,12},{1,17},{... | collective-permute-start | bytes 393224 | tf_op jit(solution)/shard_map/ppermute | solution.py:19
  102.4 5.0 %collective-permute-start.14 = (f32[256,128]{1,0:T(8,128)S(1)}, f32[256,128]{1,0:T(8,128)S(1)}, u32[]{:S(2)}, u32[]{:S(2)}) collective-permute-start(f32[256,128]{1,0:T(8,128)S(1)} %multiply_subtract_fusion), channel_id=1, source_target_pairs={{0,2},{1,3},{2,0},{3,1},{4,6},{5,7},{6,4},{7,5},{8,10},{9,11},{10,... | collective-permute-start | bytes 393224 | tf_op jit(solution)/shard_map/ppermute | solution.py:65
  107.5 1.6 %collective-permute-start.15 = (f32[2,256,128]{2,1,0:T(8,128)S(1)}, f32[2,256,128]{2,1,0:T(8,128)S(1)}, u32[]{:S(2)}, u32[]{:S(2)}) collective-permute-start(f32[2,256,128]{2,1,0:T(8,128)S(1)} %maximum_select_fusion.4), channel_id=1, source_target_pairs={{0,1},{1,0},{2,3},{3,2},{4,5},{5,4},{6,7},{7,6},{8,9},{9,8},{10,11... | collective-permute-start | bytes 786440 | tf_op jit(solution)/shard_map/ppermute | solution.py:65
  114.2 1.2 collective-permute-start.16
  115.4 3.9 %collective-permute-start.17 = (f32[64,128]{1,0:T(8,128)S(1)}, f32[64,128]{1,0:T(8,128)S(1)}, u32[]{:S(2)}, u32[]{:S(2)}) collective-permute-start(f32[64,128]{1,0:T(8,128)S(1)} %add.932), channel_id=1, source_target_pairs={{0,2},{1,3},{2,0},{3,1},{4,6},{5,7},{6,4},{7,5},{8,10},{9,11},{10,... | collective-permute-start | bytes 98312 | tf_op jit(solution)/shard_map/ppermute | solution.py:19
  120.1 9.6 %all-to-all-start.2 = ((f32[32,1,128]{2,1,0:T(1,128)}), f32[32,1,128]{2,1,0:T(1,128)S(1)}, u32[]{:S(2)}, u32[]{:S(2)}) async-start(f32[32,1,128]{2,1,0:T(1,128)} %bitcast.65), calls=%async_computation.2 | async-start | bytes 32768 | tf_op jit(solution)/shard_map/all_to_all | solution.py:30

commit v12 on v11

--- a/solution.py
+++ b/solution.py
@@ -135,10 +135,17 @@
         full_half = full_model.astype(jnp.bfloat16)
         rows = jnp.dot(select_half, full_half, preferred_element_type=jnp.float32)
         picked = rows[:n_slots].astype(jnp.bfloat16).reshape(tile_blocks.shape + rows.shape[-1:])
-        partial_value = jnp.einsum(
-            "tsrb,tsb->tr", sensitivity, picked, preferred_element_type=jnp.float32
-        )
-        ray_pred = butterfly_sum(partial_value, "region")
+        half_tiles = n_tiles // 2 if n_tiles % 16 == 0 else n_tiles
+        halves = []
+        for lo in range(0, n_tiles, half_tiles):
+            part = jnp.einsum(
+                "tsrb,tsb->tr",
+                sensitivity[lo:lo + half_tiles],
+                picked[lo:lo + half_tiles],
+                preferred_element_type=jnp.float32,
+            )
+            halves.append(butterfly_sum(part, "region"))
+        ray_pred = jnp.concatenate(halves, 0) if len(halves) > 1 else halves[0]
         face_pred = face_scale * rows[n_slots:]
         left_faces = face_pred - alpha_value * left_faces
         left_rays = ray_pred - alpha_value * left_rays

time: 132 us -> 132 us (level)
  starting transfers between devices: 20.5 us -> 23.5 us
  waiting for transfers between devices: 71 us -> 68.8 us
    ppermute x10 -> x14, starting transfers between devices: 6.09 us -> 9.07 us  [butterfly_sum(): x = x + lax.ppermute(x, axis, [(i, i ^ k) for i in range(n)])]
    ppermute x10 -> x14, waiting for transfers between devices: 38.8 us -> 36.6 us  [butterfly_sum(): x = x + lax.ppermute(x, axis, [(i, i ^ k) for i in range(n)])]
    dot_general x2 -> x4, matrix products: 6.74 us -> 6.09 us  [local(): jnp.einsum('tsrb,tsb->tr', sensitivity[lo:lo + half_tiles], picked[lo:lo...]
  transfers between devices with their start and end apart: 20 -> 24, of which waited for: 20 -> 21; matrix products, arithmetic and copies ran while one was open for 3% -> 4% of each run, Pallas kernels for 0% -> 0%
where the time goes in v12:
time: 132 us; the launch traced here: 131 us
  waiting for transfers between devices  68.8 us (52%)
  starting transfers between devices  23.5 us (18%)
  matrix products  15.6 us (12%)
  blocking collectives  9.58 us (7%)
  other arithmetic  7.12 us (5%)
  between operations  4.88 us (4%)
  local copies, waits for them, and re-layouts  1.83 us (1%)
    ppermute x14, waiting for transfers between devices, butterfly_sum(): x = x + lax.ppermute(x, axis, [(i, i ^ k) for i in range(n)])  36.6 us
    ppermute x4, waiting for transfers between devices, halving_scatter(): x = keep + lax.ppermute(send, axis, [(i, i ^ k) for i in range(n)])  12.1 us
    ppermute x4, waiting for transfers between devices, doubling_gather(): other = lax.ppermute(x, axis, [(i, i ^ k) for i in range(n)])  10.7 us
    all_to_all x2, starting transfers between devices, square_sum(): got = lax.all_to_all(spread[:, None, :], axis, 0, 0, tiled=False)  9.82 us
    all_to_all x1, blocking collectives, square_sum(): got = lax.all_to_all(spread[:, None, :], axis, 0, 0, tiled=False)  9.58 us
    all_to_all x2, waiting for transfers between devices, square_sum(): got = lax.all_to_all(spread[:, None, :], axis, 0, 0, tiled=False)  9.46 us
    ppermute x14, starting transfers between devices, butterfly_sum(): x = x + lax.ppermute(x, axis, [(i, i ^ k) for i in range(n)])  9.07 us
    dot_general x4, matrix products, local(): jnp.einsum('tsrb,tsb->tr', sensitivity[lo:lo + half_tiles], picked[lo:lo...  6.09 us
  transfers between devices with their start and end apart: 24, of which 21 were waited for; matrix products, arithmetic and copies ran while one was open for 4% of the time, Pallas kernels for 0%

profile of v12, /device:TPU:0, one launch (start us, length us, event | category | flops | bytes accessed | tf_op | source)
XLA Modules:
  0.0 131.2 jit_solution(12441534225626263081)
XLA Ops:
  0.0 1.5 %fusion.39 = f32[8,128]{1,0:T(8,128)} fusion(f32[64,128]{1,0:T(8,128)} %param.6), kind=kOutput, calls=%fused_computation.76 | convolution fusion | flops 794624 | bytes 36864 | tf_op jit(solution)/shard_map/dot_general | solution.py:27
  1.5 7.3 %all-to-all-start = ((f32[8,1,128]{2,1,0:T(1,128)}), f32[8,1,128]{2,1,0:T(1,128)S(1)}, u32[]{:S(2)}, u32[]{:S(2)}) async-start(f32[8,1,128]{2,1,0:T(1,128)} %bitcast.3), calls=%async_computation | async-start | bytes 8192 | tf_op jit(solution)/shard_map/all_to_all | solution.py:30
  8.8 0.8 copy.14
  9.8 0.8 slice_bitcast_fusion.31
  11.8 0.8 multiply_multiply_fusion.1
  12.6 2.6 %all-to-all-done = f32[8,1,128]{2,1,0:T(1,128)S(1)} async-done(((f32[8,1,128]{2,1,0:T(1,128)}), f32[8,1,128]{2,1,0:T(1,128)S(1)}, u32[]{:S(2)}, u32[]{:S(2)}) %all-to-all-start) | async-done | bytes 4128 | tf_op jit(solution)/shard_map/all_to_all | solution.py:30
  16.5 0.8 convert_bitcast_fusion.1
  17.2 2.8 %fusion.37 = f32[64,1,2,128]{3,1,2,0:T(1,128)S(1)} fusion(bf16[64,2,128,128]{3,2,1,0:T(8,128)(2,1)} %param.7, bf16[64,128,1,1]{1,0,2,3:T(8,128)(2,1)S(1)} %convert_bitcast_fusion.1), kind=kOutput, calls=%fused_computation.74 | convolution fusion | flops 4194304 | bytes 4276224 | tf_op jit(solution)/shard_map/tsrb,tr->tsb/dot_general | solution.py:98
  20.7 1.5 %collective-permute-done = f32[2,256,128]{2,1,0:T(8,128)S(1)} collective-permute-done((f32[2,256,128]{2,1,0:T(8,128)S(1)}, f32[2,256,128]{2,1,0:T(8,128)S(1)}, u32[]{:S(2)}, u32[]{:S(2)}) %collective-permute-start) | collective-permute-done | bytes 262176 | tf_op jit(solution)/shard_map/ppermute | solution.py:52
  22.3 1.6 %collective-permute-start.1 = (f32[256,128]{1,0:T(8,128)S(1)}, f32[256,128]{1,0:T(8,128)S(1)}, u32[]{:S(2)}, u32[]{:S(2)}) collective-permute-start(f32[256,128]{1,0:T(8,128)S(1)} %dynamic-slice_bitcast_fusion.3), channel_id=1, source_target_pairs={{0,2},{1,3},{2,0},{3,1},{4,6},{5,7},{6,4},{7,5},{8,10},{9,11},{10,... | collective-permute-start | bytes 393224 | tf_op jit(solution)/shard_map/ppermute | solution.py:52
  23.8 4.0 %collective-permute-done.1 = f32[256,128]{1,0:T(8,128)S(1)} collective-permute-done((f32[256,128]{1,0:T(8,128)S(1)}, f32[256,128]{1,0:T(8,128)S(1)}, u32[]{:S(2)}, u32[]{:S(2)}) %collective-permute-start.1) | collective-permute-done | bytes 131104 | tf_op jit(solution)/shard_map/ppermute | solution.py:52
  28.5 4.4 %collective-permute-done.2 = f32[256,128]{1,0:T(8,128)S(1)} collective-permute-done((f32[256,128]{1,0:T(8,128)S(1)}, f32[256,128]{1,0:T(8,128)S(1)}, u32[]{:S(2)}, u32[]{:S(2)}) %collective-permute-start.2) | collective-permute-done | bytes 131104 | tf_op jit(solution)/shard_map/ppermute | solution.py:19
  33.6 4.4 %collective-permute-done.3 = f32[256,128]{1,0:T(8,128)S(1)} collective-permute-done((f32[256,128]{1,0:T(8,128)S(1)}, f32[256,128]{1,0:T(8,128)S(1)}, u32[]{:S(2)}, u32[]{:S(2)}) %collective-permute-start.3) | collective-permute-done | bytes 131104 | tf_op jit(solution)/shard_map/ppermute | solution.py:19
  38.0 0.6 collective-permute-start.4
  38.6 6.7 %collective-permute-done.4 = f32[256,128]{1,0:T(8,128)S(1)} collective-permute-done((f32[256,128]{1,0:T(8,128)S(1)}, f32[256,128]{1,0:T(8,128)S(1)}, u32[]{:S(2)}, u32[]{:S(2)}) %collective-permute-start.4) | collective-permute-done | bytes 131104 | tf_op jit(solution)/shard_map/ppermute | solution.py:19
  45.4 1.6 %collective-permute-start.5 = (f32[256,128]{1,0:T(8,128)S(1)}, f32[256,128]{1,0:T(8,128)S(1)}, u32[]{:S(2)}, u32[]{:S(2)}) collective-permute-start(f32[256,128]{1,0:T(8,128)S(1)} %add.901), channel_id=1, source_target_pairs={{0,2},{1,3},{2,0},{3,1},{4,6},{5,7},{6,4},{7,5},{8,10},{9,11},{10,... | collective-permute-start | bytes 393224 | tf_op jit(solution)/shard_map/ppermute | solution.py:65
  47.0 3.4 %collective-permute-done.5 = f32[256,128]{1,0:T(8,128)S(1)} collective-permute-done((f32[256,128]{1,0:T(8,128)S(1)}, f32[256,128]{1,0:T(8,128)S(1)}, u32[]{:S(2)}, u32[]{:S(2)}) %collective-permute-start.5) | collective-permute-done | bytes 131104 | tf_op jit(solution)/shard_map/ppermute | solution.py:65
  50.7 1.4 %collective-permute-done.6 = f32[2,256,128]{2,1,0:T(8,128)S(1)} collective-permute-done((f32[2,256,128]{2,1,0:T(8,128)S(1)}, f32[2,256,128]{2,1,0:T(8,128)S(1)}, u32[]{:S(2)}, u32[]{:S(2)}) %collective-permute-start.6) | collective-permute-done | bytes 262176 | tf_op jit(solution)/shard_map/ppermute | solution.py:65
  52.0 0.7 multiply_reduce_fusion.1
  53.8 2.4 %fusion.2 = f32[32,1,128,1]{2,1,3,0:T(1,128)S(1)} fusion(bf16[64,2,128,128]{3,2,1,0:T(8,128)(2,1)} %param.7, bf16[32,2,128,1]{2,1,0,3:T(2,128)(2,1)S(1)} %bitcast.309), kind=kOutput, calls=%fused_computation.2 | convolution fusion | flops 2097152 | bytes 2129920 | tf_op jit(solution)/shard_map/tsrb,tsb->tr/dot_general | solution.py:141
  56.4 0.6 fusion.6
  57.4 1.5 %collective-permute-start.10 = (f32[32,128]{1,0:T(8,128)S(1)}, f32[32,128]{1,0:T(8,128)S(1)}, u32[]{:S(2)}, u32[]{:S(2)}) collective-permute-start(f32[32,128]{1,0:T(8,128)S(1)} %add.904), channel_id=1, source_target_pairs={{0,2},{1,3},{2,0},{3,1},{4,6},{5,7},{6,4},{7,5},{8,10},{9,11},{10,... | collective-permute-start | bytes 49160 | tf_op jit(solution)/shard_map/ppermute | solution.py:19
  59.0 0.8 collective-permute-start.8
  59.8 1.4 %collective-permute-done.10 = f32[32,128]{1,0:T(8,128)S(1)} collective-permute-done((f32[32,128]{1,0:T(8,128)S(1)}, f32[32,128]{1,0:T(8,128)S(1)}, u32[]{:S(2)}, u32[]{:S(2)}) %collective-permute-start.10) | collective-permute-done | bytes 16416 | tf_op jit(solution)/shard_map/ppermute | solution.py:19
  61.2 1.6 %collective-permute-done.8 = f32[32,128]{1,0:T(8,128)S(1)} collective-permute-done((f32[32,128]{1,0:T(8,128)S(1)}, f32[32,128]{1,0:T(8,128)S(1)}, u32[]{:S(2)}, u32[]{:S(2)}) %collective-permute-start.8) | collective-permute-done | bytes 16416 | tf_op jit(solution)/shard_map/ppermute | solution.py:19
  63.0 9.6 %all_to_all.15 = f32[32,1,128]{2,1,0:T(1,128)S(1)} all-to-all(f32[32,1,128]{2,1,0:T(1,128)S(1)} %bitcast.298), channel_id=1, replica_groups=mesh['dp'=8,'region'=4] {'dp','region'}, dimensions={0} | all-to-all | bytes 32768 | tf_op jit(solution)/shard_map/all_to_all | solution.py:30
  72.6 0.6 fusion.75
  74.0 2.8 %fusion.33 = f32[64,1,2,128]{3,1,2,0:T(1,128)S(1)} fusion(bf16[64,2,128,128]{3,2,1,0:T(8,128)(2,1)} %param.7, bf16[64,128,1,1]{1,0,2,3:T(8,128)(2,1)S(1)} %get-tuple-element.5), kind=kOutput, calls=%fused_computation.70 | convolution fusion | flops 4194304 | bytes 4276224 | tf_op jit(solution)/shard_map/tsrb,tr->tsb/dot_general | solution.py:98
  77.4 1.5 %collective-permute-done.11 = f32[2,256,128]{2,1,0:T(8,128)S(1)} collective-permute-done((f32[2,256,128]{2,1,0:T(8,128)S(1)}, f32[2,256,128]{2,1,0:T(8,128)S(1)}, u32[]{:S(2)}, u32[]{:S(2)}) %collective-permute-start.11) | collective-permute-done | bytes 262176 | tf_op jit(solution)/shard_map/ppermute | solution.py:52
  79.6 5.0 %collective-permute-done.12 = f32[256,128]{1,0:T(8,128)S(1)} collective-permute-done((f32[256,128]{1,0:T(8,128)S(1)}, f32[256,128]{1,0:T(8,128)S(1)}, u32[]{:S(2)}, u32[]{:S(2)}) %collective-permute-start.12) | collective-permute-done | bytes 131104 | tf_op jit(solution)/shard_map/ppermute | solution.py:52
  85.3 4.4 %collective-permute-done.13 = f32[256,128]{1,0:T(8,128)S(1)} collective-permute-done((f32[256,128]{1,0:T(8,128)S(1)}, f32[256,128]{1,0:T(8,128)S(1)}, u32[]{:S(2)}, u32[]{:S(2)}) %collective-permute-start.13) | collective-permute-done | bytes 131104 | tf_op jit(solution)/shard_map/ppermute | solution.py:19
  89.7 0.6 collective-permute-start.14
  90.3 4.4 %collective-permute-done.14 = f32[256,128]{1,0:T(8,128)S(1)} collective-permute-done((f32[256,128]{1,0:T(8,128)S(1)}, f32[256,128]{1,0:T(8,128)S(1)}, u32[]{:S(2)}, u32[]{:S(2)}) %collective-permute-start.14) | collective-permute-done | bytes 131104 | tf_op jit(solution)/shard_map/ppermute | solution.py:19
  94.7 0.7 collective-permute-start.15
  95.4 6.7 %collective-permute-done.15 = f32[256,128]{1,0:T(8,128)S(1)} collective-permute-done((f32[256,128]{1,0:T(8,128)S(1)}, f32[256,128]{1,0:T(8,128)S(1)}, u32[]{:S(2)}, u32[]{:S(2)}) %collective-permute-start.15) | collective-permute-done | bytes 131104 | tf_op jit(solution)/shard_map/ppermute | solution.py:19
  102.7 4.4 %collective-permute-done.16 = f32[256,128]{1,0:T(8,128)S(1)} collective-permute-done((f32[256,128]{1,0:T(8,128)S(1)}, f32[256,128]{1,0:T(8,128)S(1)}, u32[]{:S(2)}, u32[]{:S(2)}) %collective-permute-start.16) | collective-permute-done | bytes 131104 | tf_op jit(solution)/shard_map/ppermute | solution.py:65
  107.3 1.5 %collective-permute-done.17 = f32[2,256,128]{2,1,0:T(8,128)S(1)} collective-permute-done((f32[2,256,128]{2,1,0:T(8,128)S(1)}, f32[2,256,128]{2,1,0:T(8,128)S(1)}, u32[]{:S(2)}, u32[]{:S(2)}) %collective-permute-start.17) | collective-permute-done | bytes 262176 | tf_op jit(solution)/shard_map/ppermute | solution.py:65
  108.8 0.7 multiply_reduce_fusion
  110.5 2.4 %fusion.4 = f32[32,1,128,1]{2,1,3,0:T(1,128)S(1)} fusion(bf16[64,2,128,128]{3,2,1,0:T(8,128)(2,1)} %param.7, bf16[32,2,128,1]{2,1,0,3:T(2,128)(2,1)S(1)} %bitcast.310), kind=kOutput, calls=%fused_computation.4 | convolution fusion | flops 2097152 | bytes 2129920 | tf_op jit(solution)/shard_map/tsrb,tsb->tr/dot_general | solution.py:141
  113.1 0.6 fusion
  115.0 1.3 %collective-permute-start.21 = (f32[32,128]{1,0:T(8,128)S(1)}, f32[32,128]{1,0:T(8,128)S(1)}, u32[]{:S(2)}, u32[]{:S(2)}) collective-permute-start(f32[32,128]{1,0:T(8,128)S(1)} %add.948), channel_id=1, source_target_pairs={{0,2},{1,3},{2,0},{3,1},{4,6},{5,7},{6,4},{7,5},{8,10},{9,11},{10,... | collective-permute-start | bytes 49160 | tf_op jit(solution)/shard_map/ppermute | solution.py:19
  116.3 1.6 %collective-permute-done.19 = f32[32,128]{1,0:T(8,128)S(1)} collective-permute-done((f32[32,128]{1,0:T(8,128)S(1)}, f32[32,128]{1,0:T(8,128)S(1)}, u32[]{:S(2)}, u32[]{:S(2)}) %collective-permute-start.19) | collective-permute-done | bytes 16416 | tf_op jit(solution)/shard_map/ppermute | solution.py:19
  117.9 0.7 collective-permute-done.21
  118.7 0.8 fusion.47
  119.5 2.5 %all-to-all-start.2 = ((f32[32,1,128]{2,1,0:T(1,128)}), f32[32,1,128]{2,1,0:T(1,128)S(1)}, u32[]{:S(2)}, u32[]{:S(2)}) async-start(f32[32,1,128]{2,1,0:T(1,128)} %bitcast.75), calls=%async_computation.2 | async-start | bytes 32768 | tf_op jit(solution)/shard_map/all_to_all | solution.py:30
  122.2 6.8 %all-to-all-done.2 = f32[32,1,128]{2,1,0:T(1,128)S(1)} async-done(((f32[32,1,128]{2,1,0:T(1,128)}), f32[32,1,128]{2,1,0:T(1,128)S(1)}, u32[]{:S(2)}, u32[]{:S(2)}) %all-to-all-start.2) | async-done | bytes 16416 | tf_op jit(solution)/shard_map/all_to_all | solution.py:30
  129.1 0.6 fusion.58
  130.6 0.7 multiply_add_fusion
  (82 shorter events, 9.3 us)
Async XLA Ops:
  1.5 13.7 %all-to-all-start = ((f32[8,1,128]{2,1,0:T(1,128)}), f32[8,1,128]{2,1,0:T(1,128)S(1)}, u32[]{:S(2)}, u32[]{:S(2)}) async-start(f32[8,1,128]{2,1,0:T(1,128)} %bitcast.3), calls=%async_computation | async-start | bytes 8192 | tf_op jit(solution)/shard_map/all_to_all | solution.py:30
  20.6 1.6 %collective-permute-start = (f32[2,256,128]{2,1,0:T(8,128)S(1)}, f32[2,256,128]{2,1,0:T(8,128)S(1)}, u32[]{:S(2)}, u32[]{:S(2)}) collective-permute-start(f32[2,256,128]{2,1,0:T(8,128)S(1)} %dynamic-slice_bitcast_fusion.1), channel_id=1, source_target_pairs={{0,1},{1,0},{2,3},{3,2},{4,5},{5,4},{6,7},{7,6},{8,9},{9,8},{10,11... | collective-permute-start | bytes 786440 | tf_op jit(solution)/shard_map/ppermute | solution.py:52
  22.3 5.6 %collective-permute-start.1 = (f32[256,128]{1,0:T(8,128)S(1)}, f32[256,128]{1,0:T(8,128)S(1)}, u32[]{:S(2)}, u32[]{:S(2)}) collective-permute-start(f32[256,128]{1,0:T(8,128)S(1)} %dynamic-slice_bitcast_fusion.3), channel_id=1, source_target_pairs={{0,2},{1,3},{2,0},{3,1},{4,6},{5,7},{6,4},{7,5},{8,10},{9,11},{10,... | collective-permute-start | bytes 393224 | tf_op jit(solution)/shard_map/ppermute | solution.py:52
  27.9 5.0 %collective-permute-start.2 = (f32[256,128]{1,0:T(8,128)S(1)}, f32[256,128]{1,0:T(8,128)S(1)}, u32[]{:S(2)}, u32[]{:S(2)}) collective-permute-start(f32[256,128]{1,0:T(8,128)S(1)} %bitcast_add_fusion.3), channel_id=1, source_target_pairs={{0,4},{4,0},{8,12},{12,8},{16,20},{20,16},{24,28},{28,24},{1,5},{5... | collective-permute-start | bytes 393224 | tf_op jit(solution)/shard_map/ppermute | solution.py:19
  33.0 5.0 %collective-permute-start.3 = (f32[256,128]{1,0:T(8,128)S(1)}, f32[256,128]{1,0:T(8,128)S(1)}, u32[]{:S(2)}, u32[]{:S(2)}) collective-permute-start(f32[256,128]{1,0:T(8,128)S(1)} %add.899), channel_id=1, source_target_pairs={{0,8},{4,12},{8,0},{12,4},{16,24},{20,28},{24,16},{28,20},{1,9},{5... | collective-permute-start | bytes 393224 | tf_op jit(solution)/shard_map/ppermute | solution.py:19
  38.0 7.3 %collective-permute-start.4 = (f32[256,128]{1,0:T(8,128)S(1)}, f32[256,128]{1,0:T(8,128)S(1)}, u32[]{:S(2)}, u32[]{:S(2)}) collective-permute-start(f32[256,128]{1,0:T(8,128)S(1)} %add.900), channel_id=1, source_target_pairs={{0,16},{4,20},{8,24},{12,28},{16,0},{20,4},{24,8},{28,12},{1,17},{... | collective-permute-start | bytes 393224 | tf_op jit(solution)/shard_map/ppermute | solution.py:19
  45.4 5.0 %collective-permute-start.5 = (f32[256,128]{1,0:T(8,128)S(1)}, f32[256,128]{1,0:T(8,128)S(1)}, u32[]{:S(2)}, u32[]{:S(2)}) collective-permute-start(f32[256,128]{1,0:T(8,128)S(1)} %add.901), channel_id=1, source_target_pairs={{0,2},{1,3},{2,0},{3,1},{4,6},{5,7},{6,4},{7,5},{8,10},{9,11},{10,... | collective-permute-start | bytes 393224 | tf_op jit(solution)/shard_map/ppermute | solution.py:65
  50.4 1.6 %collective-permute-start.6 = (f32[2,256,128]{2,1,0:T(8,128)S(1)}, f32[2,256,128]{2,1,0:T(8,128)S(1)}, u32[]{:S(2)}, u32[]{:S(2)}) collective-permute-start(f32[2,256,128]{2,1,0:T(8,128)S(1)} %maximum_select_fusion.2), channel_id=1, source_target_pairs={{0,1},{1,0},{2,3},{3,2},{4,5},{5,4},{6,7},{7,6},{8,9},{9,8},{10,11... | collective-permute-start | bytes 786440 | tf_op jit(solution)/shard_map/ppermute | solution.py:65
  50.6 9.1 %copy-start.3 = (f32[32,128]{1,0:T(8,128)S(1)}, f32[32,128]{1,0:T(8,128)}, u32[]{:S(2)}) copy-start(f32[32,128]{1,0:T(8,128)} %param.10) | copy-start | bytes 49156
  50.6 12.2 %copy-start.2 = (f32[64,128]{1,0:T(8,128)S(1)}, f32[64,128]{1,0:T(8,128)}, u32[]{:S(2)}) copy-start(f32[64,128]{1,0:T(8,128)} %param.6) | copy-start | bytes 98308
  53.5 3.0 %copy-start = (bf16[64,2,128,128]{3,2,1,0:T(8,128)(2,1)S(1)}, bf16[64,2,128,128]{3,2,1,0:T(8,128)(2,1)}, u32[]{:S(2)}) copy-start(bf16[64,2,128,128]{3,2,1,0:T(8,128)(2,1)} %param.7) | copy-start | bytes 12582916
  56.2 1.2 collective-permute-start.9
  57.0 1.9 %collective-permute-start.7 = (f32[32,128]{1,0:T(8,128)S(1)}, f32[32,128]{1,0:T(8,128)S(1)}, u32[]{:S(2)}, u32[]{:S(2)}) collective-permute-start(f32[32,128]{1,0:T(8,128)S(1)} %bitcast.299), channel_id=1, source_target_pairs={{0,1},{1,0},{2,3},{3,2},{4,5},{5,4},{6,7},{7,6},{8,9},{9,8},{10,11... | collective-permute-start | bytes 49160 | tf_op jit(solution)/shard_map/ppermute | solution.py:19
  57.4 3.8 %collective-permute-start.10 = (f32[32,128]{1,0:T(8,128)S(1)}, f32[32,128]{1,0:T(8,128)S(1)}, u32[]{:S(2)}, u32[]{:S(2)}) collective-permute-start(f32[32,128]{1,0:T(8,128)S(1)} %add.904), channel_id=1, source_target_pairs={{0,2},{1,3},{2,0},{3,1},{4,6},{5,7},{6,4},{7,5},{8,10},{9,11},{10,... | collective-permute-start | bytes 49160 | tf_op jit(solution)/shard_map/ppermute | solution.py:19
  59.0 3.8 %collective-permute-start.8 = (f32[32,128]{1,0:T(8,128)S(1)}, f32[32,128]{1,0:T(8,128)S(1)}, u32[]{:S(2)}, u32[]{:S(2)}) collective-permute-start(f32[32,128]{1,0:T(8,128)S(1)} %add.902), channel_id=1, source_target_pairs={{0,2},{1,3},{2,0},{3,1},{4,6},{5,7},{6,4},{7,5},{8,10},{9,11},{10,... | collective-permute-start | bytes 49160 | tf_op jit(solution)/shard_map/ppermute | solution.py:19
  77.4 1.6 %collective-permute-start.11 = (f32[2,256,128]{2,1,0:T(8,128)S(1)}, f32[2,256,128]{2,1,0:T(8,128)S(1)}, u32[]{:S(2)}, u32[]{:S(2)}) collective-permute-start(f32[2,256,128]{2,1,0:T(8,128)S(1)} %dynamic-slice_bitcast_fusion), channel_id=1, source_target_pairs={{0,1},{1,0},{2,3},{3,2},{4,5},{5,4},{6,7},{7,6},{8,9},{9,8},{10,11... | collective-permute-start | bytes 786440 | tf_op jit(solution)/shard_map/ppermute | solution.py:52
  79.0 5.6 %collective-permute-start.12 = (f32[256,128]{1,0:T(8,128)S(1)}, f32[256,128]{1,0:T(8,128)S(1)}, u32[]{:S(2)}, u32[]{:S(2)}) collective-permute-start(f32[256,128]{1,0:T(8,128)S(1)} %dynamic-slice_bitcast_fusion.2), channel_id=1, source_target_pairs={{0,2},{1,3},{2,0},{3,1},{4,6},{5,7},{6,4},{7,5},{8,10},{9,11},{10,... | collective-permute-start | bytes 393224 | tf_op jit(solution)/shard_map/ppermute | solution.py:52
  84.6 5.0 %collective-permute-start.13 = (f32[256,128]{1,0:T(8,128)S(1)}, f32[256,128]{1,0:T(8,128)S(1)}, u32[]{:S(2)}, u32[]{:S(2)}) collective-permute-start(f32[256,128]{1,0:T(8,128)S(1)} %bitcast_add_fusion.2), channel_id=1, source_target_pairs={{0,4},{4,0},{8,12},{12,8},{16,20},{20,16},{24,28},{28,24},{1,5},{5... | collective-permute-start | bytes 393224 | tf_op jit(solution)/shard_map/ppermute | solution.py:19
  89.7 5.0 %collective-permute-start.14 = (f32[256,128]{1,0:T(8,128)S(1)}, f32[256,128]{1,0:T(8,128)S(1)}, u32[]{:S(2)}, u32[]{:S(2)}) collective-permute-start(f32[256,128]{1,0:T(8,128)S(1)} %add.943), channel_id=1, source_target_pairs={{0,8},{4,12},{8,0},{12,4},{16,24},{20,28},{24,16},{28,20},{1,9},{5... | collective-permute-start | bytes 393224 | tf_op jit(solution)/shard_map/ppermute | solution.py:19
  94.7 7.3 %collective-permute-start.15 = (f32[256,128]{1,0:T(8,128)S(1)}, f32[256,128]{1,0:T(8,128)S(1)}, u32[]{:S(2)}, u32[]{:S(2)}) collective-permute-start(f32[256,128]{1,0:T(8,128)S(1)} %add.944), channel_id=1, source_target_pairs={{0,16},{4,20},{8,24},{12,28},{16,0},{20,4},{24,8},{28,12},{1,17},{... | collective-permute-start | bytes 393224 | tf_op jit(solution)/shard_map/ppermute | solution.py:19
  102.1 5.0 %collective-permute-start.16 = (f32[256,128]{1,0:T(8,128)S(1)}, f32[256,128]{1,0:T(8,128)S(1)}, u32[]{:S(2)}, u32[]{:S(2)}) collective-permute-start(f32[256,128]{1,0:T(8,128)S(1)} %multiply_subtract_fusion), channel_id=1, source_target_pairs={{0,2},{1,3},{2,0},{3,1},{4,6},{5,7},{6,4},{7,5},{8,10},{9,11},{10,... | collective-permute-start | bytes 393224 | tf_op jit(solution)/shard_map/ppermute | solution.py:65
  107.2 1.6 %collective-permute-start.17 = (f32[2,256,128]{2,1,0:T(8,128)S(1)}, f32[2,256,128]{2,1,0:T(8,128)S(1)}, u32[]{:S(2)}, u32[]{:S(2)}) collective-permute-start(f32[2,256,128]{2,1,0:T(8,128)S(1)} %maximum_select_fusion.4), channel_id=1, source_target_pairs={{0,1},{1,0},{2,3},{3,2},{4,5},{5,4},{6,7},{7,6},{8,9},{9,8},{10,11... | collective-permute-start | bytes 786440 | tf_op jit(solution)/shard_map/ppermute | solution.py:65
  110.2 2.9 %copy-start.1 = (bf16[64,2,128,128]{3,2,1,0:T(8,128)(2,1)S(1)}, bf16[64,2,128,128]{3,2,1,0:T(8,128)(2,1)}, u32[]{:S(2)}) copy-start(bf16[64,2,128,128]{3,2,1,0:T(8,128)(2,1)} %param.7) | copy-start | bytes 12582916
  112.9 1.2 collective-permute-start.18
  113.7 1.2 collective-permute-start.20
  114.1 3.8 %collective-permute-start.19 = (f32[32,128]{1,0:T(8,128)S(1)}, f32[32,128]{1,0:T(8,128)S(1)}, u32[]{:S(2)}, u32[]{:S(2)}) collective-permute-start(f32[32,128]{1,0:T(8,128)S(1)} %add.946), channel_id=1, source_target_pairs={{0,2},{1,3},{2,0},{3,1},{4,6},{5,7},{6,4},{7,5},{8,10},{9,11},{10,... | collective-permute-start | bytes 49160 | tf_op jit(solution)/shard_map/ppermute | solution.py:19
  115.0 3.7 %collective-permute-start.21 = (f32[32,128]{1,0:T(8,128)S(1)}, f32[32,128]{1,0:T(8,128)S(1)}, u32[]{:S(2)}, u32[]{:S(2)}) collective-permute-start(f32[32,128]{1,0:T(8,128)S(1)} %add.948), channel_id=1, source_target_pairs={{0,2},{1,3},{2,0},{3,1},{4,6},{5,7},{6,4},{7,5},{8,10},{9,11},{10,... | collective-permute-start | bytes 49160 | tf_op jit(solution)/shard_map/ppermute | solution.py:19
  119.5 9.6 %all-to-all-start.2 = ((f32[32,1,128]{2,1,0:T(1,128)}), f32[32,1,128]{2,1,0:T(1,128)S(1)}, u32[]{:S(2)}, u32[]{:S(2)}) async-start(f32[32,1,128]{2,1,0:T(1,128)} %bitcast.75), calls=%async_computation.2 | async-start | bytes 32768 | tf_op jit(solution)/shard_map/all_to_all | solution.py:30

commit v13 on v12

--- a/solution.py
+++ b/solution.py
@@ -18,6 +18,22 @@
     while k < n:
         x = x + lax.ppermute(x, axis, [(i, i ^ k) for i in range(n)])
         k *= 2
+    return x
+
+
+def butterfly_sum_split(x, axis, other):
+    n, m = lax.axis_size(axis), lax.axis_size(other)
+    if n & (n - 1) or m % 2:
+        return butterfly_sum(x, axis)
+    forward = [1 << j for j in range(n.bit_length() - 1)]
+    orders = (forward, forward[::-1])
+    for stage in range(len(forward)):
+        perm = []
+        for i in range(n):
+            for j in range(m):
+                k = orders[j % 2][stage]
+                perm.append((i * m + j, (i ^ k) * m + j))
+        x = x + lax.ppermute(x, (axis, other), perm)
     return x
 
 
@@ -114,7 +130,7 @@
             preferred_element_type=jnp.float32,
         )
         piece = halving_scatter(partials, "region")
-        return butterfly_sum(piece, "dp")
+        return butterfly_sum_split(piece, "dp", "region")
 
     def normalized_field(piece):
         field = doubling_gather(piece, "region")

time: 132 us -> 133 us (level)
  waiting for transfers between devices: 68.8 us -> 71.1 us
    ppermute x0 -> x6, waiting for transfers between devices: none -> 33.3 us  [butterfly_sum_split(): x = x + lax.ppermute(x, (axis, other), perm)]
    ppermute x14 -> x8, waiting for transfers between devices: 36.6 us -> 5.55 us  [butterfly_sum(): x = x + lax.ppermute(x, axis, [(i, i ^ k) for i in range(n)])]
    ppermute x14 -> x8, starting transfers between devices: 9.07 us -> 5.31 us  [butterfly_sum(): x = x + lax.ppermute(x, axis, [(i, i ^ k) for i in range(n)])]
    ppermute x0 -> x6, starting transfers between devices: none -> 2.67 us  [butterfly_sum_split(): x = x + lax.ppermute(x, (axis, other), perm)]
where the time goes in v13:
time: 133 us; the launch traced here: 132 us
  waiting for transfers between devices  71.1 us (53%)
  starting transfers between devices  22.4 us (17%)
  matrix products  15.6 us (12%)
  blocking collectives  9.6 us (7%)
  other arithmetic  7.12 us (5%)
  between operations  4.89 us (4%)
  local copies, waits for them, and re-layouts  1.83 us (1%)
    ppermute x6, waiting for transfers between devices, butterfly_sum_split(): x = x + lax.ppermute(x, (axis, other), perm)  33.3 us
    ppermute x4, waiting for transfers between devices, halving_scatter(): x = keep + lax.ppermute(send, axis, [(i, i ^ k) for i in range(n)])  12.1 us
    ppermute x4, waiting for transfers between devices, doubling_gather(): other = lax.ppermute(x, axis, [(i, i ^ k) for i in range(n)])  10.7 us
    all_to_all x2, starting transfers between devices, square_sum(): got = lax.all_to_all(spread[:, None, :], axis, 0, 0, tiled=False)  9.82 us
    all_to_all x1, blocking collectives, square_sum(): got = lax.all_to_all(spread[:, None, :], axis, 0, 0, tiled=False)  9.6 us
    all_to_all x2, waiting for transfers between devices, square_sum(): got = lax.all_to_all(spread[:, None, :], axis, 0, 0, tiled=False)  9.46 us
    dot_general x4, matrix products, local(): jnp.einsum('tsrb,tsb->tr', sensitivity[lo:lo + half_tiles], picked[lo:lo...  6.09 us
    dot_general x2, matrix products, transposed_part(): jnp.einsum('tsrb,tr->tsb', sensitivity, rays_half, preferred_element_type...  5.68 us
  transfers between devices with their start and end apart: 24, of which 21 were waited for; matrix products, arithmetic and copies ran while one was open for 4% of the time, Pallas kernels for 0%

profile of v13, /device:TPU:0, one launch (start us, length us, event | category | flops | bytes accessed | tf_op | source)
XLA Modules:
  0.0 132.5 jit_solution(8388555183773503499)
XLA Ops:
  0.0 1.5 %fusion.39 = f32[8,128]{1,0:T(8,128)} fusion(f32[64,128]{1,0:T(8,128)} %param.6), kind=kOutput, calls=%fused_computation.76 | convolution fusion | flops 794624 | bytes 36864 | tf_op jit(solution)/shard_map/dot_general | solution.py:43
  1.5 7.3 %all-to-all-start = ((f32[8,1,128]{2,1,0:T(1,128)}), f32[8,1,128]{2,1,0:T(1,128)S(1)}, u32[]{:S(2)}, u32[]{:S(2)}) async-start(f32[8,1,128]{2,1,0:T(1,128)} %bitcast.3), calls=%async_computation | async-start | bytes 8192 | tf_op jit(solution)/shard_map/all_to_all | solution.py:46
  8.8 0.8 copy.14
  9.8 0.8 slice_bitcast_fusion.31
  11.8 0.8 multiply_multiply_fusion.1
  12.6 2.6 %all-to-all-done = f32[8,1,128]{2,1,0:T(1,128)S(1)} async-done(((f32[8,1,128]{2,1,0:T(1,128)}), f32[8,1,128]{2,1,0:T(1,128)S(1)}, u32[]{:S(2)}, u32[]{:S(2)}) %all-to-all-start) | async-done | bytes 4128 | tf_op jit(solution)/shard_map/all_to_all | solution.py:46
  16.5 0.8 convert_bitcast_fusion.1
  17.2 2.8 %fusion.37 = f32[64,1,2,128]{3,1,2,0:T(1,128)S(1)} fusion(bf16[64,2,128,128]{3,2,1,0:T(8,128)(2,1)} %param.7, bf16[64,128,1,1]{1,0,2,3:T(8,128)(2,1)S(1)} %convert_bitcast_fusion.1), kind=kOutput, calls=%fused_computation.74 | convolution fusion | flops 4194304 | bytes 4276224 | tf_op jit(solution)/shard_map/tsrb,tr->tsb/dot_general | solution.py:114
  20.7 1.5 %collective-permute-done = f32[2,256,128]{2,1,0:T(8,128)S(1)} collective-permute-done((f32[2,256,128]{2,1,0:T(8,128)S(1)}, f32[2,256,128]{2,1,0:T(8,128)S(1)}, u32[]{:S(2)}, u32[]{:S(2)}) %collective-permute-start) | collective-permute-done | bytes 262176 | tf_op jit(solution)/shard_map/ppermute | solution.py:68
  22.3 1.6 %collective-permute-start.1 = (f32[256,128]{1,0:T(8,128)S(1)}, f32[256,128]{1,0:T(8,128)S(1)}, u32[]{:S(2)}, u32[]{:S(2)}) collective-permute-start(f32[256,128]{1,0:T(8,128)S(1)} %dynamic-slice_bitcast_fusion.3), channel_id=1, source_target_pairs={{0,2},{1,3},{2,0},{3,1},{4,6},{5,7},{6,4},{7,5},{8,10},{9,11},{10,... | collective-permute-start | bytes 393224 | tf_op jit(solution)/shard_map/ppermute | solution.py:68
  23.8 4.0 %collective-permute-done.1 = f32[256,128]{1,0:T(8,128)S(1)} collective-permute-done((f32[256,128]{1,0:T(8,128)S(1)}, f32[256,128]{1,0:T(8,128)S(1)}, u32[]{:S(2)}, u32[]{:S(2)}) %collective-permute-start.1) | collective-permute-done | bytes 131104 | tf_op jit(solution)/shard_map/ppermute | solution.py:68
  27.9 0.6 collective-permute-start.2
  28.5 4.4 %collective-permute-done.2 = f32[256,128]{1,0:T(8,128)S(1)} collective-permute-done((f32[256,128]{1,0:T(8,128)S(1)}, f32[256,128]{1,0:T(8,128)S(1)}, u32[]{:S(2)}, u32[]{:S(2)}) %collective-permute-start.2) | collective-permute-done | bytes 131104 | tf_op jit(solution)/shard_map/ppermute | solution.py:36
  33.6 5.3 %collective-permute-done.3 = f32[256,128]{1,0:T(8,128)S(1)} collective-permute-done((f32[256,128]{1,0:T(8,128)S(1)}, f32[256,128]{1,0:T(8,128)S(1)}, u32[]{:S(2)}, u32[]{:S(2)}) %collective-permute-start.3) | collective-permute-done | bytes 131104 | tf_op jit(solution)/shard_map/ppermute | solution.py:36
  39.0 6.9 %collective-permute-done.4 = f32[256,128]{1,0:T(8,128)S(1)} collective-permute-done((f32[256,128]{1,0:T(8,128)S(1)}, f32[256,128]{1,0:T(8,128)S(1)}, u32[]{:S(2)}, u32[]{:S(2)}) %collective-permute-start.4) | collective-permute-done | bytes 131104 | tf_op jit(solution)/shard_map/ppermute | solution.py:36
  46.0 1.6 %collective-permute-start.5 = (f32[256,128]{1,0:T(8,128)S(1)}, f32[256,128]{1,0:T(8,128)S(1)}, u32[]{:S(2)}, u32[]{:S(2)}) collective-permute-start(f32[256,128]{1,0:T(8,128)S(1)} %add.901), channel_id=1, source_target_pairs={{0,2},{1,3},{2,0},{3,1},{4,6},{5,7},{6,4},{7,5},{8,10},{9,11},{10,... | collective-permute-start | bytes 393224 | tf_op jit(solution)/shard_map/ppermute | solution.py:81
  47.6 3.4 %collective-permute-done.5 = f32[256,128]{1,0:T(8,128)S(1)} collective-permute-done((f32[256,128]{1,0:T(8,128)S(1)}, f32[256,128]{1,0:T(8,128)S(1)}, u32[]{:S(2)}, u32[]{:S(2)}) %collective-permute-start.5) | collective-permute-done | bytes 131104 | tf_op jit(solution)/shard_map/ppermute | solution.py:81
  51.2 1.4 %collective-permute-done.6 = f32[2,256,128]{2,1,0:T(8,128)S(1)} collective-permute-done((f32[2,256,128]{2,1,0:T(8,128)S(1)}, f32[2,256,128]{2,1,0:T(8,128)S(1)}, u32[]{:S(2)}, u32[]{:S(2)}) %collective-permute-start.6) | collective-permute-done | bytes 262176 | tf_op jit(solution)/shard_map/ppermute | solution.py:81
  52.6 0.7 multiply_reduce_fusion.1
  54.4 2.4 %fusion.2 = f32[32,1,128,1]{2,1,3,0:T(1,128)S(1)} fusion(bf16[64,2,128,128]{3,2,1,0:T(8,128)(2,1)} %param.7, bf16[32,2,128,1]{2,1,0,3:T(2,128)(2,1)S(1)} %bitcast.309), kind=kOutput, calls=%fused_computation.2 | convolution fusion | flops 2097152 | bytes 2129920 | tf_op jit(solution)/shard_map/tsrb,tsb->tr/dot_general | solution.py:157
  57.0 0.6 fusion.6
  58.0 1.5 %collective-permute-start.10 = (f32[32,128]{1,0:T(8,128)S(1)}, f32[32,128]{1,0:T(8,128)S(1)}, u32[]{:S(2)}, u32[]{:S(2)}) collective-permute-start(f32[32,128]{1,0:T(8,128)S(1)} %add.904), channel_id=1, source_target_pairs={{0,2},{1,3},{2,0},{3,1},{4,6},{5,7},{6,4},{7,5},{8,10},{9,11},{10,... | collective-permute-start | bytes 49160 | tf_op jit(solution)/shard_map/ppermute | solution.py:19
  59.6 0.8 collective-permute-start.8
  60.4 1.4 %collective-permute-done.10 = f32[32,128]{1,0:T(8,128)S(1)} collective-permute-done((f32[32,128]{1,0:T(8,128)S(1)}, f32[32,128]{1,0:T(8,128)S(1)}, u32[]{:S(2)}, u32[]{:S(2)}) %collective-permute-start.10) | collective-permute-done | bytes 16416 | tf_op jit(solution)/shard_map/ppermute | solution.py:19
  61.8 1.6 %collective-permute-done.8 = f32[32,128]{1,0:T(8,128)S(1)} collective-permute-done((f32[32,128]{1,0:T(8,128)S(1)}, f32[32,128]{1,0:T(8,128)S(1)}, u32[]{:S(2)}, u32[]{:S(2)}) %collective-permute-start.8) | collective-permute-done | bytes 16416 | tf_op jit(solution)/shard_map/ppermute | solution.py:19
  63.6 9.6 %all_to_all.15 = f32[32,1,128]{2,1,0:T(1,128)S(1)} all-to-all(f32[32,1,128]{2,1,0:T(1,128)S(1)} %bitcast.298), channel_id=1, replica_groups=mesh['dp'=8,'region'=4] {'dp','region'}, dimensions={0} | all-to-all | bytes 32768 | tf_op jit(solution)/shard_map/all_to_all | solution.py:46
  73.2 0.6 fusion.75
  74.6 2.8 %fusion.33 = f32[64,1,2,128]{3,1,2,0:T(1,128)S(1)} fusion(bf16[64,2,128,128]{3,2,1,0:T(8,128)(2,1)} %param.7, bf16[64,128,1,1]{1,0,2,3:T(8,128)(2,1)S(1)} %get-tuple-element.5), kind=kOutput, calls=%fused_computation.70 | convolution fusion | flops 4194304 | bytes 4276224 | tf_op jit(solution)/shard_map/tsrb,tr->tsb/dot_general | solution.py:114
  78.1 1.5 %collective-permute-done.11 = f32[2,256,128]{2,1,0:T(8,128)S(1)} collective-permute-done((f32[2,256,128]{2,1,0:T(8,128)S(1)}, f32[2,256,128]{2,1,0:T(8,128)S(1)}, u32[]{:S(2)}, u32[]{:S(2)}) %collective-permute-start.11) | collective-permute-done | bytes 262176 | tf_op jit(solution)/shard_map/ppermute | solution.py:68
  80.2 5.0 %collective-permute-done.12 = f32[256,128]{1,0:T(8,128)S(1)} collective-permute-done((f32[256,128]{1,0:T(8,128)S(1)}, f32[256,128]{1,0:T(8,128)S(1)}, u32[]{:S(2)}, u32[]{:S(2)}) %collective-permute-start.12) | collective-permute-done | bytes 131104 | tf_op jit(solution)/shard_map/ppermute | solution.py:68
  85.3 0.6 collective-permute-start.13
  85.9 4.4 %collective-permute-done.13 = f32[256,128]{1,0:T(8,128)S(1)} collective-permute-done((f32[256,128]{1,0:T(8,128)S(1)}, f32[256,128]{1,0:T(8,128)S(1)}, u32[]{:S(2)}, u32[]{:S(2)}) %collective-permute-start.13) | collective-permute-done | bytes 131104 | tf_op jit(solution)/shard_map/ppermute | solution.py:36
  90.3 0.6 collective-permute-start.14
  91.0 5.3 %collective-permute-done.14 = f32[256,128]{1,0:T(8,128)S(1)} collective-permute-done((f32[256,128]{1,0:T(8,128)S(1)}, f32[256,128]{1,0:T(8,128)S(1)}, u32[]{:S(2)}, u32[]{:S(2)}) %collective-permute-start.14) | collective-permute-done | bytes 131104 | tf_op jit(solution)/shard_map/ppermute | solution.py:36
  96.3 7.0 %collective-permute-done.15 = f32[256,128]{1,0:T(8,128)S(1)} collective-permute-done((f32[256,128]{1,0:T(8,128)S(1)}, f32[256,128]{1,0:T(8,128)S(1)}, u32[]{:S(2)}, u32[]{:S(2)}) %collective-permute-start.15) | collective-permute-done | bytes 131104 | tf_op jit(solution)/shard_map/ppermute | solution.py:36
  103.9 4.4 %collective-permute-done.16 = f32[256,128]{1,0:T(8,128)S(1)} collective-permute-done((f32[256,128]{1,0:T(8,128)S(1)}, f32[256,128]{1,0:T(8,128)S(1)}, u32[]{:S(2)}, u32[]{:S(2)}) %collective-permute-start.16) | collective-permute-done | bytes 131104 | tf_op jit(solution)/shard_map/ppermute | solution.py:81
  108.5 1.5 %collective-permute-done.17 = f32[2,256,128]{2,1,0:T(8,128)S(1)} collective-permute-done((f32[2,256,128]{2,1,0:T(8,128)S(1)}, f32[2,256,128]{2,1,0:T(8,128)S(1)}, u32[]{:S(2)}, u32[]{:S(2)}) %collective-permute-start.17) | collective-permute-done | bytes 262176 | tf_op jit(solution)/shard_map/ppermute | solution.py:81
  110.0 0.7 multiply_reduce_fusion
  111.8 2.4 %fusion.4 = f32[32,1,128,1]{2,1,3,0:T(1,128)S(1)} fusion(bf16[64,2,128,128]{3,2,1,0:T(8,128)(2,1)} %param.7, bf16[32,2,128,1]{2,1,0,3:T(2,128)(2,1)S(1)} %bitcast.310), kind=kOutput, calls=%fused_computation.4 | convolution fusion | flops 2097152 | bytes 2129920 | tf_op jit(solution)/shard_map/tsrb,tsb->tr/dot_general | solution.py:157
  114.3 0.6 fusion
  116.2 1.3 collective-permute-start.21
  117.6 1.6 %collective-permute-done.19 = f32[32,128]{1,0:T(8,128)S(1)} collective-permute-done((f32[32,128]{1,0:T(8,128)S(1)}, f32[32,128]{1,0:T(8,128)S(1)}, u32[]{:S(2)}, u32[]{:S(2)}) %collective-permute-start.19) | collective-permute-done | bytes 16416 | tf_op jit(solution)/shard_map/ppermute | solution.py:19
  119.2 0.7 collective-permute-done.21
  119.9 0.8 fusion.47
  120.7 2.5 %all-to-all-start.2 = ((f32[32,1,128]{2,1,0:T(1,128)}), f32[32,1,128]{2,1,0:T(1,128)S(1)}, u32[]{:S(2)}, u32[]{:S(2)}) async-start(f32[32,1,128]{2,1,0:T(1,128)} %bitcast.75), calls=%async_computation.2 | async-start | bytes 32768 | tf_op jit(solution)/shard_map/all_to_all | solution.py:46
  123.5 6.8 %all-to-all-done.2 = f32[32,1,128]{2,1,0:T(1,128)S(1)} async-done(((f32[32,1,128]{2,1,0:T(1,128)}), f32[32,1,128]{2,1,0:T(1,128)S(1)}, u32[]{:S(2)}, u32[]{:S(2)}) %all-to-all-start.2) | async-done | bytes 16416 | tf_op jit(solution)/shard_map/all_to_all | solution.py:46
  130.3 0.6 fusion.58
  131.8 0.7 multiply_add_fusion
  (82 shorter events, 8.2 us)
Async XLA Ops:
  1.5 13.7 %all-to-all-start = ((f32[8,1,128]{2,1,0:T(1,128)}), f32[8,1,128]{2,1,0:T(1,128)S(1)}, u32[]{:S(2)}, u32[]{:S(2)}) async-start(f32[8,1,128]{2,1,0:T(1,128)} %bitcast.3), calls=%async_computation | async-start | bytes 8192 | tf_op jit(solution)/shard_map/all_to_all | solution.py:46
  20.6 1.6 %collective-permute-start = (f32[2,256,128]{2,1,0:T(8,128)S(1)}, f32[2,256,128]{2,1,0:T(8,128)S(1)}, u32[]{:S(2)}, u32[]{:S(2)}) collective-permute-start(f32[2,256,128]{2,1,0:T(8,128)S(1)} %dynamic-slice_bitcast_fusion.1), channel_id=1, source_target_pairs={{0,1},{1,0},{2,3},{3,2},{4,5},{5,4},{6,7},{7,6},{8,9},{9,8},{10,11... | collective-permute-start | bytes 786440 | tf_op jit(solution)/shard_map/ppermute | solution.py:68
  22.3 5.6 %collective-permute-start.1 = (f32[256,128]{1,0:T(8,128)S(1)}, f32[256,128]{1,0:T(8,128)S(1)}, u32[]{:S(2)}, u32[]{:S(2)}) collective-permute-start(f32[256,128]{1,0:T(8,128)S(1)} %dynamic-slice_bitcast_fusion.3), channel_id=1, source_target_pairs={{0,2},{1,3},{2,0},{3,1},{4,6},{5,7},{6,4},{7,5},{8,10},{9,11},{10,... | collective-permute-start | bytes 393224 | tf_op jit(solution)/shard_map/ppermute | solution.py:68
  27.9 5.0 %collective-permute-start.2 = (f32[256,128]{1,0:T(8,128)S(1)}, f32[256,128]{1,0:T(8,128)S(1)}, u32[]{:S(2)}, u32[]{:S(2)}) collective-permute-start(f32[256,128]{1,0:T(8,128)S(1)} %bitcast_add_fusion.3), channel_id=1, source_target_pairs={{0,4},{1,17},{2,6},{3,19},{4,0},{5,21},{6,2},{7,23},{8,12},{9,25},... | collective-permute-start | bytes 393224 | tf_op jit(solution)/shard_map/ppermute | solution.py:36
  33.0 5.9 %collective-permute-start.3 = (f32[256,128]{1,0:T(8,128)S(1)}, f32[256,128]{1,0:T(8,128)S(1)}, u32[]{:S(2)}, u32[]{:S(2)}) collective-permute-start(f32[256,128]{1,0:T(8,128)S(1)} %add.899), channel_id=1, source_target_pairs={{0,8},{1,9},{2,10},{3,11},{4,12},{5,13},{6,14},{7,15},{8,0},{9,1},... | collective-permute-start | bytes 393224 | tf_op jit(solution)/shard_map/ppermute | solution.py:36
  38.9 7.1 %collective-permute-start.4 = (f32[256,128]{1,0:T(8,128)S(1)}, f32[256,128]{1,0:T(8,128)S(1)}, u32[]{:S(2)}, u32[]{:S(2)}) collective-permute-start(f32[256,128]{1,0:T(8,128)S(1)} %add.900), channel_id=1, source_target_pairs={{0,16},{1,5},{2,18},{3,7},{4,20},{5,1},{6,22},{7,3},{8,24},{9,13},... | collective-permute-start | bytes 393224 | tf_op jit(solution)/shard_map/ppermute | solution.py:36
  46.0 5.0 %collective-permute-start.5 = (f32[256,128]{1,0:T(8,128)S(1)}, f32[256,128]{1,0:T(8,128)S(1)}, u32[]{:S(2)}, u32[]{:S(2)}) collective-permute-start(f32[256,128]{1,0:T(8,128)S(1)} %add.901), channel_id=1, source_target_pairs={{0,2},{1,3},{2,0},{3,1},{4,6},{5,7},{6,4},{7,5},{8,10},{9,11},{10,... | collective-permute-start | bytes 393224 | tf_op jit(solution)/shard_map/ppermute | solution.py:81
  51.0 1.6 %collective-permute-start.6 = (f32[2,256,128]{2,1,0:T(8,128)S(1)}, f32[2,256,128]{2,1,0:T(8,128)S(1)}, u32[]{:S(2)}, u32[]{:S(2)}) collective-permute-start(f32[2,256,128]{2,1,0:T(8,128)S(1)} %maximum_select_fusion.2), channel_id=1, source_target_pairs={{0,1},{1,0},{2,3},{3,2},{4,5},{5,4},{6,7},{7,6},{8,9},{9,8},{10,11... | collective-permute-start | bytes 786440 | tf_op jit(solution)/shard_map/ppermute | solution.py:81
  51.2 9.1 %copy-start.3 = (f32[32,128]{1,0:T(8,128)S(1)}, f32[32,128]{1,0:T(8,128)}, u32[]{:S(2)}) copy-start(f32[32,128]{1,0:T(8,128)} %param.10) | copy-start | bytes 49156
  51.2 12.2 %copy-start.2 = (f32[64,128]{1,0:T(8,128)S(1)}, f32[64,128]{1,0:T(8,128)}, u32[]{:S(2)}) copy-start(f32[64,128]{1,0:T(8,128)} %param.6) | copy-start | bytes 98308
  54.0 2.9 %copy-start = (bf16[64,2,128,128]{3,2,1,0:T(8,128)(2,1)S(1)}, bf16[64,2,128,128]{3,2,1,0:T(8,128)(2,1)}, u32[]{:S(2)}) copy-start(bf16[64,2,128,128]{3,2,1,0:T(8,128)(2,1)} %param.7) | copy-start | bytes 12582916
  56.8 1.2 collective-permute-start.9
  57.6 2.0 %collective-permute-start.7 = (f32[32,128]{1,0:T(8,128)S(1)}, f32[32,128]{1,0:T(8,128)S(1)}, u32[]{:S(2)}, u32[]{:S(2)}) collective-permute-start(f32[32,128]{1,0:T(8,128)S(1)} %bitcast.299), channel_id=1, source_target_pairs={{0,1},{1,0},{2,3},{3,2},{4,5},{5,4},{6,7},{7,6},{8,9},{9,8},{10,11... | collective-permute-start | bytes 49160 | tf_op jit(solution)/shard_map/ppermute | solution.py:19
  58.0 3.8 %collective-permute-start.10 = (f32[32,128]{1,0:T(8,128)S(1)}, f32[32,128]{1,0:T(8,128)S(1)}, u32[]{:S(2)}, u32[]{:S(2)}) collective-permute-start(f32[32,128]{1,0:T(8,128)S(1)} %add.904), channel_id=1, source_target_pairs={{0,2},{1,3},{2,0},{3,1},{4,6},{5,7},{6,4},{7,5},{8,10},{9,11},{10,... | collective-permute-start | bytes 49160 | tf_op jit(solution)/shard_map/ppermute | solution.py:19
  59.6 3.8 %collective-permute-start.8 = (f32[32,128]{1,0:T(8,128)S(1)}, f32[32,128]{1,0:T(8,128)S(1)}, u32[]{:S(2)}, u32[]{:S(2)}) collective-permute-start(f32[32,128]{1,0:T(8,128)S(1)} %add.902), channel_id=1, source_target_pairs={{0,2},{1,3},{2,0},{3,1},{4,6},{5,7},{6,4},{7,5},{8,10},{9,11},{10,... | collective-permute-start | bytes 49160 | tf_op jit(solution)/shard_map/ppermute | solution.py:19
  78.0 1.6 %collective-permute-start.11 = (f32[2,256,128]{2,1,0:T(8,128)S(1)}, f32[2,256,128]{2,1,0:T(8,128)S(1)}, u32[]{:S(2)}, u32[]{:S(2)}) collective-permute-start(f32[2,256,128]{2,1,0:T(8,128)S(1)} %dynamic-slice_bitcast_fusion), channel_id=1, source_target_pairs={{0,1},{1,0},{2,3},{3,2},{4,5},{5,4},{6,7},{7,6},{8,9},{9,8},{10,11... | collective-permute-start | bytes 786440 | tf_op jit(solution)/shard_map/ppermute | solution.py:68
  79.6 5.6 %collective-permute-start.12 = (f32[256,128]{1,0:T(8,128)S(1)}, f32[256,128]{1,0:T(8,128)S(1)}, u32[]{:S(2)}, u32[]{:S(2)}) collective-permute-start(f32[256,128]{1,0:T(8,128)S(1)} %dynamic-slice_bitcast_fusion.2), channel_id=1, source_target_pairs={{0,2},{1,3},{2,0},{3,1},{4,6},{5,7},{6,4},{7,5},{8,10},{9,11},{10,... | collective-permute-start | bytes 393224 | tf_op jit(solution)/shard_map/ppermute | solution.py:68
  85.3 5.0 %collective-permute-start.13 = (f32[256,128]{1,0:T(8,128)S(1)}, f32[256,128]{1,0:T(8,128)S(1)}, u32[]{:S(2)}, u32[]{:S(2)}) collective-permute-start(f32[256,128]{1,0:T(8,128)S(1)} %bitcast_add_fusion.2), channel_id=1, source_target_pairs={{0,4},{1,17},{2,6},{3,19},{4,0},{5,21},{6,2},{7,23},{8,12},{9,25},... | collective-permute-start | bytes 393224 | tf_op jit(solution)/shard_map/ppermute | solution.py:36
  90.3 5.9 %collective-permute-start.14 = (f32[256,128]{1,0:T(8,128)S(1)}, f32[256,128]{1,0:T(8,128)S(1)}, u32[]{:S(2)}, u32[]{:S(2)}) collective-permute-start(f32[256,128]{1,0:T(8,128)S(1)} %add.943), channel_id=1, source_target_pairs={{0,8},{1,9},{2,10},{3,11},{4,12},{5,13},{6,14},{7,15},{8,0},{9,1},... | collective-permute-start | bytes 393224 | tf_op jit(solution)/shard_map/ppermute | solution.py:36
  96.3 7.1 %collective-permute-start.15 = (f32[256,128]{1,0:T(8,128)S(1)}, f32[256,128]{1,0:T(8,128)S(1)}, u32[]{:S(2)}, u32[]{:S(2)}) collective-permute-start(f32[256,128]{1,0:T(8,128)S(1)} %add.944), channel_id=1, source_target_pairs={{0,16},{1,5},{2,18},{3,7},{4,20},{5,1},{6,22},{7,3},{8,24},{9,13},... | collective-permute-start | bytes 393224 | tf_op jit(solution)/shard_map/ppermute | solution.py:36
  103.3 5.0 %collective-permute-start.16 = (f32[256,128]{1,0:T(8,128)S(1)}, f32[256,128]{1,0:T(8,128)S(1)}, u32[]{:S(2)}, u32[]{:S(2)}) collective-permute-start(f32[256,128]{1,0:T(8,128)S(1)} %multiply_subtract_fusion), channel_id=1, source_target_pairs={{0,2},{1,3},{2,0},{3,1},{4,6},{5,7},{6,4},{7,5},{8,10},{9,11},{10,... | collective-permute-start | bytes 393224 | tf_op jit(solution)/shard_map/ppermute | solution.py:81
  108.4 1.6 %collective-permute-start.17 = (f32[2,256,128]{2,1,0:T(8,128)S(1)}, f32[2,256,128]{2,1,0:T(8,128)S(1)}, u32[]{:S(2)}, u32[]{:S(2)}) collective-permute-start(f32[2,256,128]{2,1,0:T(8,128)S(1)} %maximum_select_fusion.4), channel_id=1, source_target_pairs={{0,1},{1,0},{2,3},{3,2},{4,5},{5,4},{6,7},{7,6},{8,9},{9,8},{10,11... | collective-permute-start | bytes 786440 | tf_op jit(solution)/shard_map/ppermute | solution.py:81
  111.4 2.9 %copy-start.1 = (bf16[64,2,128,128]{3,2,1,0:T(8,128)(2,1)S(1)}, bf16[64,2,128,128]{3,2,1,0:T(8,128)(2,1)}, u32[]{:S(2)}) copy-start(bf16[64,2,128,128]{3,2,1,0:T(8,128)(2,1)} %param.7) | copy-start | bytes 12582916
  114.2 1.2 collective-permute-start.18
  115.0 1.2 collective-permute-start.20
  115.4 3.8 %collective-permute-start.19 = (f32[32,128]{1,0:T(8,128)S(1)}, f32[32,128]{1,0:T(8,128)S(1)}, u32[]{:S(2)}, u32[]{:S(2)}) collective-permute-start(f32[32,128]{1,0:T(8,128)S(1)} %add.946), channel_id=1, source_target_pairs={{0,2},{1,3},{2,0},{3,1},{4,6},{5,7},{6,4},{7,5},{8,10},{9,11},{10,... | collective-permute-start | bytes 49160 | tf_op jit(solution)/shard_map/ppermute | solution.py:19
  116.2 3.7 %collective-permute-start.21 = (f32[32,128]{1,0:T(8,128)S(1)}, f32[32,128]{1,0:T(8,128)S(1)}, u32[]{:S(2)}, u32[]{:S(2)}) collective-permute-start(f32[32,128]{1,0:T(8,128)S(1)} %add.948), channel_id=1, source_target_pairs={{0,2},{1,3},{2,0},{3,1},{4,6},{5,7},{6,4},{7,5},{8,10},{9,11},{10,... | collective-permute-start | bytes 49160 | tf_op jit(solution)/shard_map/ppermute | solution.py:19
  120.7 9.6 %all-to-all-start.2 = ((f32[32,1,128]{2,1,0:T(1,128)}), f32[32,1,128]{2,1,0:T(1,128)S(1)}, u32[]{:S(2)}, u32[]{:S(2)}) async-start(f32[32,1,128]{2,1,0:T(1,128)} %bitcast.75), calls=%async_computation.2 | async-start | bytes 32768 | tf_op jit(solution)/shard_map/all_to_all | solution.py:46

commit v14 on v12

--- a/solution.py
+++ b/solution.py
@@ -135,7 +135,7 @@
         full_half = full_model.astype(jnp.bfloat16)
         rows = jnp.dot(select_half, full_half, preferred_element_type=jnp.float32)
         picked = rows[:n_slots].astype(jnp.bfloat16).reshape(tile_blocks.shape + rows.shape[-1:])
-        half_tiles = n_tiles // 2 if n_tiles % 16 == 0 else n_tiles
+        half_tiles = n_tiles // 4 if n_tiles % 32 == 0 else n_tiles
         halves = []
         for lo in range(0, n_tiles, half_tiles):
             part = jnp.einsum(

time: 132 us -> 137 us (1.038)
  starting transfers between devices: 23.5 us -> 28.3 us
    ppermute x14 -> x22, starting transfers between devices: 9.07 us -> 13.9 us  [butterfly_sum(): x = x + lax.ppermute(x, axis, [(i, i ^ k) for i in range(n)])]
    dot_general x4 -> x8, matrix products: 6.09 us -> 6.99 us  [local(): jnp.einsum('tsrb,tsb->tr', sensitivity[lo:lo + half_tiles], picked[lo:lo...]
    ppermute x14 -> x22, waiting for transfers between devices: 36.6 us -> 36.1 us  [butterfly_sum(): x = x + lax.ppermute(x, axis, [(i, i ^ k) for i in range(n)])]
  transfers between devices with their start and end apart: 24 -> 32, of which waited for: 21 -> 21; matrix products, arithmetic and copies ran while one was open for 4% -> 5% of each run, Pallas kernels for 0% -> 0%
where the time goes in v14:
time: 137 us
  waiting for transfers between devices  68.3 us (50%)
  starting transfers between devices  28.3 us (21%)
  matrix products  16.5 us (12%)
  blocking collectives  9.45 us (7%)
  other arithmetic  7.15 us (5%)
  between operations  4.91 us (4%)
  local copies, waits for them, and re-layouts  2.03 us (1%)
    ppermute x22, waiting for transfers between devices, butterfly_sum(): x = x + lax.ppermute(x, axis, [(i, i ^ k) for i in range(n)])  36.1 us
    ppermute x22, starting transfers between devices, butterfly_sum(): x = x + lax.ppermute(x, axis, [(i, i ^ k) for i in range(n)])  13.9 us
    ppermute x4, waiting for transfers between devices, halving_scatter(): x = keep + lax.ppermute(send, axis, [(i, i ^ k) for i in range(n)])  12.1 us
    ppermute x4, waiting for transfers between devices, doubling_gather(): other = lax.ppermute(x, axis, [(i, i ^ k) for i in range(n)])  10.7 us
    all_to_all x2, starting transfers between devices, square_sum(): got = lax.all_to_all(spread[:, None, :], axis, 0, 0, tiled=False)  9.82 us
    all_to_all x2, waiting for transfers between devices, square_sum(): got = lax.all_to_all(spread[:, None, :], axis, 0, 0, tiled=False)  9.46 us
    all_to_all x1, blocking collectives, square_sum(): got = lax.all_to_all(spread[:, None, :], axis, 0, 0, tiled=False)  9.45 us
    dot_general x8, matrix products, local(): jnp.einsum('tsrb,tsb->tr', sensitivity[lo:lo + half_tiles], picked[lo:lo...  6.99 us
  transfers between devices with their start and end apart: 32, of which 21 were waited for; matrix products, arithmetic and copies ran while one was open for 5% of the time, Pallas kernels for 0%

profile of v14, /device:TPU:0, one launch (start us, length us, event | category | flops | bytes accessed | tf_op | source)
XLA Modules:
  0.0 136.6 jit_solution(10105347837202239522)
XLA Ops:
  0.0 1.5 %fusion.43 = f32[8,128]{1,0:T(8,128)} fusion(f32[64,128]{1,0:T(8,128)} %param.6), kind=kOutput, calls=%fused_computation.82 | convolution fusion | flops 794624 | bytes 36864 | tf_op jit(solution)/shard_map/dot_general | solution.py:27
  1.5 7.3 %all-to-all-start = ((f32[8,1,128]{2,1,0:T(1,128)}), f32[8,1,128]{2,1,0:T(1,128)S(1)}, u32[]{:S(2)}, u32[]{:S(2)}) async-start(f32[8,1,128]{2,1,0:T(1,128)} %bitcast.3), calls=%async_computation | async-start | bytes 8192 | tf_op jit(solution)/shard_map/all_to_all | solution.py:30
  8.8 0.8 copy.14
  9.8 0.8 slice_bitcast_fusion.31
  11.8 0.8 multiply_multiply_fusion.1
  12.6 2.6 %all-to-all-done = f32[8,1,128]{2,1,0:T(1,128)S(1)} async-done(((f32[8,1,128]{2,1,0:T(1,128)}), f32[8,1,128]{2,1,0:T(1,128)S(1)}, u32[]{:S(2)}, u32[]{:S(2)}) %all-to-all-start) | async-done | bytes 4128 | tf_op jit(solution)/shard_map/all_to_all | solution.py:30
  16.5 0.8 convert_bitcast_fusion.1
  17.2 2.8 %fusion.41 = f32[64,1,2,128]{3,1,2,0:T(1,128)S(1)} fusion(bf16[64,2,128,128]{3,2,1,0:T(8,128)(2,1)} %param.7, bf16[64,128,1,1]{1,0,2,3:T(8,128)(2,1)S(1)} %convert_bitcast_fusion.1), kind=kOutput, calls=%fused_computation.80 | convolution fusion | flops 4194304 | bytes 4276224 | tf_op jit(solution)/shard_map/tsrb,tr->tsb/dot_general | solution.py:98
  20.7 1.5 %collective-permute-done = f32[2,256,128]{2,1,0:T(8,128)S(1)} collective-permute-done((f32[2,256,128]{2,1,0:T(8,128)S(1)}, f32[2,256,128]{2,1,0:T(8,128)S(1)}, u32[]{:S(2)}, u32[]{:S(2)}) %collective-permute-start) | collective-permute-done | bytes 262176 | tf_op jit(solution)/shard_map/ppermute | solution.py:52
  22.3 1.6 %collective-permute-start.1 = (f32[256,128]{1,0:T(8,128)S(1)}, f32[256,128]{1,0:T(8,128)S(1)}, u32[]{:S(2)}, u32[]{:S(2)}) collective-permute-start(f32[256,128]{1,0:T(8,128)S(1)} %dynamic-slice_bitcast_fusion.3), channel_id=1, source_target_pairs={{0,2},{1,3},{2,0},{3,1},{4,6},{5,7},{6,4},{7,5},{8,10},{9,11},{10,... | collective-permute-start | bytes 393224 | tf_op jit(solution)/shard_map/ppermute | solution.py:52
  23.8 4.0 %collective-permute-done.1 = f32[256,128]{1,0:T(8,128)S(1)} collective-permute-done((f32[256,128]{1,0:T(8,128)S(1)}, f32[256,128]{1,0:T(8,128)S(1)}, u32[]{:S(2)}, u32[]{:S(2)}) %collective-permute-start.1) | collective-permute-done | bytes 131104 | tf_op jit(solution)/shard_map/ppermute | solution.py:52
  27.9 0.6 collective-permute-start.2
  28.5 4.4 %collective-permute-done.2 = f32[256,128]{1,0:T(8,128)S(1)} collective-permute-done((f32[256,128]{1,0:T(8,128)S(1)}, f32[256,128]{1,0:T(8,128)S(1)}, u32[]{:S(2)}, u32[]{:S(2)}) %collective-permute-start.2) | collective-permute-done | bytes 131104 | tf_op jit(solution)/shard_map/ppermute | solution.py:19
  33.6 4.4 %collective-permute-done.3 = f32[256,128]{1,0:T(8,128)S(1)} collective-permute-done((f32[256,128]{1,0:T(8,128)S(1)}, f32[256,128]{1,0:T(8,128)S(1)}, u32[]{:S(2)}, u32[]{:S(2)}) %collective-permute-start.3) | collective-permute-done | bytes 131104 | tf_op jit(solution)/shard_map/ppermute | solution.py:19
  38.0 0.6 collective-permute-start.4
  38.6 6.7 %collective-permute-done.4 = f32[256,128]{1,0:T(8,128)S(1)} collective-permute-done((f32[256,128]{1,0:T(8,128)S(1)}, f32[256,128]{1,0:T(8,128)S(1)}, u32[]{:S(2)}, u32[]{:S(2)}) %collective-permute-start.4) | collective-permute-done | bytes 131104 | tf_op jit(solution)/shard_map/ppermute | solution.py:19
  45.4 1.6 %collective-permute-start.5 = (f32[256,128]{1,0:T(8,128)S(1)}, f32[256,128]{1,0:T(8,128)S(1)}, u32[]{:S(2)}, u32[]{:S(2)}) collective-permute-start(f32[256,128]{1,0:T(8,128)S(1)} %add.925), channel_id=1, source_target_pairs={{0,2},{1,3},{2,0},{3,1},{4,6},{5,7},{6,4},{7,5},{8,10},{9,11},{10,... | collective-permute-start | bytes 393224 | tf_op jit(solution)/shard_map/ppermute | solution.py:65
  47.0 3.4 %collective-permute-done.5 = f32[256,128]{1,0:T(8,128)S(1)} collective-permute-done((f32[256,128]{1,0:T(8,128)S(1)}, f32[256,128]{1,0:T(8,128)S(1)}, u32[]{:S(2)}, u32[]{:S(2)}) %collective-permute-start.5) | collective-permute-done | bytes 131104 | tf_op jit(solution)/shard_map/ppermute | solution.py:65
  50.7 1.4 %collective-permute-done.6 = f32[2,256,128]{2,1,0:T(8,128)S(1)} collective-permute-done((f32[2,256,128]{2,1,0:T(8,128)S(1)}, f32[2,256,128]{2,1,0:T(8,128)S(1)}, u32[]{:S(2)}, u32[]{:S(2)}) %collective-permute-start.6) | collective-permute-done | bytes 262176 | tf_op jit(solution)/shard_map/ppermute | solution.py:65
  52.0 0.7 multiply_reduce_fusion.1
  53.8 1.8 %fusion.2 = f32[16,1,128,1]{2,1,3,0:T(1,128)S(1)} fusion(bf16[64,2,128,128]{3,2,1,0:T(8,128)(2,1)} %param.7, bf16[16,2,128,1]{2,1,0,3:T(2,128)(2,1)S(1)} %bitcast.345), kind=kOutput, calls=%fused_computation.2 | convolution fusion | flops 1048576 | bytes 1064960 | tf_op jit(solution)/shard_map/tsrb,tsb->tr/dot_general | solution.py:141
  57.8 1.5 %collective-permute-start.14 = (f32[16,128]{1,0:T(8,128)S(1)}, f32[16,128]{1,0:T(8,128)S(1)}, u32[]{:S(2)}, u32[]{:S(2)}) collective-permute-start(f32[16,128]{1,0:T(8,128)S(1)} %add.932), channel_id=1, source_target_pairs={{0,2},{1,3},{2,0},{3,1},{4,6},{5,7},{6,4},{7,5},{8,10},{9,11},{10,... | collective-permute-start | bytes 24584 | tf_op jit(solution)/shard_map/ppermute | solution.py:19
  59.9 1.5 %collective-permute-start.10 = (f32[16,128]{1,0:T(8,128)S(1)}, f32[16,128]{1,0:T(8,128)S(1)}, u32[]{:S(2)}, u32[]{:S(2)}) collective-permute-start(f32[16,128]{1,0:T(8,128)S(1)} %add.928), channel_id=1, source_target_pairs={{0,2},{1,3},{2,0},{3,1},{4,6},{5,7},{6,4},{7,5},{8,10},{9,11},{10,... | collective-permute-start | bytes 24584 | tf_op jit(solution)/shard_map/ppermute | solution.py:19
  62.0 1.0 collective-permute-done.12
  63.6 1.4 %collective-permute-done.8 = f32[16,128]{1,0:T(8,128)S(1)} collective-permute-done((f32[16,128]{1,0:T(8,128)S(1)}, f32[16,128]{1,0:T(8,128)S(1)}, u32[]{:S(2)}, u32[]{:S(2)}) %collective-permute-start.8) | collective-permute-done | bytes 8224 | tf_op jit(solution)/shard_map/ppermute | solution.py:19
  65.2 9.4 %all_to_all.15 = f32[32,1,128]{2,1,0:T(1,128)S(1)} all-to-all(f32[32,1,128]{2,1,0:T(1,128)S(1)} %bitcast.322), channel_id=1, replica_groups=mesh['dp'=8,'region'=4] {'dp','region'}, dimensions={0} | all-to-all | bytes 32768 | tf_op jit(solution)/shard_map/all_to_all | solution.py:30
  74.6 0.6 fusion.89
  76.1 2.8 %fusion.39 = f32[64,1,2,128]{3,1,2,0:T(1,128)S(1)} fusion(bf16[64,2,128,128]{3,2,1,0:T(8,128)(2,1)} %param.7, bf16[64,128,1,1]{1,0,2,3:T(8,128)(2,1)S(1)} %get-tuple-element.5), kind=kOutput, calls=%fused_computation.78 | convolution fusion | flops 4194304 | bytes 4276224 | tf_op jit(solution)/shard_map/tsrb,tr->tsb/dot_general | solution.py:98
  79.5 1.5 %collective-permute-done.15 = f32[2,256,128]{2,1,0:T(8,128)S(1)} collective-permute-done((f32[2,256,128]{2,1,0:T(8,128)S(1)}, f32[2,256,128]{2,1,0:T(8,128)S(1)}, u32[]{:S(2)}, u32[]{:S(2)}) %collective-permute-start.15) | collective-permute-done | bytes 262176 | tf_op jit(solution)/shard_map/ppermute | solution.py:52
  81.7 5.0 %collective-permute-done.16 = f32[256,128]{1,0:T(8,128)S(1)} collective-permute-done((f32[256,128]{1,0:T(8,128)S(1)}, f32[256,128]{1,0:T(8,128)S(1)}, u32[]{:S(2)}, u32[]{:S(2)}) %collective-permute-start.16) | collective-permute-done | bytes 131104 | tf_op jit(solution)/shard_map/ppermute | solution.py:52
  87.3 4.4 %collective-permute-done.17 = f32[256,128]{1,0:T(8,128)S(1)} collective-permute-done((f32[256,128]{1,0:T(8,128)S(1)}, f32[256,128]{1,0:T(8,128)S(1)}, u32[]{:S(2)}, u32[]{:S(2)}) %collective-permute-start.17) | collective-permute-done | bytes 131104 | tf_op jit(solution)/shard_map/ppermute | solution.py:19
  91.8 0.6 collective-permute-start.18
  92.4 4.4 %collective-permute-done.18 = f32[256,128]{1,0:T(8,128)S(1)} collective-permute-done((f32[256,128]{1,0:T(8,128)S(1)}, f32[256,128]{1,0:T(8,128)S(1)}, u32[]{:S(2)}, u32[]{:S(2)}) %collective-permute-start.18) | collective-permute-done | bytes 131104 | tf_op jit(solution)/shard_map/ppermute | solution.py:19
  96.8 0.7 collective-permute-start.19
  97.5 6.7 %collective-permute-done.19 = f32[256,128]{1,0:T(8,128)S(1)} collective-permute-done((f32[256,128]{1,0:T(8,128)S(1)}, f32[256,128]{1,0:T(8,128)S(1)}, u32[]{:S(2)}, u32[]{:S(2)}) %collective-permute-start.19) | collective-permute-done | bytes 131104 | tf_op jit(solution)/shard_map/ppermute | solution.py:19
  104.8 4.4 %collective-permute-done.20 = f32[256,128]{1,0:T(8,128)S(1)} collective-permute-done((f32[256,128]{1,0:T(8,128)S(1)}, f32[256,128]{1,0:T(8,128)S(1)}, u32[]{:S(2)}, u32[]{:S(2)}) %collective-permute-start.20) | collective-permute-done | bytes 131104 | tf_op jit(solution)/shard_map/ppermute | solution.py:65
  109.4 1.5 %collective-permute-done.21 = f32[2,256,128]{2,1,0:T(8,128)S(1)} collective-permute-done((f32[2,256,128]{2,1,0:T(8,128)S(1)}, f32[2,256,128]{2,1,0:T(8,128)S(1)}, u32[]{:S(2)}, u32[]{:S(2)}) %collective-permute-start.21) | collective-permute-done | bytes 262176 | tf_op jit(solution)/shard_map/ppermute | solution.py:65
  110.8 0.7 multiply_reduce_fusion
  112.6 1.8 %fusion.12 = f32[16,1,128,1]{2,1,3,0:T(1,128)S(1)} fusion(bf16[64,2,128,128]{3,2,1,0:T(8,128)(2,1)} %param.7, bf16[16,2,128,1]{2,1,0,3:T(2,128)(2,1)S(1)} %bitcast.346), kind=kOutput, calls=%fused_computation.12 | convolution fusion | flops 1048576 | bytes 1064960 | tf_op jit(solution)/shard_map/tsrb,tsb->tr/dot_general | solution.py:141
  114.5 1.6 %fusion.8 = f32[16,1,128,1]{2,1,3,0:T(1,128)S(1)} fusion(bf16[64,2,128,128]{3,2,1,0:T(8,128)(2,1)} %param.7, bf16[16,2,128,1]{2,1,0,3:T(2,128)(2,1)S(1)} %bitcast.344), kind=kOutput, calls=%fused_computation.8 | convolution fusion | flops 1048576 | bytes 1064960 | tf_op jit(solution)/shard_map/tsrb,tsb->tr/dot_general | solution.py:141
  118.3 1.5 %collective-permute-start.25 = (f32[16,128]{1,0:T(8,128)S(1)}, f32[16,128]{1,0:T(8,128)S(1)}, u32[]{:S(2)}, u32[]{:S(2)}) collective-permute-start(f32[16,128]{1,0:T(8,128)S(1)} %add.976), channel_id=1, source_target_pairs={{0,2},{1,3},{2,0},{3,1},{4,6},{5,7},{6,4},{7,5},{8,10},{9,11},{10,... | collective-permute-start | bytes 24584 | tf_op jit(solution)/shard_map/ppermute | solution.py:19
  120.4 1.5 %collective-permute-start.29 = (f32[16,128]{1,0:T(8,128)S(1)}, f32[16,128]{1,0:T(8,128)S(1)}, u32[]{:S(2)}, u32[]{:S(2)}) collective-permute-start(f32[16,128]{1,0:T(8,128)S(1)} %add.980), channel_id=1, source_target_pairs={{0,2},{1,3},{2,0},{3,1},{4,6},{5,7},{6,4},{7,5},{8,10},{9,11},{10,... | collective-permute-start | bytes 24584 | tf_op jit(solution)/shard_map/ppermute | solution.py:19
  122.0 1.5 %collective-permute-done.27 = f32[16,128]{1,0:T(8,128)S(1)} collective-permute-done((f32[16,128]{1,0:T(8,128)S(1)}, f32[16,128]{1,0:T(8,128)S(1)}, u32[]{:S(2)}, u32[]{:S(2)}) %collective-permute-start.27) | collective-permute-done | bytes 8224 | tf_op jit(solution)/shard_map/ppermute | solution.py:19
  124.1 0.8 fusion.51
  124.8 2.5 %all-to-all-start.2 = ((f32[32,1,128]{2,1,0:T(1,128)}), f32[32,1,128]{2,1,0:T(1,128)S(1)}, u32[]{:S(2)}, u32[]{:S(2)}) async-start(f32[32,1,128]{2,1,0:T(1,128)} %bitcast.95), calls=%async_computation.2 | async-start | bytes 32768 | tf_op jit(solution)/shard_map/all_to_all | solution.py:30
  127.6 6.9 %all-to-all-done.2 = f32[32,1,128]{2,1,0:T(1,128)S(1)} async-done(((f32[32,1,128]{2,1,0:T(1,128)}), f32[32,1,128]{2,1,0:T(1,128)S(1)}, u32[]{:S(2)}, u32[]{:S(2)}) %all-to-all-start.2) | async-done | bytes 16416 | tf_op jit(solution)/shard_map/all_to_all | solution.py:30
  134.4 0.6 fusion.72
  135.9 0.7 multiply_add_fusion
  (110 shorter events, 14.0 us)
Async XLA Ops:
  1.5 13.7 %all-to-all-start = ((f32[8,1,128]{2,1,0:T(1,128)}), f32[8,1,128]{2,1,0:T(1,128)S(1)}, u32[]{:S(2)}, u32[]{:S(2)}) async-start(f32[8,1,128]{2,1,0:T(1,128)} %bitcast.3), calls=%async_computation | async-start | bytes 8192 | tf_op jit(solution)/shard_map/all_to_all | solution.py:30
  20.6 1.6 %collective-permute-start = (f32[2,256,128]{2,1,0:T(8,128)S(1)}, f32[2,256,128]{2,1,0:T(8,128)S(1)}, u32[]{:S(2)}, u32[]{:S(2)}) collective-permute-start(f32[2,256,128]{2,1,0:T(8,128)S(1)} %dynamic-slice_bitcast_fusion.1), channel_id=1, source_target_pairs={{0,1},{1,0},{2,3},{3,2},{4,5},{5,4},{6,7},{7,6},{8,9},{9,8},{10,11... | collective-permute-start | bytes 786440 | tf_op jit(solution)/shard_map/ppermute | solution.py:52
  22.3 5.6 %collective-permute-start.1 = (f32[256,128]{1,0:T(8,128)S(1)}, f32[256,128]{1,0:T(8,128)S(1)}, u32[]{:S(2)}, u32[]{:S(2)}) collective-permute-start(f32[256,128]{1,0:T(8,128)S(1)} %dynamic-slice_bitcast_fusion.3), channel_id=1, source_target_pairs={{0,2},{1,3},{2,0},{3,1},{4,6},{5,7},{6,4},{7,5},{8,10},{9,11},{10,... | collective-permute-start | bytes 393224 | tf_op jit(solution)/shard_map/ppermute | solution.py:52
  27.9 5.0 %collective-permute-start.2 = (f32[256,128]{1,0:T(8,128)S(1)}, f32[256,128]{1,0:T(8,128)S(1)}, u32[]{:S(2)}, u32[]{:S(2)}) collective-permute-start(f32[256,128]{1,0:T(8,128)S(1)} %bitcast_add_fusion.3), channel_id=1, source_target_pairs={{0,4},{4,0},{8,12},{12,8},{16,20},{20,16},{24,28},{28,24},{1,5},{5... | collective-permute-start | bytes 393224 | tf_op jit(solution)/shard_map/ppermute | solution.py:19
  33.0 5.0 %collective-permute-start.3 = (f32[256,128]{1,0:T(8,128)S(1)}, f32[256,128]{1,0:T(8,128)S(1)}, u32[]{:S(2)}, u32[]{:S(2)}) collective-permute-start(f32[256,128]{1,0:T(8,128)S(1)} %add.923), channel_id=1, source_target_pairs={{0,8},{4,12},{8,0},{12,4},{16,24},{20,28},{24,16},{28,20},{1,9},{5... | collective-permute-start | bytes 393224 | tf_op jit(solution)/shard_map/ppermute | solution.py:19
  38.0 7.3 %collective-permute-start.4 = (f32[256,128]{1,0:T(8,128)S(1)}, f32[256,128]{1,0:T(8,128)S(1)}, u32[]{:S(2)}, u32[]{:S(2)}) collective-permute-start(f32[256,128]{1,0:T(8,128)S(1)} %add.924), channel_id=1, source_target_pairs={{0,16},{4,20},{8,24},{12,28},{16,0},{20,4},{24,8},{28,12},{1,17},{... | collective-permute-start | bytes 393224 | tf_op jit(solution)/shard_map/ppermute | solution.py:19
  45.4 5.0 %collective-permute-start.5 = (f32[256,128]{1,0:T(8,128)S(1)}, f32[256,128]{1,0:T(8,128)S(1)}, u32[]{:S(2)}, u32[]{:S(2)}) collective-permute-start(f32[256,128]{1,0:T(8,128)S(1)} %add.925), channel_id=1, source_target_pairs={{0,2},{1,3},{2,0},{3,1},{4,6},{5,7},{6,4},{7,5},{8,10},{9,11},{10,... | collective-permute-start | bytes 393224 | tf_op jit(solution)/shard_map/ppermute | solution.py:65
  50.4 1.6 %collective-permute-start.6 = (f32[2,256,128]{2,1,0:T(8,128)S(1)}, f32[2,256,128]{2,1,0:T(8,128)S(1)}, u32[]{:S(2)}, u32[]{:S(2)}) collective-permute-start(f32[2,256,128]{2,1,0:T(8,128)S(1)} %maximum_select_fusion.2), channel_id=1, source_target_pairs={{0,1},{1,0},{2,3},{3,2},{4,5},{5,4},{6,7},{7,6},{8,9},{9,8},{10,11... | collective-permute-start | bytes 786440 | tf_op jit(solution)/shard_map/ppermute | solution.py:65
  50.6 11.3 %copy-start.3 = (f32[32,128]{1,0:T(8,128)S(1)}, f32[32,128]{1,0:T(8,128)}, u32[]{:S(2)}) copy-start(f32[32,128]{1,0:T(8,128)} %param.10) | copy-start | bytes 49156
  50.6 14.4 %copy-start.2 = (f32[64,128]{1,0:T(8,128)S(1)}, f32[64,128]{1,0:T(8,128)}, u32[]{:S(2)}) copy-start(f32[64,128]{1,0:T(8,128)} %param.6) | copy-start | bytes 98308
  53.5 2.5 %copy-start = (bf16[64,2,128,128]{3,2,1,0:T(8,128)(2,1)S(1)}, bf16[64,2,128,128]{3,2,1,0:T(8,128)(2,1)}, u32[]{:S(2)}) copy-start(bf16[64,2,128,128]{3,2,1,0:T(8,128)(2,1)} %param.7) | copy-start | bytes 12582916
  55.6 2.2 %collective-permute-start.13 = (f32[16,128]{1,0:T(8,128)S(1)}, f32[16,128]{1,0:T(8,128)S(1)}, u32[]{:S(2)}, u32[]{:S(2)}) collective-permute-start(f32[16,128]{1,0:T(8,128)S(1)} %bitcast.329), channel_id=1, source_target_pairs={{0,1},{1,0},{2,3},{3,2},{4,5},{5,4},{6,7},{7,6},{8,9},{9,8},{10,11... | collective-permute-start | bytes 24584 | tf_op jit(solution)/shard_map/ppermute | solution.py:19
  56.3 3.0 %collective-permute-start.11 = (f32[16,128]{1,0:T(8,128)S(1)}, f32[16,128]{1,0:T(8,128)S(1)}, u32[]{:S(2)}, u32[]{:S(2)}) collective-permute-start(f32[16,128]{1,0:T(8,128)S(1)} %bitcast.327), channel_id=1, source_target_pairs={{0,1},{1,0},{2,3},{3,2},{4,5},{5,4},{6,7},{7,6},{8,9},{9,8},{10,11... | collective-permute-start | bytes 24584 | tf_op jit(solution)/shard_map/ppermute | solution.py:19
  56.9 3.0 %collective-permute-start.9 = (f32[16,128]{1,0:T(8,128)S(1)}, f32[16,128]{1,0:T(8,128)S(1)}, u32[]{:S(2)}, u32[]{:S(2)}) collective-permute-start(f32[16,128]{1,0:T(8,128)S(1)} %bitcast.325), channel_id=1, source_target_pairs={{0,1},{1,0},{2,3},{3,2},{4,5},{5,4},{6,7},{7,6},{8,9},{9,8},{10,11... | collective-permute-start | bytes 24584 | tf_op jit(solution)/shard_map/ppermute | solution.py:19
  57.6 3.7 %collective-permute-start.7 = (f32[16,128]{1,0:T(8,128)S(1)}, f32[16,128]{1,0:T(8,128)S(1)}, u32[]{:S(2)}, u32[]{:S(2)}) collective-permute-start(f32[16,128]{1,0:T(8,128)S(1)} %bitcast.323), channel_id=1, source_target_pairs={{0,1},{1,0},{2,3},{3,2},{4,5},{5,4},{6,7},{7,6},{8,9},{9,8},{10,11... | collective-permute-start | bytes 24584 | tf_op jit(solution)/shard_map/ppermute | solution.py:19
  57.8 4.2 %collective-permute-start.14 = (f32[16,128]{1,0:T(8,128)S(1)}, f32[16,128]{1,0:T(8,128)S(1)}, u32[]{:S(2)}, u32[]{:S(2)}) collective-permute-start(f32[16,128]{1,0:T(8,128)S(1)} %add.932), channel_id=1, source_target_pairs={{0,2},{1,3},{2,0},{3,1},{4,6},{5,7},{6,4},{7,5},{8,10},{9,11},{10,... | collective-permute-start | bytes 24584 | tf_op jit(solution)/shard_map/ppermute | solution.py:19
  59.3 3.7 %collective-permute-start.12 = (f32[16,128]{1,0:T(8,128)S(1)}, f32[16,128]{1,0:T(8,128)S(1)}, u32[]{:S(2)}, u32[]{:S(2)}) collective-permute-start(f32[16,128]{1,0:T(8,128)S(1)} %add.930), channel_id=1, source_target_pairs={{0,2},{1,3},{2,0},{3,1},{4,6},{5,7},{6,4},{7,5},{8,10},{9,11},{10,... | collective-permute-start | bytes 24584 | tf_op jit(solution)/shard_map/ppermute | solution.py:19
  59.9 3.7 %collective-permute-start.10 = (f32[16,128]{1,0:T(8,128)S(1)}, f32[16,128]{1,0:T(8,128)S(1)}, u32[]{:S(2)}, u32[]{:S(2)}) collective-permute-start(f32[16,128]{1,0:T(8,128)S(1)} %add.928), channel_id=1, source_target_pairs={{0,2},{1,3},{2,0},{3,1},{4,6},{5,7},{6,4},{7,5},{8,10},{9,11},{10,... | collective-permute-start | bytes 24584 | tf_op jit(solution)/shard_map/ppermute | solution.py:19
  61.4 3.7 %collective-permute-start.8 = (f32[16,128]{1,0:T(8,128)S(1)}, f32[16,128]{1,0:T(8,128)S(1)}, u32[]{:S(2)}, u32[]{:S(2)}) collective-permute-start(f32[16,128]{1,0:T(8,128)S(1)} %add.926), channel_id=1, source_target_pairs={{0,2},{1,3},{2,0},{3,1},{4,6},{5,7},{6,4},{7,5},{8,10},{9,11},{10,... | collective-permute-start | bytes 24584 | tf_op jit(solution)/shard_map/ppermute | solution.py:19
  79.4 1.6 %collective-permute-start.15 = (f32[2,256,128]{2,1,0:T(8,128)S(1)}, f32[2,256,128]{2,1,0:T(8,128)S(1)}, u32[]{:S(2)}, u32[]{:S(2)}) collective-permute-start(f32[2,256,128]{2,1,0:T(8,128)S(1)} %dynamic-slice_bitcast_fusion), channel_id=1, source_target_pairs={{0,1},{1,0},{2,3},{3,2},{4,5},{5,4},{6,7},{7,6},{8,9},{9,8},{10,11... | collective-permute-start | bytes 786440 | tf_op jit(solution)/shard_map/ppermute | solution.py:52
  81.1 5.6 %collective-permute-start.16 = (f32[256,128]{1,0:T(8,128)S(1)}, f32[256,128]{1,0:T(8,128)S(1)}, u32[]{:S(2)}, u32[]{:S(2)}) collective-permute-start(f32[256,128]{1,0:T(8,128)S(1)} %dynamic-slice_bitcast_fusion.2), channel_id=1, source_target_pairs={{0,2},{1,3},{2,0},{3,1},{4,6},{5,7},{6,4},{7,5},{8,10},{9,11},{10,... | collective-permute-start | bytes 393224 | tf_op jit(solution)/shard_map/ppermute | solution.py:52
  86.7 5.0 %collective-permute-start.17 = (f32[256,128]{1,0:T(8,128)S(1)}, f32[256,128]{1,0:T(8,128)S(1)}, u32[]{:S(2)}, u32[]{:S(2)}) collective-permute-start(f32[256,128]{1,0:T(8,128)S(1)} %bitcast_add_fusion.2), channel_id=1, source_target_pairs={{0,4},{4,0},{8,12},{12,8},{16,20},{20,16},{24,28},{28,24},{1,5},{5... | collective-permute-start | bytes 393224 | tf_op jit(solution)/shard_map/ppermute | solution.py:19
  91.8 5.0 %collective-permute-start.18 = (f32[256,128]{1,0:T(8,128)S(1)}, f32[256,128]{1,0:T(8,128)S(1)}, u32[]{:S(2)}, u32[]{:S(2)}) collective-permute-start(f32[256,128]{1,0:T(8,128)S(1)} %add.971), channel_id=1, source_target_pairs={{0,8},{4,12},{8,0},{12,4},{16,24},{20,28},{24,16},{28,20},{1,9},{5... | collective-permute-start | bytes 393224 | tf_op jit(solution)/shard_map/ppermute | solution.py:19
  96.8 7.3 %collective-permute-start.19 = (f32[256,128]{1,0:T(8,128)S(1)}, f32[256,128]{1,0:T(8,128)S(1)}, u32[]{:S(2)}, u32[]{:S(2)}) collective-permute-start(f32[256,128]{1,0:T(8,128)S(1)} %add.972), channel_id=1, source_target_pairs={{0,16},{4,20},{8,24},{12,28},{16,0},{20,4},{24,8},{28,12},{1,17},{... | collective-permute-start | bytes 393224 | tf_op jit(solution)/shard_map/ppermute | solution.py:19
  104.2 5.0 %collective-permute-start.20 = (f32[256,128]{1,0:T(8,128)S(1)}, f32[256,128]{1,0:T(8,128)S(1)}, u32[]{:S(2)}, u32[]{:S(2)}) collective-permute-start(f32[256,128]{1,0:T(8,128)S(1)} %multiply_subtract_fusion), channel_id=1, source_target_pairs={{0,2},{1,3},{2,0},{3,1},{4,6},{5,7},{6,4},{7,5},{8,10},{9,11},{10,... | collective-permute-start | bytes 393224 | tf_op jit(solution)/shard_map/ppermute | solution.py:65
  109.2 1.6 %collective-permute-start.21 = (f32[2,256,128]{2,1,0:T(8,128)S(1)}, f32[2,256,128]{2,1,0:T(8,128)S(1)}, u32[]{:S(2)}, u32[]{:S(2)}) collective-permute-start(f32[2,256,128]{2,1,0:T(8,128)S(1)} %maximum_select_fusion.4), channel_id=1, source_target_pairs={{0,1},{1,0},{2,3},{3,2},{4,5},{5,4},{6,7},{7,6},{8,9},{9,8},{10,11... | collective-permute-start | bytes 786440 | tf_op jit(solution)/shard_map/ppermute | solution.py:65
  112.3 4.2 %copy-start.1 = (bf16[64,2,128,128]{3,2,1,0:T(8,128)(2,1)S(1)}, bf16[64,2,128,128]{3,2,1,0:T(8,128)(2,1)}, u32[]{:S(2)}) copy-start(bf16[64,2,128,128]{3,2,1,0:T(8,128)(2,1)} %param.7) | copy-start | bytes 12582916
  114.4 3.4 %collective-permute-start.22 = (f32[16,128]{1,0:T(8,128)S(1)}, f32[16,128]{1,0:T(8,128)S(1)}, u32[]{:S(2)}, u32[]{:S(2)}) collective-permute-start(f32[16,128]{1,0:T(8,128)S(1)} %bitcast.337), channel_id=1, source_target_pairs={{0,1},{1,0},{2,3},{3,2},{4,5},{5,4},{6,7},{7,6},{8,9},{9,8},{10,11... | collective-permute-start | bytes 24584 | tf_op jit(solution)/shard_map/ppermute | solution.py:19
  116.1 2.2 %collective-permute-start.24 = (f32[16,128]{1,0:T(8,128)S(1)}, f32[16,128]{1,0:T(8,128)S(1)}, u32[]{:S(2)}, u32[]{:S(2)}) collective-permute-start(f32[16,128]{1,0:T(8,128)S(1)} %bitcast.335), channel_id=1, source_target_pairs={{0,1},{1,0},{2,3},{3,2},{4,5},{5,4},{6,7},{7,6},{8,9},{9,8},{10,11... | collective-permute-start | bytes 24584 | tf_op jit(solution)/shard_map/ppermute | solution.py:19
  116.9 3.0 %collective-permute-start.26 = (f32[16,128]{1,0:T(8,128)S(1)}, f32[16,128]{1,0:T(8,128)S(1)}, u32[]{:S(2)}, u32[]{:S(2)}) collective-permute-start(f32[16,128]{1,0:T(8,128)S(1)} %bitcast.333), channel_id=1, source_target_pairs={{0,1},{1,0},{2,3},{3,2},{4,5},{5,4},{6,7},{7,6},{8,9},{9,8},{10,11... | collective-permute-start | bytes 24584 | tf_op jit(solution)/shard_map/ppermute | solution.py:19
  117.4 3.0 %collective-permute-start.28 = (f32[16,128]{1,0:T(8,128)S(1)}, f32[16,128]{1,0:T(8,128)S(1)}, u32[]{:S(2)}, u32[]{:S(2)}) collective-permute-start(f32[16,128]{1,0:T(8,128)S(1)} %bitcast.331), channel_id=1, source_target_pairs={{0,1},{1,0},{2,3},{3,2},{4,5},{5,4},{6,7},{7,6},{8,9},{9,8},{10,11... | collective-permute-start | bytes 24584 | tf_op jit(solution)/shard_map/ppermute | solution.py:19
  117.8 4.2 %collective-permute-start.23 = (f32[16,128]{1,0:T(8,128)S(1)}, f32[16,128]{1,0:T(8,128)S(1)}, u32[]{:S(2)}, u32[]{:S(2)}) collective-permute-start(f32[16,128]{1,0:T(8,128)S(1)} %add.974), channel_id=1, source_target_pairs={{0,2},{1,3},{2,0},{3,1},{4,6},{5,7},{6,4},{7,5},{8,10},{9,11},{10,... | collective-permute-start | bytes 24584 | tf_op jit(solution)/shard_map/ppermute | solution.py:19
  118.3 3.7 %collective-permute-start.25 = (f32[16,128]{1,0:T(8,128)S(1)}, f32[16,128]{1,0:T(8,128)S(1)}, u32[]{:S(2)}, u32[]{:S(2)}) collective-permute-start(f32[16,128]{1,0:T(8,128)S(1)} %add.976), channel_id=1, source_target_pairs={{0,2},{1,3},{2,0},{3,1},{4,6},{5,7},{6,4},{7,5},{8,10},{9,11},{10,... | collective-permute-start | bytes 24584 | tf_op jit(solution)/shard_map/ppermute | solution.py:19
  119.9 3.7 %collective-permute-start.27 = (f32[16,128]{1,0:T(8,128)S(1)}, f32[16,128]{1,0:T(8,128)S(1)}, u32[]{:S(2)}, u32[]{:S(2)}) collective-permute-start(f32[16,128]{1,0:T(8,128)S(1)} %add.978), channel_id=1, source_target_pairs={{0,2},{1,3},{2,0},{3,1},{4,6},{5,7},{6,4},{7,5},{8,10},{9,11},{10,... | collective-permute-start | bytes 24584 | tf_op jit(solution)/shard_map/ppermute | solution.py:19
  120.4 3.7 %collective-permute-start.29 = (f32[16,128]{1,0:T(8,128)S(1)}, f32[16,128]{1,0:T(8,128)S(1)}, u32[]{:S(2)}, u32[]{:S(2)}) collective-permute-start(f32[16,128]{1,0:T(8,128)S(1)} %add.980), channel_id=1, source_target_pairs={{0,2},{1,3},{2,0},{3,1},{4,6},{5,7},{6,4},{7,5},{8,10},{9,11},{10,... | collective-permute-start | bytes 24584 | tf_op jit(solution)/shard_map/ppermute | solution.py:19
  124.8 9.6 %all-to-all-start.2 = ((f32[32,1,128]{2,1,0:T(1,128)}), f32[32,1,128]{2,1,0:T(1,128)S(1)}, u32[]{:S(2)}, u32[]{:S(2)}) async-start(f32[32,1,128]{2,1,0:T(1,128)} %bitcast.95), calls=%async_computation.2 | async-start | bytes 32768 | tf_op jit(solution)/shard_map/all_to_all | solution.py:30

commit v15 on v12

--- a/solution.py
+++ b/solution.py
@@ -24,8 +24,14 @@
 def square_sum(rows, axis):
     n = lax.psum(1, axis)
     squares = rows * rows
+    high = lax.reduce_precision(squares, exponent_bits=8, mantissa_bits=7)
+    rest = squares - high
+    middle = lax.reduce_precision(rest, exponent_bits=8, mantissa_bits=7)
+    parts = jnp.concatenate(
+        [high.astype(jnp.bfloat16), middle.astype(jnp.bfloat16), (rest - middle).astype(jnp.bfloat16)], 0
+    )
     spread = jnp.dot(
-        jnp.ones((n, squares.shape[0]), jnp.float32), squares, precision=lax.Precision.HIGHEST
+        jnp.ones((n, parts.shape[0]), jnp.bfloat16), parts, preferred_element_type=jnp.float32
     )
     got = lax.all_to_all(spread[:, None, :], axis, 0, 0, tiled=False)
     total = got[0]

time: 132 us -> 132 us (level)
  no operation moved by 1% of the time
where the time goes in v15:
time: 132 us; the launch traced here: 131 us
  waiting for transfers between devices  68.8 us (52%)
  starting transfers between devices  23.5 us (18%)
  matrix products  14.8 us (11%)
  blocking collectives  9.58 us (7%)
  other arithmetic  7.92 us (6%)
  between operations  4.89 us (4%)
  local copies, waits for them, and re-layouts  1.83 us (1%)
    ppermute x14, waiting for transfers between devices, butterfly_sum(): x = x + lax.ppermute(x, axis, [(i, i ^ k) for i in range(n)])  36.6 us
    ppermute x4, waiting for transfers between devices, halving_scatter(): x = keep + lax.ppermute(send, axis, [(i, i ^ k) for i in range(n)])  12.1 us
    ppermute x4, waiting for transfers between devices, doubling_gather(): other = lax.ppermute(x, axis, [(i, i ^ k) for i in range(n)])  10.7 us
    all_to_all x2, starting transfers between devices, square_sum(): got = lax.all_to_all(spread[:, None, :], axis, 0, 0, tiled=False)  9.82 us
    all_to_all x1, blocking collectives, square_sum(): got = lax.all_to_all(spread[:, None, :], axis, 0, 0, tiled=False)  9.58 us
    all_to_all x2, waiting for transfers between devices, square_sum(): got = lax.all_to_all(spread[:, None, :], axis, 0, 0, tiled=False)  9.46 us
    ppermute x14, starting transfers between devices, butterfly_sum(): x = x + lax.ppermute(x, axis, [(i, i ^ k) for i in range(n)])  9.07 us
    dot_general x4, matrix products, local(): jnp.einsum('tsrb,tsb->tr', sensitivity[lo:lo + half_tiles], picked[lo:lo...  6.09 us
  transfers between devices with their start and end apart: 24, of which 21 were waited for; matrix products, arithmetic and copies ran while one was open for 4% of the time, Pallas kernels for 0%

profile of v15, /device:TPU:0, one launch (start us, length us, event | category | flops | bytes accessed | tf_op | source)
XLA Modules:
  0.0 131.3 jit_solution(15786963186924914099)
XLA Ops:
  0.0 0.8 reduce-precision_convert_fusion.5
  0.8 0.7 fusion.31
  1.5 7.3 %all-to-all-start = ((f32[8,1,128]{2,1,0:T(1,128)}), f32[8,1,128]{2,1,0:T(1,128)S(1)}, u32[]{:S(2)}, u32[]{:S(2)}) async-start(f32[8,1,128]{2,1,0:T(1,128)} %bitcast.3), calls=%async_computation | async-start | bytes 8192 | tf_op jit(solution)/shard_map/all_to_all | solution.py:36
  8.8 0.8 copy.14
  9.8 0.8 slice_bitcast_fusion.31
  11.8 0.8 multiply_multiply_fusion.1
  12.6 2.6 %all-to-all-done = f32[8,1,128]{2,1,0:T(1,128)S(1)} async-done(((f32[8,1,128]{2,1,0:T(1,128)}), f32[8,1,128]{2,1,0:T(1,128)S(1)}, u32[]{:S(2)}, u32[]{:S(2)}) %all-to-all-start) | async-done | bytes 4128 | tf_op jit(solution)/shard_map/all_to_all | solution.py:36
  16.5 0.8 convert_bitcast_fusion.1
  17.2 2.8 %fusion.56 = f32[64,1,2,128]{3,1,2,0:T(1,128)S(1)} fusion(bf16[64,2,128,128]{3,2,1,0:T(8,128)(2,1)} %param.7, bf16[64,128,1,1]{1,0,2,3:T(8,128)(2,1)S(1)} %convert_bitcast_fusion.1), kind=kOutput, calls=%fused_computation.105 | convolution fusion | flops 4194304 | bytes 4276224 | tf_op jit(solution)/shard_map/tsrb,tr->tsb/dot_general | solution.py:104
  20.8 1.5 %collective-permute-done = f32[2,256,128]{2,1,0:T(8,128)S(1)} collective-permute-done((f32[2,256,128]{2,1,0:T(8,128)S(1)}, f32[2,256,128]{2,1,0:T(8,128)S(1)}, u32[]{:S(2)}, u32[]{:S(2)}) %collective-permute-start) | collective-permute-done | bytes 262176 | tf_op jit(solution)/shard_map/ppermute | solution.py:58
  22.3 1.6 %collective-permute-start.1 = (f32[256,128]{1,0:T(8,128)S(1)}, f32[256,128]{1,0:T(8,128)S(1)}, u32[]{:S(2)}, u32[]{:S(2)}) collective-permute-start(f32[256,128]{1,0:T(8,128)S(1)} %dynamic-slice_bitcast_fusion.3), channel_id=1, source_target_pairs={{0,2},{1,3},{2,0},{3,1},{4,6},{5,7},{6,4},{7,5},{8,10},{9,11},{10,... | collective-permute-start | bytes 393224 | tf_op jit(solution)/shard_map/ppermute | solution.py:58
  23.8 4.0 %collective-permute-done.1 = f32[256,128]{1,0:T(8,128)S(1)} collective-permute-done((f32[256,128]{1,0:T(8,128)S(1)}, f32[256,128]{1,0:T(8,128)S(1)}, u32[]{:S(2)}, u32[]{:S(2)}) %collective-permute-start.1) | collective-permute-done | bytes 131104 | tf_op jit(solution)/shard_map/ppermute | solution.py:58
  28.5 4.4 %collective-permute-done.2 = f32[256,128]{1,0:T(8,128)S(1)} collective-permute-done((f32[256,128]{1,0:T(8,128)S(1)}, f32[256,128]{1,0:T(8,128)S(1)}, u32[]{:S(2)}, u32[]{:S(2)}) %collective-permute-start.2) | collective-permute-done | bytes 131104 | tf_op jit(solution)/shard_map/ppermute | solution.py:19
  33.6 4.4 %collective-permute-done.3 = f32[256,128]{1,0:T(8,128)S(1)} collective-permute-done((f32[256,128]{1,0:T(8,128)S(1)}, f32[256,128]{1,0:T(8,128)S(1)}, u32[]{:S(2)}, u32[]{:S(2)}) %collective-permute-start.3) | collective-permute-done | bytes 131104 | tf_op jit(solution)/shard_map/ppermute | solution.py:19
  38.6 6.7 %collective-permute-done.4 = f32[256,128]{1,0:T(8,128)S(1)} collective-permute-done((f32[256,128]{1,0:T(8,128)S(1)}, f32[256,128]{1,0:T(8,128)S(1)}, u32[]{:S(2)}, u32[]{:S(2)}) %collective-permute-start.4) | collective-permute-done | bytes 131104 | tf_op jit(solution)/shard_map/ppermute | solution.py:19
  45.4 1.6 %collective-permute-start.5 = (f32[256,128]{1,0:T(8,128)S(1)}, f32[256,128]{1,0:T(8,128)S(1)}, u32[]{:S(2)}, u32[]{:S(2)}) collective-permute-start(f32[256,128]{1,0:T(8,128)S(1)} %add.901), channel_id=1, source_target_pairs={{0,2},{1,3},{2,0},{3,1},{4,6},{5,7},{6,4},{7,5},{8,10},{9,11},{10,... | collective-permute-start | bytes 393224 | tf_op jit(solution)/shard_map/ppermute | solution.py:71
  47.0 3.4 %collective-permute-done.5 = f32[256,128]{1,0:T(8,128)S(1)} collective-permute-done((f32[256,128]{1,0:T(8,128)S(1)}, f32[256,128]{1,0:T(8,128)S(1)}, u32[]{:S(2)}, u32[]{:S(2)}) %collective-permute-start.5) | collective-permute-done | bytes 131104 | tf_op jit(solution)/shard_map/ppermute | solution.py:71
  50.7 1.4 %collective-permute-done.6 = f32[2,256,128]{2,1,0:T(8,128)S(1)} collective-permute-done((f32[2,256,128]{2,1,0:T(8,128)S(1)}, f32[2,256,128]{2,1,0:T(8,128)S(1)}, u32[]{:S(2)}, u32[]{:S(2)}) %collective-permute-start.6) | collective-permute-done | bytes 262176 | tf_op jit(solution)/shard_map/ppermute | solution.py:71
  52.0 0.7 multiply_reduce_fusion.1
  53.8 2.4 %fusion.2 = f32[32,1,128,1]{2,1,3,0:T(1,128)S(1)} fusion(bf16[64,2,128,128]{3,2,1,0:T(8,128)(2,1)} %param.7, bf16[32,2,128,1]{2,1,0,3:T(2,128)(2,1)S(1)} %bitcast.309), kind=kOutput, calls=%fused_computation.2 | convolution fusion | flops 2097152 | bytes 2129920 | tf_op jit(solution)/shard_map/tsrb,tsb->tr/dot_general | solution.py:147
  56.4 0.6 fusion.6
  57.5 1.5 %collective-permute-start.10 = (f32[32,128]{1,0:T(8,128)S(1)}, f32[32,128]{1,0:T(8,128)S(1)}, u32[]{:S(2)}, u32[]{:S(2)}) collective-permute-start(f32[32,128]{1,0:T(8,128)S(1)} %add.904), channel_id=1, source_target_pairs={{0,2},{1,3},{2,0},{3,1},{4,6},{5,7},{6,4},{7,5},{8,10},{9,11},{10,... | collective-permute-start | bytes 49160 | tf_op jit(solution)/shard_map/ppermute | solution.py:19
  59.0 0.8 collective-permute-start.8
  59.9 1.4 %collective-permute-done.10 = f32[32,128]{1,0:T(8,128)S(1)} collective-permute-done((f32[32,128]{1,0:T(8,128)S(1)}, f32[32,128]{1,0:T(8,128)S(1)}, u32[]{:S(2)}, u32[]{:S(2)}) %collective-permute-start.10) | collective-permute-done | bytes 16416 | tf_op jit(solution)/shard_map/ppermute | solution.py:19
  61.3 1.6 %collective-permute-done.8 = f32[32,128]{1,0:T(8,128)S(1)} collective-permute-done((f32[32,128]{1,0:T(8,128)S(1)}, f32[32,128]{1,0:T(8,128)S(1)}, u32[]{:S(2)}, u32[]{:S(2)}) %collective-permute-start.8) | collective-permute-done | bytes 16416 | tf_op jit(solution)/shard_map/ppermute | solution.py:19
  63.0 9.6 %all_to_all.15 = f32[32,1,128]{2,1,0:T(1,128)S(1)} all-to-all(f32[32,1,128]{2,1,0:T(1,128)S(1)} %bitcast.306), channel_id=1, replica_groups=mesh['dp'=8,'region'=4] {'dp','region'}, dimensions={0} | all-to-all | bytes 32768 | tf_op jit(solution)/shard_map/all_to_all | solution.py:36
  72.6 0.6 fusion.88
  74.0 2.8 %fusion.52 = f32[64,1,2,128]{3,1,2,0:T(1,128)S(1)} fusion(bf16[64,2,128,128]{3,2,1,0:T(8,128)(2,1)} %param.7, bf16[64,128,1,1]{1,0,2,3:T(8,128)(2,1)S(1)} %get-tuple-element.5), kind=kOutput, calls=%fused_computation.101 | convolution fusion | flops 4194304 | bytes 4276224 | tf_op jit(solution)/shard_map/tsrb,tr->tsb/dot_general | solution.py:104
  77.4 1.5 %collective-permute-done.11 = f32[2,256,128]{2,1,0:T(8,128)S(1)} collective-permute-done((f32[2,256,128]{2,1,0:T(8,128)S(1)}, f32[2,256,128]{2,1,0:T(8,128)S(1)}, u32[]{:S(2)}, u32[]{:S(2)}) %collective-permute-start.11) | collective-permute-done | bytes 262176 | tf_op jit(solution)/shard_map/ppermute | solution.py:58
  79.6 5.0 %collective-permute-done.12 = f32[256,128]{1,0:T(8,128)S(1)} collective-permute-done((f32[256,128]{1,0:T(8,128)S(1)}, f32[256,128]{1,0:T(8,128)S(1)}, u32[]{:S(2)}, u32[]{:S(2)}) %collective-permute-start.12) | collective-permute-done | bytes 131104 | tf_op jit(solution)/shard_map/ppermute | solution.py:58
  85.3 4.4 %collective-permute-done.13 = f32[256,128]{1,0:T(8,128)S(1)} collective-permute-done((f32[256,128]{1,0:T(8,128)S(1)}, f32[256,128]{1,0:T(8,128)S(1)}, u32[]{:S(2)}, u32[]{:S(2)}) %collective-permute-start.13) | collective-permute-done | bytes 131104 | tf_op jit(solution)/shard_map/ppermute | solution.py:19
  89.7 0.6 collective-permute-start.14
  90.3 4.4 %collective-permute-done.14 = f32[256,128]{1,0:T(8,128)S(1)} collective-permute-done((f32[256,128]{1,0:T(8,128)S(1)}, f32[256,128]{1,0:T(8,128)S(1)}, u32[]{:S(2)}, u32[]{:S(2)}) %collective-permute-start.14) | collective-permute-done | bytes 131104 | tf_op jit(solution)/shard_map/ppermute | solution.py:19
  94.8 0.7 collective-permute-start.15
  95.4 6.7 %collective-permute-done.15 = f32[256,128]{1,0:T(8,128)S(1)} collective-permute-done((f32[256,128]{1,0:T(8,128)S(1)}, f32[256,128]{1,0:T(8,128)S(1)}, u32[]{:S(2)}, u32[]{:S(2)}) %collective-permute-start.15) | collective-permute-done | bytes 131104 | tf_op jit(solution)/shard_map/ppermute | solution.py:19
  102.7 4.4 %collective-permute-done.16 = f32[256,128]{1,0:T(8,128)S(1)} collective-permute-done((f32[256,128]{1,0:T(8,128)S(1)}, f32[256,128]{1,0:T(8,128)S(1)}, u32[]{:S(2)}, u32[]{:S(2)}) %collective-permute-start.16) | collective-permute-done | bytes 131104 | tf_op jit(solution)/shard_map/ppermute | solution.py:71
  107.3 1.5 %collective-permute-done.17 = f32[2,256,128]{2,1,0:T(8,128)S(1)} collective-permute-done((f32[2,256,128]{2,1,0:T(8,128)S(1)}, f32[2,256,128]{2,1,0:T(8,128)S(1)}, u32[]{:S(2)}, u32[]{:S(2)}) %collective-permute-start.17) | collective-permute-done | bytes 262176 | tf_op jit(solution)/shard_map/ppermute | solution.py:71
  108.8 0.7 multiply_reduce_fusion
  110.5 2.4 %fusion.4 = f32[32,1,128,1]{2,1,3,0:T(1,128)S(1)} fusion(bf16[64,2,128,128]{3,2,1,0:T(8,128)(2,1)} %param.7, bf16[32,2,128,1]{2,1,0,3:T(2,128)(2,1)S(1)} %bitcast.310), kind=kOutput, calls=%fused_computation.4 | convolution fusion | flops 2097152 | bytes 2129920 | tf_op jit(solution)/shard_map/tsrb,tsb->tr/dot_general | solution.py:147
  113.1 0.6 fusion
  115.0 1.3 %collective-permute-start.21 = (f32[32,128]{1,0:T(8,128)S(1)}, f32[32,128]{1,0:T(8,128)S(1)}, u32[]{:S(2)}, u32[]{:S(2)}) collective-permute-start(f32[32,128]{1,0:T(8,128)S(1)} %add.948), channel_id=1, source_target_pairs={{0,2},{1,3},{2,0},{3,1},{4,6},{5,7},{6,4},{7,5},{8,10},{9,11},{10,... | collective-permute-start | bytes 49160 | tf_op jit(solution)/shard_map/ppermute | solution.py:19
  116.4 1.6 %collective-permute-done.19 = f32[32,128]{1,0:T(8,128)S(1)} collective-permute-done((f32[32,128]{1,0:T(8,128)S(1)}, f32[32,128]{1,0:T(8,128)S(1)}, u32[]{:S(2)}, u32[]{:S(2)}) %collective-permute-start.19) | collective-permute-done | bytes 16416 | tf_op jit(solution)/shard_map/ppermute | solution.py:19
  118.0 0.7 collective-permute-done.21
  118.7 0.7 fusion.43
  119.5 2.5 %all-to-all-start.2 = ((f32[32,1,128]{2,1,0:T(1,128)}), f32[32,1,128]{2,1,0:T(1,128)S(1)}, u32[]{:S(2)}, u32[]{:S(2)}) async-start(f32[32,1,128]{2,1,0:T(1,128)} %bitcast.75), calls=%async_computation.2 | async-start | bytes 32768 | tf_op jit(solution)/shard_map/all_to_all | solution.py:36
  122.3 6.9 %all-to-all-done.2 = f32[32,1,128]{2,1,0:T(1,128)S(1)} async-done(((f32[32,1,128]{2,1,0:T(1,128)}), f32[32,1,128]{2,1,0:T(1,128)S(1)}, u32[]{:S(2)}, u32[]{:S(2)}) %all-to-all-start.2) | async-done | bytes 16416 | tf_op jit(solution)/shard_map/all_to_all | solution.py:36
  129.1 0.6 fusion.71
  130.6 0.7 multiply_add_fusion
  (85 shorter events, 9.9 us)
Async XLA Ops:
  1.5 13.7 %all-to-all-start = ((f32[8,1,128]{2,1,0:T(1,128)}), f32[8,1,128]{2,1,0:T(1,128)S(1)}, u32[]{:S(2)}, u32[]{:S(2)}) async-start(f32[8,1,128]{2,1,0:T(1,128)} %bitcast.3), calls=%async_computation | async-start | bytes 8192 | tf_op jit(solution)/shard_map/all_to_all | solution.py:36
  20.6 1.6 %collective-permute-start = (f32[2,256,128]{2,1,0:T(8,128)S(1)}, f32[2,256,128]{2,1,0:T(8,128)S(1)}, u32[]{:S(2)}, u32[]{:S(2)}) collective-permute-start(f32[2,256,128]{2,1,0:T(8,128)S(1)} %dynamic-slice_bitcast_fusion.1), channel_id=1, source_target_pairs={{0,1},{1,0},{2,3},{3,2},{4,5},{5,4},{6,7},{7,6},{8,9},{9,8},{10,11... | collective-permute-start | bytes 786440 | tf_op jit(solution)/shard_map/ppermute | solution.py:58
  22.3 5.6 %collective-permute-start.1 = (f32[256,128]{1,0:T(8,128)S(1)}, f32[256,128]{1,0:T(8,128)S(1)}, u32[]{:S(2)}, u32[]{:S(2)}) collective-permute-start(f32[256,128]{1,0:T(8,128)S(1)} %dynamic-slice_bitcast_fusion.3), channel_id=1, source_target_pairs={{0,2},{1,3},{2,0},{3,1},{4,6},{5,7},{6,4},{7,5},{8,10},{9,11},{10,... | collective-permute-start | bytes 393224 | tf_op jit(solution)/shard_map/ppermute | solution.py:58
  27.9 5.0 %collective-permute-start.2 = (f32[256,128]{1,0:T(8,128)S(1)}, f32[256,128]{1,0:T(8,128)S(1)}, u32[]{:S(2)}, u32[]{:S(2)}) collective-permute-start(f32[256,128]{1,0:T(8,128)S(1)} %bitcast_add_fusion.3), channel_id=1, source_target_pairs={{0,4},{4,0},{8,12},{12,8},{16,20},{20,16},{24,28},{28,24},{1,5},{5... | collective-permute-start | bytes 393224 | tf_op jit(solution)/shard_map/ppermute | solution.py:19
  33.0 5.0 %collective-permute-start.3 = (f32[256,128]{1,0:T(8,128)S(1)}, f32[256,128]{1,0:T(8,128)S(1)}, u32[]{:S(2)}, u32[]{:S(2)}) collective-permute-start(f32[256,128]{1,0:T(8,128)S(1)} %add.899), channel_id=1, source_target_pairs={{0,8},{4,12},{8,0},{12,4},{16,24},{20,28},{24,16},{28,20},{1,9},{5... | collective-permute-start | bytes 393224 | tf_op jit(solution)/shard_map/ppermute | solution.py:19
  38.0 7.3 %collective-permute-start.4 = (f32[256,128]{1,0:T(8,128)S(1)}, f32[256,128]{1,0:T(8,128)S(1)}, u32[]{:S(2)}, u32[]{:S(2)}) collective-permute-start(f32[256,128]{1,0:T(8,128)S(1)} %add.900), channel_id=1, source_target_pairs={{0,16},{4,20},{8,24},{12,28},{16,0},{20,4},{24,8},{28,12},{1,17},{... | collective-permute-start | bytes 393224 | tf_op jit(solution)/shard_map/ppermute | solution.py:19
  45.4 5.0 %collective-permute-start.5 = (f32[256,128]{1,0:T(8,128)S(1)}, f32[256,128]{1,0:T(8,128)S(1)}, u32[]{:S(2)}, u32[]{:S(2)}) collective-permute-start(f32[256,128]{1,0:T(8,128)S(1)} %add.901), channel_id=1, source_target_pairs={{0,2},{1,3},{2,0},{3,1},{4,6},{5,7},{6,4},{7,5},{8,10},{9,11},{10,... | collective-permute-start | bytes 393224 | tf_op jit(solution)/shard_map/ppermute | solution.py:71
  50.4 1.6 %collective-permute-start.6 = (f32[2,256,128]{2,1,0:T(8,128)S(1)}, f32[2,256,128]{2,1,0:T(8,128)S(1)}, u32[]{:S(2)}, u32[]{:S(2)}) collective-permute-start(f32[2,256,128]{2,1,0:T(8,128)S(1)} %maximum_select_fusion.2), channel_id=1, source_target_pairs={{0,1},{1,0},{2,3},{3,2},{4,5},{5,4},{6,7},{7,6},{8,9},{9,8},{10,11... | collective-permute-start | bytes 786440 | tf_op jit(solution)/shard_map/ppermute | solution.py:71
  50.6 9.1 %copy-start.3 = (f32[32,128]{1,0:T(8,128)S(1)}, f32[32,128]{1,0:T(8,128)}, u32[]{:S(2)}) copy-start(f32[32,128]{1,0:T(8,128)} %param.10) | copy-start | bytes 49156
  50.7 12.2 %copy-start.2 = (f32[64,128]{1,0:T(8,128)S(1)}, f32[64,128]{1,0:T(8,128)}, u32[]{:S(2)}) copy-start(f32[64,128]{1,0:T(8,128)} %param.6) | copy-start | bytes 98308
  53.5 2.9 %copy-start = (bf16[64,2,128,128]{3,2,1,0:T(8,128)(2,1)S(1)}, bf16[64,2,128,128]{3,2,1,0:T(8,128)(2,1)}, u32[]{:S(2)}) copy-start(bf16[64,2,128,128]{3,2,1,0:T(8,128)(2,1)} %param.7) | copy-start | bytes 12582916
  56.2 1.2 collective-permute-start.9
  57.0 2.0 %collective-permute-start.7 = (f32[32,128]{1,0:T(8,128)S(1)}, f32[32,128]{1,0:T(8,128)S(1)}, u32[]{:S(2)}, u32[]{:S(2)}) collective-permute-start(f32[32,128]{1,0:T(8,128)S(1)} %bitcast.298), channel_id=1, source_target_pairs={{0,1},{1,0},{2,3},{3,2},{4,5},{5,4},{6,7},{7,6},{8,9},{9,8},{10,11... | collective-permute-start | bytes 49160 | tf_op jit(solution)/shard_map/ppermute | solution.py:19
  57.5 3.8 %collective-permute-start.10 = (f32[32,128]{1,0:T(8,128)S(1)}, f32[32,128]{1,0:T(8,128)S(1)}, u32[]{:S(2)}, u32[]{:S(2)}) collective-permute-start(f32[32,128]{1,0:T(8,128)S(1)} %add.904), channel_id=1, source_target_pairs={{0,2},{1,3},{2,0},{3,1},{4,6},{5,7},{6,4},{7,5},{8,10},{9,11},{10,... | collective-permute-start | bytes 49160 | tf_op jit(solution)/shard_map/ppermute | solution.py:19
  59.0 3.8 %collective-permute-start.8 = (f32[32,128]{1,0:T(8,128)S(1)}, f32[32,128]{1,0:T(8,128)S(1)}, u32[]{:S(2)}, u32[]{:S(2)}) collective-permute-start(f32[32,128]{1,0:T(8,128)S(1)} %add.902), channel_id=1, source_target_pairs={{0,2},{1,3},{2,0},{3,1},{4,6},{5,7},{6,4},{7,5},{8,10},{9,11},{10,... | collective-permute-start | bytes 49160 | tf_op jit(solution)/shard_map/ppermute | solution.py:19
  77.4 1.6 %collective-permute-start.11 = (f32[2,256,128]{2,1,0:T(8,128)S(1)}, f32[2,256,128]{2,1,0:T(8,128)S(1)}, u32[]{:S(2)}, u32[]{:S(2)}) collective-permute-start(f32[2,256,128]{2,1,0:T(8,128)S(1)} %dynamic-slice_bitcast_fusion), channel_id=1, source_target_pairs={{0,1},{1,0},{2,3},{3,2},{4,5},{5,4},{6,7},{7,6},{8,9},{9,8},{10,11... | collective-permute-start | bytes 786440 | tf_op jit(solution)/shard_map/ppermute | solution.py:58
  79.0 5.6 %collective-permute-start.12 = (f32[256,128]{1,0:T(8,128)S(1)}, f32[256,128]{1,0:T(8,128)S(1)}, u32[]{:S(2)}, u32[]{:S(2)}) collective-permute-start(f32[256,128]{1,0:T(8,128)S(1)} %dynamic-slice_bitcast_fusion.2), channel_id=1, source_target_pairs={{0,2},{1,3},{2,0},{3,1},{4,6},{5,7},{6,4},{7,5},{8,10},{9,11},{10,... | collective-permute-start | bytes 393224 | tf_op jit(solution)/shard_map/ppermute | solution.py:58
  84.7 5.0 %collective-permute-start.13 = (f32[256,128]{1,0:T(8,128)S(1)}, f32[256,128]{1,0:T(8,128)S(1)}, u32[]{:S(2)}, u32[]{:S(2)}) collective-permute-start(f32[256,128]{1,0:T(8,128)S(1)} %bitcast_add_fusion.2), channel_id=1, source_target_pairs={{0,4},{4,0},{8,12},{12,8},{16,20},{20,16},{24,28},{28,24},{1,5},{5... | collective-permute-start | bytes 393224 | tf_op jit(solution)/shard_map/ppermute | solution.py:19
  89.7 5.0 %collective-permute-start.14 = (f32[256,128]{1,0:T(8,128)S(1)}, f32[256,128]{1,0:T(8,128)S(1)}, u32[]{:S(2)}, u32[]{:S(2)}) collective-permute-start(f32[256,128]{1,0:T(8,128)S(1)} %add.943), channel_id=1, source_target_pairs={{0,8},{4,12},{8,0},{12,4},{16,24},{20,28},{24,16},{28,20},{1,9},{5... | collective-permute-start | bytes 393224 | tf_op jit(solution)/shard_map/ppermute | solution.py:19
  94.8 7.3 %collective-permute-start.15 = (f32[256,128]{1,0:T(8,128)S(1)}, f32[256,128]{1,0:T(8,128)S(1)}, u32[]{:S(2)}, u32[]{:S(2)}) collective-permute-start(f32[256,128]{1,0:T(8,128)S(1)} %add.944), channel_id=1, source_target_pairs={{0,16},{4,20},{8,24},{12,28},{16,0},{20,4},{24,8},{28,12},{1,17},{... | collective-permute-start | bytes 393224 | tf_op jit(solution)/shard_map/ppermute | solution.py:19
  102.1 5.0 %collective-permute-start.16 = (f32[256,128]{1,0:T(8,128)S(1)}, f32[256,128]{1,0:T(8,128)S(1)}, u32[]{:S(2)}, u32[]{:S(2)}) collective-permute-start(f32[256,128]{1,0:T(8,128)S(1)} %multiply_subtract_fusion), channel_id=1, source_target_pairs={{0,2},{1,3},{2,0},{3,1},{4,6},{5,7},{6,4},{7,5},{8,10},{9,11},{10,... | collective-permute-start | bytes 393224 | tf_op jit(solution)/shard_map/ppermute | solution.py:71
  107.2 1.6 %collective-permute-start.17 = (f32[2,256,128]{2,1,0:T(8,128)S(1)}, f32[2,256,128]{2,1,0:T(8,128)S(1)}, u32[]{:S(2)}, u32[]{:S(2)}) collective-permute-start(f32[2,256,128]{2,1,0:T(8,128)S(1)} %maximum_select_fusion.4), channel_id=1, source_target_pairs={{0,1},{1,0},{2,3},{3,2},{4,5},{5,4},{6,7},{7,6},{8,9},{9,8},{10,11... | collective-permute-start | bytes 786440 | tf_op jit(solution)/shard_map/ppermute | solution.py:71
  110.2 2.9 %copy-start.1 = (bf16[64,2,128,128]{3,2,1,0:T(8,128)(2,1)S(1)}, bf16[64,2,128,128]{3,2,1,0:T(8,128)(2,1)}, u32[]{:S(2)}) copy-start(bf16[64,2,128,128]{3,2,1,0:T(8,128)(2,1)} %param.7) | copy-start | bytes 12582916
  112.9 1.2 collective-permute-start.18
  113.7 1.2 collective-permute-start.20
  114.1 3.8 %collective-permute-start.19 = (f32[32,128]{1,0:T(8,128)S(1)}, f32[32,128]{1,0:T(8,128)S(1)}, u32[]{:S(2)}, u32[]{:S(2)}) collective-permute-start(f32[32,128]{1,0:T(8,128)S(1)} %add.946), channel_id=1, source_target_pairs={{0,2},{1,3},{2,0},{3,1},{4,6},{5,7},{6,4},{7,5},{8,10},{9,11},{10,... | collective-permute-start | bytes 49160 | tf_op jit(solution)/shard_map/ppermute | solution.py:19
  115.0 3.7 %collective-permute-start.21 = (f32[32,128]{1,0:T(8,128)S(1)}, f32[32,128]{1,0:T(8,128)S(1)}, u32[]{:S(2)}, u32[]{:S(2)}) collective-permute-start(f32[32,128]{1,0:T(8,128)S(1)} %add.948), channel_id=1, source_target_pairs={{0,2},{1,3},{2,0},{3,1},{4,6},{5,7},{6,4},{7,5},{8,10},{9,11},{10,... | collective-permute-start | bytes 49160 | tf_op jit(solution)/shard_map/ppermute | solution.py:19
  119.5 9.6 %all-to-all-start.2 = ((f32[32,1,128]{2,1,0:T(1,128)}), f32[32,1,128]{2,1,0:T(1,128)S(1)}, u32[]{:S(2)}, u32[]{:S(2)}) async-start(f32[32,1,128]{2,1,0:T(1,128)} %bitcast.75), calls=%async_computation.2 | async-start | bytes 32768 | tf_op jit(solution)/shard_map/all_to_all | solution.py:36

commit v16 on v14

--- a/solution.py
+++ b/solution.py
@@ -135,13 +135,15 @@
         full_half = full_model.astype(jnp.bfloat16)
         rows = jnp.dot(select_half, full_half, preferred_element_type=jnp.float32)
         picked = rows[:n_slots].astype(jnp.bfloat16).reshape(tile_blocks.shape + rows.shape[-1:])
-        half_tiles = n_tiles // 4 if n_tiles % 32 == 0 else n_tiles
+        cut = 3 * n_tiles // 4 if n_tiles % 32 == 0 else n_tiles
         halves = []
-        for lo in range(0, n_tiles, half_tiles):
+        for lo, hi in ((0, cut), (cut, n_tiles)):
+            if hi == lo:
+                continue
             part = jnp.einsum(
                 "tsrb,tsb->tr",
-                sensitivity[lo:lo + half_tiles],
-                picked[lo:lo + half_tiles],
+                sensitivity[lo:hi],
+                picked[lo:hi],
                 preferred_element_type=jnp.float32,
             )
             halves.append(butterfly_sum(part, "region"))

time: 137 us -> 136 us (level)
  starting transfers between devices: 28.3 us -> 23.4 us
  waiting for transfers between devices: 68.3 us -> 70.4 us
  matrix products: 16.5 us -> 18.3 us
    ppermute x22 -> x14, starting transfers between devices: 13.9 us -> 9.03 us  [butterfly_sum(): x = x + lax.ppermute(x, axis, [(i, i ^ k) for i in range(n)])]
    ppermute x22 -> x14, waiting for transfers between devices: 36.1 us -> 38.2 us  [butterfly_sum(): x = x + lax.ppermute(x, axis, [(i, i ^ k) for i in range(n)])]
    dot_general x8 -> x4, matrix products: 6.99 us -> 8.79 us  [local(): jnp.einsum('tsrb,tsb->tr', sensitivity[lo:hi], picked[lo:hi], preferred_e...]
  transfers between devices with their start and end apart: 32 -> 24, of which waited for: 21 -> 22; matrix products, arithmetic and copies ran while one was open for 5% -> 5% of each run, Pallas kernels for 0% -> 0%
where the time goes in v16:
time: 136 us; the launch traced here: 135 us
  waiting for transfers between devices  70.4 us (52%)
  starting transfers between devices  23.4 us (17%)
  matrix products  18.3 us (13%)
  blocking collectives  9.44 us (7%)
  other arithmetic  7.12 us (5%)
  between operations  4.89 us (4%)
  local copies, waits for them, and re-layouts  1.82 us (1%)
    ppermute x14, waiting for transfers between devices, butterfly_sum(): x = x + lax.ppermute(x, axis, [(i, i ^ k) for i in range(n)])  38.2 us
    ppermute x4, waiting for transfers between devices, halving_scatter(): x = keep + lax.ppermute(send, axis, [(i, i ^ k) for i in range(n)])  12.1 us
    ppermute x4, waiting for transfers between devices, doubling_gather(): other = lax.ppermute(x, axis, [(i, i ^ k) for i in range(n)])  10.7 us
    all_to_all x2, starting transfers between devices, square_sum(): got = lax.all_to_all(spread[:, None, :], axis, 0, 0, tiled=False)  9.82 us
    all_to_all x2, waiting for transfers between devices, square_sum(): got = lax.all_to_all(spread[:, None, :], axis, 0, 0, tiled=False)  9.46 us
    all_to_all x1, blocking collectives, square_sum(): got = lax.all_to_all(spread[:, None, :], axis, 0, 0, tiled=False)  9.44 us
    ppermute x14, starting transfers between devices, butterfly_sum(): x = x + lax.ppermute(x, axis, [(i, i ^ k) for i in range(n)])  9.03 us
    dot_general x4, matrix products, local(): jnp.einsum('tsrb,tsb->tr', sensitivity[lo:hi], picked[lo:hi], preferred_e...  8.79 us
  transfers between devices with their start and end apart: 24, of which 22 were waited for; matrix products, arithmetic and copies ran while one was open for 5% of the time, Pallas kernels for 0%

profile of v16, /device:TPU:0, one launch (start us, length us, event | category | flops | bytes accessed | tf_op | source)
XLA Modules:
  0.0 135.3 jit_solution(14557114423900720994)
XLA Ops:
  0.0 1.5 %fusion.37 = f32[8,128]{1,0:T(8,128)} fusion(f32[64,128]{1,0:T(8,128)} %param.6), kind=kOutput, calls=%fused_computation.74 | convolution fusion | flops 794624 | bytes 36864 | tf_op jit(solution)/shard_map/dot_general | solution.py:27
  1.5 7.3 %all-to-all-start = ((f32[8,1,128]{2,1,0:T(1,128)}), f32[8,1,128]{2,1,0:T(1,128)S(1)}, u32[]{:S(2)}, u32[]{:S(2)}) async-start(f32[8,1,128]{2,1,0:T(1,128)} %bitcast.3), calls=%async_computation | async-start | bytes 8192 | tf_op jit(solution)/shard_map/all_to_all | solution.py:30
  8.8 0.8 copy.14
  9.8 0.8 slice_bitcast_fusion.31
  11.8 0.8 multiply_multiply_fusion.1
  12.6 2.6 %all-to-all-done = f32[8,1,128]{2,1,0:T(1,128)S(1)} async-done(((f32[8,1,128]{2,1,0:T(1,128)}), f32[8,1,128]{2,1,0:T(1,128)S(1)}, u32[]{:S(2)}, u32[]{:S(2)}) %all-to-all-start) | async-done | bytes 4128 | tf_op jit(solution)/shard_map/all_to_all | solution.py:30
  16.5 0.8 convert_bitcast_fusion.1
  17.2 2.8 %fusion.35 = f32[64,1,2,128]{3,1,2,0:T(1,128)S(1)} fusion(bf16[64,2,128,128]{3,2,1,0:T(8,128)(2,1)} %param.7, bf16[64,128,1,1]{1,0,2,3:T(8,128)(2,1)S(1)} %convert_bitcast_fusion.1), kind=kOutput, calls=%fused_computation.72 | convolution fusion | flops 4194304 | bytes 4276224 | tf_op jit(solution)/shard_map/tsrb,tr->tsb/dot_general | solution.py:98
  20.7 1.5 %collective-permute-done = f32[2,256,128]{2,1,0:T(8,128)S(1)} collective-permute-done((f32[2,256,128]{2,1,0:T(8,128)S(1)}, f32[2,256,128]{2,1,0:T(8,128)S(1)}, u32[]{:S(2)}, u32[]{:S(2)}) %collective-permute-start) | collective-permute-done | bytes 262176 | tf_op jit(solution)/shard_map/ppermute | solution.py:52
  22.3 1.6 %collective-permute-start.1 = (f32[256,128]{1,0:T(8,128)S(1)}, f32[256,128]{1,0:T(8,128)S(1)}, u32[]{:S(2)}, u32[]{:S(2)}) collective-permute-start(f32[256,128]{1,0:T(8,128)S(1)} %dynamic-slice_bitcast_fusion.3), channel_id=1, source_target_pairs={{0,2},{1,3},{2,0},{3,1},{4,6},{5,7},{6,4},{7,5},{8,10},{9,11},{10,... | collective-permute-start | bytes 393224 | tf_op jit(solution)/shard_map/ppermute | solution.py:52
  23.8 4.0 %collective-permute-done.1 = f32[256,128]{1,0:T(8,128)S(1)} collective-permute-done((f32[256,128]{1,0:T(8,128)S(1)}, f32[256,128]{1,0:T(8,128)S(1)}, u32[]{:S(2)}, u32[]{:S(2)}) %collective-permute-start.1) | collective-permute-done | bytes 131104 | tf_op jit(solution)/shard_map/ppermute | solution.py:52
  28.5 4.4 %collective-permute-done.2 = f32[256,128]{1,0:T(8,128)S(1)} collective-permute-done((f32[256,128]{1,0:T(8,128)S(1)}, f32[256,128]{1,0:T(8,128)S(1)}, u32[]{:S(2)}, u32[]{:S(2)}) %collective-permute-start.2) | collective-permute-done | bytes 131104 | tf_op jit(solution)/shard_map/ppermute | solution.py:19
  33.6 4.4 %collective-permute-done.3 = f32[256,128]{1,0:T(8,128)S(1)} collective-permute-done((f32[256,128]{1,0:T(8,128)S(1)}, f32[256,128]{1,0:T(8,128)S(1)}, u32[]{:S(2)}, u32[]{:S(2)}) %collective-permute-start.3) | collective-permute-done | bytes 131104 | tf_op jit(solution)/shard_map/ppermute | solution.py:19
  38.6 6.7 %collective-permute-done.4 = f32[256,128]{1,0:T(8,128)S(1)} collective-permute-done((f32[256,128]{1,0:T(8,128)S(1)}, f32[256,128]{1,0:T(8,128)S(1)}, u32[]{:S(2)}, u32[]{:S(2)}) %collective-permute-start.4) | collective-permute-done | bytes 131104 | tf_op jit(solution)/shard_map/ppermute | solution.py:19
  45.4 1.6 %collective-permute-start.5 = (f32[256,128]{1,0:T(8,128)S(1)}, f32[256,128]{1,0:T(8,128)S(1)}, u32[]{:S(2)}, u32[]{:S(2)}) collective-permute-start(f32[256,128]{1,0:T(8,128)S(1)} %add.901), channel_id=1, source_target_pairs={{0,2},{1,3},{2,0},{3,1},{4,6},{5,7},{6,4},{7,5},{8,10},{9,11},{10,... | collective-permute-start | bytes 393224 | tf_op jit(solution)/shard_map/ppermute | solution.py:65
  47.0 3.4 %collective-permute-done.5 = f32[256,128]{1,0:T(8,128)S(1)} collective-permute-done((f32[256,128]{1,0:T(8,128)S(1)}, f32[256,128]{1,0:T(8,128)S(1)}, u32[]{:S(2)}, u32[]{:S(2)}) %collective-permute-start.5) | collective-permute-done | bytes 131104 | tf_op jit(solution)/shard_map/ppermute | solution.py:65
  50.7 1.4 %collective-permute-done.6 = f32[2,256,128]{2,1,0:T(8,128)S(1)} collective-permute-done((f32[2,256,128]{2,1,0:T(8,128)S(1)}, f32[2,256,128]{2,1,0:T(8,128)S(1)}, u32[]{:S(2)}, u32[]{:S(2)}) %collective-permute-start.6) | collective-permute-done | bytes 262176 | tf_op jit(solution)/shard_map/ppermute | solution.py:65
  52.0 0.7 multiply_reduce_fusion.1
  53.8 2.8 %fusion.2 = f32[48,1,128,1]{2,1,3,0:T(1,128)S(1)} fusion(bf16[64,2,128,128]{3,2,1,0:T(8,128)(2,1)} %param.7, bf16[48,2,128,1]{2,1,0,3:T(2,128)(2,1)S(1)} %bitcast.300), kind=kOutput, calls=%fused_computation.2 | convolution fusion | flops 3145728 | bytes 3194880 | tf_op jit(solution)/shard_map/tsrb,tsb->tr/dot_general | solution.py:143
  56.8 1.6 %fusion.6 = f32[16,1,128,1]{2,1,3,0:T(1,128)S(1)} fusion(bf16[64,2,128,128]{3,2,1,0:T(8,128)(2,1)} %param.7, bf16[16,2,128,1]{2,1,0,3:T(2,128)(2,1)S(1)} %bitcast.309), kind=kOutput, calls=%fused_computation.6 | convolution fusion | flops 1048576 | bytes 1064960 | tf_op jit(solution)/shard_map/tsrb,tsb->tr/dot_general | solution.py:143
  58.8 0.8 collective-permute-done.9
  59.6 1.5 %collective-permute-start.10 = (f32[16,128]{1,0:T(8,128)S(1)}, f32[16,128]{1,0:T(8,128)S(1)}, u32[]{:S(2)}, u32[]{:S(2)}) collective-permute-start(f32[16,128]{1,0:T(8,128)S(1)} %add.904), channel_id=1, source_target_pairs={{0,2},{1,3},{2,0},{3,1},{4,6},{5,7},{6,4},{7,5},{8,10},{9,11},{10,... | collective-permute-start | bytes 24584 | tf_op jit(solution)/shard_map/ppermute | solution.py:19
  61.8 1.5 %collective-permute-done.10 = f32[16,128]{1,0:T(8,128)S(1)} collective-permute-done((f32[16,128]{1,0:T(8,128)S(1)}, f32[16,128]{1,0:T(8,128)S(1)}, u32[]{:S(2)}, u32[]{:S(2)}) %collective-permute-start.10) | collective-permute-done | bytes 8224 | tf_op jit(solution)/shard_map/ppermute | solution.py:19
  63.2 1.7 %collective-permute-done.8 = f32[48,128]{1,0:T(8,128)S(1)} collective-permute-done((f32[48,128]{1,0:T(8,128)S(1)}, f32[48,128]{1,0:T(8,128)S(1)}, u32[]{:S(2)}, u32[]{:S(2)}) %collective-permute-start.8) | collective-permute-done | bytes 24608 | tf_op jit(solution)/shard_map/ppermute | solution.py:19
  65.2 9.4 %all_to_all.15 = f32[32,1,128]{2,1,0:T(1,128)S(1)} all-to-all(f32[32,1,128]{2,1,0:T(1,128)S(1)} %bitcast.298), channel_id=1, replica_groups=mesh['dp'=8,'region'=4] {'dp','region'}, dimensions={0} | all-to-all | bytes 32768 | tf_op jit(solution)/shard_map/all_to_all | solution.py:30
  74.6 0.6 fusion.75
  76.0 2.8 %fusion.33 = f32[64,1,2,128]{3,1,2,0:T(1,128)S(1)} fusion(bf16[64,2,128,128]{3,2,1,0:T(8,128)(2,1)} %param.7, bf16[64,128,1,1]{1,0,2,3:T(8,128)(2,1)S(1)} %get-tuple-element.5), kind=kOutput, calls=%fused_computation.70 | convolution fusion | flops 4194304 | bytes 4276224 | tf_op jit(solution)/shard_map/tsrb,tr->tsb/dot_general | solution.py:98
  79.5 1.5 %collective-permute-done.11 = f32[2,256,128]{2,1,0:T(8,128)S(1)} collective-permute-done((f32[2,256,128]{2,1,0:T(8,128)S(1)}, f32[2,256,128]{2,1,0:T(8,128)S(1)}, u32[]{:S(2)}, u32[]{:S(2)}) %collective-permute-start.11) | collective-permute-done | bytes 262176 | tf_op jit(solution)/shard_map/ppermute | solution.py:52
  81.7 5.0 %collective-permute-done.12 = f32[256,128]{1,0:T(8,128)S(1)} collective-permute-done((f32[256,128]{1,0:T(8,128)S(1)}, f32[256,128]{1,0:T(8,128)S(1)}, u32[]{:S(2)}, u32[]{:S(2)}) %collective-permute-start.12) | collective-permute-done | bytes 131104 | tf_op jit(solution)/shard_map/ppermute | solution.py:52
  87.3 4.4 %collective-permute-done.13 = f32[256,128]{1,0:T(8,128)S(1)} collective-permute-done((f32[256,128]{1,0:T(8,128)S(1)}, f32[256,128]{1,0:T(8,128)S(1)}, u32[]{:S(2)}, u32[]{:S(2)}) %collective-permute-start.13) | collective-permute-done | bytes 131104 | tf_op jit(solution)/shard_map/ppermute | solution.py:19
  91.8 0.6 collective-permute-start.14
  92.4 4.4 %collective-permute-done.14 = f32[256,128]{1,0:T(8,128)S(1)} collective-permute-done((f32[256,128]{1,0:T(8,128)S(1)}, f32[256,128]{1,0:T(8,128)S(1)}, u32[]{:S(2)}, u32[]{:S(2)}) %collective-permute-start.14) | collective-permute-done | bytes 131104 | tf_op jit(solution)/shard_map/ppermute | solution.py:19
  96.8 0.7 collective-permute-start.15
  97.5 6.7 %collective-permute-done.15 = f32[256,128]{1,0:T(8,128)S(1)} collective-permute-done((f32[256,128]{1,0:T(8,128)S(1)}, f32[256,128]{1,0:T(8,128)S(1)}, u32[]{:S(2)}, u32[]{:S(2)}) %collective-permute-start.15) | collective-permute-done | bytes 131104 | tf_op jit(solution)/shard_map/ppermute | solution.py:19
  104.8 4.4 %collective-permute-done.16 = f32[256,128]{1,0:T(8,128)S(1)} collective-permute-done((f32[256,128]{1,0:T(8,128)S(1)}, f32[256,128]{1,0:T(8,128)S(1)}, u32[]{:S(2)}, u32[]{:S(2)}) %collective-permute-start.16) | collective-permute-done | bytes 131104 | tf_op jit(solution)/shard_map/ppermute | solution.py:65
  109.3 1.5 %collective-permute-done.17 = f32[2,256,128]{2,1,0:T(8,128)S(1)} collective-permute-done((f32[2,256,128]{2,1,0:T(8,128)S(1)}, f32[2,256,128]{2,1,0:T(8,128)S(1)}, u32[]{:S(2)}, u32[]{:S(2)}) %collective-permute-start.17) | collective-permute-done | bytes 262176 | tf_op jit(solution)/shard_map/ppermute | solution.py:65
  110.8 0.7 multiply_reduce_fusion
  112.6 2.8 %fusion = f32[48,1,128,1]{2,1,3,0:T(1,128)S(1)} fusion(bf16[64,2,128,128]{3,2,1,0:T(8,128)(2,1)} %param.7, bf16[48,2,128,1]{2,1,0,3:T(2,128)(2,1)S(1)} %bitcast.299), kind=kOutput, calls=%fused_computation | convolution fusion | flops 3145728 | bytes 3194880 | tf_op jit(solution)/shard_map/tsrb,tsb->tr/dot_general | solution.py:143
  115.5 1.6 %fusion.4 = f32[16,1,128,1]{2,1,3,0:T(1,128)S(1)} fusion(bf16[64,2,128,128]{3,2,1,0:T(8,128)(2,1)} %param.7, bf16[16,2,128,1]{2,1,0,3:T(2,128)(2,1)S(1)} %bitcast.310), kind=kOutput, calls=%fused_computation.4 | convolution fusion | flops 1048576 | bytes 1064960 | tf_op jit(solution)/shard_map/tsrb,tsb->tr/dot_general | solution.py:143
  117.5 0.8 collective-permute-done.20
  118.9 1.6 %collective-permute-start.19 = (f32[48,128]{1,0:T(8,128)S(1)}, f32[48,128]{1,0:T(8,128)S(1)}, u32[]{:S(2)}, u32[]{:S(2)}) collective-permute-start(f32[48,128]{1,0:T(8,128)S(1)} %add.946), channel_id=1, source_target_pairs={{0,2},{1,3},{2,0},{3,1},{4,6},{5,7},{6,4},{7,5},{8,10},{9,11},{10,... | collective-permute-start | bytes 73736 | tf_op jit(solution)/shard_map/ppermute | solution.py:19
  120.5 1.5 %collective-permute-done.21 = f32[16,128]{1,0:T(8,128)S(1)} collective-permute-done((f32[16,128]{1,0:T(8,128)S(1)}, f32[16,128]{1,0:T(8,128)S(1)}, u32[]{:S(2)}, u32[]{:S(2)}) %collective-permute-start.21) | collective-permute-done | bytes 8224 | tf_op jit(solution)/shard_map/ppermute | solution.py:19
  122.0 0.8 collective-permute-done.19
  122.8 0.8 fusion.45
  123.6 2.5 %all-to-all-start.2 = ((f32[32,1,128]{2,1,0:T(1,128)}), f32[32,1,128]{2,1,0:T(1,128)S(1)}, u32[]{:S(2)}, u32[]{:S(2)}) async-start(f32[32,1,128]{2,1,0:T(1,128)} %bitcast.75), calls=%async_computation.2 | async-start | bytes 32768 | tf_op jit(solution)/shard_map/all_to_all | solution.py:30
  126.3 6.9 %all-to-all-done.2 = f32[32,1,128]{2,1,0:T(1,128)S(1)} async-done(((f32[32,1,128]{2,1,0:T(1,128)}), f32[32,1,128]{2,1,0:T(1,128)S(1)}, u32[]{:S(2)}, u32[]{:S(2)}) %all-to-all-start.2) | async-done | bytes 16416 | tf_op jit(solution)/shard_map/all_to_all | solution.py:30
  133.2 0.6 fusion.58
  134.6 0.7 multiply_add_fusion
  (80 shorter events, 10.2 us)
Async XLA Ops:
  1.5 13.7 %all-to-all-start = ((f32[8,1,128]{2,1,0:T(1,128)}), f32[8,1,128]{2,1,0:T(1,128)S(1)}, u32[]{:S(2)}, u32[]{:S(2)}) async-start(f32[8,1,128]{2,1,0:T(1,128)} %bitcast.3), calls=%async_computation | async-start | bytes 8192 | tf_op jit(solution)/shard_map/all_to_all | solution.py:30
  20.6 1.6 %collective-permute-start = (f32[2,256,128]{2,1,0:T(8,128)S(1)}, f32[2,256,128]{2,1,0:T(8,128)S(1)}, u32[]{:S(2)}, u32[]{:S(2)}) collective-permute-start(f32[2,256,128]{2,1,0:T(8,128)S(1)} %dynamic-slice_bitcast_fusion.1), channel_id=1, source_target_pairs={{0,1},{1,0},{2,3},{3,2},{4,5},{5,4},{6,7},{7,6},{8,9},{9,8},{10,11... | collective-permute-start | bytes 786440 | tf_op jit(solution)/shard_map/ppermute | solution.py:52
  22.3 5.6 %collective-permute-start.1 = (f32[256,128]{1,0:T(8,128)S(1)}, f32[256,128]{1,0:T(8,128)S(1)}, u32[]{:S(2)}, u32[]{:S(2)}) collective-permute-start(f32[256,128]{1,0:T(8,128)S(1)} %dynamic-slice_bitcast_fusion.3), channel_id=1, source_target_pairs={{0,2},{1,3},{2,0},{3,1},{4,6},{5,7},{6,4},{7,5},{8,10},{9,11},{10,... | collective-permute-start | bytes 393224 | tf_op jit(solution)/shard_map/ppermute | solution.py:52
  27.9 5.0 %collective-permute-start.2 = (f32[256,128]{1,0:T(8,128)S(1)}, f32[256,128]{1,0:T(8,128)S(1)}, u32[]{:S(2)}, u32[]{:S(2)}) collective-permute-start(f32[256,128]{1,0:T(8,128)S(1)} %bitcast_add_fusion.3), channel_id=1, source_target_pairs={{0,4},{4,0},{8,12},{12,8},{16,20},{20,16},{24,28},{28,24},{1,5},{5... | collective-permute-start | bytes 393224 | tf_op jit(solution)/shard_map/ppermute | solution.py:19
  33.0 5.0 %collective-permute-start.3 = (f32[256,128]{1,0:T(8,128)S(1)}, f32[256,128]{1,0:T(8,128)S(1)}, u32[]{:S(2)}, u32[]{:S(2)}) collective-permute-start(f32[256,128]{1,0:T(8,128)S(1)} %add.899), channel_id=1, source_target_pairs={{0,8},{4,12},{8,0},{12,4},{16,24},{20,28},{24,16},{28,20},{1,9},{5... | collective-permute-start | bytes 393224 | tf_op jit(solution)/shard_map/ppermute | solution.py:19
  38.0 7.3 %collective-permute-start.4 = (f32[256,128]{1,0:T(8,128)S(1)}, f32[256,128]{1,0:T(8,128)S(1)}, u32[]{:S(2)}, u32[]{:S(2)}) collective-permute-start(f32[256,128]{1,0:T(8,128)S(1)} %add.900), channel_id=1, source_target_pairs={{0,16},{4,20},{8,24},{12,28},{16,0},{20,4},{24,8},{28,12},{1,17},{... | collective-permute-start | bytes 393224 | tf_op jit(solution)/shard_map/ppermute | solution.py:19
  45.4 5.0 %collective-permute-start.5 = (f32[256,128]{1,0:T(8,128)S(1)}, f32[256,128]{1,0:T(8,128)S(1)}, u32[]{:S(2)}, u32[]{:S(2)}) collective-permute-start(f32[256,128]{1,0:T(8,128)S(1)} %add.901), channel_id=1, source_target_pairs={{0,2},{1,3},{2,0},{3,1},{4,6},{5,7},{6,4},{7,5},{8,10},{9,11},{10,... | collective-permute-start | bytes 393224 | tf_op jit(solution)/shard_map/ppermute | solution.py:65
  50.4 1.6 %collective-permute-start.6 = (f32[2,256,128]{2,1,0:T(8,128)S(1)}, f32[2,256,128]{2,1,0:T(8,128)S(1)}, u32[]{:S(2)}, u32[]{:S(2)}) collective-permute-start(f32[2,256,128]{2,1,0:T(8,128)S(1)} %maximum_select_fusion.2), channel_id=1, source_target_pairs={{0,1},{1,0},{2,3},{3,2},{4,5},{5,4},{6,7},{7,6},{8,9},{9,8},{10,11... | collective-permute-start | bytes 786440 | tf_op jit(solution)/shard_map/ppermute | solution.py:65
  50.6 11.1 %copy-start.1 = (f32[32,128]{1,0:T(8,128)S(1)}, f32[32,128]{1,0:T(8,128)}, u32[]{:S(2)}) copy-start(f32[32,128]{1,0:T(8,128)} %param.10) | copy-start | bytes 49156
  50.6 14.4 %copy-start = (f32[64,128]{1,0:T(8,128)S(1)}, f32[64,128]{1,0:T(8,128)}, u32[]{:S(2)}) copy-start(f32[64,128]{1,0:T(8,128)} %param.6) | copy-start | bytes 98308
  56.6 4.5 %collective-permute-start.7 = (f32[48,128]{1,0:T(8,128)S(1)}, f32[48,128]{1,0:T(8,128)S(1)}, u32[]{:S(2)}, u32[]{:S(2)}) collective-permute-start(f32[48,128]{1,0:T(8,128)S(1)} %bitcast.301), channel_id=1, source_target_pairs={{0,1},{1,0},{2,3},{3,2},{4,5},{5,4},{6,7},{7,6},{8,9},{9,8},{10,11... | collective-permute-start | bytes 73736 | tf_op jit(solution)/shard_map/ppermute | solution.py:19
  58.4 1.2 collective-permute-start.9
  59.6 3.7 %collective-permute-start.10 = (f32[16,128]{1,0:T(8,128)S(1)}, f32[16,128]{1,0:T(8,128)S(1)}, u32[]{:S(2)}, u32[]{:S(2)}) collective-permute-start(f32[16,128]{1,0:T(8,128)S(1)} %add.904), channel_id=1, source_target_pairs={{0,2},{1,3},{2,0},{3,1},{4,6},{5,7},{6,4},{7,5},{8,10},{9,11},{10,... | collective-permute-start | bytes 24584 | tf_op jit(solution)/shard_map/ppermute | solution.py:19
  61.1 3.9 %collective-permute-start.8 = (f32[48,128]{1,0:T(8,128)S(1)}, f32[48,128]{1,0:T(8,128)S(1)}, u32[]{:S(2)}, u32[]{:S(2)}) collective-permute-start(f32[48,128]{1,0:T(8,128)S(1)} %add.902), channel_id=1, source_target_pairs={{0,2},{1,3},{2,0},{3,1},{4,6},{5,7},{6,4},{7,5},{8,10},{9,11},{10,... | collective-permute-start | bytes 73736 | tf_op jit(solution)/shard_map/ppermute | solution.py:19
  79.4 1.6 %collective-permute-start.11 = (f32[2,256,128]{2,1,0:T(8,128)S(1)}, f32[2,256,128]{2,1,0:T(8,128)S(1)}, u32[]{:S(2)}, u32[]{:S(2)}) collective-permute-start(f32[2,256,128]{2,1,0:T(8,128)S(1)} %dynamic-slice_bitcast_fusion), channel_id=1, source_target_pairs={{0,1},{1,0},{2,3},{3,2},{4,5},{5,4},{6,7},{7,6},{8,9},{9,8},{10,11... | collective-permute-start | bytes 786440 | tf_op jit(solution)/shard_map/ppermute | solution.py:52
  81.1 5.6 %collective-permute-start.12 = (f32[256,128]{1,0:T(8,128)S(1)}, f32[256,128]{1,0:T(8,128)S(1)}, u32[]{:S(2)}, u32[]{:S(2)}) collective-permute-start(f32[256,128]{1,0:T(8,128)S(1)} %dynamic-slice_bitcast_fusion.2), channel_id=1, source_target_pairs={{0,2},{1,3},{2,0},{3,1},{4,6},{5,7},{6,4},{7,5},{8,10},{9,11},{10,... | collective-permute-start | bytes 393224 | tf_op jit(solution)/shard_map/ppermute | solution.py:52
  86.7 5.0 %collective-permute-start.13 = (f32[256,128]{1,0:T(8,128)S(1)}, f32[256,128]{1,0:T(8,128)S(1)}, u32[]{:S(2)}, u32[]{:S(2)}) collective-permute-start(f32[256,128]{1,0:T(8,128)S(1)} %bitcast_add_fusion.2), channel_id=1, source_target_pairs={{0,4},{4,0},{8,12},{12,8},{16,20},{20,16},{24,28},{28,24},{1,5},{5... | collective-permute-start | bytes 393224 | tf_op jit(solution)/shard_map/ppermute | solution.py:19
  91.8 5.0 %collective-permute-start.14 = (f32[256,128]{1,0:T(8,128)S(1)}, f32[256,128]{1,0:T(8,128)S(1)}, u32[]{:S(2)}, u32[]{:S(2)}) collective-permute-start(f32[256,128]{1,0:T(8,128)S(1)} %add.943), channel_id=1, source_target_pairs={{0,8},{4,12},{8,0},{12,4},{16,24},{20,28},{24,16},{28,20},{1,9},{5... | collective-permute-start | bytes 393224 | tf_op jit(solution)/shard_map/ppermute | solution.py:19
  96.8 7.3 %collective-permute-start.15 = (f32[256,128]{1,0:T(8,128)S(1)}, f32[256,128]{1,0:T(8,128)S(1)}, u32[]{:S(2)}, u32[]{:S(2)}) collective-permute-start(f32[256,128]{1,0:T(8,128)S(1)} %add.944), channel_id=1, source_target_pairs={{0,16},{4,20},{8,24},{12,28},{16,0},{20,4},{24,8},{28,12},{1,17},{... | collective-permute-start | bytes 393224 | tf_op jit(solution)/shard_map/ppermute | solution.py:19
  104.2 5.0 %collective-permute-start.16 = (f32[256,128]{1,0:T(8,128)S(1)}, f32[256,128]{1,0:T(8,128)S(1)}, u32[]{:S(2)}, u32[]{:S(2)}) collective-permute-start(f32[256,128]{1,0:T(8,128)S(1)} %multiply_subtract_fusion), channel_id=1, source_target_pairs={{0,2},{1,3},{2,0},{3,1},{4,6},{5,7},{6,4},{7,5},{8,10},{9,11},{10,... | collective-permute-start | bytes 393224 | tf_op jit(solution)/shard_map/ppermute | solution.py:65
  109.2 1.6 %collective-permute-start.17 = (f32[2,256,128]{2,1,0:T(8,128)S(1)}, f32[2,256,128]{2,1,0:T(8,128)S(1)}, u32[]{:S(2)}, u32[]{:S(2)}) collective-permute-start(f32[2,256,128]{2,1,0:T(8,128)S(1)} %maximum_select_fusion.4), channel_id=1, source_target_pairs={{0,1},{1,0},{2,3},{3,2},{4,5},{5,4},{6,7},{7,6},{8,9},{9,8},{10,11... | collective-permute-start | bytes 786440 | tf_op jit(solution)/shard_map/ppermute | solution.py:65
  115.4 3.5 %collective-permute-start.18 = (f32[48,128]{1,0:T(8,128)S(1)}, f32[48,128]{1,0:T(8,128)S(1)}, u32[]{:S(2)}, u32[]{:S(2)}) collective-permute-start(f32[48,128]{1,0:T(8,128)S(1)} %bitcast.303), channel_id=1, source_target_pairs={{0,1},{1,0},{2,3},{3,2},{4,5},{5,4},{6,7},{7,6},{8,9},{9,8},{10,11... | collective-permute-start | bytes 73736 | tf_op jit(solution)/shard_map/ppermute | solution.py:19
  117.1 1.2 collective-permute-start.20
  118.4 3.7 %collective-permute-start.21 = (f32[16,128]{1,0:T(8,128)S(1)}, f32[16,128]{1,0:T(8,128)S(1)}, u32[]{:S(2)}, u32[]{:S(2)}) collective-permute-start(f32[16,128]{1,0:T(8,128)S(1)} %add.948), channel_id=1, source_target_pairs={{0,2},{1,3},{2,0},{3,1},{4,6},{5,7},{6,4},{7,5},{8,10},{9,11},{10,... | collective-permute-start | bytes 24584 | tf_op jit(solution)/shard_map/ppermute | solution.py:19
  118.9 3.9 %collective-permute-start.19 = (f32[48,128]{1,0:T(8,128)S(1)}, f32[48,128]{1,0:T(8,128)S(1)}, u32[]{:S(2)}, u32[]{:S(2)}) collective-permute-start(f32[48,128]{1,0:T(8,128)S(1)} %add.946), channel_id=1, source_target_pairs={{0,2},{1,3},{2,0},{3,1},{4,6},{5,7},{6,4},{7,5},{8,10},{9,11},{10,... | collective-permute-start | bytes 73736 | tf_op jit(solution)/shard_map/ppermute | solution.py:19
  123.6 9.6 %all-to-all-start.2 = ((f32[32,1,128]{2,1,0:T(1,128)}), f32[32,1,128]{2,1,0:T(1,128)S(1)}, u32[]{:S(2)}, u32[]{:S(2)}) async-start(f32[32,1,128]{2,1,0:T(1,128)} %bitcast.75), calls=%async_computation.2 | async-start | bytes 32768 | tf_op jit(solution)/shard_map/all_to_all | solution.py:30

commit v17 on v12

--- a/solution.py
+++ b/solution.py
@@ -10,14 +10,13 @@
 smooth_weight = 1.0
 
 
-def butterfly_sum(x, axis):
+def butterfly_sum(x, axis, reverse=False):
     n = lax.axis_size(axis)
     if n & (n - 1):
         return lax.psum(x, axis)
-    k = 1
-    while k < n:
+    steps = [1 << j for j in range(n.bit_length() - 1)]
+    for k in steps[::-1] if reverse else steps:
         x = x + lax.ppermute(x, axis, [(i, i ^ k) for i in range(n)])
-        k *= 2
     return x
 
 
@@ -144,7 +143,7 @@
                 picked[lo:lo + half_tiles],
                 preferred_element_type=jnp.float32,
             )
-            halves.append(butterfly_sum(part, "region"))
+            halves.append(butterfly_sum(part, "region", reverse=len(halves) % 2 == 1))
         ray_pred = jnp.concatenate(halves, 0) if len(halves) > 1 else halves[0]
         face_pred = face_scale * rows[n_slots:]
         left_faces = face_pred - alpha_value * left_faces

time: 132 us -> 134 us (1.015)
  no operation moved by 1% of the time
where the time goes in v17:
time: 134 us; the launch traced here: 133 us
  waiting for transfers between devices  69.7 us (52%)
  starting transfers between devices  23.5 us (18%)
  matrix products  15.6 us (12%)
  blocking collectives  10.4 us (8%)
  other arithmetic  7.13 us (5%)
  between operations  4.9 us (4%)
  local copies, waits for them, and re-layouts  1.83 us (1%)
    ppermute x14, waiting for transfers between devices, butterfly_sum(): x = x + lax.ppermute(x, axis, [(i, i ^ k) for i in range(n)])  37.6 us
    ppermute x4, waiting for transfers between devices, halving_scatter(): x = keep + lax.ppermute(send, axis, [(i, i ^ k) for i in range(n)])  12.1 us
    ppermute x4, waiting for transfers between devices, doubling_gather(): other = lax.ppermute(x, axis, [(i, i ^ k) for i in range(n)])  10.7 us
    all_to_all x1, blocking collectives, square_sum(): got = lax.all_to_all(spread[:, None, :], axis, 0, 0, tiled=False)  10.4 us
    all_to_all x2, starting transfers between devices, square_sum(): got = lax.all_to_all(spread[:, None, :], axis, 0, 0, tiled=False)  9.82 us
    all_to_all x2, waiting for transfers between devices, square_sum(): got = lax.all_to_all(spread[:, None, :], axis, 0, 0, tiled=False)  9.46 us
    ppermute x14, starting transfers between devices, butterfly_sum(): x = x + lax.ppermute(x, axis, [(i, i ^ k) for i in range(n)])  9.1 us
    dot_general x4, matrix products, local(): jnp.einsum('tsrb,tsb->tr', sensitivity[lo:lo + half_tiles], picked[lo:lo...  6.09 us
  transfers between devices with their start and end apart: 24, of which 21 were waited for; matrix products, arithmetic and copies ran while one was open for 4% of the time, Pallas kernels for 0%

profile of v17, /device:TPU:0, one launch (start us, length us, event | category | flops | bytes accessed | tf_op | source)
XLA Modules:
  0.0 133.0 jit_solution(7612342317166692327)
XLA Ops:
  0.0 1.5 %fusion.39 = f32[8,128]{1,0:T(8,128)} fusion(f32[64,128]{1,0:T(8,128)} %param.6), kind=kOutput, calls=%fused_computation.76 | convolution fusion | flops 794624 | bytes 36864 | tf_op jit(solution)/shard_map/dot_general | solution.py:26
  1.5 7.3 %all-to-all-start = ((f32[8,1,128]{2,1,0:T(1,128)}), f32[8,1,128]{2,1,0:T(1,128)S(1)}, u32[]{:S(2)}, u32[]{:S(2)}) async-start(f32[8,1,128]{2,1,0:T(1,128)} %bitcast.3), calls=%async_computation | async-start | bytes 8192 | tf_op jit(solution)/shard_map/all_to_all | solution.py:29
  8.8 0.8 copy.14
  9.8 0.8 slice_bitcast_fusion.31
  11.8 0.8 multiply_multiply_fusion.1
  12.6 2.6 %all-to-all-done = f32[8,1,128]{2,1,0:T(1,128)S(1)} async-done(((f32[8,1,128]{2,1,0:T(1,128)}), f32[8,1,128]{2,1,0:T(1,128)S(1)}, u32[]{:S(2)}, u32[]{:S(2)}) %all-to-all-start) | async-done | bytes 4128 | tf_op jit(solution)/shard_map/all_to_all | solution.py:29
  16.5 0.8 convert_bitcast_fusion.1
  17.2 2.8 %fusion.37 = f32[64,1,2,128]{3,1,2,0:T(1,128)S(1)} fusion(bf16[64,2,128,128]{3,2,1,0:T(8,128)(2,1)} %param.7, bf16[64,128,1,1]{1,0,2,3:T(8,128)(2,1)S(1)} %convert_bitcast_fusion.1), kind=kOutput, calls=%fused_computation.74 | convolution fusion | flops 4194304 | bytes 4276224 | tf_op jit(solution)/shard_map/tsrb,tr->tsb/dot_general | solution.py:97
  20.7 1.5 %collective-permute-done = f32[2,256,128]{2,1,0:T(8,128)S(1)} collective-permute-done((f32[2,256,128]{2,1,0:T(8,128)S(1)}, f32[2,256,128]{2,1,0:T(8,128)S(1)}, u32[]{:S(2)}, u32[]{:S(2)}) %collective-permute-start) | collective-permute-done | bytes 262176 | tf_op jit(solution)/shard_map/ppermute | solution.py:51
  22.3 1.6 %collective-permute-start.1 = (f32[256,128]{1,0:T(8,128)S(1)}, f32[256,128]{1,0:T(8,128)S(1)}, u32[]{:S(2)}, u32[]{:S(2)}) collective-permute-start(f32[256,128]{1,0:T(8,128)S(1)} %dynamic-slice_bitcast_fusion.3), channel_id=1, source_target_pairs={{0,2},{1,3},{2,0},{3,1},{4,6},{5,7},{6,4},{7,5},{8,10},{9,11},{10,... | collective-permute-start | bytes 393224 | tf_op jit(solution)/shard_map/ppermute | solution.py:51
  23.8 4.0 %collective-permute-done.1 = f32[256,128]{1,0:T(8,128)S(1)} collective-permute-done((f32[256,128]{1,0:T(8,128)S(1)}, f32[256,128]{1,0:T(8,128)S(1)}, u32[]{:S(2)}, u32[]{:S(2)}) %collective-permute-start.1) | collective-permute-done | bytes 131104 | tf_op jit(solution)/shard_map/ppermute | solution.py:51
  27.9 0.6 collective-permute-start.2
  28.5 4.4 %collective-permute-done.2 = f32[256,128]{1,0:T(8,128)S(1)} collective-permute-done((f32[256,128]{1,0:T(8,128)S(1)}, f32[256,128]{1,0:T(8,128)S(1)}, u32[]{:S(2)}, u32[]{:S(2)}) %collective-permute-start.2) | collective-permute-done | bytes 131104 | tf_op jit(solution)/shard_map/ppermute | solution.py:19
  33.6 4.4 %collective-permute-done.3 = f32[256,128]{1,0:T(8,128)S(1)} collective-permute-done((f32[256,128]{1,0:T(8,128)S(1)}, f32[256,128]{1,0:T(8,128)S(1)}, u32[]{:S(2)}, u32[]{:S(2)}) %collective-permute-start.3) | collective-permute-done | bytes 131104 | tf_op jit(solution)/shard_map/ppermute | solution.py:19
  38.0 0.6 collective-permute-start.4
  38.6 6.7 %collective-permute-done.4 = f32[256,128]{1,0:T(8,128)S(1)} collective-permute-done((f32[256,128]{1,0:T(8,128)S(1)}, f32[256,128]{1,0:T(8,128)S(1)}, u32[]{:S(2)}, u32[]{:S(2)}) %collective-permute-start.4) | collective-permute-done | bytes 131104 | tf_op jit(solution)/shard_map/ppermute | solution.py:19
  45.4 1.6 %collective-permute-start.5 = (f32[256,128]{1,0:T(8,128)S(1)}, f32[256,128]{1,0:T(8,128)S(1)}, u32[]{:S(2)}, u32[]{:S(2)}) collective-permute-start(f32[256,128]{1,0:T(8,128)S(1)} %add.901), channel_id=1, source_target_pairs={{0,2},{1,3},{2,0},{3,1},{4,6},{5,7},{6,4},{7,5},{8,10},{9,11},{10,... | collective-permute-start | bytes 393224 | tf_op jit(solution)/shard_map/ppermute | solution.py:64
  47.0 3.4 %collective-permute-done.5 = f32[256,128]{1,0:T(8,128)S(1)} collective-permute-done((f32[256,128]{1,0:T(8,128)S(1)}, f32[256,128]{1,0:T(8,128)S(1)}, u32[]{:S(2)}, u32[]{:S(2)}) %collective-permute-start.5) | collective-permute-done | bytes 131104 | tf_op jit(solution)/shard_map/ppermute | solution.py:64
  50.7 1.4 %collective-permute-done.6 = f32[2,256,128]{2,1,0:T(8,128)S(1)} collective-permute-done((f32[2,256,128]{2,1,0:T(8,128)S(1)}, f32[2,256,128]{2,1,0:T(8,128)S(1)}, u32[]{:S(2)}, u32[]{:S(2)}) %collective-permute-start.6) | collective-permute-done | bytes 262176 | tf_op jit(solution)/shard_map/ppermute | solution.py:64
  52.0 0.7 multiply_reduce_fusion.1
  53.8 2.4 %fusion.2 = f32[32,1,128,1]{2,1,3,0:T(1,128)S(1)} fusion(bf16[64,2,128,128]{3,2,1,0:T(8,128)(2,1)} %param.7, bf16[32,2,128,1]{2,1,0,3:T(2,128)(2,1)S(1)} %bitcast.309), kind=kOutput, calls=%fused_computation.2 | convolution fusion | flops 2097152 | bytes 2129920 | tf_op jit(solution)/shard_map/tsrb,tsb->tr/dot_general | solution.py:140
  56.2 1.5 %collective-permute-start.9 = (f32[32,128]{1,0:T(8,128)S(1)}, f32[32,128]{1,0:T(8,128)S(1)}, u32[]{:S(2)}, u32[]{:S(2)}) collective-permute-start(f32[32,128]{1,0:T(8,128)S(1)} %bitcast.301), channel_id=1, source_target_pairs={{0,2},{1,3},{2,0},{3,1},{4,6},{5,7},{6,4},{7,5},{8,10},{9,11},{10,... | collective-permute-start | bytes 49160 | tf_op jit(solution)/shard_map/ppermute | solution.py:19
  57.7 0.6 fusion.6
  58.4 1.6 %collective-permute-done.9 = f32[32,128]{1,0:T(8,128)S(1)} collective-permute-done((f32[32,128]{1,0:T(8,128)S(1)}, f32[32,128]{1,0:T(8,128)S(1)}, u32[]{:S(2)}, u32[]{:S(2)}) %collective-permute-start.9) | collective-permute-done | bytes 16416 | tf_op jit(solution)/shard_map/ppermute | solution.py:19
  60.0 1.6 %collective-permute-start.8 = (f32[32,128]{1,0:T(8,128)S(1)}, f32[32,128]{1,0:T(8,128)S(1)}, u32[]{:S(2)}, u32[]{:S(2)}) collective-permute-start(f32[32,128]{1,0:T(8,128)S(1)} %add.902), channel_id=1, source_target_pairs={{0,2},{1,3},{2,0},{3,1},{4,6},{5,7},{6,4},{7,5},{8,10},{9,11},{10,... | collective-permute-start | bytes 49160 | tf_op jit(solution)/shard_map/ppermute | solution.py:19
  61.7 2.2 %collective-permute-done.8 = f32[32,128]{1,0:T(8,128)S(1)} collective-permute-done((f32[32,128]{1,0:T(8,128)S(1)}, f32[32,128]{1,0:T(8,128)S(1)}, u32[]{:S(2)}, u32[]{:S(2)}) %collective-permute-start.8) | collective-permute-done | bytes 16416 | tf_op jit(solution)/shard_map/ppermute | solution.py:19
  64.0 10.4 %all_to_all.15 = f32[32,1,128]{2,1,0:T(1,128)S(1)} all-to-all(f32[32,1,128]{2,1,0:T(1,128)S(1)} %bitcast.298), channel_id=1, replica_groups=mesh['dp'=8,'region'=4] {'dp','region'}, dimensions={0} | all-to-all | bytes 32768 | tf_op jit(solution)/shard_map/all_to_all | solution.py:29
  74.4 0.6 fusion.75
  75.8 2.8 %fusion.33 = f32[64,1,2,128]{3,1,2,0:T(1,128)S(1)} fusion(bf16[64,2,128,128]{3,2,1,0:T(8,128)(2,1)} %param.7, bf16[64,128,1,1]{1,0,2,3:T(8,128)(2,1)S(1)} %get-tuple-element.5), kind=kOutput, calls=%fused_computation.70 | convolution fusion | flops 4194304 | bytes 4276224 | tf_op jit(solution)/shard_map/tsrb,tr->tsb/dot_general | solution.py:97
  79.3 1.5 %collective-permute-done.11 = f32[2,256,128]{2,1,0:T(8,128)S(1)} collective-permute-done((f32[2,256,128]{2,1,0:T(8,128)S(1)}, f32[2,256,128]{2,1,0:T(8,128)S(1)}, u32[]{:S(2)}, u32[]{:S(2)}) %collective-permute-start.11) | collective-permute-done | bytes 262176 | tf_op jit(solution)/shard_map/ppermute | solution.py:51
  81.4 5.0 %collective-permute-done.12 = f32[256,128]{1,0:T(8,128)S(1)} collective-permute-done((f32[256,128]{1,0:T(8,128)S(1)}, f32[256,128]{1,0:T(8,128)S(1)}, u32[]{:S(2)}, u32[]{:S(2)}) %collective-permute-start.12) | collective-permute-done | bytes 131104 | tf_op jit(solution)/shard_map/ppermute | solution.py:51
  87.1 4.4 %collective-permute-done.13 = f32[256,128]{1,0:T(8,128)S(1)} collective-permute-done((f32[256,128]{1,0:T(8,128)S(1)}, f32[256,128]{1,0:T(8,128)S(1)}, u32[]{:S(2)}, u32[]{:S(2)}) %collective-permute-start.13) | collective-permute-done | bytes 131104 | tf_op jit(solution)/shard_map/ppermute | solution.py:19
  91.5 0.6 collective-permute-start.14
  92.2 4.4 %collective-permute-done.14 = f32[256,128]{1,0:T(8,128)S(1)} collective-permute-done((f32[256,128]{1,0:T(8,128)S(1)}, f32[256,128]{1,0:T(8,128)S(1)}, u32[]{:S(2)}, u32[]{:S(2)}) %collective-permute-start.14) | collective-permute-done | bytes 131104 | tf_op jit(solution)/shard_map/ppermute | solution.py:19
  96.6 0.7 collective-permute-start.15
  97.2 6.7 %collective-permute-done.15 = f32[256,128]{1,0:T(8,128)S(1)} collective-permute-done((f32[256,128]{1,0:T(8,128)S(1)}, f32[256,128]{1,0:T(8,128)S(1)}, u32[]{:S(2)}, u32[]{:S(2)}) %collective-permute-start.15) | collective-permute-done | bytes 131104 | tf_op jit(solution)/shard_map/ppermute | solution.py:19
  104.5 4.4 %collective-permute-done.16 = f32[256,128]{1,0:T(8,128)S(1)} collective-permute-done((f32[256,128]{1,0:T(8,128)S(1)}, f32[256,128]{1,0:T(8,128)S(1)}, u32[]{:S(2)}, u32[]{:S(2)}) %collective-permute-start.16) | collective-permute-done | bytes 131104 | tf_op jit(solution)/shard_map/ppermute | solution.py:64
  109.1 1.5 %collective-permute-done.17 = f32[2,256,128]{2,1,0:T(8,128)S(1)} collective-permute-done((f32[2,256,128]{2,1,0:T(8,128)S(1)}, f32[2,256,128]{2,1,0:T(8,128)S(1)}, u32[]{:S(2)}, u32[]{:S(2)}) %collective-permute-start.17) | collective-permute-done | bytes 262176 | tf_op jit(solution)/shard_map/ppermute | solution.py:64
  110.6 0.7 multiply_reduce_fusion
  112.3 2.4 %fusion.4 = f32[32,1,128,1]{2,1,3,0:T(1,128)S(1)} fusion(bf16[64,2,128,128]{3,2,1,0:T(8,128)(2,1)} %param.7, bf16[32,2,128,1]{2,1,0,3:T(2,128)(2,1)S(1)} %bitcast.310), kind=kOutput, calls=%fused_computation.4 | convolution fusion | flops 2097152 | bytes 2129920 | tf_op jit(solution)/shard_map/tsrb,tsb->tr/dot_general | solution.py:140
  114.9 0.6 fusion
  116.1 1.6 %collective-permute-start.19 = (f32[32,128]{1,0:T(8,128)S(1)}, f32[32,128]{1,0:T(8,128)S(1)}, u32[]{:S(2)}, u32[]{:S(2)}) collective-permute-start(f32[32,128]{1,0:T(8,128)S(1)} %add.946), channel_id=1, source_target_pairs={{0,2},{1,3},{2,0},{3,1},{4,6},{5,7},{6,4},{7,5},{8,10},{9,11},{10,... | collective-permute-start | bytes 49160 | tf_op jit(solution)/shard_map/ppermute | solution.py:19
  117.7 1.6 %collective-permute-done.20 = f32[32,128]{1,0:T(8,128)S(1)} collective-permute-done((f32[32,128]{1,0:T(8,128)S(1)}, f32[32,128]{1,0:T(8,128)S(1)}, u32[]{:S(2)}, u32[]{:S(2)}) %collective-permute-start.20) | collective-permute-done | bytes 16416 | tf_op jit(solution)/shard_map/ppermute | solution.py:19
  120.5 0.8 fusion.47
  121.3 2.5 %all-to-all-start.2 = ((f32[32,1,128]{2,1,0:T(1,128)}), f32[32,1,128]{2,1,0:T(1,128)S(1)}, u32[]{:S(2)}, u32[]{:S(2)}) async-start(f32[32,1,128]{2,1,0:T(1,128)} %bitcast.75), calls=%async_computation.2 | async-start | bytes 32768 | tf_op jit(solution)/shard_map/all_to_all | solution.py:29
  124.0 6.8 %all-to-all-done.2 = f32[32,1,128]{2,1,0:T(1,128)S(1)} async-done(((f32[32,1,128]{2,1,0:T(1,128)}), f32[32,1,128]{2,1,0:T(1,128)S(1)}, u32[]{:S(2)}, u32[]{:S(2)}) %all-to-all-start.2) | async-done | bytes 16416 | tf_op jit(solution)/shard_map/all_to_all | solution.py:29
  130.9 0.6 fusion.58
  132.4 0.7 multiply_add_fusion
  (82 shorter events, 8.5 us)
Async XLA Ops:
  1.5 13.7 %all-to-all-start = ((f32[8,1,128]{2,1,0:T(1,128)}), f32[8,1,128]{2,1,0:T(1,128)S(1)}, u32[]{:S(2)}, u32[]{:S(2)}) async-start(f32[8,1,128]{2,1,0:T(1,128)} %bitcast.3), calls=%async_computation | async-start | bytes 8192 | tf_op jit(solution)/shard_map/all_to_all | solution.py:29
  20.6 1.6 %collective-permute-start = (f32[2,256,128]{2,1,0:T(8,128)S(1)}, f32[2,256,128]{2,1,0:T(8,128)S(1)}, u32[]{:S(2)}, u32[]{:S(2)}) collective-permute-start(f32[2,256,128]{2,1,0:T(8,128)S(1)} %dynamic-slice_bitcast_fusion.1), channel_id=1, source_target_pairs={{0,1},{1,0},{2,3},{3,2},{4,5},{5,4},{6,7},{7,6},{8,9},{9,8},{10,11... | collective-permute-start | bytes 786440 | tf_op jit(solution)/shard_map/ppermute | solution.py:51
  22.3 5.6 %collective-permute-start.1 = (f32[256,128]{1,0:T(8,128)S(1)}, f32[256,128]{1,0:T(8,128)S(1)}, u32[]{:S(2)}, u32[]{:S(2)}) collective-permute-start(f32[256,128]{1,0:T(8,128)S(1)} %dynamic-slice_bitcast_fusion.3), channel_id=1, source_target_pairs={{0,2},{1,3},{2,0},{3,1},{4,6},{5,7},{6,4},{7,5},{8,10},{9,11},{10,... | collective-permute-start | bytes 393224 | tf_op jit(solution)/shard_map/ppermute | solution.py:51
  27.9 5.0 %collective-permute-start.2 = (f32[256,128]{1,0:T(8,128)S(1)}, f32[256,128]{1,0:T(8,128)S(1)}, u32[]{:S(2)}, u32[]{:S(2)}) collective-permute-start(f32[256,128]{1,0:T(8,128)S(1)} %bitcast_add_fusion.3), channel_id=1, source_target_pairs={{0,4},{4,0},{8,12},{12,8},{16,20},{20,16},{24,28},{28,24},{1,5},{5... | collective-permute-start | bytes 393224 | tf_op jit(solution)/shard_map/ppermute | solution.py:19
  33.0 5.0 %collective-permute-start.3 = (f32[256,128]{1,0:T(8,128)S(1)}, f32[256,128]{1,0:T(8,128)S(1)}, u32[]{:S(2)}, u32[]{:S(2)}) collective-permute-start(f32[256,128]{1,0:T(8,128)S(1)} %add.899), channel_id=1, source_target_pairs={{0,8},{4,12},{8,0},{12,4},{16,24},{20,28},{24,16},{28,20},{1,9},{5... | collective-permute-start | bytes 393224 | tf_op jit(solution)/shard_map/ppermute | solution.py:19
  38.0 7.3 %collective-permute-start.4 = (f32[256,128]{1,0:T(8,128)S(1)}, f32[256,128]{1,0:T(8,128)S(1)}, u32[]{:S(2)}, u32[]{:S(2)}) collective-permute-start(f32[256,128]{1,0:T(8,128)S(1)} %add.900), channel_id=1, source_target_pairs={{0,16},{4,20},{8,24},{12,28},{16,0},{20,4},{24,8},{28,12},{1,17},{... | collective-permute-start | bytes 393224 | tf_op jit(solution)/shard_map/ppermute | solution.py:19
  45.4 5.0 %collective-permute-start.5 = (f32[256,128]{1,0:T(8,128)S(1)}, f32[256,128]{1,0:T(8,128)S(1)}, u32[]{:S(2)}, u32[]{:S(2)}) collective-permute-start(f32[256,128]{1,0:T(8,128)S(1)} %add.901), channel_id=1, source_target_pairs={{0,2},{1,3},{2,0},{3,1},{4,6},{5,7},{6,4},{7,5},{8,10},{9,11},{10,... | collective-permute-start | bytes 393224 | tf_op jit(solution)/shard_map/ppermute | solution.py:64
  50.4 1.6 %collective-permute-start.6 = (f32[2,256,128]{2,1,0:T(8,128)S(1)}, f32[2,256,128]{2,1,0:T(8,128)S(1)}, u32[]{:S(2)}, u32[]{:S(2)}) collective-permute-start(f32[2,256,128]{2,1,0:T(8,128)S(1)} %maximum_select_fusion.2), channel_id=1, source_target_pairs={{0,1},{1,0},{2,3},{3,2},{4,5},{5,4},{6,7},{7,6},{8,9},{9,8},{10,11... | collective-permute-start | bytes 786440 | tf_op jit(solution)/shard_map/ppermute | solution.py:64
  50.6 11.0 %copy-start.3 = (f32[32,128]{1,0:T(8,128)S(1)}, f32[32,128]{1,0:T(8,128)}, u32[]{:S(2)}) copy-start(f32[32,128]{1,0:T(8,128)} %param.10) | copy-start | bytes 49156
  50.6 13.2 %copy-start.2 = (f32[64,128]{1,0:T(8,128)S(1)}, f32[64,128]{1,0:T(8,128)}, u32[]{:S(2)}) copy-start(f32[64,128]{1,0:T(8,128)} %param.6) | copy-start | bytes 98308
  53.5 4.3 %copy-start = (bf16[64,2,128,128]{3,2,1,0:T(8,128)(2,1)S(1)}, bf16[64,2,128,128]{3,2,1,0:T(8,128)(2,1)}, u32[]{:S(2)}) copy-start(bf16[64,2,128,128]{3,2,1,0:T(8,128)(2,1)} %param.7) | copy-start | bytes 12582916
  56.2 3.8 %collective-permute-start.9 = (f32[32,128]{1,0:T(8,128)S(1)}, f32[32,128]{1,0:T(8,128)S(1)}, u32[]{:S(2)}, u32[]{:S(2)}) collective-permute-start(f32[32,128]{1,0:T(8,128)S(1)} %bitcast.301), channel_id=1, source_target_pairs={{0,2},{1,3},{2,0},{3,1},{4,6},{5,7},{6,4},{7,5},{8,10},{9,11},{10,... | collective-permute-start | bytes 49160 | tf_op jit(solution)/shard_map/ppermute | solution.py:19
  58.4 1.6 %collective-permute-start.7 = (f32[32,128]{1,0:T(8,128)S(1)}, f32[32,128]{1,0:T(8,128)S(1)}, u32[]{:S(2)}, u32[]{:S(2)}) collective-permute-start(f32[32,128]{1,0:T(8,128)S(1)} %bitcast.299), channel_id=1, source_target_pairs={{0,1},{1,0},{2,3},{3,2},{4,5},{5,4},{6,7},{7,6},{8,9},{9,8},{10,11... | collective-permute-start | bytes 49160 | tf_op jit(solution)/shard_map/ppermute | solution.py:19
  60.0 1.7 %collective-permute-start.10 = (f32[32,128]{1,0:T(8,128)S(1)}, f32[32,128]{1,0:T(8,128)S(1)}, u32[]{:S(2)}, u32[]{:S(2)}) collective-permute-start(f32[32,128]{1,0:T(8,128)S(1)} %add.904), channel_id=1, source_target_pairs={{0,1},{1,0},{2,3},{3,2},{4,5},{5,4},{6,7},{7,6},{8,9},{9,8},{10,11... | collective-permute-start | bytes 49160 | tf_op jit(solution)/shard_map/ppermute | solution.py:19
  60.0 3.8 %collective-permute-start.8 = (f32[32,128]{1,0:T(8,128)S(1)}, f32[32,128]{1,0:T(8,128)S(1)}, u32[]{:S(2)}, u32[]{:S(2)}) collective-permute-start(f32[32,128]{1,0:T(8,128)S(1)} %add.902), channel_id=1, source_target_pairs={{0,2},{1,3},{2,0},{3,1},{4,6},{5,7},{6,4},{7,5},{8,10},{9,11},{10,... | collective-permute-start | bytes 49160 | tf_op jit(solution)/shard_map/ppermute | solution.py:19
  79.2 1.6 %collective-permute-start.11 = (f32[2,256,128]{2,1,0:T(8,128)S(1)}, f32[2,256,128]{2,1,0:T(8,128)S(1)}, u32[]{:S(2)}, u32[]{:S(2)}) collective-permute-start(f32[2,256,128]{2,1,0:T(8,128)S(1)} %dynamic-slice_bitcast_fusion), channel_id=1, source_target_pairs={{0,1},{1,0},{2,3},{3,2},{4,5},{5,4},{6,7},{7,6},{8,9},{9,8},{10,11... | collective-permute-start | bytes 786440 | tf_op jit(solution)/shard_map/ppermute | solution.py:51
  80.8 5.6 %collective-permute-start.12 = (f32[256,128]{1,0:T(8,128)S(1)}, f32[256,128]{1,0:T(8,128)S(1)}, u32[]{:S(2)}, u32[]{:S(2)}) collective-permute-start(f32[256,128]{1,0:T(8,128)S(1)} %dynamic-slice_bitcast_fusion.2), channel_id=1, source_target_pairs={{0,2},{1,3},{2,0},{3,1},{4,6},{5,7},{6,4},{7,5},{8,10},{9,11},{10,... | collective-permute-start | bytes 393224 | tf_op jit(solution)/shard_map/ppermute | solution.py:51
  86.5 5.0 %collective-permute-start.13 = (f32[256,128]{1,0:T(8,128)S(1)}, f32[256,128]{1,0:T(8,128)S(1)}, u32[]{:S(2)}, u32[]{:S(2)}) collective-permute-start(f32[256,128]{1,0:T(8,128)S(1)} %bitcast_add_fusion.2), channel_id=1, source_target_pairs={{0,4},{4,0},{8,12},{12,8},{16,20},{20,16},{24,28},{28,24},{1,5},{5... | collective-permute-start | bytes 393224 | tf_op jit(solution)/shard_map/ppermute | solution.py:19
  91.5 5.0 %collective-permute-start.14 = (f32[256,128]{1,0:T(8,128)S(1)}, f32[256,128]{1,0:T(8,128)S(1)}, u32[]{:S(2)}, u32[]{:S(2)}) collective-permute-start(f32[256,128]{1,0:T(8,128)S(1)} %add.943), channel_id=1, source_target_pairs={{0,8},{4,12},{8,0},{12,4},{16,24},{20,28},{24,16},{28,20},{1,9},{5... | collective-permute-start | bytes 393224 | tf_op jit(solution)/shard_map/ppermute | solution.py:19
  96.6 7.3 %collective-permute-start.15 = (f32[256,128]{1,0:T(8,128)S(1)}, f32[256,128]{1,0:T(8,128)S(1)}, u32[]{:S(2)}, u32[]{:S(2)}) collective-permute-start(f32[256,128]{1,0:T(8,128)S(1)} %add.944), channel_id=1, source_target_pairs={{0,16},{4,20},{8,24},{12,28},{16,0},{20,4},{24,8},{28,12},{1,17},{... | collective-permute-start | bytes 393224 | tf_op jit(solution)/shard_map/ppermute | solution.py:19
  103.9 5.0 %collective-permute-start.16 = (f32[256,128]{1,0:T(8,128)S(1)}, f32[256,128]{1,0:T(8,128)S(1)}, u32[]{:S(2)}, u32[]{:S(2)}) collective-permute-start(f32[256,128]{1,0:T(8,128)S(1)} %multiply_subtract_fusion), channel_id=1, source_target_pairs={{0,2},{1,3},{2,0},{3,1},{4,6},{5,7},{6,4},{7,5},{8,10},{9,11},{10,... | collective-permute-start | bytes 393224 | tf_op jit(solution)/shard_map/ppermute | solution.py:64
  109.0 1.6 %collective-permute-start.17 = (f32[2,256,128]{2,1,0:T(8,128)S(1)}, f32[2,256,128]{2,1,0:T(8,128)S(1)}, u32[]{:S(2)}, u32[]{:S(2)}) collective-permute-start(f32[2,256,128]{2,1,0:T(8,128)S(1)} %maximum_select_fusion.4), channel_id=1, source_target_pairs={{0,1},{1,0},{2,3},{3,2},{4,5},{5,4},{6,7},{7,6},{8,9},{9,8},{10,11... | collective-permute-start | bytes 786440 | tf_op jit(solution)/shard_map/ppermute | solution.py:64
  112.0 2.9 %copy-start.1 = (bf16[64,2,128,128]{3,2,1,0:T(8,128)(2,1)S(1)}, bf16[64,2,128,128]{3,2,1,0:T(8,128)(2,1)}, u32[]{:S(2)}) copy-start(bf16[64,2,128,128]{3,2,1,0:T(8,128)(2,1)} %param.7) | copy-start | bytes 12582916
  114.7 1.4 %collective-permute-start.18 = (f32[32,128]{1,0:T(8,128)S(1)}, f32[32,128]{1,0:T(8,128)S(1)}, u32[]{:S(2)}, u32[]{:S(2)}) collective-permute-start(f32[32,128]{1,0:T(8,128)S(1)} %bitcast.305), channel_id=1, source_target_pairs={{0,1},{1,0},{2,3},{3,2},{4,5},{5,4},{6,7},{7,6},{8,9},{9,8},{10,11... | collective-permute-start | bytes 49160 | tf_op jit(solution)/shard_map/ppermute | solution.py:19
  115.5 3.8 %collective-permute-start.20 = (f32[32,128]{1,0:T(8,128)S(1)}, f32[32,128]{1,0:T(8,128)S(1)}, u32[]{:S(2)}, u32[]{:S(2)}) collective-permute-start(f32[32,128]{1,0:T(8,128)S(1)} %bitcast.303), channel_id=1, source_target_pairs={{0,2},{1,3},{2,0},{3,1},{4,6},{5,7},{6,4},{7,5},{8,10},{9,11},{10,... | collective-permute-start | bytes 49160 | tf_op jit(solution)/shard_map/ppermute | solution.py:19
  116.1 3.8 %collective-permute-start.19 = (f32[32,128]{1,0:T(8,128)S(1)}, f32[32,128]{1,0:T(8,128)S(1)}, u32[]{:S(2)}, u32[]{:S(2)}) collective-permute-start(f32[32,128]{1,0:T(8,128)S(1)} %add.946), channel_id=1, source_target_pairs={{0,2},{1,3},{2,0},{3,1},{4,6},{5,7},{6,4},{7,5},{8,10},{9,11},{10,... | collective-permute-start | bytes 49160 | tf_op jit(solution)/shard_map/ppermute | solution.py:19
  119.3 1.2 collective-permute-start.21
  121.3 9.6 %all-to-all-start.2 = ((f32[32,1,128]{2,1,0:T(1,128)}), f32[32,1,128]{2,1,0:T(1,128)S(1)}, u32[]{:S(2)}, u32[]{:S(2)}) async-start(f32[32,1,128]{2,1,0:T(1,128)} %bitcast.75), calls=%async_computation.2 | async-start | bytes 32768 | tf_op jit(solution)/shard_map/all_to_all | solution.py:29

commit v18 on v12

--- a/solution.py
+++ b/solution.py
@@ -68,6 +68,30 @@
         x = jnp.where(upper, jnp.stack([other, x], place), jnp.stack([x, other], place))
         k //= 2
     return x.reshape((n * rows,) + x.shape[-1:])
+
+
+def gather_with_norm(x, axis):
+    n = lax.axis_size(axis)
+    if n & (n - 1):
+        field = lax.all_gather(x, axis, axis=0, tiled=True)
+        return field, jnp.sum(field * field)
+    me = lax.axis_index(axis)
+    rows = x.shape[0]
+    sums = jnp.sum(x * x, axis=(-2, -1))
+    k = n // 2
+    while k >= 1:
+        other = lax.ppermute(x, axis, [(i, i ^ k) for i in range(n)])
+        other_sums = jnp.sum(other * other, axis=(-2, -1))
+        upper = (me // k) % 2 == 1
+        place = x.ndim - 2
+        x = jnp.where(upper, jnp.stack([other, x], place), jnp.stack([x, other], place))
+        sums = jnp.where(upper, jnp.stack([other_sums, sums], place), jnp.stack([sums, other_sums], place))
+        k //= 2
+    sums = sums.reshape(n)
+    total = sums[0]
+    for j in range(1, n):
+        total = total + sums[j]
+    return x.reshape((n * rows,) + x.shape[-1:]), total
 
 
 def local(travel_times, sensitivity, tile_blocks, face_blocks, face_weights, face_count):
@@ -117,8 +141,8 @@
         return butterfly_sum(piece, "dp")
 
     def normalized_field(piece):
-        field = doubling_gather(piece, "region")
-        alpha = jnp.sqrt(jnp.sum(field * field))
+        field, squares = gather_with_norm(piece, "region")
+        alpha = jnp.sqrt(squares)
         field = field / alpha
         return field, lax.dynamic_slice_in_dim(field, region * NB_DEV, NB_DEV, 0), alpha
 

time: 132 us -> 139 us (1.053)
  between operations: 4.88 us -> 9.15 us
  other arithmetic: 7.12 us -> 11.2 us
  waiting for transfers between devices: 68.8 us -> 66.3 us
  local copies, waits for them, and re-layouts: 1.83 us -> 3.44 us
    ppermute x4, waiting for transfers between devices: 10.7 us -> 7.82 us  [gather_with_norm(): other = lax.ppermute(x, axis, [(i, i ^ k) for i in range(n)])]
    select_n x4 -> x8, other arithmetic: 0.08 us -> 2.8 us  [the longest x4 2.72 us: gather_with_norm(): jnp.where(upper, jnp.stack([other_sums, sums], place), jnp.stack([sums, o...]
    reduce_sum x2 -> x6, other arithmetic: 1.47 us -> 2.88 us  [the longest x4 1.61 us: gather_with_norm(): other_sums = jnp.sum(other * other, axis=(-2, -1))]
  transfers between devices with their start and end apart: 24 -> 24, of which waited for: 21 -> 21; matrix products, arithmetic and copies ran while one was open for 4% -> 6% of each run, Pallas kernels for 0% -> 0%
where the time goes in v18:
time: 139 us; the launch traced here: 138 us
  waiting for transfers between devices  66.3 us (48%)
  starting transfers between devices  23.2 us (17%)
  matrix products  15.2 us (11%)
  other arithmetic  11.2 us (8%)
  blocking collectives  9.81 us (7%)
  between operations  9.15 us (7%)
  local copies, waits for them, and re-layouts  3.44 us (2%)
    ppermute x14, waiting for transfers between devices, butterfly_sum(): x = x + lax.ppermute(x, axis, [(i, i ^ k) for i in range(n)])  37 us
    ppermute x4, waiting for transfers between devices, halving_scatter(): x = keep + lax.ppermute(send, axis, [(i, i ^ k) for i in range(n)])  12.1 us
    all_to_all x2, starting transfers between devices, square_sum(): got = lax.all_to_all(spread[:, None, :], axis, 0, 0, tiled=False)  9.82 us
    all_to_all x1, blocking collectives, square_sum(): got = lax.all_to_all(spread[:, None, :], axis, 0, 0, tiled=False)  9.81 us
    all_to_all x2, waiting for transfers between devices, square_sum(): got = lax.all_to_all(spread[:, None, :], axis, 0, 0, tiled=False)  9.46 us
    ppermute x14, starting transfers between devices, butterfly_sum(): x = x + lax.ppermute(x, axis, [(i, i ^ k) for i in range(n)])  8.96 us
    ppermute x4, waiting for transfers between devices, gather_with_norm(): other = lax.ppermute(x, axis, [(i, i ^ k) for i in range(n)])  7.82 us
    dot_general x4, matrix products, local(): jnp.einsum('tsrb,tsb->tr', sensitivity[lo:lo + half_tiles], picked[lo:lo...  5.75 us
  transfers between devices with their start and end apart: 24, of which 21 were waited for; matrix products, arithmetic and copies ran while one was open for 6% of the time, Pallas kernels for 0%

profile of v18, /device:TPU:0, one launch (start us, length us, event | category | flops | bytes accessed | tf_op | source)
XLA Modules:
  0.0 138.4 jit_solution(13378327292836591713)
XLA Ops:
  0.0 1.5 %fusion.39 = f32[8,128]{1,0:T(8,128)} fusion(f32[64,128]{1,0:T(8,128)} %param.6), kind=kOutput, calls=%fused_computation.80 | convolution fusion | flops 794624 | bytes 36864 | tf_op jit(solution)/shard_map/dot_general | solution.py:27
  1.5 7.3 %all-to-all-start = ((f32[8,1,128]{2,1,0:T(1,128)}), f32[8,1,128]{2,1,0:T(1,128)S(1)}, u32[]{:S(2)}, u32[]{:S(2)}) async-start(f32[8,1,128]{2,1,0:T(1,128)} %bitcast.3), calls=%async_computation | async-start | bytes 8192 | tf_op jit(solution)/shard_map/all_to_all | solution.py:30
  8.8 0.8 copy.18
  9.8 0.8 slice_bitcast_fusion.31
  11.8 0.8 multiply_multiply_fusion.1
  12.6 2.6 %all-to-all-done = f32[8,1,128]{2,1,0:T(1,128)S(1)} async-done(((f32[8,1,128]{2,1,0:T(1,128)}), f32[8,1,128]{2,1,0:T(1,128)S(1)}, u32[]{:S(2)}, u32[]{:S(2)}) %all-to-all-start) | async-done | bytes 4128 | tf_op jit(solution)/shard_map/all_to_all | solution.py:30
  16.5 0.8 convert_bitcast_fusion.1
  17.2 2.8 %fusion.37 = f32[64,1,2,128]{3,1,2,0:T(1,128)S(1)} fusion(bf16[64,2,128,128]{3,2,1,0:T(8,128)(2,1)} %param.7, bf16[64,128,1,1]{1,0,2,3:T(8,128)(2,1)S(1)} %convert_bitcast_fusion.1), kind=kOutput, calls=%fused_computation.78 | convolution fusion | flops 4194304 | bytes 4276224 | tf_op jit(solution)/shard_map/tsrb,tr->tsb/dot_general | solution.py:122
  20.7 1.5 %collective-permute-done = f32[2,256,128]{2,1,0:T(8,128)S(1)} collective-permute-done((f32[2,256,128]{2,1,0:T(8,128)S(1)}, f32[2,256,128]{2,1,0:T(8,128)S(1)}, u32[]{:S(2)}, u32[]{:S(2)}) %collective-permute-start) | collective-permute-done | bytes 262176 | tf_op jit(solution)/shard_map/ppermute | solution.py:52
  22.3 1.6 %collective-permute-start.1 = (f32[256,128]{1,0:T(8,128)S(1)}, f32[256,128]{1,0:T(8,128)S(1)}, u32[]{:S(2)}, u32[]{:S(2)}) collective-permute-start(f32[256,128]{1,0:T(8,128)S(1)} %dynamic-slice_bitcast_fusion.3), channel_id=1, source_target_pairs={{0,2},{1,3},{2,0},{3,1},{4,6},{5,7},{6,4},{7,5},{8,10},{9,11},{10,... | collective-permute-start | bytes 393224 | tf_op jit(solution)/shard_map/ppermute | solution.py:52
  23.8 4.0 %collective-permute-done.1 = f32[256,128]{1,0:T(8,128)S(1)} collective-permute-done((f32[256,128]{1,0:T(8,128)S(1)}, f32[256,128]{1,0:T(8,128)S(1)}, u32[]{:S(2)}, u32[]{:S(2)}) %collective-permute-start.1) | collective-permute-done | bytes 131104 | tf_op jit(solution)/shard_map/ppermute | solution.py:52
  28.5 4.4 %collective-permute-done.2 = f32[256,128]{1,0:T(8,128)S(1)} collective-permute-done((f32[256,128]{1,0:T(8,128)S(1)}, f32[256,128]{1,0:T(8,128)S(1)}, u32[]{:S(2)}, u32[]{:S(2)}) %collective-permute-start.2) | collective-permute-done | bytes 131104 | tf_op jit(solution)/shard_map/ppermute | solution.py:19
  33.6 4.4 %collective-permute-done.3 = f32[256,128]{1,0:T(8,128)S(1)} collective-permute-done((f32[256,128]{1,0:T(8,128)S(1)}, f32[256,128]{1,0:T(8,128)S(1)}, u32[]{:S(2)}, u32[]{:S(2)}) %collective-permute-start.3) | collective-permute-done | bytes 131104 | tf_op jit(solution)/shard_map/ppermute | solution.py:19
  38.7 6.6 %collective-permute-done.4 = f32[256,128]{1,0:T(8,128)S(1)} collective-permute-done((f32[256,128]{1,0:T(8,128)S(1)}, f32[256,128]{1,0:T(8,128)S(1)}, u32[]{:S(2)}, u32[]{:S(2)}) %collective-permute-start.4) | collective-permute-done | bytes 131104 | tf_op jit(solution)/shard_map/ppermute | solution.py:19
  45.3 0.6 multiply_reduce_fusion.4
  46.0 1.5 %collective-permute-start.5 = (f32[256,128]{1,0:T(8,128)S(1)}, f32[256,128]{1,0:T(8,128)S(1)}, u32[]{:S(2)}, u32[]{:S(2)}) collective-permute-start(f32[256,128]{1,0:T(8,128)S(1)} %get-tuple-element.10), channel_id=1, source_target_pairs={{0,2},{1,3},{2,0},{3,1},{4,6},{5,7},{6,4},{7,5},{8,10},{9,11},{10,... | collective-permute-start | bytes 393224 | tf_op jit(solution)/shard_map/ppermute | solution.py:83
  47.6 3.4 %collective-permute-done.5 = f32[256,128]{1,0:T(8,128)S(1)} collective-permute-done((f32[256,128]{1,0:T(8,128)S(1)}, f32[256,128]{1,0:T(8,128)S(1)}, u32[]{:S(2)}, u32[]{:S(2)}) %collective-permute-start.5) | collective-permute-done | bytes 131104 | tf_op jit(solution)/shard_map/ppermute | solution.py:83
  51.0 0.7 multiply_reduce_fusion.5
  51.7 1.3 broadcast_select_fusion.1
  53.5 0.6 fusion.104
  57.3 2.2 %fusion.2 = f32[32,1,128,1]{2,1,3,0:T(1,128)S(1)} fusion(bf16[64,2,128,128]{3,2,1,0:T(8,128)(2,1)} %param.7, bf16[32,2,128,1]{2,1,0,3:T(2,128)(2,1)S(1)} %bitcast.315), kind=kOutput, calls=%fused_computation.2 | convolution fusion | flops 2097152 | bytes 2129920 | tf_op jit(solution)/shard_map/tsrb,tsb->tr/dot_general | solution.py:165
  60.0 0.6 fusion.6
  60.9 1.5 %collective-permute-start.10 = (f32[32,128]{1,0:T(8,128)S(1)}, f32[32,128]{1,0:T(8,128)S(1)}, u32[]{:S(2)}, u32[]{:S(2)}) collective-permute-start(f32[32,128]{1,0:T(8,128)S(1)} %add.931), channel_id=1, source_target_pairs={{0,2},{1,3},{2,0},{3,1},{4,6},{5,7},{6,4},{7,5},{8,10},{9,11},{10,... | collective-permute-start | bytes 49160 | tf_op jit(solution)/shard_map/ppermute | solution.py:19
  62.4 1.0 collective-permute-start.8
  63.4 1.2 collective-permute-done.10
  64.6 1.6 %collective-permute-done.8 = f32[32,128]{1,0:T(8,128)S(1)} collective-permute-done((f32[32,128]{1,0:T(8,128)S(1)}, f32[32,128]{1,0:T(8,128)S(1)}, u32[]{:S(2)}, u32[]{:S(2)}) %collective-permute-start.8) | collective-permute-done | bytes 16416 | tf_op jit(solution)/shard_map/ppermute | solution.py:19
  66.3 9.8 %all_to_all.15 = f32[32,1,128]{2,1,0:T(1,128)S(1)} all-to-all(f32[32,1,128]{2,1,0:T(1,128)S(1)} %bitcast.304), channel_id=1, replica_groups=mesh['dp'=8,'region'=4] {'dp','region'}, dimensions={0} | all-to-all | bytes 32768 | tf_op jit(solution)/shard_map/all_to_all | solution.py:30
  77.6 2.8 %fusion.33 = f32[64,1,2,128]{3,1,2,0:T(1,128)S(1)} fusion(bf16[64,2,128,128]{3,2,1,0:T(8,128)(2,1)} %param.7, bf16[64,128,1,1]{1,0,2,3:T(8,128)(2,1)S(1)} %get-tuple-element.7), kind=kOutput, calls=%fused_computation.74 | convolution fusion | flops 4194304 | bytes 4276224 | tf_op jit(solution)/shard_map/tsrb,tr->tsb/dot_general | solution.py:122
  81.0 1.5 %collective-permute-done.11 = f32[2,256,128]{2,1,0:T(8,128)S(1)} collective-permute-done((f32[2,256,128]{2,1,0:T(8,128)S(1)}, f32[2,256,128]{2,1,0:T(8,128)S(1)}, u32[]{:S(2)}, u32[]{:S(2)}) %collective-permute-start.11) | collective-permute-done | bytes 262176 | tf_op jit(solution)/shard_map/ppermute | solution.py:52
  83.2 5.0 %collective-permute-done.12 = f32[256,128]{1,0:T(8,128)S(1)} collective-permute-done((f32[256,128]{1,0:T(8,128)S(1)}, f32[256,128]{1,0:T(8,128)S(1)}, u32[]{:S(2)}, u32[]{:S(2)}) %collective-permute-start.12) | collective-permute-done | bytes 131104 | tf_op jit(solution)/shard_map/ppermute | solution.py:52
  88.9 4.4 %collective-permute-done.13 = f32[256,128]{1,0:T(8,128)S(1)} collective-permute-done((f32[256,128]{1,0:T(8,128)S(1)}, f32[256,128]{1,0:T(8,128)S(1)}, u32[]{:S(2)}, u32[]{:S(2)}) %collective-permute-start.13) | collective-permute-done | bytes 131104 | tf_op jit(solution)/shard_map/ppermute | solution.py:19
  93.3 0.6 collective-permute-start.14
  93.9 4.4 %collective-permute-done.14 = f32[256,128]{1,0:T(8,128)S(1)} collective-permute-done((f32[256,128]{1,0:T(8,128)S(1)}, f32[256,128]{1,0:T(8,128)S(1)}, u32[]{:S(2)}, u32[]{:S(2)}) %collective-permute-start.14) | collective-permute-done | bytes 131104 | tf_op jit(solution)/shard_map/ppermute | solution.py:19
  98.3 0.7 collective-permute-start.15
  99.0 6.7 %collective-permute-done.15 = f32[256,128]{1,0:T(8,128)S(1)} collective-permute-done((f32[256,128]{1,0:T(8,128)S(1)}, f32[256,128]{1,0:T(8,128)S(1)}, u32[]{:S(2)}, u32[]{:S(2)}) %collective-permute-start.15) | collective-permute-done | bytes 131104 | tf_op jit(solution)/shard_map/ppermute | solution.py:19
  105.7 0.6 multiply_reduce_fusion.2
  106.9 4.4 %collective-permute-done.16 = f32[256,128]{1,0:T(8,128)S(1)} collective-permute-done((f32[256,128]{1,0:T(8,128)S(1)}, f32[256,128]{1,0:T(8,128)S(1)}, u32[]{:S(2)}, u32[]{:S(2)}) %collective-permute-start.16) | collective-permute-done | bytes 131104 | tf_op jit(solution)/shard_map/ppermute | solution.py:83
  111.4 0.7 multiply_reduce_fusion.3
  112.0 1.4 broadcast_select_fusion
  117.6 2.2 %fusion.4 = f32[32,1,128,1]{2,1,3,0:T(1,128)S(1)} fusion(bf16[64,2,128,128]{3,2,1,0:T(8,128)(2,1)} %param.7, bf16[32,2,128,1]{2,1,0,3:T(2,128)(2,1)S(1)} %bitcast.316), kind=kOutput, calls=%fused_computation.4 | convolution fusion | flops 2097152 | bytes 2129920 | tf_op jit(solution)/shard_map/tsrb,tsb->tr/dot_general | solution.py:165
  120.3 0.6 fusion
  122.2 1.1 collective-permute-start.21
  123.3 1.6 %collective-permute-done.19 = f32[32,128]{1,0:T(8,128)S(1)} collective-permute-done((f32[32,128]{1,0:T(8,128)S(1)}, f32[32,128]{1,0:T(8,128)S(1)}, u32[]{:S(2)}, u32[]{:S(2)}) %collective-permute-start.19) | collective-permute-done | bytes 16416 | tf_op jit(solution)/shard_map/ppermute | solution.py:19
  124.9 1.0 collective-permute-done.21
  125.9 0.8 fusion.47
  126.7 2.5 %all-to-all-start.2 = ((f32[32,1,128]{2,1,0:T(1,128)}), f32[32,1,128]{2,1,0:T(1,128)S(1)}, u32[]{:S(2)}, u32[]{:S(2)}) async-start(f32[32,1,128]{2,1,0:T(1,128)} %bitcast.83), calls=%async_computation.2 | async-start | bytes 32768 | tf_op jit(solution)/shard_map/all_to_all | solution.py:30
  129.4 6.9 %all-to-all-done.2 = f32[32,1,128]{2,1,0:T(1,128)S(1)} async-done(((f32[32,1,128]{2,1,0:T(1,128)}), f32[32,1,128]{2,1,0:T(1,128)S(1)}, u32[]{:S(2)}, u32[]{:S(2)}) %all-to-all-start.2) | async-done | bytes 16416 | tf_op jit(solution)/shard_map/all_to_all | solution.py:30
  137.8 0.7 multiply_add_fusion
  (94 shorter events, 12.8 us)
Async XLA Ops:
  1.5 13.7 %all-to-all-start = ((f32[8,1,128]{2,1,0:T(1,128)}), f32[8,1,128]{2,1,0:T(1,128)S(1)}, u32[]{:S(2)}, u32[]{:S(2)}) async-start(f32[8,1,128]{2,1,0:T(1,128)} %bitcast.3), calls=%async_computation | async-start | bytes 8192 | tf_op jit(solution)/shard_map/all_to_all | solution.py:30
  20.6 1.6 %collective-permute-start = (f32[2,256,128]{2,1,0:T(8,128)S(1)}, f32[2,256,128]{2,1,0:T(8,128)S(1)}, u32[]{:S(2)}, u32[]{:S(2)}) collective-permute-start(f32[2,256,128]{2,1,0:T(8,128)S(1)} %dynamic-slice_bitcast_fusion.1), channel_id=1, source_target_pairs={{0,1},{1,0},{2,3},{3,2},{4,5},{5,4},{6,7},{7,6},{8,9},{9,8},{10,11... | collective-permute-start | bytes 786440 | tf_op jit(solution)/shard_map/ppermute | solution.py:52
  22.3 5.6 %collective-permute-start.1 = (f32[256,128]{1,0:T(8,128)S(1)}, f32[256,128]{1,0:T(8,128)S(1)}, u32[]{:S(2)}, u32[]{:S(2)}) collective-permute-start(f32[256,128]{1,0:T(8,128)S(1)} %dynamic-slice_bitcast_fusion.3), channel_id=1, source_target_pairs={{0,2},{1,3},{2,0},{3,1},{4,6},{5,7},{6,4},{7,5},{8,10},{9,11},{10,... | collective-permute-start | bytes 393224 | tf_op jit(solution)/shard_map/ppermute | solution.py:52
  27.9 5.0 %collective-permute-start.2 = (f32[256,128]{1,0:T(8,128)S(1)}, f32[256,128]{1,0:T(8,128)S(1)}, u32[]{:S(2)}, u32[]{:S(2)}) collective-permute-start(f32[256,128]{1,0:T(8,128)S(1)} %bitcast_add_fusion.3), channel_id=1, source_target_pairs={{0,4},{4,0},{8,12},{12,8},{16,20},{20,16},{24,28},{28,24},{1,5},{5... | collective-permute-start | bytes 393224 | tf_op jit(solution)/shard_map/ppermute | solution.py:19
  33.0 5.0 %collective-permute-start.3 = (f32[256,128]{1,0:T(8,128)S(1)}, f32[256,128]{1,0:T(8,128)S(1)}, u32[]{:S(2)}, u32[]{:S(2)}) collective-permute-start(f32[256,128]{1,0:T(8,128)S(1)} %add.923), channel_id=1, source_target_pairs={{0,8},{4,12},{8,0},{12,4},{16,24},{20,28},{24,16},{28,20},{1,9},{5... | collective-permute-start | bytes 393224 | tf_op jit(solution)/shard_map/ppermute | solution.py:19
  38.0 7.3 %collective-permute-start.4 = (f32[256,128]{1,0:T(8,128)S(1)}, f32[256,128]{1,0:T(8,128)S(1)}, u32[]{:S(2)}, u32[]{:S(2)}) collective-permute-start(f32[256,128]{1,0:T(8,128)S(1)} %add.924), channel_id=1, source_target_pairs={{0,16},{4,20},{8,24},{12,28},{16,0},{20,4},{24,8},{28,12},{1,17},{... | collective-permute-start | bytes 393224 | tf_op jit(solution)/shard_map/ppermute | solution.py:19
  46.0 5.0 %collective-permute-start.5 = (f32[256,128]{1,0:T(8,128)S(1)}, f32[256,128]{1,0:T(8,128)S(1)}, u32[]{:S(2)}, u32[]{:S(2)}) collective-permute-start(f32[256,128]{1,0:T(8,128)S(1)} %get-tuple-element.10), channel_id=1, source_target_pairs={{0,2},{1,3},{2,0},{3,1},{4,6},{5,7},{6,4},{7,5},{8,10},{9,11},{10,... | collective-permute-start | bytes 393224 | tf_op jit(solution)/shard_map/ppermute | solution.py:83
  51.0 2.1 %collective-permute-start.6 = (f32[2,256,128]{2,1,0:T(8,128)S(1)}, f32[2,256,128]{2,1,0:T(8,128)S(1)}, u32[]{:S(2)}, u32[]{:S(2)}) collective-permute-start(f32[2,256,128]{2,1,0:T(8,128)S(1)} %maximum_select_fusion.2), channel_id=1, source_target_pairs={{0,1},{1,0},{2,3},{3,2},{4,5},{5,4},{6,7},{7,6},{8,9},{9,8},{10,11... | collective-permute-start | bytes 786440 | tf_op jit(solution)/shard_map/ppermute | solution.py:83
  53.1 10.3 %copy-start.3 = (f32[32,128]{1,0:T(8,128)S(1)}, f32[32,128]{1,0:T(8,128)}, u32[]{:S(2)}) copy-start(f32[32,128]{1,0:T(8,128)} %param.10) | copy-start | bytes 49156
  53.1 13.1 %copy-start.2 = (f32[64,128]{1,0:T(8,128)S(1)}, f32[64,128]{1,0:T(8,128)}, u32[]{:S(2)}) copy-start(f32[64,128]{1,0:T(8,128)} %param.6) | copy-start | bytes 98308
  53.4 6.6 %copy-start = (bf16[64,2,128,128]{3,2,1,0:T(8,128)(2,1)S(1)}, bf16[64,2,128,128]{3,2,1,0:T(8,128)(2,1)}, u32[]{:S(2)}) copy-start(bf16[64,2,128,128]{3,2,1,0:T(8,128)(2,1)} %param.7) | copy-start | bytes 12582916
  59.5 1.4 collective-permute-start.9
  60.7 1.7 %collective-permute-start.7 = (f32[32,128]{1,0:T(8,128)S(1)}, f32[32,128]{1,0:T(8,128)S(1)}, u32[]{:S(2)}, u32[]{:S(2)}) collective-permute-start(f32[32,128]{1,0:T(8,128)S(1)} %bitcast.305), channel_id=1, source_target_pairs={{0,1},{1,0},{2,3},{3,2},{4,5},{5,4},{6,7},{7,6},{8,9},{9,8},{10,11... | collective-permute-start | bytes 49160 | tf_op jit(solution)/shard_map/ppermute | solution.py:19
  60.9 3.7 %collective-permute-start.10 = (f32[32,128]{1,0:T(8,128)S(1)}, f32[32,128]{1,0:T(8,128)S(1)}, u32[]{:S(2)}, u32[]{:S(2)}) collective-permute-start(f32[32,128]{1,0:T(8,128)S(1)} %add.931), channel_id=1, source_target_pairs={{0,2},{1,3},{2,0},{3,1},{4,6},{5,7},{6,4},{7,5},{8,10},{9,11},{10,... | collective-permute-start | bytes 49160 | tf_op jit(solution)/shard_map/ppermute | solution.py:19
  62.4 3.8 %collective-permute-start.8 = (f32[32,128]{1,0:T(8,128)S(1)}, f32[32,128]{1,0:T(8,128)S(1)}, u32[]{:S(2)}, u32[]{:S(2)}) collective-permute-start(f32[32,128]{1,0:T(8,128)S(1)} %add.929), channel_id=1, source_target_pairs={{0,2},{1,3},{2,0},{3,1},{4,6},{5,7},{6,4},{7,5},{8,10},{9,11},{10,... | collective-permute-start | bytes 49160 | tf_op jit(solution)/shard_map/ppermute | solution.py:19
  81.0 1.6 %collective-permute-start.11 = (f32[2,256,128]{2,1,0:T(8,128)S(1)}, f32[2,256,128]{2,1,0:T(8,128)S(1)}, u32[]{:S(2)}, u32[]{:S(2)}) collective-permute-start(f32[2,256,128]{2,1,0:T(8,128)S(1)} %dynamic-slice_bitcast_fusion), channel_id=1, source_target_pairs={{0,1},{1,0},{2,3},{3,2},{4,5},{5,4},{6,7},{7,6},{8,9},{9,8},{10,11... | collective-permute-start | bytes 786440 | tf_op jit(solution)/shard_map/ppermute | solution.py:52
  82.6 5.6 %collective-permute-start.12 = (f32[256,128]{1,0:T(8,128)S(1)}, f32[256,128]{1,0:T(8,128)S(1)}, u32[]{:S(2)}, u32[]{:S(2)}) collective-permute-start(f32[256,128]{1,0:T(8,128)S(1)} %dynamic-slice_bitcast_fusion.2), channel_id=1, source_target_pairs={{0,2},{1,3},{2,0},{3,1},{4,6},{5,7},{6,4},{7,5},{8,10},{9,11},{10,... | collective-permute-start | bytes 393224 | tf_op jit(solution)/shard_map/ppermute | solution.py:52
  88.2 5.0 %collective-permute-start.13 = (f32[256,128]{1,0:T(8,128)S(1)}, f32[256,128]{1,0:T(8,128)S(1)}, u32[]{:S(2)}, u32[]{:S(2)}) collective-permute-start(f32[256,128]{1,0:T(8,128)S(1)} %bitcast_add_fusion.2), channel_id=1, source_target_pairs={{0,4},{4,0},{8,12},{12,8},{16,20},{20,16},{24,28},{28,24},{1,5},{5... | collective-permute-start | bytes 393224 | tf_op jit(solution)/shard_map/ppermute | solution.py:19
  93.3 5.0 %collective-permute-start.14 = (f32[256,128]{1,0:T(8,128)S(1)}, f32[256,128]{1,0:T(8,128)S(1)}, u32[]{:S(2)}, u32[]{:S(2)}) collective-permute-start(f32[256,128]{1,0:T(8,128)S(1)} %add.970), channel_id=1, source_target_pairs={{0,8},{4,12},{8,0},{12,4},{16,24},{20,28},{24,16},{28,20},{1,9},{5... | collective-permute-start | bytes 393224 | tf_op jit(solution)/shard_map/ppermute | solution.py:19
  98.3 7.3 %collective-permute-start.15 = (f32[256,128]{1,0:T(8,128)S(1)}, f32[256,128]{1,0:T(8,128)S(1)}, u32[]{:S(2)}, u32[]{:S(2)}) collective-permute-start(f32[256,128]{1,0:T(8,128)S(1)} %add.971), channel_id=1, source_target_pairs={{0,16},{4,20},{8,24},{12,28},{16,0},{20,4},{24,8},{28,12},{1,17},{... | collective-permute-start | bytes 393224 | tf_op jit(solution)/shard_map/ppermute | solution.py:19
  106.3 5.0 %collective-permute-start.16 = (f32[256,128]{1,0:T(8,128)S(1)}, f32[256,128]{1,0:T(8,128)S(1)}, u32[]{:S(2)}, u32[]{:S(2)}) collective-permute-start(f32[256,128]{1,0:T(8,128)S(1)} %get-tuple-element.6), channel_id=1, source_target_pairs={{0,2},{1,3},{2,0},{3,1},{4,6},{5,7},{6,4},{7,5},{8,10},{9,11},{10,... | collective-permute-start | bytes 393224 | tf_op jit(solution)/shard_map/ppermute | solution.py:83
  111.3 2.1 %collective-permute-start.17 = (f32[2,256,128]{2,1,0:T(8,128)S(1)}, f32[2,256,128]{2,1,0:T(8,128)S(1)}, u32[]{:S(2)}, u32[]{:S(2)}) collective-permute-start(f32[2,256,128]{2,1,0:T(8,128)S(1)} %maximum_select_fusion.4), channel_id=1, source_target_pairs={{0,1},{1,0},{2,3},{3,2},{4,5},{5,4},{6,7},{7,6},{8,9},{9,8},{10,11... | collective-permute-start | bytes 786440 | tf_op jit(solution)/shard_map/ppermute | solution.py:83
  113.8 6.5 %copy-start.1 = (bf16[64,2,128,128]{3,2,1,0:T(8,128)(2,1)S(1)}, bf16[64,2,128,128]{3,2,1,0:T(8,128)(2,1)}, u32[]{:S(2)}) copy-start(bf16[64,2,128,128]{3,2,1,0:T(8,128)(2,1)} %param.7) | copy-start | bytes 12582916
  119.8 1.4 collective-permute-start.18
  120.9 1.2 collective-permute-start.20
  121.1 3.7 %collective-permute-start.19 = (f32[32,128]{1,0:T(8,128)S(1)}, f32[32,128]{1,0:T(8,128)S(1)}, u32[]{:S(2)}, u32[]{:S(2)}) collective-permute-start(f32[32,128]{1,0:T(8,128)S(1)} %add.976), channel_id=1, source_target_pairs={{0,2},{1,3},{2,0},{3,1},{4,6},{5,7},{6,4},{7,5},{8,10},{9,11},{10,... | collective-permute-start | bytes 49160 | tf_op jit(solution)/shard_map/ppermute | solution.py:19
  122.2 3.7 %collective-permute-start.21 = (f32[32,128]{1,0:T(8,128)S(1)}, f32[32,128]{1,0:T(8,128)S(1)}, u32[]{:S(2)}, u32[]{:S(2)}) collective-permute-start(f32[32,128]{1,0:T(8,128)S(1)} %add.978), channel_id=1, source_target_pairs={{0,2},{1,3},{2,0},{3,1},{4,6},{5,7},{6,4},{7,5},{8,10},{9,11},{10,... | collective-permute-start | bytes 49160 | tf_op jit(solution)/shard_map/ppermute | solution.py:19
  126.7 9.6 %all-to-all-start.2 = ((f32[32,1,128]{2,1,0:T(1,128)}), f32[32,1,128]{2,1,0:T(1,128)S(1)}, u32[]{:S(2)}, u32[]{:S(2)}) async-start(f32[32,1,128]{2,1,0:T(1,128)} %bitcast.83), calls=%async_computation.2 | async-start | bytes 32768 | tf_op jit(solution)/shard_map/all_to_all | solution.py:30

commit v19 on v17

--- a/solution.py
+++ b/solution.py
@@ -10,12 +10,15 @@
 smooth_weight = 1.0
 
 
-def butterfly_sum(x, axis, reverse=False):
+def butterfly_sum(x, axis, first=1):
     n = lax.axis_size(axis)
     if n & (n - 1):
         return lax.psum(x, axis)
     steps = [1 << j for j in range(n.bit_length() - 1)]
-    for k in steps[::-1] if reverse else steps:
+    if first in steps:
+        steps.remove(first)
+        steps.insert(0, first)
+    for k in steps:
         x = x + lax.ppermute(x, axis, [(i, i ^ k) for i in range(n)])
     return x
 
@@ -113,7 +116,7 @@
             preferred_element_type=jnp.float32,
         )
         piece = halving_scatter(partials, "region")
-        return butterfly_sum(piece, "dp")
+        return butterfly_sum(piece, "dp", first=2)
 
     def normalized_field(piece):
         field = doubling_gather(piece, "region")
@@ -143,7 +146,7 @@
                 picked[lo:lo + half_tiles],
                 preferred_element_type=jnp.float32,
             )
-            halves.append(butterfly_sum(part, "region", reverse=len(halves) % 2 == 1))
+            halves.append(butterfly_sum(part, "region"))
         ray_pred = jnp.concatenate(halves, 0) if len(halves) > 1 else halves[0]
         face_pred = face_scale * rows[n_slots:]
         left_faces = face_pred - alpha_value * left_faces

time: 134 us -> 132 us (0.985)
  no operation moved by 1% of the time
where the time goes in v19:
time: 132 us; the launch traced here: 131 us
  waiting for transfers between devices  68.7 us (52%)
  starting transfers between devices  23.5 us (18%)
  matrix products  15.6 us (12%)
  blocking collectives  9.6 us (7%)
  other arithmetic  7.12 us (5%)
  between operations  4.88 us (4%)
  local copies, waits for them, and re-layouts  1.83 us (1%)
    ppermute x14, waiting for transfers between devices, butterfly_sum(): x = x + lax.ppermute(x, axis, [(i, i ^ k) for i in range(n)])  36.6 us
    ppermute x4, waiting for transfers between devices, halving_scatter(): x = keep + lax.ppermute(send, axis, [(i, i ^ k) for i in range(n)])  12.1 us
    ppermute x4, waiting for transfers between devices, doubling_gather(): other = lax.ppermute(x, axis, [(i, i ^ k) for i in range(n)])  10.7 us
    all_to_all x2, starting transfers between devices, square_sum(): got = lax.all_to_all(spread[:, None, :], axis, 0, 0, tiled=False)  9.82 us
    all_to_all x1, blocking collectives, square_sum(): got = lax.all_to_all(spread[:, None, :], axis, 0, 0, tiled=False)  9.6 us
    all_to_all x2, waiting for transfers between devices, square_sum(): got = lax.all_to_all(spread[:, None, :], axis, 0, 0, tiled=False)  9.46 us
    ppermute x14, starting transfers between devices, butterfly_sum(): x = x + lax.ppermute(x, axis, [(i, i ^ k) for i in range(n)])  9.08 us
    dot_general x4, matrix products, local(): jnp.einsum('tsrb,tsb->tr', sensitivity[lo:lo + half_tiles], picked[lo:lo...  6.09 us
  transfers between devices with their start and end apart: 24, of which 21 were waited for; matrix products, arithmetic and copies ran while one was open for 4% of the time, Pallas kernels for 0%

profile of v19, /device:TPU:0, one launch (start us, length us, event | category | flops | bytes accessed | tf_op | source)
XLA Modules:
  0.0 131.2 jit_solution(8756360487735067378)
XLA Ops:
  0.0 1.5 %fusion.39 = f32[8,128]{1,0:T(8,128)} fusion(f32[64,128]{1,0:T(8,128)} %param.6), kind=kOutput, calls=%fused_computation.76 | convolution fusion | flops 794624 | bytes 36864 | tf_op jit(solution)/shard_map/dot_general | solution.py:29
  1.5 7.3 %all-to-all-start = ((f32[8,1,128]{2,1,0:T(1,128)}), f32[8,1,128]{2,1,0:T(1,128)S(1)}, u32[]{:S(2)}, u32[]{:S(2)}) async-start(f32[8,1,128]{2,1,0:T(1,128)} %bitcast.3), calls=%async_computation | async-start | bytes 8192 | tf_op jit(solution)/shard_map/all_to_all | solution.py:32
  8.8 0.8 copy.14
  9.8 0.8 slice_bitcast_fusion.31
  11.8 0.8 multiply_multiply_fusion.1
  12.6 2.6 %all-to-all-done = f32[8,1,128]{2,1,0:T(1,128)S(1)} async-done(((f32[8,1,128]{2,1,0:T(1,128)}), f32[8,1,128]{2,1,0:T(1,128)S(1)}, u32[]{:S(2)}, u32[]{:S(2)}) %all-to-all-start) | async-done | bytes 4128 | tf_op jit(solution)/shard_map/all_to_all | solution.py:32
  16.5 0.8 convert_bitcast_fusion.1
  17.2 2.8 %fusion.37 = f32[64,1,2,128]{3,1,2,0:T(1,128)S(1)} fusion(bf16[64,2,128,128]{3,2,1,0:T(8,128)(2,1)} %param.7, bf16[64,128,1,1]{1,0,2,3:T(8,128)(2,1)S(1)} %convert_bitcast_fusion.1), kind=kOutput, calls=%fused_computation.74 | convolution fusion | flops 4194304 | bytes 4276224 | tf_op jit(solution)/shard_map/tsrb,tr->tsb/dot_general | solution.py:100
  20.7 1.5 %collective-permute-done = f32[2,256,128]{2,1,0:T(8,128)S(1)} collective-permute-done((f32[2,256,128]{2,1,0:T(8,128)S(1)}, f32[2,256,128]{2,1,0:T(8,128)S(1)}, u32[]{:S(2)}, u32[]{:S(2)}) %collective-permute-start) | collective-permute-done | bytes 262176 | tf_op jit(solution)/shard_map/ppermute | solution.py:54
  22.3 1.6 %collective-permute-start.1 = (f32[256,128]{1,0:T(8,128)S(1)}, f32[256,128]{1,0:T(8,128)S(1)}, u32[]{:S(2)}, u32[]{:S(2)}) collective-permute-start(f32[256,128]{1,0:T(8,128)S(1)} %dynamic-slice_bitcast_fusion.3), channel_id=1, source_target_pairs={{0,2},{1,3},{2,0},{3,1},{4,6},{5,7},{6,4},{7,5},{8,10},{9,11},{10,... | collective-permute-start | bytes 393224 | tf_op jit(solution)/shard_map/ppermute | solution.py:54
  23.8 4.0 %collective-permute-done.1 = f32[256,128]{1,0:T(8,128)S(1)} collective-permute-done((f32[256,128]{1,0:T(8,128)S(1)}, f32[256,128]{1,0:T(8,128)S(1)}, u32[]{:S(2)}, u32[]{:S(2)}) %collective-permute-start.1) | collective-permute-done | bytes 131104 | tf_op jit(solution)/shard_map/ppermute | solution.py:54
  28.5 4.4 %collective-permute-done.2 = f32[256,128]{1,0:T(8,128)S(1)} collective-permute-done((f32[256,128]{1,0:T(8,128)S(1)}, f32[256,128]{1,0:T(8,128)S(1)}, u32[]{:S(2)}, u32[]{:S(2)}) %collective-permute-start.2) | collective-permute-done | bytes 131104 | tf_op jit(solution)/shard_map/ppermute | solution.py:22
  33.6 4.4 %collective-permute-done.3 = f32[256,128]{1,0:T(8,128)S(1)} collective-permute-done((f32[256,128]{1,0:T(8,128)S(1)}, f32[256,128]{1,0:T(8,128)S(1)}, u32[]{:S(2)}, u32[]{:S(2)}) %collective-permute-start.3) | collective-permute-done | bytes 131104 | tf_op jit(solution)/shard_map/ppermute | solution.py:22
  38.0 0.6 collective-permute-start.4
  38.6 6.7 %collective-permute-done.4 = f32[256,128]{1,0:T(8,128)S(1)} collective-permute-done((f32[256,128]{1,0:T(8,128)S(1)}, f32[256,128]{1,0:T(8,128)S(1)}, u32[]{:S(2)}, u32[]{:S(2)}) %collective-permute-start.4) | collective-permute-done | bytes 131104 | tf_op jit(solution)/shard_map/ppermute | solution.py:22
  45.3 1.6 %collective-permute-start.5 = (f32[256,128]{1,0:T(8,128)S(1)}, f32[256,128]{1,0:T(8,128)S(1)}, u32[]{:S(2)}, u32[]{:S(2)}) collective-permute-start(f32[256,128]{1,0:T(8,128)S(1)} %add.901), channel_id=1, source_target_pairs={{0,2},{1,3},{2,0},{3,1},{4,6},{5,7},{6,4},{7,5},{8,10},{9,11},{10,... | collective-permute-start | bytes 393224 | tf_op jit(solution)/shard_map/ppermute | solution.py:67
  47.0 3.4 %collective-permute-done.5 = f32[256,128]{1,0:T(8,128)S(1)} collective-permute-done((f32[256,128]{1,0:T(8,128)S(1)}, f32[256,128]{1,0:T(8,128)S(1)}, u32[]{:S(2)}, u32[]{:S(2)}) %collective-permute-start.5) | collective-permute-done | bytes 131104 | tf_op jit(solution)/shard_map/ppermute | solution.py:67
  50.6 1.4 %collective-permute-done.6 = f32[2,256,128]{2,1,0:T(8,128)S(1)} collective-permute-done((f32[2,256,128]{2,1,0:T(8,128)S(1)}, f32[2,256,128]{2,1,0:T(8,128)S(1)}, u32[]{:S(2)}, u32[]{:S(2)}) %collective-permute-start.6) | collective-permute-done | bytes 262176 | tf_op jit(solution)/shard_map/ppermute | solution.py:67
  52.0 0.7 multiply_reduce_fusion.1
  53.8 2.4 %fusion.2 = f32[32,1,128,1]{2,1,3,0:T(1,128)S(1)} fusion(bf16[64,2,128,128]{3,2,1,0:T(8,128)(2,1)} %param.7, bf16[32,2,128,1]{2,1,0,3:T(2,128)(2,1)S(1)} %bitcast.309), kind=kOutput, calls=%fused_computation.2 | convolution fusion | flops 2097152 | bytes 2129920 | tf_op jit(solution)/shard_map/tsrb,tsb->tr/dot_general | solution.py:143
  56.4 0.6 fusion.6
  57.4 1.6 %collective-permute-start.10 = (f32[32,128]{1,0:T(8,128)S(1)}, f32[32,128]{1,0:T(8,128)S(1)}, u32[]{:S(2)}, u32[]{:S(2)}) collective-permute-start(f32[32,128]{1,0:T(8,128)S(1)} %add.904), channel_id=1, source_target_pairs={{0,2},{1,3},{2,0},{3,1},{4,6},{5,7},{6,4},{7,5},{8,10},{9,11},{10,... | collective-permute-start | bytes 49160 | tf_op jit(solution)/shard_map/ppermute | solution.py:22
  59.0 0.8 collective-permute-start.8
  59.8 1.4 %collective-permute-done.10 = f32[32,128]{1,0:T(8,128)S(1)} collective-permute-done((f32[32,128]{1,0:T(8,128)S(1)}, f32[32,128]{1,0:T(8,128)S(1)}, u32[]{:S(2)}, u32[]{:S(2)}) %collective-permute-start.10) | collective-permute-done | bytes 16416 | tf_op jit(solution)/shard_map/ppermute | solution.py:22
  61.2 1.6 %collective-permute-done.8 = f32[32,128]{1,0:T(8,128)S(1)} collective-permute-done((f32[32,128]{1,0:T(8,128)S(1)}, f32[32,128]{1,0:T(8,128)S(1)}, u32[]{:S(2)}, u32[]{:S(2)}) %collective-permute-start.8) | collective-permute-done | bytes 16416 | tf_op jit(solution)/shard_map/ppermute | solution.py:22
  63.0 9.6 %all_to_all.15 = f32[32,1,128]{2,1,0:T(1,128)S(1)} all-to-all(f32[32,1,128]{2,1,0:T(1,128)S(1)} %bitcast.298), channel_id=1, replica_groups=mesh['dp'=8,'region'=4] {'dp','region'}, dimensions={0} | all-to-all | bytes 32768 | tf_op jit(solution)/shard_map/all_to_all | solution.py:32
  72.6 0.6 fusion.75
  74.0 2.8 %fusion.33 = f32[64,1,2,128]{3,1,2,0:T(1,128)S(1)} fusion(bf16[64,2,128,128]{3,2,1,0:T(8,128)(2,1)} %param.7, bf16[64,128,1,1]{1,0,2,3:T(8,128)(2,1)S(1)} %get-tuple-element.5), kind=kOutput, calls=%fused_computation.70 | convolution fusion | flops 4194304 | bytes 4276224 | tf_op jit(solution)/shard_map/tsrb,tr->tsb/dot_general | solution.py:100
  77.4 1.5 %collective-permute-done.11 = f32[2,256,128]{2,1,0:T(8,128)S(1)} collective-permute-done((f32[2,256,128]{2,1,0:T(8,128)S(1)}, f32[2,256,128]{2,1,0:T(8,128)S(1)}, u32[]{:S(2)}, u32[]{:S(2)}) %collective-permute-start.11) | collective-permute-done | bytes 262176 | tf_op jit(solution)/shard_map/ppermute | solution.py:54
  79.6 5.0 %collective-permute-done.12 = f32[256,128]{1,0:T(8,128)S(1)} collective-permute-done((f32[256,128]{1,0:T(8,128)S(1)}, f32[256,128]{1,0:T(8,128)S(1)}, u32[]{:S(2)}, u32[]{:S(2)}) %collective-permute-start.12) | collective-permute-done | bytes 131104 | tf_op jit(solution)/shard_map/ppermute | solution.py:54
  84.6 0.6 collective-permute-start.13
  85.3 4.4 %collective-permute-done.13 = f32[256,128]{1,0:T(8,128)S(1)} collective-permute-done((f32[256,128]{1,0:T(8,128)S(1)}, f32[256,128]{1,0:T(8,128)S(1)}, u32[]{:S(2)}, u32[]{:S(2)}) %collective-permute-start.13) | collective-permute-done | bytes 131104 | tf_op jit(solution)/shard_map/ppermute | solution.py:22
  90.3 4.4 %collective-permute-done.14 = f32[256,128]{1,0:T(8,128)S(1)} collective-permute-done((f32[256,128]{1,0:T(8,128)S(1)}, f32[256,128]{1,0:T(8,128)S(1)}, u32[]{:S(2)}, u32[]{:S(2)}) %collective-permute-start.14) | collective-permute-done | bytes 131104 | tf_op jit(solution)/shard_map/ppermute | solution.py:22
  94.8 0.7 collective-permute-start.15
  95.4 6.7 %collective-permute-done.15 = f32[256,128]{1,0:T(8,128)S(1)} collective-permute-done((f32[256,128]{1,0:T(8,128)S(1)}, f32[256,128]{1,0:T(8,128)S(1)}, u32[]{:S(2)}, u32[]{:S(2)}) %collective-permute-start.15) | collective-permute-done | bytes 131104 | tf_op jit(solution)/shard_map/ppermute | solution.py:22
  102.7 4.4 %collective-permute-done.16 = f32[256,128]{1,0:T(8,128)S(1)} collective-permute-done((f32[256,128]{1,0:T(8,128)S(1)}, f32[256,128]{1,0:T(8,128)S(1)}, u32[]{:S(2)}, u32[]{:S(2)}) %collective-permute-start.16) | collective-permute-done | bytes 131104 | tf_op jit(solution)/shard_map/ppermute | solution.py:67
  107.3 1.5 %collective-permute-done.17 = f32[2,256,128]{2,1,0:T(8,128)S(1)} collective-permute-done((f32[2,256,128]{2,1,0:T(8,128)S(1)}, f32[2,256,128]{2,1,0:T(8,128)S(1)}, u32[]{:S(2)}, u32[]{:S(2)}) %collective-permute-start.17) | collective-permute-done | bytes 262176 | tf_op jit(solution)/shard_map/ppermute | solution.py:67
  108.8 0.7 multiply_reduce_fusion
  110.5 2.4 %fusion.4 = f32[32,1,128,1]{2,1,3,0:T(1,128)S(1)} fusion(bf16[64,2,128,128]{3,2,1,0:T(8,128)(2,1)} %param.7, bf16[32,2,128,1]{2,1,0,3:T(2,128)(2,1)S(1)} %bitcast.310), kind=kOutput, calls=%fused_computation.4 | convolution fusion | flops 2097152 | bytes 2129920 | tf_op jit(solution)/shard_map/tsrb,tsb->tr/dot_general | solution.py:143
  113.1 0.6 fusion
  115.0 1.3 %collective-permute-start.21 = (f32[32,128]{1,0:T(8,128)S(1)}, f32[32,128]{1,0:T(8,128)S(1)}, u32[]{:S(2)}, u32[]{:S(2)}) collective-permute-start(f32[32,128]{1,0:T(8,128)S(1)} %add.948), channel_id=1, source_target_pairs={{0,2},{1,3},{2,0},{3,1},{4,6},{5,7},{6,4},{7,5},{8,10},{9,11},{10,... | collective-permute-start | bytes 49160 | tf_op jit(solution)/shard_map/ppermute | solution.py:22
  116.4 1.6 %collective-permute-done.19 = f32[32,128]{1,0:T(8,128)S(1)} collective-permute-done((f32[32,128]{1,0:T(8,128)S(1)}, f32[32,128]{1,0:T(8,128)S(1)}, u32[]{:S(2)}, u32[]{:S(2)}) %collective-permute-start.19) | collective-permute-done | bytes 16416 | tf_op jit(solution)/shard_map/ppermute | solution.py:22
  117.9 0.7 collective-permute-done.21
  118.7 0.8 fusion.47
  119.5 2.5 %all-to-all-start.2 = ((f32[32,1,128]{2,1,0:T(1,128)}), f32[32,1,128]{2,1,0:T(1,128)S(1)}, u32[]{:S(2)}, u32[]{:S(2)}) async-start(f32[32,1,128]{2,1,0:T(1,128)} %bitcast.75), calls=%async_computation.2 | async-start | bytes 32768 | tf_op jit(solution)/shard_map/all_to_all | solution.py:32
  122.3 6.8 %all-to-all-done.2 = f32[32,1,128]{2,1,0:T(1,128)S(1)} async-done(((f32[32,1,128]{2,1,0:T(1,128)}), f32[32,1,128]{2,1,0:T(1,128)S(1)}, u32[]{:S(2)}, u32[]{:S(2)}) %all-to-all-start.2) | async-done | bytes 16416 | tf_op jit(solution)/shard_map/all_to_all | solution.py:32
  129.1 0.6 fusion.58
  130.6 0.7 multiply_add_fusion
  (82 shorter events, 9.3 us)
Async XLA Ops:
  1.5 13.7 %all-to-all-start = ((f32[8,1,128]{2,1,0:T(1,128)}), f32[8,1,128]{2,1,0:T(1,128)S(1)}, u32[]{:S(2)}, u32[]{:S(2)}) async-start(f32[8,1,128]{2,1,0:T(1,128)} %bitcast.3), calls=%async_computation | async-start | bytes 8192 | tf_op jit(solution)/shard_map/all_to_all | solution.py:32
  20.6 1.6 %collective-permute-start = (f32[2,256,128]{2,1,0:T(8,128)S(1)}, f32[2,256,128]{2,1,0:T(8,128)S(1)}, u32[]{:S(2)}, u32[]{:S(2)}) collective-permute-start(f32[2,256,128]{2,1,0:T(8,128)S(1)} %dynamic-slice_bitcast_fusion.1), channel_id=1, source_target_pairs={{0,1},{1,0},{2,3},{3,2},{4,5},{5,4},{6,7},{7,6},{8,9},{9,8},{10,11... | collective-permute-start | bytes 786440 | tf_op jit(solution)/shard_map/ppermute | solution.py:54
  22.3 5.6 %collective-permute-start.1 = (f32[256,128]{1,0:T(8,128)S(1)}, f32[256,128]{1,0:T(8,128)S(1)}, u32[]{:S(2)}, u32[]{:S(2)}) collective-permute-start(f32[256,128]{1,0:T(8,128)S(1)} %dynamic-slice_bitcast_fusion.3), channel_id=1, source_target_pairs={{0,2},{1,3},{2,0},{3,1},{4,6},{5,7},{6,4},{7,5},{8,10},{9,11},{10,... | collective-permute-start | bytes 393224 | tf_op jit(solution)/shard_map/ppermute | solution.py:54
  27.9 5.0 %collective-permute-start.2 = (f32[256,128]{1,0:T(8,128)S(1)}, f32[256,128]{1,0:T(8,128)S(1)}, u32[]{:S(2)}, u32[]{:S(2)}) collective-permute-start(f32[256,128]{1,0:T(8,128)S(1)} %bitcast_add_fusion.3), channel_id=1, source_target_pairs={{0,8},{4,12},{8,0},{12,4},{16,24},{20,28},{24,16},{28,20},{1,9},{5... | collective-permute-start | bytes 393224 | tf_op jit(solution)/shard_map/ppermute | solution.py:22
  33.0 5.0 %collective-permute-start.3 = (f32[256,128]{1,0:T(8,128)S(1)}, f32[256,128]{1,0:T(8,128)S(1)}, u32[]{:S(2)}, u32[]{:S(2)}) collective-permute-start(f32[256,128]{1,0:T(8,128)S(1)} %add.899), channel_id=1, source_target_pairs={{0,4},{4,0},{8,12},{12,8},{16,20},{20,16},{24,28},{28,24},{1,5},{5... | collective-permute-start | bytes 393224 | tf_op jit(solution)/shard_map/ppermute | solution.py:22
  38.0 7.3 %collective-permute-start.4 = (f32[256,128]{1,0:T(8,128)S(1)}, f32[256,128]{1,0:T(8,128)S(1)}, u32[]{:S(2)}, u32[]{:S(2)}) collective-permute-start(f32[256,128]{1,0:T(8,128)S(1)} %add.900), channel_id=1, source_target_pairs={{0,16},{4,20},{8,24},{12,28},{16,0},{20,4},{24,8},{28,12},{1,17},{... | collective-permute-start | bytes 393224 | tf_op jit(solution)/shard_map/ppermute | solution.py:22
  45.3 5.0 %collective-permute-start.5 = (f32[256,128]{1,0:T(8,128)S(1)}, f32[256,128]{1,0:T(8,128)S(1)}, u32[]{:S(2)}, u32[]{:S(2)}) collective-permute-start(f32[256,128]{1,0:T(8,128)S(1)} %add.901), channel_id=1, source_target_pairs={{0,2},{1,3},{2,0},{3,1},{4,6},{5,7},{6,4},{7,5},{8,10},{9,11},{10,... | collective-permute-start | bytes 393224 | tf_op jit(solution)/shard_map/ppermute | solution.py:67
  50.4 1.6 %collective-permute-start.6 = (f32[2,256,128]{2,1,0:T(8,128)S(1)}, f32[2,256,128]{2,1,0:T(8,128)S(1)}, u32[]{:S(2)}, u32[]{:S(2)}) collective-permute-start(f32[2,256,128]{2,1,0:T(8,128)S(1)} %maximum_select_fusion.2), channel_id=1, source_target_pairs={{0,1},{1,0},{2,3},{3,2},{4,5},{5,4},{6,7},{7,6},{8,9},{9,8},{10,11... | collective-permute-start | bytes 786440 | tf_op jit(solution)/shard_map/ppermute | solution.py:67
  50.6 9.1 %copy-start.3 = (f32[32,128]{1,0:T(8,128)S(1)}, f32[32,128]{1,0:T(8,128)}, u32[]{:S(2)}) copy-start(f32[32,128]{1,0:T(8,128)} %param.10) | copy-start | bytes 49156
  50.6 12.2 %copy-start.2 = (f32[64,128]{1,0:T(8,128)S(1)}, f32[64,128]{1,0:T(8,128)}, u32[]{:S(2)}) copy-start(f32[64,128]{1,0:T(8,128)} %param.6) | copy-start | bytes 98308
  53.4 2.9 %copy-start = (bf16[64,2,128,128]{3,2,1,0:T(8,128)(2,1)S(1)}, bf16[64,2,128,128]{3,2,1,0:T(8,128)(2,1)}, u32[]{:S(2)}) copy-start(bf16[64,2,128,128]{3,2,1,0:T(8,128)(2,1)} %param.7) | copy-start | bytes 12582916
  56.2 1.2 collective-permute-start.9
  57.0 2.0 %collective-permute-start.7 = (f32[32,128]{1,0:T(8,128)S(1)}, f32[32,128]{1,0:T(8,128)S(1)}, u32[]{:S(2)}, u32[]{:S(2)}) collective-permute-start(f32[32,128]{1,0:T(8,128)S(1)} %bitcast.299), channel_id=1, source_target_pairs={{0,1},{1,0},{2,3},{3,2},{4,5},{5,4},{6,7},{7,6},{8,9},{9,8},{10,11... | collective-permute-start | bytes 49160 | tf_op jit(solution)/shard_map/ppermute | solution.py:22
  57.4 3.8 %collective-permute-start.10 = (f32[32,128]{1,0:T(8,128)S(1)}, f32[32,128]{1,0:T(8,128)S(1)}, u32[]{:S(2)}, u32[]{:S(2)}) collective-permute-start(f32[32,128]{1,0:T(8,128)S(1)} %add.904), channel_id=1, source_target_pairs={{0,2},{1,3},{2,0},{3,1},{4,6},{5,7},{6,4},{7,5},{8,10},{9,11},{10,... | collective-permute-start | bytes 49160 | tf_op jit(solution)/shard_map/ppermute | solution.py:22
  59.0 3.8 %collective-permute-start.8 = (f32[32,128]{1,0:T(8,128)S(1)}, f32[32,128]{1,0:T(8,128)S(1)}, u32[]{:S(2)}, u32[]{:S(2)}) collective-permute-start(f32[32,128]{1,0:T(8,128)S(1)} %add.902), channel_id=1, source_target_pairs={{0,2},{1,3},{2,0},{3,1},{4,6},{5,7},{6,4},{7,5},{8,10},{9,11},{10,... | collective-permute-start | bytes 49160 | tf_op jit(solution)/shard_map/ppermute | solution.py:22
  77.4 1.6 %collective-permute-start.11 = (f32[2,256,128]{2,1,0:T(8,128)S(1)}, f32[2,256,128]{2,1,0:T(8,128)S(1)}, u32[]{:S(2)}, u32[]{:S(2)}) collective-permute-start(f32[2,256,128]{2,1,0:T(8,128)S(1)} %dynamic-slice_bitcast_fusion), channel_id=1, source_target_pairs={{0,1},{1,0},{2,3},{3,2},{4,5},{5,4},{6,7},{7,6},{8,9},{9,8},{10,11... | collective-permute-start | bytes 786440 | tf_op jit(solution)/shard_map/ppermute | solution.py:54
  79.0 5.6 %collective-permute-start.12 = (f32[256,128]{1,0:T(8,128)S(1)}, f32[256,128]{1,0:T(8,128)S(1)}, u32[]{:S(2)}, u32[]{:S(2)}) collective-permute-start(f32[256,128]{1,0:T(8,128)S(1)} %dynamic-slice_bitcast_fusion.2), channel_id=1, source_target_pairs={{0,2},{1,3},{2,0},{3,1},{4,6},{5,7},{6,4},{7,5},{8,10},{9,11},{10,... | collective-permute-start | bytes 393224 | tf_op jit(solution)/shard_map/ppermute | solution.py:54
  84.6 5.0 %collective-permute-start.13 = (f32[256,128]{1,0:T(8,128)S(1)}, f32[256,128]{1,0:T(8,128)S(1)}, u32[]{:S(2)}, u32[]{:S(2)}) collective-permute-start(f32[256,128]{1,0:T(8,128)S(1)} %bitcast_add_fusion.2), channel_id=1, source_target_pairs={{0,8},{4,12},{8,0},{12,4},{16,24},{20,28},{24,16},{28,20},{1,9},{5... | collective-permute-start | bytes 393224 | tf_op jit(solution)/shard_map/ppermute | solution.py:22
  89.7 5.0 %collective-permute-start.14 = (f32[256,128]{1,0:T(8,128)S(1)}, f32[256,128]{1,0:T(8,128)S(1)}, u32[]{:S(2)}, u32[]{:S(2)}) collective-permute-start(f32[256,128]{1,0:T(8,128)S(1)} %add.943), channel_id=1, source_target_pairs={{0,4},{4,0},{8,12},{12,8},{16,20},{20,16},{24,28},{28,24},{1,5},{5... | collective-permute-start | bytes 393224 | tf_op jit(solution)/shard_map/ppermute | solution.py:22
  94.8 7.3 %collective-permute-start.15 = (f32[256,128]{1,0:T(8,128)S(1)}, f32[256,128]{1,0:T(8,128)S(1)}, u32[]{:S(2)}, u32[]{:S(2)}) collective-permute-start(f32[256,128]{1,0:T(8,128)S(1)} %add.944), channel_id=1, source_target_pairs={{0,16},{4,20},{8,24},{12,28},{16,0},{20,4},{24,8},{28,12},{1,17},{... | collective-permute-start | bytes 393224 | tf_op jit(solution)/shard_map/ppermute | solution.py:22
  102.1 5.0 %collective-permute-start.16 = (f32[256,128]{1,0:T(8,128)S(1)}, f32[256,128]{1,0:T(8,128)S(1)}, u32[]{:S(2)}, u32[]{:S(2)}) collective-permute-start(f32[256,128]{1,0:T(8,128)S(1)} %multiply_subtract_fusion), channel_id=1, source_target_pairs={{0,2},{1,3},{2,0},{3,1},{4,6},{5,7},{6,4},{7,5},{8,10},{9,11},{10,... | collective-permute-start | bytes 393224 | tf_op jit(solution)/shard_map/ppermute | solution.py:67
  107.2 1.6 %collective-permute-start.17 = (f32[2,256,128]{2,1,0:T(8,128)S(1)}, f32[2,256,128]{2,1,0:T(8,128)S(1)}, u32[]{:S(2)}, u32[]{:S(2)}) collective-permute-start(f32[2,256,128]{2,1,0:T(8,128)S(1)} %maximum_select_fusion.4), channel_id=1, source_target_pairs={{0,1},{1,0},{2,3},{3,2},{4,5},{5,4},{6,7},{7,6},{8,9},{9,8},{10,11... | collective-permute-start | bytes 786440 | tf_op jit(solution)/shard_map/ppermute | solution.py:67
  110.2 2.9 %copy-start.1 = (bf16[64,2,128,128]{3,2,1,0:T(8,128)(2,1)S(1)}, bf16[64,2,128,128]{3,2,1,0:T(8,128)(2,1)}, u32[]{:S(2)}) copy-start(bf16[64,2,128,128]{3,2,1,0:T(8,128)(2,1)} %param.7) | copy-start | bytes 12582916
  112.9 1.2 collective-permute-start.18
  113.7 1.2 collective-permute-start.20
  114.1 3.8 %collective-permute-start.19 = (f32[32,128]{1,0:T(8,128)S(1)}, f32[32,128]{1,0:T(8,128)S(1)}, u32[]{:S(2)}, u32[]{:S(2)}) collective-permute-start(f32[32,128]{1,0:T(8,128)S(1)} %add.946), channel_id=1, source_target_pairs={{0,2},{1,3},{2,0},{3,1},{4,6},{5,7},{6,4},{7,5},{8,10},{9,11},{10,... | collective-permute-start | bytes 49160 | tf_op jit(solution)/shard_map/ppermute | solution.py:22
  115.0 3.7 %collective-permute-start.21 = (f32[32,128]{1,0:T(8,128)S(1)}, f32[32,128]{1,0:T(8,128)S(1)}, u32[]{:S(2)}, u32[]{:S(2)}) collective-permute-start(f32[32,128]{1,0:T(8,128)S(1)} %add.948), channel_id=1, source_target_pairs={{0,2},{1,3},{2,0},{3,1},{4,6},{5,7},{6,4},{7,5},{8,10},{9,11},{10,... | collective-permute-start | bytes 49160 | tf_op jit(solution)/shard_map/ppermute | solution.py:22
  119.5 9.6 %all-to-all-start.2 = ((f32[32,1,128]{2,1,0:T(1,128)}), f32[32,1,128]{2,1,0:T(1,128)S(1)}, u32[]{:S(2)}, u32[]{:S(2)}) async-start(f32[32,1,128]{2,1,0:T(1,128)} %bitcast.75), calls=%async_computation.2 | async-start | bytes 32768 | tf_op jit(solution)/shard_map/all_to_all | solution.py:32
